TPU v7x, 32 devices: a whole 2x2x4 slice. The times are simulated.
32 devices in a mesh: groups: 2 (over y), clus: 4 (over z), pair: 2 (over x), rhs: 2 (over core).
Axes of the slice: x: 2, y: 2, z: 4, core: 2. Of those that a mesh axis runs over, the one named last changes fastest.
Arguments:
- rhs_field: float32 [16, 16384], P('rhs', ('groups', 'clus')), parts along dimension 1, may hold values from -6 to 6
- coefficients: float32 [4], replicated, may hold values from -1 to 1
- near_blocks: bfloat16 [256, 256, 256], P(('groups', 'clus', 'pair')), parts along dimension 0, may hold values from -0.125 to 0.125
- near_tgt: int32 [256], P(('groups', 'clus', 'pair')), parts along dimension 0, may hold values from 0 to 31, as said below
- near_src: int32 [256], P(('groups', 'clus', 'pair')), parts along dimension 0, may hold values from 0 to 31, as said below
- row_basis: bfloat16 [64, 16, 256], P(('groups', 'clus')), parts along dimension 0, may hold values from -0.25 to 0.25
- col_basis: bfloat16 [1024, 16, 256], P(('groups', 'clus', 'pair')), parts along dimension 0, may hold values from -0.375 to 0.375
- far_src: int32 [1024], P(('groups', 'clus', 'pair')), parts along dimension 0, may hold values from 0 to 31, as said below
- far_tgt: int32 [1024], P(('groups', 'clus', 'pair')), parts along dimension 0, may hold values from 0 to 31, as said below
Outputs:
- preconditioned: float32 [16, 16384], P('rhs', ('groups', 'clus')), parts along dimension 1
There are 2 independent parts, one for each index of `groups`. A program takes and returns all parts, laid end to end along the dimension named above; an argument that names none is the same for every part. Nothing has to cross between parts.
Inputs may be any that keep to these rules, and one draw needn't show every extreme that they name: `near_tgt`: the rows are in aligned blocks of 16, one a device in the order of clus then pair; the block of clus index c names clusters c * 8 to (c + 1) * 8 - 1. `near_src`: in each aligned block of 16 rows (one a device, clus then pair, clus index c), exactly 2 rows name clusters of clus index c - 1 and exactly 2 name clusters of clus index c + 1 (both taken modulo the number of clus indices; cluster // 8 is a cluster's clus index), and all others name clusters of clus index c. `far_src`: the rows are in aligned blocks of 64, one a device in the order of clus then pair; the block of clus index c names clusters c * 8 to (c + 1) * 8 - 1. `far_tgt`: never equal to far_src of the same row.
All inputs are finite; a program needn't handle non-finite values.
Results may differ from a plain program's by a relative error of at most 0.0047.
Values may be sent and summed in bfloat16 or wider, within the bound.
No kernel may reach another device: no remote copies, remote signals or barrier semaphores. Data moves between devices by JAX's collectives and lax.ppermute only.
A program may use at most 64 MiB of HBM per device.

v0:
```python
import jax
import jax.numpy as jnp
from jax import lax
from jax.sharding import PartitionSpec as P


def shards(
    rhs_field, coefficients, near_blocks, near_tgt, near_src, row_basis, col_basis, far_src, far_tgt
):
    rhs_here = rhs_field.shape[0]
    clusters_here = row_basis.shape[0]
    rank_size = row_basis.shape[1]
    leaf_size = row_basis.shape[2]
    peer_count = lax.axis_size("clus")
    cluster_count = clusters_here * peer_count
    degree_top = coefficients.shape[0] - 1
    my_index = lax.axis_index("clus")
    my_base = my_index * clusters_here
    source = rhs_field.reshape(rhs_here, clusters_here, leaf_size)
    target_local = near_tgt - my_base
    target_hot = (target_local[:, None] == jnp.arange(clusters_here)[None, :]).astype(jnp.float32)
    far_local = far_src - my_base
    far_hot = (far_tgt[:, None] == jnp.arange(cluster_count)[None, :]).astype(jnp.float32)
    iterate = (coefficients[degree_top] * source).astype(jnp.bfloat16)
    result = source
    for step in range(degree_top):
        degree = degree_top - 1 - step
        every_cluster = lax.all_gather(iterate, "clus", axis=1, tiled=True)
        gathered = every_cluster[:, near_src, :]
        contrib = jnp.einsum(
            "rjs,jts->rjt", gathered, near_blocks, preferred_element_type=jnp.float32
        )
        near_part = jnp.einsum("rjt,jc->rct", contrib, target_hot, precision=lax.Precision.HIGHEST)
        far_input = iterate[:, far_local, :]
        coef = jnp.einsum("rjl,jkl->jrk", far_input, col_basis, preferred_element_type=jnp.float32)
        coef = coef.reshape(coef.shape[0], rhs_here * rank_size)
        partial_value = jnp.einsum("jc,jm->cm", far_hot, coef, precision=lax.Precision.HIGHEST)
        group_coef = lax.psum_scatter(partial_value, "clus", scatter_dimension=0, tiled=True)
        coef_sum, near_sum = lax.psum((group_coef, near_part), "pair")
        coef_sum = coef_sum.reshape(clusters_here, rhs_here, rank_size)
        far_field = jnp.einsum(
            "crk,ckl->rcl", coef_sum, row_basis.astype(jnp.float32), precision=lax.Precision.HIGHEST
        )
        result = near_sum + far_field + coefficients[degree] * source
        iterate = result.astype(jnp.bfloat16)
    return result.reshape(rhs_here, clusters_here * leaf_size)


def solution(mesh):
    return jax.shard_map(
        shards,
        mesh=mesh,
        in_specs=(
            P("rhs", ("groups", "clus")),
            P(),
            P(("groups", "clus", "pair"), None, None),
            P(("groups", "clus", "pair")),
            P(("groups", "clus", "pair")),
            P(("groups", "clus"), None, None),
            P(("groups", "clus", "pair"), None, None),
            P(("groups", "clus", "pair")),
            P(("groups", "clus", "pair")),
        ),
        out_specs=P("rhs", ("groups", "clus")),
        check_vma=False,
    )
```

profile of v0, /device:TPU:0, one launch (start us, length us, event | category | flops | bytes accessed | tf_op | source)
XLA Modules:
  0.0 191.1 jit_solution(16882531839466192800)
XLA Ops:
  6.6 1.5 fusion.32
  8.1 3.4 %multiply_convert_fusion = (bf16[8,2048]{1,0:T(8,128)(2,1)S(1)}, f32[8,2048]{1,0:T(8,128)S(1)}, f32[8,2048]{1,0:T(8,128)S(1)}, f32[8,2048]{1,0:T(8,128)S(1)}) fusion(f32[8,2048]{1,0:T(8,128)} %param.9, f32[]{:T(128)} %bitcast.1, f32[]{:T(128)} %bitcast.9, f32[]{:T(128)} %bitcast.23, f32[]{:T(128)} %bitcast.16), kind=kLoop, calls=%fused_computation.33 | loop fusion | flops 81920 | bytes 294928 | tf_op jit(solution)/shard_map/convert_element_type | solution.py:24
  11.5 15.1 %all_gather.9 = bf16[8,32,256]{2,0,1:T(8,128)(2,1)S(1)} all-gather(bf16[8,8,256]{2,0,1:T(8,128)(2,1)S(1)} %bitcast.89), channel_id=1, replica_groups=mesh['groups'=2,'clus'=4,'pair'=2,'rhs'=2] {'clus'}, dimensions={1}, use_global_device_ids=true | all-gather | bytes 163840 | tf_op jit(solution)/shard_map/all_gather | solution.py:28
  26.6 0.7 compare_select_fusion.1
  27.2 0.6 gather_fusion
  27.8 0.7 convolution_bitcast_fusion.2
  28.5 0.8 convolution_bitcast_fusion.5
  29.4 0.6 gather_fusion.1
  30.4 0.3 fusion.20
  30.7 19.1 %all-reduce = f32[32,128]{1,0:T(8,128)S(1)} all-reduce(f32[32,128]{1,0:T(8,128)S(1)} %fusion.20), channel_id=2, replica_groups=mesh['groups'=2,'clus'=4,'pair'=2,'rhs'=2] {'clus'}, use_global_device_ids=true, to_apply=%region_1.0.clone | all-reduce | flops 4096 | bytes 32768
  49.8 0.6 dynamic-slice
  51.1 8.3 %psum.43 = f32[8,8,16]{2,1,0:T(8,128)S(1)} all-reduce(f32[8,8,16]{2,1,0:T(8,128)S(1)} %reshape.34), channel_id=1, replica_groups=mesh['groups'=2,'clus'=4,'pair'=2,'rhs'=2] {'pair'}, use_global_device_ids=true, to_apply=%region_2.0 | all-reduce | flops 1024 | bytes 8192 | tf_op jit(solution)/shard_map/psum | solution.py:39
  59.7 0.9 fusion.11
  60.6 13.4 %all_gather.10 = bf16[8,32,256]{2,1,0:T(8,128)(2,1)S(1)} all-gather(bf16[8,8,256]{2,1,0:T(8,128)(2,1)S(1)} %fusion.11), channel_id=1, replica_groups=mesh['groups'=2,'clus'=4,'pair'=2,'rhs'=2] {'clus'}, dimensions={1}, use_global_device_ids=true | all-gather | bytes 163840 | tf_op jit(solution)/shard_map/all_gather | solution.py:28
  74.0 0.6 gather_fusion.3
  75.2 15.6 %all-reduce.1 = f32[32,128]{1,0:T(8,128)S(1)} all-reduce(f32[32,128]{1,0:T(8,128)S(1)} %fusion.18), channel_id=3, replica_groups=mesh['groups'=2,'clus'=4,'pair'=2,'rhs'=2] {'clus'}, use_global_device_ids=true, to_apply=%region_4.0.clone | all-reduce | flops 4096 | bytes 32768
  90.9 7.4 %psum.45 = f32[8,8,16]{2,1,0:T(8,128)S(1)} all-reduce(f32[8,8,16]{2,1,0:T(8,128)S(1)} %reshape.36), channel_id=1, replica_groups=mesh['groups'=2,'clus'=4,'pair'=2,'rhs'=2] {'pair'}, use_global_device_ids=true, to_apply=%region_5.0 | all-reduce | flops 1024 | bytes 8192 | tf_op jit(solution)/shard_map/psum | solution.py:39
  98.4 0.6 gather_fusion.2
  98.9 0.6 convolution_bitcast_fusion.1
  99.6 0.8 convolution_bitcast_fusion.4
  100.7 19.3 %all-reduce.9.cloned.1.call-done = f32[8,8,256]{2,1,0:T(8,128)} async-done(((f32[8,8,256]{2,1,0:T(8,128)}), f32[8,8,256]{2,1,0:T(8,128)}) %all-reduce.9.cloned.1.call-update) | async-done | bytes 65552 | tf_op jit(solution)/shard_map/psum | solution.py:39
  119.9 0.9 fusion.10
  120.8 13.4 %all_gather.11 = bf16[8,32,256]{2,1,0:T(8,128)(2,1)S(1)} all-gather(bf16[8,8,256]{2,1,0:T(8,128)(2,1)S(1)} %fusion.10), channel_id=1, replica_groups=mesh['groups'=2,'clus'=4,'pair'=2,'rhs'=2] {'clus'}, dimensions={1}, use_global_device_ids=true | all-gather | bytes 163840 | tf_op jit(solution)/shard_map/all_gather | solution.py:28
  134.2 0.6 gather_fusion.5
  135.5 18.8 %all-reduce.2 = f32[32,128]{1,0:T(8,128)S(1)} all-reduce(f32[32,128]{1,0:T(8,128)S(1)} %fusion.16), channel_id=4, replica_groups=mesh['groups'=2,'clus'=4,'pair'=2,'rhs'=2] {'clus'}, use_global_device_ids=true, to_apply=%region_7.0.clone | all-reduce | flops 4096 | bytes 32768
  154.3 7.4 %psum.47 = f32[8,8,16]{2,1,0:T(8,128)S(1)} all-reduce(f32[8,8,16]{2,1,0:T(8,128)S(1)} %reshape.38), channel_id=1, replica_groups=mesh['groups'=2,'clus'=4,'pair'=2,'rhs'=2] {'pair'}, use_global_device_ids=true, to_apply=%region_8.0 | all-reduce | flops 1024 | bytes 8192 | tf_op jit(solution)/shard_map/psum | solution.py:39
  161.9 0.6 gather_fusion.4
  162.4 0.6 convolution_bitcast_fusion
  163.1 0.8 convolution_bitcast_fusion.3
  164.1 18.9 %all-reduce.11.cloned.1.call-done = f32[8,8,256]{2,1,0:T(8,128)} async-done(((f32[8,8,256]{2,1,0:T(8,128)}), f32[8,8,256]{2,1,0:T(8,128)}) %all-reduce.11.cloned.1.call-update) | async-done | bytes 65552 | tf_op jit(solution)/shard_map/psum | solution.py:39
  183.0 0.9 fusion.9
  183.9 0.7 copy.41
  (46 shorter events, 2.7 us)
Async XLA Ops:
  6.5 21.3 %copy-start = (bf16[16,256,256]{2,1,0:T(8,128)(2,1)S(1)}, bf16[16,256,256]{2,1,0:T(8,128)(2,1)}, u32[]{:S(2)}) copy-start(bf16[16,256,256]{2,1,0:T(8,128)(2,1)} %param.11) | copy-start | bytes 6291460
  6.5 22.0 %copy-start.4 = (s32[16]{0:T(128)S(1)}, s32[16]{0:T(128)}, u32[]{:S(2)}) copy-start(s32[16]{0:T(128)} %param.12) | copy-start | bytes 196
  6.5 22.9 %copy-start.5 = (s32[64]{0:T(128)S(1)}, s32[64]{0:T(128)}, u32[]{:S(2)}) copy-start(s32[64]{0:T(128)} %param.16) | copy-start | bytes 772
  6.5 23.5 %copy-start.1 = (bf16[64,16,256]{2,1,0:T(8,128)(2,1)S(1)}, bf16[64,16,256]{2,1,0:T(8,128)(2,1)}, u32[]{:S(2)}) copy-start(bf16[64,16,256]{2,1,0:T(8,128)(2,1)} %param.15) | copy-start | bytes 1572868
  6.5 53.1 %all-reduce.7.cloned.1.call-start = ((), (), s32[]{:S(2)}) async-start(), calls=%async_computation | async-start | bytes 131072 | tf_op jit(solution)/shard_map/psum | solution.py:39
  27.8 2.6 %copy-start.3 = (s32[64]{0:T(128)S(1)}, s32[64]{0:T(128)}, u32[]{:S(2)}) copy-start(s32[64]{0:T(128)} %param.17) | copy-start | bytes 772
  27.8 22.0 %copy-start.6 = (u32[32]{0:T(128)S(1)}, u32[32]{0:T(128)}, u32[]{:S(2)}) copy-start(u32[32]{0:T(128)} %constant.15) | copy-start | bytes 388
  27.8 31.7 %copy-start.2 = (bf16[8,16,256]{2,1,0:T(8,128)(2,1)S(1)}, bf16[8,16,256]{2,1,0:T(8,128)(2,1)}, u32[]{:S(2)}) copy-start(bf16[8,16,256]{2,1,0:T(8,128)(2,1)} %param.14) | copy-start | bytes 196612
  29.4 90.6 %all-reduce.9.cloned.1.call-start = ((), (), s32[]{:S(2)}) async-start(), calls=%async_computation.1 | async-start | bytes 131072 | tf_op jit(solution)/shard_map/psum | solution.py:39
  100.4 82.6 %all-reduce.11.cloned.1.call-start = ((), (), s32[]{:S(2)}) async-start(), calls=%async_computation.2 | async-start | bytes 131072 | tf_op jit(solution)/shard_map/psum | solution.py:39
Sparse Core Ops, SparseCore 0:
  29.5 22.1 all-reduce.6
  100.6 19.3 all-reduce.8
  164.1 18.8 all-reduce.10
where the time goes:
time: 192 us; the launch traced here: 191 us
  blocking collectives  119 us (62%)
  waiting for transfers between devices  38.2 us (20%)
  between operations  14 us (7%)
  local copies, waits for them, and re-layouts  7.12 us (4%)
  other arithmetic  6.71 us (3%)
  matrix products  6.37 us (3%)
    unnamed x3, blocking collectives  53.5 us
    all_gather x3, blocking collectives, shards(): every_cluster = lax.all_gather(iterate, 'clus', axis=1, tiled=True)  41.9 us
    psum x3, waiting for transfers between devices, shards(): coef_sum, near_sum = lax.psum((group_coef, near_part), 'pair')  38.2 us
    psum x3, blocking collectives, shards(): coef_sum, near_sum = lax.psum((group_coef, near_part), 'pair')  23.1 us
  transfers between devices with their start and end apart: 3, of which 2 were waited for; matrix products, arithmetic and copies ran while one was open for 1% of the time, Pallas kernels for 0%

commit v1 on v0

v1 whole, which is shorter than its diff:
```python
import jax
import jax.numpy as jnp
from jax import lax
from jax.sharding import PartitionSpec as P


def shift(value, axis, count, step):
    return lax.ppermute(value, axis, [(i, (i + step) % count) for i in range(count)])


def pair_total(value, pair_count, pair_index):
    if pair_count == 1:
        return value
    if pair_count == 2:
        return value + shift(value, "pair", 2, 1)
    received = [value] + [shift(value, "pair", pair_count, s) for s in range(1, pair_count)]
    stacked = jnp.stack(received)
    order = (pair_index - jnp.arange(pair_count)) % pair_count
    canonical = stacked[order]
    total = canonical[0]
    for q in range(1, pair_count):
        total = total + canonical[q]
    return total


def shards(
    rhs_field, coefficients, near_blocks, near_tgt, near_src, row_basis, col_basis, far_src, far_tgt
):
    rhs_here = rhs_field.shape[0]
    clusters_here = row_basis.shape[0]
    rank_size = row_basis.shape[1]
    leaf_size = row_basis.shape[2]
    peer_count = lax.axis_size("clus")
    pair_count = lax.axis_size("pair")
    cluster_count = clusters_here * peer_count
    degree_top = coefficients.shape[0] - 1
    my_index = lax.axis_index("clus")
    pair_index = lax.axis_index("pair")
    my_base = my_index * clusters_here
    source = rhs_field.reshape(rhs_here, clusters_here, leaf_size)

    target_local = near_tgt - my_base
    target_hot = (target_local[:, None] == jnp.arange(clusters_here)[None, :]).astype(jnp.float32)
    relative = (near_src // clusters_here - my_index) % peer_count
    slot = jnp.where(relative == 0, 0, jnp.where(relative == 1, 1, 2))
    near_index = slot * clusters_here + near_src % clusters_here

    far_local = far_src - my_base
    far_hot = (far_tgt[:, None] == jnp.arange(cluster_count)[None, :]).astype(jnp.float32)
    row_f32 = row_basis.astype(jnp.float32)

    iterate = (coefficients[degree_top] * source).astype(jnp.bfloat16)
    result = source
    for step in range(degree_top):
        degree = degree_top - 1 - step
        with jax.named_scope("neighbour_iterates"):
            if peer_count > 1:
                from_minus = shift(iterate, "clus", peer_count, 1)
                from_plus = shift(iterate, "clus", peer_count, peer_count - 1)
            else:
                from_minus = iterate
                from_plus = iterate
        with jax.named_scope("far_partial"):
            far_input = iterate[:, far_local, :]
            coef = jnp.einsum(
                "rjl,jkl->jrk", far_input, col_basis, preferred_element_type=jnp.float32
            )
            coef = coef.reshape(coef.shape[0], rhs_here * rank_size)
            partial_value = jnp.einsum("jc,jm->cm", far_hot, coef, precision=lax.Precision.HIGHEST)
            partial_value = partial_value.reshape(peer_count, clusters_here, rhs_here * rank_size)
        with jax.named_scope("far_slices"):
            far_mine = partial_value[my_index]
            for s in range(1, peer_count):
                outgoing = partial_value[(my_index + s) % peer_count]
                far_mine = far_mine + shift(outgoing, "clus", peer_count, s)
        with jax.named_scope("near_partial"):
            extended = jnp.concatenate([iterate, from_plus, from_minus], axis=1)
            gathered = extended[:, near_index, :]
            contrib = jnp.einsum(
                "rjs,jts->rjt", gathered, near_blocks, preferred_element_type=jnp.float32
            )
            near_part = jnp.einsum(
                "rjt,jc->rct", contrib, target_hot, precision=lax.Precision.HIGHEST
            )
        with jax.named_scope("pair_sums"):
            near_flat = near_part.reshape(rhs_here, clusters_here * leaf_size)
            far_flat = far_mine.reshape(clusters_here, rhs_here, rank_size)
            far_flat = far_flat.transpose(1, 0, 2).reshape(rhs_here, clusters_here * rank_size)
            packed = jnp.concatenate([near_flat, far_flat], axis=1)
            packed = pair_total(packed, pair_count, pair_index)
            near_sum = packed[:, : clusters_here * leaf_size].reshape(
                rhs_here, clusters_here, leaf_size
            )
            coef_sum = packed[:, clusters_here * leaf_size :].reshape(
                rhs_here, clusters_here, rank_size
            )
        with jax.named_scope("far_field"):
            far_field = jnp.einsum(
                "rck,ckl->rcl", coef_sum, row_f32, precision=lax.Precision.HIGHEST
            )
        result = near_sum + far_field + coefficients[degree] * source
        iterate = result.astype(jnp.bfloat16)
    return result.reshape(rhs_here, clusters_here * leaf_size)


def solution(mesh):
    return jax.shard_map(
        shards,
        mesh=mesh,
        in_specs=(
            P("rhs", ("groups", "clus")),
            P(),
            P(("groups", "clus", "pair"), None, None),
            P(("groups", "clus", "pair")),
            P(("groups", "clus", "pair")),
            P(("groups", "clus"), None, None),
            P(("groups", "clus", "pair"), None, None),
            P(("groups", "clus", "pair")),
            P(("groups", "clus", "pair")),
        ),
        out_specs=P("rhs", ("groups", "clus")),
        check_vma=False,
    )
```

time: 192 us -> 64.8 us (0.34)
  blocking collectives: 119 us -> 0 us
  starting transfers between devices: 0.12 us -> 26.4 us
  waiting for transfers between devices: 38.2 us -> 21.1 us
  between operations: 14 us -> 0.46 us
    unnamed x3 -> x0, blocking collectives: 53.5 us -> none
    all_gather x3 -> x0, blocking collectives: 41.9 us -> none  [shards(): every_cluster = lax.all_gather(iterate, 'clus', axis=1, tiled=True)]
    psum x3 -> x0, waiting for transfers between devices: 38.2 us -> none  [shards(): coef_sum, near_sum = lax.psum((group_coef, near_part), 'pair')]
    ppermute x0 -> x18, starting transfers between devices: none -> 26.4 us  [shift(): lax.ppermute(value, axis, [(i, (i + step) % count) for i in range(count)])]
    psum x3 -> x0, blocking collectives: 23.1 us -> none  [shards(): coef_sum, near_sum = lax.psum((group_coef, near_part), 'pair')]
    ppermute x0 -> x18, waiting for transfers between devices: none -> 21.1 us  [shift(): lax.ppermute(value, axis, [(i, (i + step) % count) for i in range(count)])]
  transfers between devices with their start and end apart: 3 -> 18, of which waited for: 2 -> 12; matrix products, arithmetic and copies ran while one was open for 1% -> 5% of each run, Pallas kernels for 0% -> 0%
where the time goes in v1:
time: 64.8 us; the launch traced here: 64.5 us
  starting transfers between devices  26.4 us (41%)
  waiting for transfers between devices  21.1 us (33%)
  local copies, waits for them, and re-layouts  6.34 us (10%)
  matrix products  5.31 us (8%)
  other arithmetic  4.9 us (8%)
    ppermute x18, starting transfers between devices, shift(): lax.ppermute(value, axis, [(i, (i + step) % count) for i in range(count)])  26.4 us
    ppermute x18, waiting for transfers between devices, shift(): lax.ppermute(value, axis, [(i, (i + step) % count) for i in range(count)])  21.1 us
    convert_element_type x1, other arithmetic, shards(): iterate = (coefficients[degree_top] * source).astype(jnp.bfloat16)  3.43 us
    dot_general x3, matrix products, shards(): jnp.einsum('rjs,jts->rjt', gathered, near_blocks, preferred_element_type=...  1.91 us
    gather x3, local copies, waits for them, and re-layouts, shards(): far_input = iterate[:, far_local, :]  1.79 us
    dot_general x3, matrix products, shards(): jnp.einsum('rjl,jkl->jrk', far_input, col_basis, preferred_element_type=j...  1.72 us
    gather x3, local copies, waits for them, and re-layouts, shards(): gathered = extended[:, near_index, :]  1.67 us
    slice x1, local copies, waits for them, and re-layouts, shards(): iterate = (coefficients[degree_top] * source).astype(jnp.bfloat16)  1.52 us
  transfers between devices with their start and end apart: 18, of which 12 were waited for; matrix products, arithmetic and copies ran while one was open for 5% of the time, Pallas kernels for 0%

profile of v1, /device:TPU:0, one launch (start us, length us, event | category | flops | bytes accessed | tf_op | source)
XLA Modules:
  0.0 64.5 jit_solution(3337499495705589240)
XLA Ops:
  0.0 1.5 %fusion.43 = (f32[1]{0:T(128)}, f32[1]{0:T(128)}, f32[1]{0:T(128)}, f32[1]{0:T(128)}) fusion(f32[4]{0:T(128)} %param.10), kind=kLoop, calls=%fused_computation.100 | loop fusion | bytes 32 | tf_op jit(solution)/shard_map/slice | solution.py:52
  1.5 3.4 %multiply_convert_fusion = (bf16[8,2048]{1,0:T(8,128)(2,1)S(1)}, f32[8,2048]{1,0:T(8,128)S(1)}, f32[8,2048]{1,0:T(8,128)S(1)}, f32[8,2048]{1,0:T(8,128)S(1)}) fusion(f32[8,2048]{1,0:T(8,128)} %param.9, f32[]{:T(128)} %bitcast.1, f32[]{:T(128)} %bitcast.16, f32[]{:T(128)} %bitcast.46, f32[]{:T(128)} %bitcast.31), kind=kLoop, calls=%fused_computation.33 | loop fusion | flops 81920 | bytes 294928 | tf_op jit(solution)/shard_map/convert_element_type | solution.py:52
  5.0 5.1 %collective-permute-start = (bf16[8,8,256]{2,0,1:T(8,128)(2,1)S(1)}, bf16[8,8,256]{2,0,1:T(8,128)(2,1)S(1)}, u32[]{:S(2)}, u32[]{:S(2)}) collective-permute-start(bf16[8,8,256]{2,0,1:T(8,128)(2,1)S(1)} %bitcast.119), channel_id=1, source_target_pairs={{0,12},{4,0},{8,4},{12,8},{1,13},{5,1},{9,5},{13,9},{2,14},{6,2},{... | collective-permute-start | bytes 98312 | tf_op jit(solution)/shard_map/neighbour_iterates/ppermute | solution.py:8
  10.1 0.7 %compare_select_fusion = s32[64]{0:T(128)S(1)} fusion(s32[64]{0:T(128)} %param.16, s32[]{:T(128)S(6)} %mul.40), kind=kLoop, calls=%fused_computation.80 | loop fusion | flops 256 | bytes 516 | tf_op jit(solution)/shard_map/far_partial/select_n | solution.py:64
  10.7 0.6 gather_fusion.1
  11.3 1.3 %fusion.4 = f32[64,8,16]{2,1,0:T(8,128)S(1)} fusion(bf16[64,16,256]{2,1,0:T(8,128)(2,1)} %param.15, bf16[64,8,256]{2,1,0:T(8,128)(2,1)S(1)} %gather_fusion.1), kind=kOutput, calls=%fused_computation.19 | convolution fusion | flops 4194304 | bytes 819200 | tf_op jit(solution)/shard_map/far_partial/rjl,jkl->jrk/dot_general | solution.py:65
  13.1 4.4 %collective-permute-start.3 = (f32[8,128]{1,0:T(8,128)S(1)}, f32[8,128]{1,0:T(8,128)S(1)}, u32[]{:S(2)}, u32[]{:S(2)}) collective-permute-start(f32[8,128]{1,0:T(8,128)S(1)} %get-tuple-element.17), channel_id=1, source_target_pairs={{0,8},{4,12},{8,0},{12,4},{1,9},{5,13},{9,1},{13,5},{2,10},{6,14},... | collective-permute-start | bytes 12296 | tf_op jit(solution)/shard_map/far_slices/ppermute | solution.py:8
  17.5 1.0 %collective-permute-done.2 = f32[8,128]{1,0:T(8,128)S(1)} collective-permute-done((f32[8,128]{1,0:T(8,128)S(1)}, f32[8,128]{1,0:T(8,128)S(1)}, u32[]{:S(2)}, u32[]{:S(2)}) %collective-permute-start.2) | collective-permute-done | bytes 4128 | tf_op jit(solution)/shard_map/far_slices/ppermute | solution.py:8
  19.0 2.0 %collective-permute-done.4 = f32[8,128]{1,0:T(8,128)S(1)} collective-permute-done((f32[8,128]{1,0:T(8,128)S(1)}, f32[8,128]{1,0:T(8,128)S(1)}, u32[]{:S(2)}, u32[]{:S(2)}) %collective-permute-start.4) | collective-permute-done | bytes 4128 | tf_op jit(solution)/shard_map/far_slices/ppermute | solution.py:8
  21.9 0.6 convolution_bitcast_fusion.2
  22.8 1.6 %collective-permute-start.5 = (f32[8,2176]{1,0:T(8,128)S(1)}, f32[8,2176]{1,0:T(8,128)S(1)}, u32[]{:S(2)}, u32[]{:S(2)}) collective-permute-start(f32[8,2176]{1,0:T(8,128)S(1)} %constant_dynamic-update-slice_fusion), channel_id=1, source_target_pairs={{0,2},{2,0},{1,3},{3,1},{4,6},{6,4},{5,7},{7,5},{8,10},{10,8},{9,1... | collective-permute-start | bytes 208904 | tf_op jit(solution)/shard_map/pair_sums/ppermute | solution.py:8
  24.3 2.8 %collective-permute-done.5 = f32[8,2176]{1,0:T(8,128)S(1)} collective-permute-done((f32[8,2176]{1,0:T(8,128)S(1)}, f32[8,2176]{1,0:T(8,128)S(1)}, u32[]{:S(2)}, u32[]{:S(2)}) %collective-permute-start.5) | collective-permute-done | bytes 69664 | tf_op jit(solution)/shard_map/pair_sums/ppermute | solution.py:8
  27.4 0.6 gather_fusion.3
  28.7 1.9 %collective-permute-start.10 = (f32[8,128]{1,0:T(8,128)S(1)}, f32[8,128]{1,0:T(8,128)S(1)}, u32[]{:S(2)}, u32[]{:S(2)}) collective-permute-start(f32[8,128]{1,0:T(8,128)S(1)} %get-tuple-element.13), channel_id=1, source_target_pairs={{0,12},{4,0},{8,4},{12,8},{1,13},{5,1},{9,5},{13,9},{2,14},{6,2},{... | collective-permute-start | bytes 12296 | tf_op jit(solution)/shard_map/far_slices/ppermute | solution.py:8
  30.8 0.9 %collective-permute-start.9 = (f32[8,128]{1,0:T(8,128)S(1)}, f32[8,128]{1,0:T(8,128)S(1)}, u32[]{:S(2)}, u32[]{:S(2)}) collective-permute-start(f32[8,128]{1,0:T(8,128)S(1)} %get-tuple-element.14), channel_id=1, source_target_pairs={{0,8},{4,12},{8,0},{12,4},{1,9},{5,13},{9,1},{13,5},{2,10},{6,14},... | collective-permute-start | bytes 12296 | tf_op jit(solution)/shard_map/far_slices/ppermute | solution.py:8
  31.7 2.7 %collective-permute-start.6 = (bf16[8,8,256]{2,0,1:T(8,128)(2,1)S(1)}, bf16[8,8,256]{2,0,1:T(8,128)(2,1)S(1)}, u32[]{:S(2)}, u32[]{:S(2)}) collective-permute-start(bf16[8,8,256]{2,0,1:T(8,128)(2,1)S(1)} %add_convert_fusion.1), channel_id=1, source_target_pairs={{0,12},{4,0},{8,4},{12,8},{1,13},{5,1},{9,5},{13,9},{2,14},{6,2},{... | collective-permute-start | bytes 98312 | tf_op jit(solution)/shard_map/neighbour_iterates/ppermute | solution.py:8
  35.0 1.0 %collective-permute-done.8 = f32[8,128]{1,0:T(8,128)S(1)} collective-permute-done((f32[8,128]{1,0:T(8,128)S(1)}, f32[8,128]{1,0:T(8,128)S(1)}, u32[]{:S(2)}, u32[]{:S(2)}) %collective-permute-start.8) | collective-permute-done | bytes 4128 | tf_op jit(solution)/shard_map/far_slices/ppermute | solution.py:8
  36.2 0.7 %collective-permute-done.6 = bf16[8,8,256]{2,0,1:T(8,128)(2,1)S(1)} collective-permute-done((bf16[8,8,256]{2,0,1:T(8,128)(2,1)S(1)}, bf16[8,8,256]{2,0,1:T(8,128)(2,1)S(1)}, u32[]{:S(2)}, u32[]{:S(2)}) %collective-permute-start.6) | collective-permute-done | bytes 32800 | tf_op jit(solution)/shard_map/neighbour_iterates/ppermute | solution.py:8
  36.9 3.3 %collective-permute-done.7 = bf16[8,8,256]{2,0,1:T(8,128)(2,1)S(1)} collective-permute-done((bf16[8,8,256]{2,0,1:T(8,128)(2,1)S(1)}, bf16[8,8,256]{2,0,1:T(8,128)(2,1)S(1)}, u32[]{:S(2)}, u32[]{:S(2)}) %collective-permute-start.7) | collective-permute-done | bytes 32800 | tf_op jit(solution)/shard_map/neighbour_iterates/ppermute | solution.py:8
  40.7 0.6 convolution_bitcast_fusion.1
  41.6 1.6 %collective-permute-start.11 = (f32[8,2176]{1,0:T(8,128)S(1)}, f32[8,2176]{1,0:T(8,128)S(1)}, u32[]{:S(2)}, u32[]{:S(2)}) collective-permute-start(f32[8,2176]{1,0:T(8,128)S(1)} %constant_dynamic-update-slice_fusion.2), channel_id=1, source_target_pairs={{0,2},{2,0},{1,3},{3,1},{4,6},{6,4},{5,7},{7,5},{8,10},{10,8},{9,1... | collective-permute-start | bytes 208904 | tf_op jit(solution)/shard_map/pair_sums/ppermute | solution.py:8
  43.2 2.8 %collective-permute-done.11 = f32[8,2176]{1,0:T(8,128)S(1)} collective-permute-done((f32[8,2176]{1,0:T(8,128)S(1)}, f32[8,2176]{1,0:T(8,128)S(1)}, u32[]{:S(2)}, u32[]{:S(2)}) %collective-permute-start.11) | collective-permute-done | bytes 69664 | tf_op jit(solution)/shard_map/pair_sums/ppermute | solution.py:8
  46.3 0.6 gather_fusion.5
  48.1 3.2 %collective-permute-start.16 = (f32[8,128]{1,0:T(8,128)S(1)}, f32[8,128]{1,0:T(8,128)S(1)}, u32[]{:S(2)}, u32[]{:S(2)}) collective-permute-start(f32[8,128]{1,0:T(8,128)S(1)} %get-tuple-element.10), channel_id=1, source_target_pairs={{0,12},{4,0},{8,4},{12,8},{1,13},{5,1},{9,5},{13,9},{2,14},{6,2},{... | collective-permute-start | bytes 12296 | tf_op jit(solution)/shard_map/far_slices/ppermute | solution.py:8
  51.4 0.6 collective-permute-start.12
  52.0 1.4 %collective-permute-start.13 = (bf16[8,8,256]{2,0,1:T(8,128)(2,1)S(1)}, bf16[8,8,256]{2,0,1:T(8,128)(2,1)S(1)}, u32[]{:S(2)}, u32[]{:S(2)}) collective-permute-start(bf16[8,8,256]{2,0,1:T(8,128)(2,1)S(1)} %add_convert_fusion), channel_id=1, source_target_pairs={{0,4},{4,8},{8,12},{12,0},{1,5},{5,9},{9,13},{13,1},{2,6},{6,10},{... | collective-permute-start | bytes 98312 | tf_op jit(solution)/shard_map/neighbour_iterates/ppermute | solution.py:8
  53.7 1.6 %collective-permute-done.12 = bf16[8,8,256]{2,0,1:T(8,128)(2,1)S(1)} collective-permute-done((bf16[8,8,256]{2,0,1:T(8,128)(2,1)S(1)}, bf16[8,8,256]{2,0,1:T(8,128)(2,1)S(1)}, u32[]{:S(2)}, u32[]{:S(2)}) %collective-permute-start.12) | collective-permute-done | bytes 32800 | tf_op jit(solution)/shard_map/neighbour_iterates/ppermute | solution.py:8
  55.3 2.4 %collective-permute-done.13 = bf16[8,8,256]{2,0,1:T(8,128)(2,1)S(1)} collective-permute-done((bf16[8,8,256]{2,0,1:T(8,128)(2,1)S(1)}, bf16[8,8,256]{2,0,1:T(8,128)(2,1)S(1)}, u32[]{:S(2)}, u32[]{:S(2)}) %collective-permute-start.13) | collective-permute-done | bytes 32800 | tf_op jit(solution)/shard_map/neighbour_iterates/ppermute | solution.py:8
  58.3 0.6 convolution_bitcast_fusion
  59.2 1.6 %collective-permute-start.17 = (f32[8,2176]{1,0:T(8,128)S(1)}, f32[8,2176]{1,0:T(8,128)S(1)}, u32[]{:S(2)}, u32[]{:S(2)}) collective-permute-start(f32[8,2176]{1,0:T(8,128)S(1)} %constant_dynamic-update-slice_fusion.4), channel_id=1, source_target_pairs={{0,2},{2,0},{1,3},{3,1},{4,6},{6,4},{5,7},{7,5},{8,10},{10,8},{9,1... | collective-permute-start | bytes 208904 | tf_op jit(solution)/shard_map/pair_sums/ppermute | solution.py:8
  60.8 2.8 %collective-permute-done.17 = f32[8,2176]{1,0:T(8,128)S(1)} collective-permute-done((f32[8,2176]{1,0:T(8,128)S(1)}, f32[8,2176]{1,0:T(8,128)S(1)}, u32[]{:S(2)}, u32[]{:S(2)}) %collective-permute-start.17) | collective-permute-done | bytes 69664 | tf_op jit(solution)/shard_map/pair_sums/ppermute | solution.py:8
  63.9 0.6 add_add_fusion
  (90 shorter events, 7.5 us)
Async XLA Ops:
  0.0 21.8 %copy-start = (bf16[16,256,256]{2,1,0:T(8,128)(2,1)S(1)}, bf16[16,256,256]{2,1,0:T(8,128)(2,1)}, u32[]{:S(2)}) copy-start(bf16[16,256,256]{2,1,0:T(8,128)(2,1)} %param.11) | copy-start | bytes 6291460
  0.0 12.8 %copy-start.3 = (s32[64]{0:T(128)S(1)}, s32[64]{0:T(128)}, u32[]{:S(2)}) copy-start(s32[64]{0:T(128)} %param.17) | copy-start | bytes 772
  0.0 17.5 %copy-start.4 = (s32[16]{0:T(128)S(1)}, s32[16]{0:T(128)}, u32[]{:S(2)}) copy-start(s32[16]{0:T(128)} %param.13) | copy-start | bytes 196
  0.0 17.5 %copy-start.5 = (s32[16]{0:T(128)S(1)}, s32[16]{0:T(128)}, u32[]{:S(2)}) copy-start(s32[16]{0:T(128)} %param.12) | copy-start | bytes 196
  5.0 16.3 %collective-permute-start = (bf16[8,8,256]{2,0,1:T(8,128)(2,1)S(1)}, bf16[8,8,256]{2,0,1:T(8,128)(2,1)S(1)}, u32[]{:S(2)}, u32[]{:S(2)}) collective-permute-start(bf16[8,8,256]{2,0,1:T(8,128)(2,1)S(1)} %bitcast.119), channel_id=1, source_target_pairs={{0,12},{4,0},{8,4},{12,8},{1,13},{5,1},{9,5},{13,9},{2,14},{6,2},{... | collective-permute-start | bytes 98312 | tf_op jit(solution)/shard_map/neighbour_iterates/ppermute | solution.py:8
  10.1 11.2 %collective-permute-start.1 = (bf16[8,8,256]{2,0,1:T(8,128)(2,1)S(1)}, bf16[8,8,256]{2,0,1:T(8,128)(2,1)S(1)}, u32[]{:S(2)}, u32[]{:S(2)}) collective-permute-start(bf16[8,8,256]{2,0,1:T(8,128)(2,1)S(1)} %bitcast.120), channel_id=1, source_target_pairs={{0,4},{4,8},{8,12},{12,0},{1,5},{5,9},{9,13},{13,1},{2,6},{6,10},{... | collective-permute-start | bytes 98312 | tf_op jit(solution)/shard_map/neighbour_iterates/ppermute | solution.py:8
  12.6 14.6 %copy-start.2 = (bf16[8,16,256]{2,1,0:T(8,128)(2,1)S(1)}, bf16[8,16,256]{2,1,0:T(8,128)(2,1)}, u32[]{:S(2)}) copy-start(bf16[8,16,256]{2,1,0:T(8,128)(2,1)} %param.14) | copy-start | bytes 196612
  13.0 5.5 %collective-permute-start.2 = (f32[8,128]{1,0:T(8,128)S(1)}, f32[8,128]{1,0:T(8,128)S(1)}, u32[]{:S(2)}, u32[]{:S(2)}) collective-permute-start(f32[8,128]{1,0:T(8,128)S(1)} %get-tuple-element.15), channel_id=1, source_target_pairs={{0,4},{4,8},{8,12},{12,0},{1,5},{5,9},{9,13},{13,1},{2,6},{6,10},{... | collective-permute-start | bytes 12296 | tf_op jit(solution)/shard_map/far_slices/ppermute | solution.py:8
  13.1 6.0 %collective-permute-start.3 = (f32[8,128]{1,0:T(8,128)S(1)}, f32[8,128]{1,0:T(8,128)S(1)}, u32[]{:S(2)}, u32[]{:S(2)}) collective-permute-start(f32[8,128]{1,0:T(8,128)S(1)} %get-tuple-element.17), channel_id=1, source_target_pairs={{0,8},{4,12},{8,0},{12,4},{1,9},{5,13},{9,1},{13,5},{2,10},{6,14},... | collective-permute-start | bytes 12296 | tf_op jit(solution)/shard_map/far_slices/ppermute | solution.py:8
  17.5 3.6 %collective-permute-start.4 = (f32[8,128]{1,0:T(8,128)S(1)}, f32[8,128]{1,0:T(8,128)S(1)}, u32[]{:S(2)}, u32[]{:S(2)}) collective-permute-start(f32[8,128]{1,0:T(8,128)S(1)} %get-tuple-element.16), channel_id=1, source_target_pairs={{0,12},{4,0},{8,4},{12,8},{1,13},{5,1},{9,5},{13,9},{2,14},{6,2},{... | collective-permute-start | bytes 12296 | tf_op jit(solution)/shard_map/far_slices/ppermute | solution.py:8
  21.3 6.8 %copy-start.1 = (bf16[64,16,256]{2,1,0:T(8,128)(2,1)S(1)}, bf16[64,16,256]{2,1,0:T(8,128)(2,1)}, u32[]{:S(2)}) copy-start(bf16[64,16,256]{2,1,0:T(8,128)(2,1)} %param.15) | copy-start | bytes 1572868
  22.8 4.4 %collective-permute-start.5 = (f32[8,2176]{1,0:T(8,128)S(1)}, f32[8,2176]{1,0:T(8,128)S(1)}, u32[]{:S(2)}, u32[]{:S(2)}) collective-permute-start(f32[8,2176]{1,0:T(8,128)S(1)} %constant_dynamic-update-slice_fusion), channel_id=1, source_target_pairs={{0,2},{2,0},{1,3},{3,1},{4,6},{6,4},{5,7},{7,5},{8,10},{10,8},{9,1... | collective-permute-start | bytes 208904 | tf_op jit(solution)/shard_map/pair_sums/ppermute | solution.py:8
  28.7 6.3 %collective-permute-start.10 = (f32[8,128]{1,0:T(8,128)S(1)}, f32[8,128]{1,0:T(8,128)S(1)}, u32[]{:S(2)}, u32[]{:S(2)}) collective-permute-start(f32[8,128]{1,0:T(8,128)S(1)} %get-tuple-element.13), channel_id=1, source_target_pairs={{0,12},{4,0},{8,4},{12,8},{1,13},{5,1},{9,5},{13,9},{2,14},{6,2},{... | collective-permute-start | bytes 12296 | tf_op jit(solution)/shard_map/far_slices/ppermute | solution.py:8
  30.6 5.4 %collective-permute-start.8 = (f32[8,128]{1,0:T(8,128)S(1)}, f32[8,128]{1,0:T(8,128)S(1)}, u32[]{:S(2)}, u32[]{:S(2)}) collective-permute-start(f32[8,128]{1,0:T(8,128)S(1)} %get-tuple-element.12), channel_id=1, source_target_pairs={{0,4},{4,8},{8,12},{12,0},{1,5},{5,9},{9,13},{13,1},{2,6},{6,10},{... | collective-permute-start | bytes 12296 | tf_op jit(solution)/shard_map/far_slices/ppermute | solution.py:8
  30.8 5.2 %collective-permute-start.9 = (f32[8,128]{1,0:T(8,128)S(1)}, f32[8,128]{1,0:T(8,128)S(1)}, u32[]{:S(2)}, u32[]{:S(2)}) collective-permute-start(f32[8,128]{1,0:T(8,128)S(1)} %get-tuple-element.14), channel_id=1, source_target_pairs={{0,8},{4,12},{8,0},{12,4},{1,9},{5,13},{9,1},{13,5},{2,10},{6,14},... | collective-permute-start | bytes 12296 | tf_op jit(solution)/shard_map/far_slices/ppermute | solution.py:8
  31.7 5.2 %collective-permute-start.6 = (bf16[8,8,256]{2,0,1:T(8,128)(2,1)S(1)}, bf16[8,8,256]{2,0,1:T(8,128)(2,1)S(1)}, u32[]{:S(2)}, u32[]{:S(2)}) collective-permute-start(bf16[8,8,256]{2,0,1:T(8,128)(2,1)S(1)} %add_convert_fusion.1), channel_id=1, source_target_pairs={{0,12},{4,0},{8,4},{12,8},{1,13},{5,1},{9,5},{13,9},{2,14},{6,2},{... | collective-permute-start | bytes 98312 | tf_op jit(solution)/shard_map/neighbour_iterates/ppermute | solution.py:8
  34.4 5.7 %collective-permute-start.7 = (bf16[8,8,256]{2,0,1:T(8,128)(2,1)S(1)}, bf16[8,8,256]{2,0,1:T(8,128)(2,1)S(1)}, u32[]{:S(2)}, u32[]{:S(2)}) collective-permute-start(bf16[8,8,256]{2,0,1:T(8,128)(2,1)S(1)} %add_convert_fusion.1), channel_id=1, source_target_pairs={{0,4},{4,8},{8,12},{12,0},{1,5},{5,9},{9,13},{13,1},{2,6},{6,10},{... | collective-permute-start | bytes 98312 | tf_op jit(solution)/shard_map/neighbour_iterates/ppermute | solution.py:8
  41.6 4.4 %collective-permute-start.11 = (f32[8,2176]{1,0:T(8,128)S(1)}, f32[8,2176]{1,0:T(8,128)S(1)}, u32[]{:S(2)}, u32[]{:S(2)}) collective-permute-start(f32[8,2176]{1,0:T(8,128)S(1)} %constant_dynamic-update-slice_fusion.2), channel_id=1, source_target_pairs={{0,2},{2,0},{1,3},{3,1},{4,6},{6,4},{5,7},{7,5},{8,10},{10,8},{9,1... | collective-permute-start | bytes 208904 | tf_op jit(solution)/shard_map/pair_sums/ppermute | solution.py:8
  47.5 5.9 %collective-permute-start.14 = (f32[8,128]{1,0:T(8,128)S(1)}, f32[8,128]{1,0:T(8,128)S(1)}, u32[]{:S(2)}, u32[]{:S(2)}) collective-permute-start(f32[8,128]{1,0:T(8,128)S(1)} %get-tuple-element.9), channel_id=1, source_target_pairs={{0,4},{4,8},{8,12},{12,0},{1,5},{5,9},{9,13},{13,1},{2,6},{6,10},{... | collective-permute-start | bytes 12296 | tf_op jit(solution)/shard_map/far_slices/ppermute | solution.py:8
  47.6 5.8 %collective-permute-start.15 = (f32[8,128]{1,0:T(8,128)S(1)}, f32[8,128]{1,0:T(8,128)S(1)}, u32[]{:S(2)}, u32[]{:S(2)}) collective-permute-start(f32[8,128]{1,0:T(8,128)S(1)} %get-tuple-element.11), channel_id=1, source_target_pairs={{0,8},{4,12},{8,0},{12,4},{1,9},{5,13},{9,1},{13,5},{2,10},{6,14},... | collective-permute-start | bytes 12296 | tf_op jit(solution)/shard_map/far_slices/ppermute | solution.py:8
  48.1 5.4 %collective-permute-start.16 = (f32[8,128]{1,0:T(8,128)S(1)}, f32[8,128]{1,0:T(8,128)S(1)}, u32[]{:S(2)}, u32[]{:S(2)}) collective-permute-start(f32[8,128]{1,0:T(8,128)S(1)} %get-tuple-element.10), channel_id=1, source_target_pairs={{0,12},{4,0},{8,4},{12,8},{1,13},{5,1},{9,5},{13,9},{2,14},{6,2},{... | collective-permute-start | bytes 12296 | tf_op jit(solution)/shard_map/far_slices/ppermute | solution.py:8
  51.4 3.9 %collective-permute-start.12 = (bf16[8,8,256]{2,0,1:T(8,128)(2,1)S(1)}, bf16[8,8,256]{2,0,1:T(8,128)(2,1)S(1)}, u32[]{:S(2)}, u32[]{:S(2)}) collective-permute-start(bf16[8,8,256]{2,0,1:T(8,128)(2,1)S(1)} %add_convert_fusion), channel_id=1, source_target_pairs={{0,12},{4,0},{8,4},{12,8},{1,13},{5,1},{9,5},{13,9},{2,14},{6,2},{... | collective-permute-start | bytes 98312 | tf_op jit(solution)/shard_map/neighbour_iterates/ppermute | solution.py:8
  52.0 5.7 %collective-permute-start.13 = (bf16[8,8,256]{2,0,1:T(8,128)(2,1)S(1)}, bf16[8,8,256]{2,0,1:T(8,128)(2,1)S(1)}, u32[]{:S(2)}, u32[]{:S(2)}) collective-permute-start(bf16[8,8,256]{2,0,1:T(8,128)(2,1)S(1)} %add_convert_fusion), channel_id=1, source_target_pairs={{0,4},{4,8},{8,12},{12,0},{1,5},{5,9},{9,13},{13,1},{2,6},{6,10},{... | collective-permute-start | bytes 98312 | tf_op jit(solution)/shard_map/neighbour_iterates/ppermute | solution.py:8
  59.2 4.4 %collective-permute-start.17 = (f32[8,2176]{1,0:T(8,128)S(1)}, f32[8,2176]{1,0:T(8,128)S(1)}, u32[]{:S(2)}, u32[]{:S(2)}) collective-permute-start(f32[8,2176]{1,0:T(8,128)S(1)} %constant_dynamic-update-slice_fusion.4), channel_id=1, source_target_pairs={{0,2},{2,0},{1,3},{3,1},{4,6},{6,4},{5,7},{7,5},{8,10},{10,8},{9,1... | collective-permute-start | bytes 208904 | tf_op jit(solution)/shard_map/pair_sums/ppermute | solution.py:8

commit v2 on v1

--- a/solution.py
+++ b/solution.py
@@ -53,13 +53,6 @@
     result = source
     for step in range(degree_top):
         degree = degree_top - 1 - step
-        with jax.named_scope("neighbour_iterates"):
-            if peer_count > 1:
-                from_minus = shift(iterate, "clus", peer_count, 1)
-                from_plus = shift(iterate, "clus", peer_count, peer_count - 1)
-            else:
-                from_minus = iterate
-                from_plus = iterate
         with jax.named_scope("far_partial"):
             far_input = iterate[:, far_local, :]
             coef = jnp.einsum(
@@ -67,12 +60,31 @@
             )
             coef = coef.reshape(coef.shape[0], rhs_here * rank_size)
             partial_value = jnp.einsum("jc,jm->cm", far_hot, coef, precision=lax.Precision.HIGHEST)
-            partial_value = partial_value.reshape(peer_count, clusters_here, rhs_here * rank_size)
-        with jax.named_scope("far_slices"):
+            partial_value = partial_value.reshape(peer_count, clusters_here, rhs_here, rank_size)
+            partial_value = partial_value.transpose(0, 2, 1, 3).reshape(
+                peer_count, rhs_here, clusters_here * rank_size
+            )
+        with jax.named_scope("clus_exchange"):
             far_mine = partial_value[my_index]
+            iterate_wide = iterate.reshape(rhs_here, clusters_here * leaf_size).astype(jnp.float32)
+            iterate_size = clusters_here * leaf_size
+            from_minus = iterate
+            from_plus = iterate
             for s in range(1, peer_count):
                 outgoing = partial_value[(my_index + s) % peer_count]
-                far_mine = far_mine + shift(outgoing, "clus", peer_count, s)
+                carries_iterate = s == 1 or s == peer_count - 1
+                if carries_iterate:
+                    outgoing = jnp.concatenate([iterate_wide, outgoing], axis=1)
+                incoming = shift(outgoing, "clus", peer_count, s)
+                if carries_iterate:
+                    neighbour = incoming[:, :iterate_size].astype(jnp.bfloat16)
+                    neighbour = neighbour.reshape(rhs_here, clusters_here, leaf_size)
+                    if s == 1:
+                        from_minus = neighbour
+                    if s == peer_count - 1:
+                        from_plus = neighbour
+                    incoming = incoming[:, iterate_size:]
+                far_mine = far_mine + incoming
         with jax.named_scope("near_partial"):
             extended = jnp.concatenate([iterate, from_plus, from_minus], axis=1)
             gathered = extended[:, near_index, :]
@@ -84,9 +96,7 @@
             )
         with jax.named_scope("pair_sums"):
             near_flat = near_part.reshape(rhs_here, clusters_here * leaf_size)
-            far_flat = far_mine.reshape(clusters_here, rhs_here, rank_size)
-            far_flat = far_flat.transpose(1, 0, 2).reshape(rhs_here, clusters_here * rank_size)
-            packed = jnp.concatenate([near_flat, far_flat], axis=1)
+            packed = jnp.concatenate([near_flat, far_mine], axis=1)
             packed = pair_total(packed, pair_count, pair_index)
             near_sum = packed[:, : clusters_here * leaf_size].reshape(
                 rhs_here, clusters_here, leaf_size

time: 64.8 us -> 56 us (0.86)
  starting transfers between devices: 26.4 us -> 18.5 us
  waiting for transfers between devices: 21.1 us -> 19.5 us
  matrix products: 5.31 us -> 6.06 us
    ppermute x18 -> x12, starting transfers between devices: 26.4 us -> 18.5 us  [shift(): lax.ppermute(value, axis, [(i, (i + step) % count) for i in range(count)])]
    ppermute x18 -> x12, waiting for transfers between devices: 21.1 us -> 19.5 us  [shift(): lax.ppermute(value, axis, [(i, (i + step) % count) for i in range(count)])]
    dot_general x3, matrix products: 0.55 us -> 1.29 us  [shards(): jnp.einsum('jc,jm->cm', far_hot, coef, precision=lax.Precision.HIGHEST)]
    convert_element_type x1 -> x3, other arithmetic: 3.43 us -> 3.45 us  [shards(): iterate.reshape(rhs_here, clusters_here * leaf_size).astype(jnp.float32)]
  transfers between devices with their start and end apart: 18 -> 12, of which waited for: 12 -> 8; matrix products, arithmetic and copies ran while one was open for 5% -> 8% of each run, Pallas kernels for 0% -> 0%
where the time goes in v2:
time: 56 us; the launch traced here: 55.7 us
  waiting for transfers between devices  19.5 us (35%)
  starting transfers between devices  18.5 us (33%)
  local copies, waits for them, and re-layouts  6.13 us (11%)
  matrix products  6.06 us (11%)
  other arithmetic  4.99 us (9%)
    ppermute x12, waiting for transfers between devices, shift(): lax.ppermute(value, axis, [(i, (i + step) % count) for i in range(count)])  19.5 us
    ppermute x12, starting transfers between devices, shift(): lax.ppermute(value, axis, [(i, (i + step) % count) for i in range(count)])  18.5 us
    convert_element_type x3, other arithmetic, shards(): iterate.reshape(rhs_here, clusters_here * leaf_size).astype(jnp.float32)  3.45 us
    dot_general x3, matrix products, shards(): jnp.einsum('rjs,jts->rjt', gathered, near_blocks, preferred_element_type=...  1.91 us
    gather x3, local copies, waits for them, and re-layouts, shards(): far_input = iterate[:, far_local, :]  1.79 us
    dot_general x3, matrix products, shards(): jnp.einsum('rjl,jkl->jrk', far_input, col_basis, preferred_element_type=j...  1.73 us
    gather x3, local copies, waits for them, and re-layouts, shards(): gathered = extended[:, near_index, :]  1.67 us
    slice x1, local copies, waits for them, and re-layouts, shards(): iterate = (coefficients[degree_top] * source).astype(jnp.bfloat16)  1.51 us
  transfers between devices with their start and end apart: 12, of which 8 were waited for; matrix products, arithmetic and copies ran while one was open for 8% of the time, Pallas kernels for 0%

profile of v2, /device:TPU:0, one launch (start us, length us, event | category | flops | bytes accessed | tf_op | source)
XLA Modules:
  0.0 55.7 jit_solution(2178642171841069514)
XLA Ops:
  0.1 1.5 %fusion.53 = (f32[1]{0:T(128)}, f32[1]{0:T(128)}, f32[1]{0:T(128)}, f32[1]{0:T(128)}) fusion(f32[4]{0:T(128)} %param.10), kind=kLoop, calls=%fused_computation.122 | loop fusion | bytes 32 | tf_op jit(solution)/shard_map/slice | solution.py:52
  1.6 0.7 %compare_select_fusion.1 = s32[64]{0:T(128)S(1)} fusion(s32[64]{0:T(128)} %param.16, s32[]{:T(128)S(6)} %mul.41), kind=kLoop, calls=%fused_computation.99 | loop fusion | flops 256 | bytes 516 | tf_op jit(solution)/shard_map/far_partial/select_n | solution.py:57
  2.2 3.4 %fusion.52 = (f32[8,2048]{1,0:T(8,128)S(1)}, bf16[8,2048]{1,0:T(8,128)(2,1)S(1)}, f32[8,2048]{1,0:T(8,128)S(1)}, f32[8,2048]{1,0:T(8,128)S(1)}, f32[8,2048]{1,0:T(8,128)S(1)}) fusion(f32[8,2048]{1,0:T(8,128)} %param.9, f32[]{:T(128)} %bitcast.1, f32[]{:T(128)} %bitcast.22, f32[]{:T(128)} %bitcast.65, f32[]{:T(128)} %bitcast.44), kind=kLoop, calls=%fused_computation.121 | loop fusion | flops 98304 | bytes 360464 | tf_op jit(solution)/shard_map/clus_exchange/convert_element_type | solution.py:69
  5.7 0.6 %gather_fusion = bf16[64,8,256]{2,1,0:T(8,128)(2,1)S(1)} fusion(bf16[8,8,256]{2,0,1:T(8,128)(2,1)S(1)} %bitcast.155, s32[1024]{0:T(1024)S(1)} %pad_clamp_fusion.1), kind=kCustom, calls=%fused_computation | custom fusion | bytes 524544 | tf_op jit(solution)/shard_map/far_partial/gather | solution.py:57
  6.3 1.3 %fusion.4 = f32[64,8,16]{2,1,0:T(8,128)S(1)} fusion(bf16[64,16,256]{2,1,0:T(8,128)(2,1)} %param.15, bf16[64,8,256]{2,1,0:T(8,128)(2,1)S(1)} %gather_fusion), kind=kOutput, calls=%fused_computation.19 | convolution fusion | flops 4194304 | bytes 819200 | tf_op jit(solution)/shard_map/far_partial/rjl,jkl->jrk/dot_general | solution.py:58
  7.7 0.4 convolution_bitcast_fusion.2
  8.3 5.1 %collective-permute-start = (f32[8,2176]{1,0:T(8,128)S(1)}, f32[8,2176]{1,0:T(8,128)S(1)}, u32[]{:S(2)}, u32[]{:S(2)}) collective-permute-start(f32[8,2176]{1,0:T(8,128)S(1)} %get-tuple-element.12), channel_id=1, source_target_pairs={{0,12},{4,0},{8,4},{12,8},{1,13},{5,1},{9,5},{13,9},{2,14},{6,2},{... | collective-permute-start | bytes 208904 | tf_op jit(solution)/shard_map/clus_exchange/ppermute | solution.py:8
  13.4 1.0 %collective-permute-start.1 = (f32[8,2176]{1,0:T(8,128)S(1)}, f32[8,2176]{1,0:T(8,128)S(1)}, u32[]{:S(2)}, u32[]{:S(2)}) collective-permute-start(f32[8,2176]{1,0:T(8,128)S(1)} %get-tuple-element.11), channel_id=1, source_target_pairs={{0,4},{4,8},{8,12},{12,0},{1,5},{5,9},{9,13},{13,1},{2,6},{6,10},{... | collective-permute-start | bytes 208904 | tf_op jit(solution)/shard_map/clus_exchange/ppermute | solution.py:8
  14.5 5.0 %collective-permute-done.1 = f32[8,2176]{1,0:T(8,128)S(1)} collective-permute-done((f32[8,2176]{1,0:T(8,128)S(1)}, f32[8,2176]{1,0:T(8,128)S(1)}, u32[]{:S(2)}, u32[]{:S(2)}) %collective-permute-start.1) | collective-permute-done | bytes 69664 | tf_op jit(solution)/shard_map/clus_exchange/ppermute | solution.py:8
  19.6 0.6 %gather_fusion.1 = bf16[16,8,256]{2,1,0:T(8,128)(2,1)S(1)} fusion(bf16[8,24,256]{2,0,1:T(8,128)(2,1)S(1)} %pad_maximum_fusion, s32[1024]{0:T(1024)S(1)} %pad_clamp_fusion), kind=kCustom, calls=%fused_computation.1 | custom fusion | bytes 131136 | tf_op jit(solution)/shard_map/near_partial/gather | solution.py:90
  20.2 0.6 %fusion.19 = f32[16,8,256]{2,1,0:T(8,128)S(1)} fusion(bf16[16,256,256]{2,1,0:T(8,128)(2,1)S(1)} %copy-done, bf16[16,8,256]{2,1,0:T(8,128)(2,1)S(1)} %gather_fusion.1), kind=kOutput, calls=%fused_computation.52 | convolution fusion | flops 16777216 | bytes 2293760 | tf_op jit(solution)/shard_map/near_partial/rjs,jts->rjt/dot_general | solution.py:91
  21.1 1.6 %collective-permute-start.3 = (f32[8,2176]{1,0:T(8,128)S(1)}, f32[8,2176]{1,0:T(8,128)S(1)}, u32[]{:S(2)}, u32[]{:S(2)}) collective-permute-start(f32[8,2176]{1,0:T(8,128)S(1)} %pad_maximum_fusion.5), channel_id=1, source_target_pairs={{0,2},{2,0},{1,3},{3,1},{4,6},{6,4},{5,7},{7,5},{8,10},{10,8},{9,1... | collective-permute-start | bytes 208904 | tf_op jit(solution)/shard_map/pair_sums/ppermute | solution.py:8
  22.7 2.8 %collective-permute-done.3 = f32[8,2176]{1,0:T(8,128)S(1)} collective-permute-done((f32[8,2176]{1,0:T(8,128)S(1)}, f32[8,2176]{1,0:T(8,128)S(1)}, u32[]{:S(2)}, u32[]{:S(2)}) %collective-permute-start.3) | collective-permute-done | bytes 69664 | tf_op jit(solution)/shard_map/pair_sums/ppermute | solution.py:8
  25.8 0.6 %gather_fusion.2 = bf16[64,8,256]{2,1,0:T(8,128)(2,1)S(1)} fusion(bf16[8,8,256]{2,0,1:T(8,128)(2,1)S(1)} %add_convert_fusion.1, s32[1024]{0:T(1024)S(1)} %pad_clamp_fusion.1), kind=kCustom, calls=%fused_computation.2 | custom fusion | bytes 524544 | tf_op jit(solution)/shard_map/far_partial/gather | solution.py:57
  26.8 0.4 convolution_bitcast_fusion.1
  27.4 3.8 %collective-permute-start.4 = (f32[8,2176]{1,0:T(8,128)S(1)}, f32[8,2176]{1,0:T(8,128)S(1)}, u32[]{:S(2)}, u32[]{:S(2)}) collective-permute-start(f32[8,2176]{1,0:T(8,128)S(1)} %get-tuple-element.10), channel_id=1, source_target_pairs={{0,12},{4,0},{8,4},{12,8},{1,13},{5,1},{9,5},{13,9},{2,14},{6,2},{... | collective-permute-start | bytes 208904 | tf_op jit(solution)/shard_map/clus_exchange/ppermute | solution.py:8
  31.2 2.4 %collective-permute-done.5 = f32[8,2176]{1,0:T(8,128)S(1)} collective-permute-done((f32[8,2176]{1,0:T(8,128)S(1)}, f32[8,2176]{1,0:T(8,128)S(1)}, u32[]{:S(2)}, u32[]{:S(2)}) %collective-permute-start.5) | collective-permute-done | bytes 69664 | tf_op jit(solution)/shard_map/clus_exchange/ppermute | solution.py:8
  33.6 0.6 %gather_fusion.3 = bf16[16,8,256]{2,1,0:T(8,128)(2,1)S(1)} fusion(bf16[8,24,256]{2,0,1:T(8,128)(2,1)S(1)} %pad_maximum_fusion.1, s32[1024]{0:T(1024)S(1)} %pad_clamp_fusion), kind=kCustom, calls=%fused_computation.3 | custom fusion | bytes 131136 | tf_op jit(solution)/shard_map/near_partial/gather | solution.py:90
  34.2 0.6 %fusion.17 = f32[16,8,256]{2,1,0:T(8,128)S(1)} fusion(bf16[16,256,256]{2,1,0:T(8,128)(2,1)S(1)} %copy-done, bf16[16,8,256]{2,1,0:T(8,128)(2,1)S(1)} %gather_fusion.3), kind=kOutput, calls=%fused_computation.50 | convolution fusion | flops 16777216 | bytes 2293760 | tf_op jit(solution)/shard_map/near_partial/rjs,jts->rjt/dot_general | solution.py:91
  35.1 0.6 %collective-permute-done.6 = f32[8,128]{1,0:T(8,128)S(1)} collective-permute-done((f32[8,128]{1,0:T(8,128)S(1)}, f32[8,128]{1,0:T(8,128)S(1)}, u32[]{:S(2)}, u32[]{:S(2)}) %collective-permute-start.6) | collective-permute-done | bytes 4128 | tf_op jit(solution)/shard_map/clus_exchange/ppermute | solution.py:8
  35.8 1.6 %collective-permute-start.7 = (f32[8,2176]{1,0:T(8,128)S(1)}, f32[8,2176]{1,0:T(8,128)S(1)}, u32[]{:S(2)}, u32[]{:S(2)}) collective-permute-start(f32[8,2176]{1,0:T(8,128)S(1)} %pad_maximum_fusion.8), channel_id=1, source_target_pairs={{0,2},{2,0},{1,3},{3,1},{4,6},{6,4},{5,7},{7,5},{8,10},{10,8},{9,1... | collective-permute-start | bytes 208904 | tf_op jit(solution)/shard_map/pair_sums/ppermute | solution.py:8
  37.3 2.8 %collective-permute-done.7 = f32[8,2176]{1,0:T(8,128)S(1)} collective-permute-done((f32[8,2176]{1,0:T(8,128)S(1)}, f32[8,2176]{1,0:T(8,128)S(1)}, u32[]{:S(2)}, u32[]{:S(2)}) %collective-permute-start.7) | collective-permute-done | bytes 69664 | tf_op jit(solution)/shard_map/pair_sums/ppermute | solution.py:8
  40.4 0.6 %gather_fusion.4 = bf16[64,8,256]{2,1,0:T(8,128)(2,1)S(1)} fusion(bf16[8,8,256]{2,0,1:T(8,128)(2,1)S(1)} %add_convert_fusion, s32[1024]{0:T(1024)S(1)} %pad_clamp_fusion.1), kind=kCustom, calls=%fused_computation.4 | custom fusion | bytes 524544 | tf_op jit(solution)/shard_map/far_partial/gather | solution.py:57
  41.4 0.4 convolution_bitcast_fusion
  42.1 3.8 %collective-permute-start.8 = (f32[8,2176]{1,0:T(8,128)S(1)}, f32[8,2176]{1,0:T(8,128)S(1)}, u32[]{:S(2)}, u32[]{:S(2)}) collective-permute-start(f32[8,2176]{1,0:T(8,128)S(1)} %get-tuple-element.8), channel_id=1, source_target_pairs={{0,12},{4,0},{8,4},{12,8},{1,13},{5,1},{9,5},{13,9},{2,14},{6,2},{... | collective-permute-start | bytes 208904 | tf_op jit(solution)/shard_map/clus_exchange/ppermute | solution.py:8
  45.9 2.4 %collective-permute-done.9 = f32[8,2176]{1,0:T(8,128)S(1)} collective-permute-done((f32[8,2176]{1,0:T(8,128)S(1)}, f32[8,2176]{1,0:T(8,128)S(1)}, u32[]{:S(2)}, u32[]{:S(2)}) %collective-permute-start.9) | collective-permute-done | bytes 69664 | tf_op jit(solution)/shard_map/clus_exchange/ppermute | solution.py:8
  48.3 0.6 %gather_fusion.5 = bf16[16,8,256]{2,1,0:T(8,128)(2,1)S(1)} fusion(bf16[8,24,256]{2,0,1:T(8,128)(2,1)S(1)} %pad_maximum_fusion.2, s32[1024]{0:T(1024)S(1)} %pad_clamp_fusion), kind=kCustom, calls=%fused_computation.5 | custom fusion | bytes 131136 | tf_op jit(solution)/shard_map/near_partial/gather | solution.py:90
  48.9 0.6 %fusion.15 = f32[16,8,256]{2,1,0:T(8,128)S(1)} fusion(bf16[16,256,256]{2,1,0:T(8,128)(2,1)S(1)} %copy-done, bf16[16,8,256]{2,1,0:T(8,128)(2,1)S(1)} %gather_fusion.5), kind=kOutput, calls=%fused_computation.48 | convolution fusion | flops 16777216 | bytes 2293760 | tf_op jit(solution)/shard_map/near_partial/rjs,jts->rjt/dot_general | solution.py:91
  49.8 0.6 %collective-permute-done.10 = f32[8,128]{1,0:T(8,128)S(1)} collective-permute-done((f32[8,128]{1,0:T(8,128)S(1)}, f32[8,128]{1,0:T(8,128)S(1)}, u32[]{:S(2)}, u32[]{:S(2)}) %collective-permute-start.10) | collective-permute-done | bytes 4128 | tf_op jit(solution)/shard_map/clus_exchange/ppermute | solution.py:8
  50.4 1.6 %collective-permute-start.11 = (f32[8,2176]{1,0:T(8,128)S(1)}, f32[8,2176]{1,0:T(8,128)S(1)}, u32[]{:S(2)}, u32[]{:S(2)}) collective-permute-start(f32[8,2176]{1,0:T(8,128)S(1)} %pad_maximum_fusion.11), channel_id=1, source_target_pairs={{0,2},{2,0},{1,3},{3,1},{4,6},{6,4},{5,7},{7,5},{8,10},{10,8},{9,1... | collective-permute-start | bytes 208904 | tf_op jit(solution)/shard_map/pair_sums/ppermute | solution.py:8
  52.0 2.8 %collective-permute-done.11 = f32[8,2176]{1,0:T(8,128)S(1)} collective-permute-done((f32[8,2176]{1,0:T(8,128)S(1)}, f32[8,2176]{1,0:T(8,128)S(1)}, u32[]{:S(2)}, u32[]{:S(2)}) %collective-permute-start.11) | collective-permute-done | bytes 69664 | tf_op jit(solution)/shard_map/pair_sums/ppermute | solution.py:8
  55.1 0.6 %add_add_fusion = f32[8,8,256]{2,0,1:T(8,128)} fusion(f32[8,8,256]{2,0,1:T(8,128)S(1)} %bitcast.168, f32[8,8,256]{2,0,1:T(8,128)S(1)} %bitcast.167, f32[8,8,256]{2,0,1:T(8,128)S(1)} %convolution_bitcast_fusion.3), kind=kLoop, calls=%fused_computation.54 | loop fusion | flops 32768 | bytes 262144 | tf_op jit(solution)/shard_map/add | solution.py:111
  (80 shorter events, 3.1 us)
Async XLA Ops:
  0.0 20.2 %copy-start = (bf16[16,256,256]{2,1,0:T(8,128)(2,1)S(1)}, bf16[16,256,256]{2,1,0:T(8,128)(2,1)}, u32[]{:S(2)}) copy-start(bf16[16,256,256]{2,1,0:T(8,128)(2,1)} %param.11) | copy-start | bytes 6291460
  0.0 7.7 %copy-start.3 = (s32[64]{0:T(128)S(1)}, s32[64]{0:T(128)}, u32[]{:S(2)}) copy-start(s32[64]{0:T(128)} %param.17) | copy-start | bytes 772
  0.0 14.4 %copy-start.4 = (s32[16]{0:T(128)S(1)}, s32[16]{0:T(128)}, u32[]{:S(2)}) copy-start(s32[16]{0:T(128)} %param.13) | copy-start | bytes 196
  0.0 14.5 %copy-start.5 = (s32[16]{0:T(128)S(1)}, s32[16]{0:T(128)}, u32[]{:S(2)}) copy-start(s32[16]{0:T(128)} %param.12) | copy-start | bytes 196
  7.7 17.9 %copy-start.2 = (bf16[8,16,256]{2,1,0:T(8,128)(2,1)S(1)}, bf16[8,16,256]{2,1,0:T(8,128)(2,1)}, u32[]{:S(2)}) copy-start(bf16[8,16,256]{2,1,0:T(8,128)(2,1)} %param.14) | copy-start | bytes 196612
  8.3 11.2 %collective-permute-start = (f32[8,2176]{1,0:T(8,128)S(1)}, f32[8,2176]{1,0:T(8,128)S(1)}, u32[]{:S(2)}, u32[]{:S(2)}) collective-permute-start(f32[8,2176]{1,0:T(8,128)S(1)} %get-tuple-element.12), channel_id=1, source_target_pairs={{0,12},{4,0},{8,4},{12,8},{1,13},{5,1},{9,5},{13,9},{2,14},{6,2},{... | collective-permute-start | bytes 208904 | tf_op jit(solution)/shard_map/clus_exchange/ppermute | solution.py:8
  13.4 7.6 %collective-permute-start.2 = (f32[8,128]{1,0:T(8,128)S(1)}, f32[8,128]{1,0:T(8,128)S(1)}, u32[]{:S(2)}, u32[]{:S(2)}) collective-permute-start(f32[8,128]{1,0:T(8,128)S(1)} %get-tuple-element.23), channel_id=1, source_target_pairs={{0,8},{4,12},{8,0},{12,4},{1,9},{5,13},{9,1},{13,5},{2,10},{6,14},... | collective-permute-start | bytes 12296 | tf_op jit(solution)/shard_map/clus_exchange/ppermute | solution.py:8
  13.4 6.1 %collective-permute-start.1 = (f32[8,2176]{1,0:T(8,128)S(1)}, f32[8,2176]{1,0:T(8,128)S(1)}, u32[]{:S(2)}, u32[]{:S(2)}) collective-permute-start(f32[8,2176]{1,0:T(8,128)S(1)} %get-tuple-element.11), channel_id=1, source_target_pairs={{0,4},{4,8},{8,12},{12,0},{1,5},{5,9},{9,13},{13,1},{2,6},{6,10},{... | collective-permute-start | bytes 208904 | tf_op jit(solution)/shard_map/clus_exchange/ppermute | solution.py:8
  19.6 6.8 %copy-start.1 = (bf16[64,16,256]{2,1,0:T(8,128)(2,1)S(1)}, bf16[64,16,256]{2,1,0:T(8,128)(2,1)}, u32[]{:S(2)}) copy-start(bf16[64,16,256]{2,1,0:T(8,128)(2,1)} %param.15) | copy-start | bytes 1572868
  21.1 4.4 %collective-permute-start.3 = (f32[8,2176]{1,0:T(8,128)S(1)}, f32[8,2176]{1,0:T(8,128)S(1)}, u32[]{:S(2)}, u32[]{:S(2)}) collective-permute-start(f32[8,2176]{1,0:T(8,128)S(1)} %pad_maximum_fusion.5), channel_id=1, source_target_pairs={{0,2},{2,0},{1,3},{3,1},{4,6},{6,4},{5,7},{7,5},{8,10},{10,8},{9,1... | collective-permute-start | bytes 208904 | tf_op jit(solution)/shard_map/pair_sums/ppermute | solution.py:8
  27.4 6.2 %collective-permute-start.5 = (f32[8,2176]{1,0:T(8,128)S(1)}, f32[8,2176]{1,0:T(8,128)S(1)}, u32[]{:S(2)}, u32[]{:S(2)}) collective-permute-start(f32[8,2176]{1,0:T(8,128)S(1)} %get-tuple-element.9), channel_id=1, source_target_pairs={{0,4},{4,8},{8,12},{12,0},{1,5},{5,9},{9,13},{13,1},{2,6},{6,10},{... | collective-permute-start | bytes 208904 | tf_op jit(solution)/shard_map/clus_exchange/ppermute | solution.py:8
  27.4 6.2 %collective-permute-start.4 = (f32[8,2176]{1,0:T(8,128)S(1)}, f32[8,2176]{1,0:T(8,128)S(1)}, u32[]{:S(2)}, u32[]{:S(2)}) collective-permute-start(f32[8,2176]{1,0:T(8,128)S(1)} %get-tuple-element.10), channel_id=1, source_target_pairs={{0,12},{4,0},{8,4},{12,8},{1,13},{5,1},{9,5},{13,9},{2,14},{6,2},{... | collective-permute-start | bytes 208904 | tf_op jit(solution)/shard_map/clus_exchange/ppermute | solution.py:8
  31.2 4.5 %collective-permute-start.6 = (f32[8,128]{1,0:T(8,128)S(1)}, f32[8,128]{1,0:T(8,128)S(1)}, u32[]{:S(2)}, u32[]{:S(2)}) collective-permute-start(f32[8,128]{1,0:T(8,128)S(1)} %get-tuple-element.20), channel_id=1, source_target_pairs={{0,8},{4,12},{8,0},{12,4},{1,9},{5,13},{9,1},{13,5},{2,10},{6,14},... | collective-permute-start | bytes 12296 | tf_op jit(solution)/shard_map/clus_exchange/ppermute | solution.py:8
  35.8 4.4 %collective-permute-start.7 = (f32[8,2176]{1,0:T(8,128)S(1)}, f32[8,2176]{1,0:T(8,128)S(1)}, u32[]{:S(2)}, u32[]{:S(2)}) collective-permute-start(f32[8,2176]{1,0:T(8,128)S(1)} %pad_maximum_fusion.8), channel_id=1, source_target_pairs={{0,2},{2,0},{1,3},{3,1},{4,6},{6,4},{5,7},{7,5},{8,10},{10,8},{9,1... | collective-permute-start | bytes 208904 | tf_op jit(solution)/shard_map/pair_sums/ppermute | solution.py:8
  42.0 6.3 %collective-permute-start.9 = (f32[8,2176]{1,0:T(8,128)S(1)}, f32[8,2176]{1,0:T(8,128)S(1)}, u32[]{:S(2)}, u32[]{:S(2)}) collective-permute-start(f32[8,2176]{1,0:T(8,128)S(1)} %get-tuple-element.7), channel_id=1, source_target_pairs={{0,4},{4,8},{8,12},{12,0},{1,5},{5,9},{9,13},{13,1},{2,6},{6,10},{... | collective-permute-start | bytes 208904 | tf_op jit(solution)/shard_map/clus_exchange/ppermute | solution.py:8
  42.1 6.2 %collective-permute-start.8 = (f32[8,2176]{1,0:T(8,128)S(1)}, f32[8,2176]{1,0:T(8,128)S(1)}, u32[]{:S(2)}, u32[]{:S(2)}) collective-permute-start(f32[8,2176]{1,0:T(8,128)S(1)} %get-tuple-element.8), channel_id=1, source_target_pairs={{0,12},{4,0},{8,4},{12,8},{1,13},{5,1},{9,5},{13,9},{2,14},{6,2},{... | collective-permute-start | bytes 208904 | tf_op jit(solution)/shard_map/clus_exchange/ppermute | solution.py:8
  45.9 4.5 %collective-permute-start.10 = (f32[8,128]{1,0:T(8,128)S(1)}, f32[8,128]{1,0:T(8,128)S(1)}, u32[]{:S(2)}, u32[]{:S(2)}) collective-permute-start(f32[8,128]{1,0:T(8,128)S(1)} %get-tuple-element.17), channel_id=1, source_target_pairs={{0,8},{4,12},{8,0},{12,4},{1,9},{5,13},{9,1},{13,5},{2,10},{6,14},... | collective-permute-start | bytes 12296 | tf_op jit(solution)/shard_map/clus_exchange/ppermute | solution.py:8
  50.4 4.4 %collective-permute-start.11 = (f32[8,2176]{1,0:T(8,128)S(1)}, f32[8,2176]{1,0:T(8,128)S(1)}, u32[]{:S(2)}, u32[]{:S(2)}) collective-permute-start(f32[8,2176]{1,0:T(8,128)S(1)} %pad_maximum_fusion.11), channel_id=1, source_target_pairs={{0,2},{2,0},{1,3},{3,1},{4,6},{6,4},{5,7},{7,5},{8,10},{10,8},{9,1... | collective-permute-start | bytes 208904 | tf_op jit(solution)/shard_map/pair_sums/ppermute | solution.py:8

commit v3 on v2

--- a/solution.py
+++ b/solution.py
@@ -49,24 +49,24 @@
     far_hot = (far_tgt[:, None] == jnp.arange(cluster_count)[None, :]).astype(jnp.float32)
     row_f32 = row_basis.astype(jnp.float32)
 
-    iterate = (coefficients[degree_top] * source).astype(jnp.bfloat16)
-    result = source
-    for step in range(degree_top):
-        degree = degree_top - 1 - step
+    stream_count = 2 if rhs_here % 2 == 0 else 1
+    rhs_stream = rhs_here // stream_count
+
+    def product(iterate, source_part, degree):
         with jax.named_scope("far_partial"):
             far_input = iterate[:, far_local, :]
             coef = jnp.einsum(
                 "rjl,jkl->jrk", far_input, col_basis, preferred_element_type=jnp.float32
             )
-            coef = coef.reshape(coef.shape[0], rhs_here * rank_size)
+            coef = coef.reshape(coef.shape[0], rhs_stream * rank_size)
             partial_value = jnp.einsum("jc,jm->cm", far_hot, coef, precision=lax.Precision.HIGHEST)
-            partial_value = partial_value.reshape(peer_count, clusters_here, rhs_here, rank_size)
+            partial_value = partial_value.reshape(peer_count, clusters_here, rhs_stream, rank_size)
             partial_value = partial_value.transpose(0, 2, 1, 3).reshape(
-                peer_count, rhs_here, clusters_here * rank_size
+                peer_count, rhs_stream, clusters_here * rank_size
             )
         with jax.named_scope("clus_exchange"):
             far_mine = partial_value[my_index]
-            iterate_wide = iterate.reshape(rhs_here, clusters_here * leaf_size).astype(jnp.float32)
+            iterate_wide = iterate.reshape(rhs_stream, clusters_here * leaf_size).astype(jnp.float32)
             iterate_size = clusters_here * leaf_size
             from_minus = iterate
             from_plus = iterate
@@ -78,7 +78,7 @@
                 incoming = shift(outgoing, "clus", peer_count, s)
                 if carries_iterate:
                     neighbour = incoming[:, :iterate_size].astype(jnp.bfloat16)
-                    neighbour = neighbour.reshape(rhs_here, clusters_here, leaf_size)
+                    neighbour = neighbour.reshape(rhs_stream, clusters_here, leaf_size)
                     if s == 1:
                         from_minus = neighbour
                     if s == peer_count - 1:
@@ -95,21 +95,29 @@
                 "rjt,jc->rct", contrib, target_hot, precision=lax.Precision.HIGHEST
             )
         with jax.named_scope("pair_sums"):
-            near_flat = near_part.reshape(rhs_here, clusters_here * leaf_size)
+            near_flat = near_part.reshape(rhs_stream, clusters_here * leaf_size)
             packed = jnp.concatenate([near_flat, far_mine], axis=1)
             packed = pair_total(packed, pair_count, pair_index)
             near_sum = packed[:, : clusters_here * leaf_size].reshape(
-                rhs_here, clusters_here, leaf_size
+                rhs_stream, clusters_here, leaf_size
             )
             coef_sum = packed[:, clusters_here * leaf_size :].reshape(
-                rhs_here, clusters_here, rank_size
+                rhs_stream, clusters_here, rank_size
             )
         with jax.named_scope("far_field"):
             far_field = jnp.einsum(
                 "rck,ckl->rcl", coef_sum, row_f32, precision=lax.Precision.HIGHEST
             )
-        result = near_sum + far_field + coefficients[degree] * source
-        iterate = result.astype(jnp.bfloat16)
+        return near_sum + far_field + coefficients[degree] * source_part
+
+    sources = [source[k * rhs_stream : (k + 1) * rhs_stream] for k in range(stream_count)]
+    iterates = [(coefficients[degree_top] * part).astype(jnp.bfloat16) for part in sources]
+    results = sources
+    for step in range(degree_top):
+        degree = degree_top - 1 - step
+        results = [product(iterates[k], sources[k], degree) for k in range(stream_count)]
+        iterates = [part.astype(jnp.bfloat16) for part in results]
+    result = jnp.concatenate(results, axis=0)
     return result.reshape(rhs_here, clusters_here * leaf_size)
 
 

time: 56 us -> 75.6 us (1.35)
  starting transfers between devices: 18.5 us -> 33.3 us
  waiting for transfers between devices: 19.5 us -> 13.9 us
  local copies, waits for them, and re-layouts: 6.13 us -> 11.3 us
  matrix products: 6.06 us -> 10.4 us
    ppermute x12 -> x24, starting transfers between devices: 18.5 us -> 33.3 us  [shift(): lax.ppermute(value, axis, [(i, (i + step) % count) for i in range(count)])]
    ppermute x12 -> x24, waiting for transfers between devices: 19.5 us -> 13.9 us  [shift(): lax.ppermute(value, axis, [(i, (i + step) % count) for i in range(count)])]
    dot_general x15 -> x30, matrix products: 6.06 us -> 10.4 us  [the longest x6 3.82 us: product(): jnp.einsum('rjs,jts->rjt', gathered, near_blocks, preferred_element_type=...]
    gather x6 -> x12, local copies, waits for them, and re-layouts: 3.46 us -> 7.71 us  [the longest x6 4.15 us: product(): far_input = iterate[:, far_local, :]]
    concatenate x9 -> x19, other arithmetic: 0.1 us -> 1.03 us  [the longest x1 0.65 us: shards(): result = jnp.concatenate(results, axis=0)]
    slice x13 -> x25, local copies, waits for them, and re-layouts: 1.57 us -> 1.64 us  [the longest x1 1.51 us: shards(): coefficients[degree_top] * part]
    convert_element_type x5 -> x9, other arithmetic: 3.48 us -> 3.53 us  [the longest x5 3.47 us: product(): iterate.reshape(rhs_stream, clusters_here * leaf_size).astype(jnp.float32)]
  transfers between devices with their start and end apart: 12 -> 24, of which waited for: 8 -> 6; matrix products, arithmetic and copies ran while one was open for 8% -> 18% of each run, Pallas kernels for 0% -> 0%
where the time goes in v3:
time: 75.6 us; the launch traced here: 75.4 us
  starting transfers between devices  33.3 us (44%)
  waiting for transfers between devices  13.9 us (18%)
  local copies, waits for them, and re-layouts  11.3 us (15%)
  matrix products  10.4 us (14%)
  other arithmetic  5.45 us (7%)
  between operations  0.96 us (1%)
    ppermute x24, starting transfers between devices, shift(): lax.ppermute(value, axis, [(i, (i + step) % count) for i in range(count)])  33.3 us
    ppermute x24, waiting for transfers between devices, shift(): lax.ppermute(value, axis, [(i, (i + step) % count) for i in range(count)])  13.9 us
    gather x6, local copies, waits for them, and re-layouts, product(): far_input = iterate[:, far_local, :]  4.15 us
    dot_general x6, matrix products, product(): jnp.einsum('rjs,jts->rjt', gathered, near_blocks, preferred_element_type=...  3.82 us
    gather x6, local copies, waits for them, and re-layouts, product(): gathered = extended[:, near_index, :]  3.56 us
    convert_element_type x5, other arithmetic, product(): iterate.reshape(rhs_stream, clusters_here * leaf_size).astype(jnp.float32)  3.47 us
    dot_general x6, matrix products, product(): jnp.einsum('rjl,jkl->jrk', far_input, col_basis, preferred_element_type=j...  2.41 us
    dot_general x6, matrix products, product(): jnp.einsum('jc,jm->cm', far_hot, coef, precision=lax.Precision.HIGHEST)  2.27 us
  transfers between devices with their start and end apart: 24, of which 6 were waited for; matrix products, arithmetic and copies ran while one was open for 18% of the time, Pallas kernels for 0%

profile of v3, /device:TPU:0, one launch (start us, length us, event | category | flops | bytes accessed | tf_op | source)
XLA Modules:
  0.0 75.4 jit_solution(16188868301578403808)
XLA Ops:
  0.1 1.5 %fusion.138 = (f32[1]{0:T(128)}, f32[1]{0:T(128)}, f32[1]{0:T(128)}, f32[1]{0:T(128)}) fusion(f32[4]{0:T(128)} %param.10), kind=kLoop, calls=%fused_computation.254 | loop fusion | bytes 32 | tf_op jit(solution)/shard_map/slice | solution.py:114
  2.3 3.4 %fusion.136 = (f32[4,2048]{1,0:T(4,128)S(1)}, bf16[4,2048]{1,0:T(4,128)(2,1)S(1)}, f32[4,2048]{1,0:T(4,128)S(1)}, f32[4,2048]{1,0:T(4,128)S(1)}, f32[4,2048]{1,0...) fusion(f32[8,2048]{1,0:T(8,128)} %param.9, ...), kind=kLoop, calls=%fused_computation.252 | loop fusion | flops 98304 | bytes 360464 | tf_op jit(solution)/shard_map/clus_exchange/convert_element_type | solution.py:69
  5.7 0.7 gather_fusion.6
  6.4 1.3 %fusion.4 = f32[64,4,16]{2,1,0:T(4,128)S(1)} fusion(bf16[64,16,256]{2,1,0:T(8,128)(2,1)} %param.15, bf16[64,4,256]{2,1,0:T(4,128)(2,1)S(1)} %gather_fusion.6), kind=kOutput, calls=%fused_computation.34 | convolution fusion | flops 2097152 | bytes 671744 | tf_op jit(solution)/shard_map/far_partial/rjl,jkl->jrk/dot_general | solution.py:58
  7.8 0.9 %convolution_bitcast_fusion.2 = f32[4,4,8,16]{3,2,1,0:T(8,128)S(1)} fusion(f32[64,4,16]{0,2,1:T(8,128)S(1)} %copy.22, s32[4,8]{1,0:T(4,128)S(1)} %multiply_add_fusion, s32[64]{0:T(128)} %param.17), kind=kOutput, calls=%fused_computation.14 | convolution fusion | flops 1574912 | bytes 24960 | tf_op jit(solution)/shard_map/far_partial/jc,jm->cm/dot_general | solution.py:62
  8.8 4.1 %collective-permute-start.14 = (f32[4,128]{1,0:T(4,128)S(1)}, f32[4,128]{1,0:T(4,128)S(1)}, u32[]{:S(2)}, u32[]{:S(2)}) collective-permute-start(f32[4,128]{1,0:T(4,128)S(1)} %get-tuple-element.45), channel_id=1, source_target_pairs={{0,8},{4,12},{8,0},{12,4},{1,9},{5,13},{9,1},{13,5},{2,10},{6,14},... | collective-permute-start | bytes 6152 | tf_op jit(solution)/shard_map/clus_exchange/ppermute | solution.py:8
  13.0 1.4 %collective-permute-start.12 = (f32[4,2176]{1,0:T(4,128)S(1)}, f32[4,2176]{1,0:T(4,128)S(1)}, u32[]{:S(2)}, u32[]{:S(2)}) collective-permute-start(f32[4,2176]{1,0:T(4,128)S(1)} %get-tuple-element.28), channel_id=1, source_target_pairs={{0,12},{4,0},{8,4},{12,8},{1,13},{5,1},{9,5},{13,9},{2,14},{6,2},{... | collective-permute-start | bytes 104456 | tf_op jit(solution)/shard_map/clus_exchange/ppermute | solution.py:8
  16.5 1.1 %collective-permute-start.2 = (f32[4,128]{1,0:T(4,128)S(1)}, f32[4,128]{1,0:T(4,128)S(1)}, u32[]{:S(2)}, u32[]{:S(2)}) collective-permute-start(f32[4,128]{1,0:T(4,128)S(1)} %get-tuple-element.36), channel_id=1, source_target_pairs={{0,8},{4,12},{8,0},{12,4},{1,9},{5,13},{9,1},{13,5},{2,10},{6,14},... | collective-permute-start | bytes 6152 | tf_op jit(solution)/shard_map/clus_exchange/ppermute | solution.py:8
  17.6 3.0 %collective-permute-start = (f32[4,2176]{1,0:T(4,128)S(1)}, f32[4,2176]{1,0:T(4,128)S(1)}, u32[]{:S(2)}, u32[]{:S(2)}) collective-permute-start(f32[4,2176]{1,0:T(4,128)S(1)} %get-tuple-element.22), channel_id=1, source_target_pairs={{0,12},{4,0},{8,4},{12,8},{1,13},{5,1},{9,5},{13,9},{2,14},{6,2},{... | collective-permute-start | bytes 104456 | tf_op jit(solution)/shard_map/clus_exchange/ppermute | solution.py:8
  22.3 1.6 %collective-permute-start.15 = (f32[4,2176]{1,0:T(4,128)S(1)}, f32[4,2176]{1,0:T(4,128)S(1)}, u32[]{:S(2)}, u32[]{:S(2)}) collective-permute-start(f32[4,2176]{1,0:T(4,128)S(1)} %pad_maximum_fusion.18), channel_id=1, source_target_pairs={{0,2},{2,0},{1,3},{3,1},{4,6},{6,4},{5,7},{7,5},{8,10},{10,8},{9,1... | collective-permute-start | bytes 104456 | tf_op jit(solution)/shard_map/pair_sums/ppermute | solution.py:8
  23.8 2.6 %collective-permute-done.1 = f32[4,2176]{1,0:T(4,128)S(1)} collective-permute-done((f32[4,2176]{1,0:T(4,128)S(1)}, f32[4,2176]{1,0:T(4,128)S(1)}, u32[]{:S(2)}, u32[]{:S(2)}) %collective-permute-start.1) | collective-permute-done | bytes 34848 | tf_op jit(solution)/shard_map/clus_exchange/ppermute | solution.py:8
  28.0 1.6 %collective-permute-start.3 = (f32[4,2176]{1,0:T(4,128)S(1)}, f32[4,2176]{1,0:T(4,128)S(1)}, u32[]{:S(2)}, u32[]{:S(2)}) collective-permute-start(f32[4,2176]{1,0:T(4,128)S(1)} %pad_maximum_fusion.9), channel_id=1, source_target_pairs={{0,2},{2,0},{1,3},{3,1},{4,6},{6,4},{5,7},{7,5},{8,10},{10,8},{9,1... | collective-permute-start | bytes 104456 | tf_op jit(solution)/shard_map/pair_sums/ppermute | solution.py:8
  29.6 2.4 %collective-permute-done.3 = f32[4,2176]{1,0:T(4,128)S(1)} collective-permute-done((f32[4,2176]{1,0:T(4,128)S(1)}, f32[4,2176]{1,0:T(4,128)S(1)}, u32[]{:S(2)}, u32[]{:S(2)}) %collective-permute-start.3) | collective-permute-done | bytes 34848 | tf_op jit(solution)/shard_map/pair_sums/ppermute | solution.py:8
  32.3 0.7 gather_fusion.8
  33.9 1.6 %collective-permute-start.16 = (f32[4,2176]{1,0:T(4,128)S(1)}, f32[4,2176]{1,0:T(4,128)S(1)}, u32[]{:S(2)}, u32[]{:S(2)}) collective-permute-start(f32[4,2176]{1,0:T(4,128)S(1)} %get-tuple-element.26), channel_id=1, source_target_pairs={{0,12},{4,0},{8,4},{12,8},{1,13},{5,1},{9,5},{13,9},{2,14},{6,2},{... | collective-permute-start | bytes 104456 | tf_op jit(solution)/shard_map/clus_exchange/ppermute | solution.py:8
  36.2 0.7 gather_fusion.2
  37.7 3.0 %collective-permute-start.6 = (f32[4,128]{1,0:T(4,128)S(1)}, f32[4,128]{1,0:T(4,128)S(1)}, u32[]{:S(2)}, u32[]{:S(2)}) collective-permute-start(f32[4,128]{1,0:T(4,128)S(1)} %get-tuple-element.33), channel_id=1, source_target_pairs={{0,8},{4,12},{8,0},{12,4},{1,9},{5,13},{9,1},{13,5},{2,10},{6,14},... | collective-permute-start | bytes 6152 | tf_op jit(solution)/shard_map/clus_exchange/ppermute | solution.py:8
  40.6 1.3 %collective-permute-start.4 = (f32[4,2176]{1,0:T(4,128)S(1)}, f32[4,2176]{1,0:T(4,128)S(1)}, u32[]{:S(2)}, u32[]{:S(2)}) collective-permute-start(f32[4,2176]{1,0:T(4,128)S(1)} %get-tuple-element.20), channel_id=1, source_target_pairs={{0,12},{4,0},{8,4},{12,8},{1,13},{5,1},{9,5},{13,9},{2,14},{6,2},{... | collective-permute-start | bytes 104456 | tf_op jit(solution)/shard_map/clus_exchange/ppermute | solution.py:8
  41.9 0.8 %collective-permute-start.5 = (f32[4,2176]{1,0:T(4,128)S(1)}, f32[4,2176]{1,0:T(4,128)S(1)}, u32[]{:S(2)}, u32[]{:S(2)}) collective-permute-start(f32[4,2176]{1,0:T(4,128)S(1)} %get-tuple-element.19), channel_id=1, source_target_pairs={{0,4},{4,8},{8,12},{12,0},{1,5},{5,9},{9,13},{13,1},{2,6},{6,10},{... | collective-permute-start | bytes 104456 | tf_op jit(solution)/shard_map/clus_exchange/ppermute | solution.py:8
  44.3 1.6 %collective-permute-start.19 = (f32[4,2176]{1,0:T(4,128)S(1)}, f32[4,2176]{1,0:T(4,128)S(1)}, u32[]{:S(2)}, u32[]{:S(2)}) collective-permute-start(f32[4,2176]{1,0:T(4,128)S(1)} %pad_maximum_fusion.21), channel_id=1, source_target_pairs={{0,2},{2,0},{1,3},{3,1},{4,6},{6,4},{5,7},{7,5},{8,10},{10,8},{9,1... | collective-permute-start | bytes 104456 | tf_op jit(solution)/shard_map/pair_sums/ppermute | solution.py:8
  45.8 1.8 %collective-permute-done.5 = f32[4,2176]{1,0:T(4,128)S(1)} collective-permute-done((f32[4,2176]{1,0:T(4,128)S(1)}, f32[4,2176]{1,0:T(4,128)S(1)}, u32[]{:S(2)}, u32[]{:S(2)}) %collective-permute-start.5) | collective-permute-done | bytes 34848 | tf_op jit(solution)/shard_map/clus_exchange/ppermute | solution.py:8
  49.2 1.3 %collective-permute-start.7 = (f32[4,2176]{1,0:T(4,128)S(1)}, f32[4,2176]{1,0:T(4,128)S(1)}, u32[]{:S(2)}, u32[]{:S(2)}) collective-permute-start(f32[4,2176]{1,0:T(4,128)S(1)} %pad_maximum_fusion.12), channel_id=1, source_target_pairs={{0,2},{2,0},{1,3},{3,1},{4,6},{6,4},{5,7},{7,5},{8,10},{10,8},{9,1... | collective-permute-start | bytes 104456 | tf_op jit(solution)/shard_map/pair_sums/ppermute | solution.py:8
  50.6 2.6 %collective-permute-done.7 = f32[4,2176]{1,0:T(4,128)S(1)} collective-permute-done((f32[4,2176]{1,0:T(4,128)S(1)}, f32[4,2176]{1,0:T(4,128)S(1)}, u32[]{:S(2)}, u32[]{:S(2)}) %collective-permute-start.7) | collective-permute-done | bytes 34848 | tf_op jit(solution)/shard_map/pair_sums/ppermute | solution.py:8
  53.5 0.7 gather_fusion.10
  55.1 1.4 %collective-permute-start.20 = (f32[4,2176]{1,0:T(4,128)S(1)}, f32[4,2176]{1,0:T(4,128)S(1)}, u32[]{:S(2)}, u32[]{:S(2)}) collective-permute-start(f32[4,2176]{1,0:T(4,128)S(1)} %get-tuple-element.24), channel_id=1, source_target_pairs={{0,12},{4,0},{8,4},{12,8},{1,13},{5,1},{9,5},{13,9},{2,14},{6,2},{... | collective-permute-start | bytes 104456 | tf_op jit(solution)/shard_map/clus_exchange/ppermute | solution.py:8
  58.9 3.0 %collective-permute-start.10 = (f32[4,128]{1,0:T(4,128)S(1)}, f32[4,128]{1,0:T(4,128)S(1)}, u32[]{:S(2)}, u32[]{:S(2)}) collective-permute-start(f32[4,128]{1,0:T(4,128)S(1)} %get-tuple-element.30), channel_id=1, source_target_pairs={{0,8},{4,12},{8,0},{12,4},{1,9},{5,13},{9,1},{13,5},{2,10},{6,14},... | collective-permute-start | bytes 6152 | tf_op jit(solution)/shard_map/clus_exchange/ppermute | solution.py:8
  61.8 1.0 %collective-permute-start.8 = (f32[4,2176]{1,0:T(4,128)S(1)}, f32[4,2176]{1,0:T(4,128)S(1)}, u32[]{:S(2)}, u32[]{:S(2)}) collective-permute-start(f32[4,2176]{1,0:T(4,128)S(1)} %get-tuple-element.18), channel_id=1, source_target_pairs={{0,12},{4,0},{8,4},{12,8},{1,13},{5,1},{9,5},{13,9},{2,14},{6,2},{... | collective-permute-start | bytes 104456 | tf_op jit(solution)/shard_map/clus_exchange/ppermute | solution.py:8
  62.9 1.1 %collective-permute-start.9 = (f32[4,2176]{1,0:T(4,128)S(1)}, f32[4,2176]{1,0:T(4,128)S(1)}, u32[]{:S(2)}, u32[]{:S(2)}) collective-permute-start(f32[4,2176]{1,0:T(4,128)S(1)} %get-tuple-element.17), channel_id=1, source_target_pairs={{0,4},{4,8},{8,12},{12,0},{1,5},{5,9},{9,13},{13,1},{2,6},{6,10},{... | collective-permute-start | bytes 104456 | tf_op jit(solution)/shard_map/clus_exchange/ppermute | solution.py:8
  65.5 1.3 %collective-permute-start.23 = (f32[4,2176]{1,0:T(4,128)S(1)}, f32[4,2176]{1,0:T(4,128)S(1)}, u32[]{:S(2)}, u32[]{:S(2)}) collective-permute-start(f32[4,2176]{1,0:T(4,128)S(1)} %pad_maximum_fusion.24), channel_id=1, source_target_pairs={{0,2},{2,0},{1,3},{3,1},{4,6},{6,4},{5,7},{7,5},{8,10},{10,8},{9,1... | collective-permute-start | bytes 104456 | tf_op jit(solution)/shard_map/pair_sums/ppermute | solution.py:8
  66.8 1.8 %collective-permute-done.9 = f32[4,2176]{1,0:T(4,128)S(1)} collective-permute-done((f32[4,2176]{1,0:T(4,128)S(1)}, f32[4,2176]{1,0:T(4,128)S(1)}, u32[]{:S(2)}, u32[]{:S(2)}) %collective-permute-start.9) | collective-permute-done | bytes 34848 | tf_op jit(solution)/shard_map/clus_exchange/ppermute | solution.py:8
  70.2 1.3 %collective-permute-start.11 = (f32[4,2176]{1,0:T(4,128)S(1)}, f32[4,2176]{1,0:T(4,128)S(1)}, u32[]{:S(2)}, u32[]{:S(2)}) collective-permute-start(f32[4,2176]{1,0:T(4,128)S(1)} %pad_maximum_fusion.15), channel_id=1, source_target_pairs={{0,2},{2,0},{1,3},{3,1},{4,6},{6,4},{5,7},{7,5},{8,10},{10,8},{9,1... | collective-permute-start | bytes 104456 | tf_op jit(solution)/shard_map/pair_sums/ppermute | solution.py:8
  71.5 2.6 %collective-permute-done.11 = f32[4,2176]{1,0:T(4,128)S(1)} collective-permute-done((f32[4,2176]{1,0:T(4,128)S(1)}, f32[4,2176]{1,0:T(4,128)S(1)}, u32[]{:S(2)}, u32[]{:S(2)}) %collective-permute-start.11) | collective-permute-done | bytes 34848 | tf_op jit(solution)/shard_map/pair_sums/ppermute | solution.py:8
  (172 shorter events, 19.4 us)
Async XLA Ops:
  0.0 21.4 %copy-start = (bf16[16,256,256]{2,1,0:T(8,128)(2,1)S(1)}, bf16[16,256,256]{2,1,0:T(8,128)(2,1)}, u32[]{:S(2)}) copy-start(bf16[16,256,256]{2,1,0:T(8,128)(2,1)} %param.11) | copy-start | bytes 6291460
  0.0 15.7 %copy-start.1 = (bf16[64,16,256]{2,1,0:T(8,128)(2,1)S(1)}, bf16[64,16,256]{2,1,0:T(8,128)(2,1)}, u32[]{:S(2)}) copy-start(bf16[64,16,256]{2,1,0:T(8,128)(2,1)} %param.15) | copy-start | bytes 1572868
  0.0 16.1 %copy-start.3 = (s32[64]{0:T(128)S(1)}, s32[64]{0:T(128)}, u32[]{:S(2)}) copy-start(s32[64]{0:T(128)} %param.17) | copy-start | bytes 772
  0.0 20.6 %copy-start.4 = (s32[16]{0:T(128)S(1)}, s32[16]{0:T(128)}, u32[]{:S(2)}) copy-start(s32[16]{0:T(128)} %param.13) | copy-start | bytes 196
  0.0 20.6 %copy-start.5 = (s32[16]{0:T(128)S(1)}, s32[16]{0:T(128)}, u32[]{:S(2)}) copy-start(s32[16]{0:T(128)} %param.12) | copy-start | bytes 196
  8.8 13.4 %collective-permute-start.14 = (f32[4,128]{1,0:T(4,128)S(1)}, f32[4,128]{1,0:T(4,128)S(1)}, u32[]{:S(2)}, u32[]{:S(2)}) collective-permute-start(f32[4,128]{1,0:T(4,128)S(1)} %get-tuple-element.45), channel_id=1, source_target_pairs={{0,8},{4,12},{8,0},{12,4},{1,9},{5,13},{9,1},{13,5},{2,10},{6,14},... | collective-permute-start | bytes 6152 | tf_op jit(solution)/shard_map/clus_exchange/ppermute | solution.py:8
  13.0 7.8 %collective-permute-start.12 = (f32[4,2176]{1,0:T(4,128)S(1)}, f32[4,2176]{1,0:T(4,128)S(1)}, u32[]{:S(2)}, u32[]{:S(2)}) collective-permute-start(f32[4,2176]{1,0:T(4,128)S(1)} %get-tuple-element.28), channel_id=1, source_target_pairs={{0,12},{4,0},{8,4},{12,8},{1,13},{5,1},{9,5},{13,9},{2,14},{6,2},{... | collective-permute-start | bytes 104456 | tf_op jit(solution)/shard_map/clus_exchange/ppermute | solution.py:8
  14.4 6.3 %collective-permute-start.13 = (f32[4,2176]{1,0:T(4,128)S(1)}, f32[4,2176]{1,0:T(4,128)S(1)}, u32[]{:S(2)}, u32[]{:S(2)}) collective-permute-start(f32[4,2176]{1,0:T(4,128)S(1)} %get-tuple-element.27), channel_id=1, source_target_pairs={{0,4},{4,8},{8,12},{12,0},{1,5},{5,9},{9,13},{13,1},{2,6},{6,10},{... | collective-permute-start | bytes 104456 | tf_op jit(solution)/shard_map/clus_exchange/ppermute | solution.py:8
  16.5 11.4 %collective-permute-start.2 = (f32[4,128]{1,0:T(4,128)S(1)}, f32[4,128]{1,0:T(4,128)S(1)}, u32[]{:S(2)}, u32[]{:S(2)}) collective-permute-start(f32[4,128]{1,0:T(4,128)S(1)} %get-tuple-element.36), channel_id=1, source_target_pairs={{0,8},{4,12},{8,0},{12,4},{1,9},{5,13},{9,1},{13,5},{2,10},{6,14},... | collective-permute-start | bytes 6152 | tf_op jit(solution)/shard_map/clus_exchange/ppermute | solution.py:8
  17.6 8.8 %collective-permute-start = (f32[4,2176]{1,0:T(4,128)S(1)}, f32[4,2176]{1,0:T(4,128)S(1)}, u32[]{:S(2)}, u32[]{:S(2)}) collective-permute-start(f32[4,2176]{1,0:T(4,128)S(1)} %get-tuple-element.22), channel_id=1, source_target_pairs={{0,12},{4,0},{8,4},{12,8},{1,13},{5,1},{9,5},{13,9},{2,14},{6,2},{... | collective-permute-start | bytes 104456 | tf_op jit(solution)/shard_map/clus_exchange/ppermute | solution.py:8
  20.6 5.8 %collective-permute-start.1 = (f32[4,2176]{1,0:T(4,128)S(1)}, f32[4,2176]{1,0:T(4,128)S(1)}, u32[]{:S(2)}, u32[]{:S(2)}) collective-permute-start(f32[4,2176]{1,0:T(4,128)S(1)} %get-tuple-element.21), channel_id=1, source_target_pairs={{0,4},{4,8},{8,12},{12,0},{1,5},{5,9},{9,13},{13,1},{2,6},{6,10},{... | collective-permute-start | bytes 104456 | tf_op jit(solution)/shard_map/clus_exchange/ppermute | solution.py:8
  22.0 10.1 %copy-start.2 = (bf16[8,16,256]{2,1,0:T(8,128)(2,1)S(1)}, bf16[8,16,256]{2,1,0:T(8,128)(2,1)}, u32[]{:S(2)}) copy-start(bf16[8,16,256]{2,1,0:T(8,128)(2,1)} %param.14) | copy-start | bytes 196612
  22.3 7.3 %collective-permute-start.15 = (f32[4,2176]{1,0:T(4,128)S(1)}, f32[4,2176]{1,0:T(4,128)S(1)}, u32[]{:S(2)}, u32[]{:S(2)}) collective-permute-start(f32[4,2176]{1,0:T(4,128)S(1)} %pad_maximum_fusion.18), channel_id=1, source_target_pairs={{0,2},{2,0},{1,3},{3,1},{4,6},{6,4},{5,7},{7,5},{8,10},{10,8},{9,1... | collective-permute-start | bytes 104456 | tf_op jit(solution)/shard_map/pair_sums/ppermute | solution.py:8
  28.0 4.0 %collective-permute-start.3 = (f32[4,2176]{1,0:T(4,128)S(1)}, f32[4,2176]{1,0:T(4,128)S(1)}, u32[]{:S(2)}, u32[]{:S(2)}) collective-permute-start(f32[4,2176]{1,0:T(4,128)S(1)} %pad_maximum_fusion.9), channel_id=1, source_target_pairs={{0,2},{2,0},{1,3},{3,1},{4,6},{6,4},{5,7},{7,5},{8,10},{10,8},{9,1... | collective-permute-start | bytes 104456 | tf_op jit(solution)/shard_map/pair_sums/ppermute | solution.py:8
  33.7 10.5 %collective-permute-start.18 = (f32[4,128]{1,0:T(4,128)S(1)}, f32[4,128]{1,0:T(4,128)S(1)}, u32[]{:S(2)}, u32[]{:S(2)}) collective-permute-start(f32[4,128]{1,0:T(4,128)S(1)} %get-tuple-element.42), channel_id=1, source_target_pairs={{0,8},{4,12},{8,0},{12,4},{1,9},{5,13},{9,1},{13,5},{2,10},{6,14},... | collective-permute-start | bytes 6152 | tf_op jit(solution)/shard_map/clus_exchange/ppermute | solution.py:8
  33.9 8.9 %collective-permute-start.16 = (f32[4,2176]{1,0:T(4,128)S(1)}, f32[4,2176]{1,0:T(4,128)S(1)}, u32[]{:S(2)}, u32[]{:S(2)}) collective-permute-start(f32[4,2176]{1,0:T(4,128)S(1)} %get-tuple-element.26), channel_id=1, source_target_pairs={{0,12},{4,0},{8,4},{12,8},{1,13},{5,1},{9,5},{13,9},{2,14},{6,2},{... | collective-permute-start | bytes 104456 | tf_op jit(solution)/shard_map/clus_exchange/ppermute | solution.py:8
  35.4 6.5 %collective-permute-start.17 = (f32[4,2176]{1,0:T(4,128)S(1)}, f32[4,2176]{1,0:T(4,128)S(1)}, u32[]{:S(2)}, u32[]{:S(2)}) collective-permute-start(f32[4,2176]{1,0:T(4,128)S(1)} %get-tuple-element.25), channel_id=1, source_target_pairs={{0,4},{4,8},{8,12},{12,0},{1,5},{5,9},{9,13},{13,1},{2,6},{6,10},{... | collective-permute-start | bytes 104456 | tf_op jit(solution)/shard_map/clus_exchange/ppermute | solution.py:8
  37.7 11.5 %collective-permute-start.6 = (f32[4,128]{1,0:T(4,128)S(1)}, f32[4,128]{1,0:T(4,128)S(1)}, u32[]{:S(2)}, u32[]{:S(2)}) collective-permute-start(f32[4,128]{1,0:T(4,128)S(1)} %get-tuple-element.33), channel_id=1, source_target_pairs={{0,8},{4,12},{8,0},{12,4},{1,9},{5,13},{9,1},{13,5},{2,10},{6,14},... | collective-permute-start | bytes 6152 | tf_op jit(solution)/shard_map/clus_exchange/ppermute | solution.py:8
  40.6 7.0 %collective-permute-start.4 = (f32[4,2176]{1,0:T(4,128)S(1)}, f32[4,2176]{1,0:T(4,128)S(1)}, u32[]{:S(2)}, u32[]{:S(2)}) collective-permute-start(f32[4,2176]{1,0:T(4,128)S(1)} %get-tuple-element.20), channel_id=1, source_target_pairs={{0,12},{4,0},{8,4},{12,8},{1,13},{5,1},{9,5},{13,9},{2,14},{6,2},{... | collective-permute-start | bytes 104456 | tf_op jit(solution)/shard_map/clus_exchange/ppermute | solution.py:8
  41.9 5.7 %collective-permute-start.5 = (f32[4,2176]{1,0:T(4,128)S(1)}, f32[4,2176]{1,0:T(4,128)S(1)}, u32[]{:S(2)}, u32[]{:S(2)}) collective-permute-start(f32[4,2176]{1,0:T(4,128)S(1)} %get-tuple-element.19), channel_id=1, source_target_pairs={{0,4},{4,8},{8,12},{12,0},{1,5},{5,9},{9,13},{13,1},{2,6},{6,10},{... | collective-permute-start | bytes 104456 | tf_op jit(solution)/shard_map/clus_exchange/ppermute | solution.py:8
  44.3 6.2 %collective-permute-start.19 = (f32[4,2176]{1,0:T(4,128)S(1)}, f32[4,2176]{1,0:T(4,128)S(1)}, u32[]{:S(2)}, u32[]{:S(2)}) collective-permute-start(f32[4,2176]{1,0:T(4,128)S(1)} %pad_maximum_fusion.21), channel_id=1, source_target_pairs={{0,2},{2,0},{1,3},{3,1},{4,6},{6,4},{5,7},{7,5},{8,10},{10,8},{9,1... | collective-permute-start | bytes 104456 | tf_op jit(solution)/shard_map/pair_sums/ppermute | solution.py:8
  49.2 4.0 %collective-permute-start.7 = (f32[4,2176]{1,0:T(4,128)S(1)}, f32[4,2176]{1,0:T(4,128)S(1)}, u32[]{:S(2)}, u32[]{:S(2)}) collective-permute-start(f32[4,2176]{1,0:T(4,128)S(1)} %pad_maximum_fusion.12), channel_id=1, source_target_pairs={{0,2},{2,0},{1,3},{3,1},{4,6},{6,4},{5,7},{7,5},{8,10},{10,8},{9,1... | collective-permute-start | bytes 104456 | tf_op jit(solution)/shard_map/pair_sums/ppermute | solution.py:8
  55.0 10.5 %collective-permute-start.22 = (f32[4,128]{1,0:T(4,128)S(1)}, f32[4,128]{1,0:T(4,128)S(1)}, u32[]{:S(2)}, u32[]{:S(2)}) collective-permute-start(f32[4,128]{1,0:T(4,128)S(1)} %get-tuple-element.39), channel_id=1, source_target_pairs={{0,8},{4,12},{8,0},{12,4},{1,9},{5,13},{9,1},{13,5},{2,10},{6,14},... | collective-permute-start | bytes 6152 | tf_op jit(solution)/shard_map/clus_exchange/ppermute | solution.py:8
  55.1 8.9 %collective-permute-start.20 = (f32[4,2176]{1,0:T(4,128)S(1)}, f32[4,2176]{1,0:T(4,128)S(1)}, u32[]{:S(2)}, u32[]{:S(2)}) collective-permute-start(f32[4,2176]{1,0:T(4,128)S(1)} %get-tuple-element.24), channel_id=1, source_target_pairs={{0,12},{4,0},{8,4},{12,8},{1,13},{5,1},{9,5},{13,9},{2,14},{6,2},{... | collective-permute-start | bytes 104456 | tf_op jit(solution)/shard_map/clus_exchange/ppermute | solution.py:8
  56.5 6.4 %collective-permute-start.21 = (f32[4,2176]{1,0:T(4,128)S(1)}, f32[4,2176]{1,0:T(4,128)S(1)}, u32[]{:S(2)}, u32[]{:S(2)}) collective-permute-start(f32[4,2176]{1,0:T(4,128)S(1)} %get-tuple-element.23), channel_id=1, source_target_pairs={{0,4},{4,8},{8,12},{12,0},{1,5},{5,9},{9,13},{13,1},{2,6},{6,10},{... | collective-permute-start | bytes 104456 | tf_op jit(solution)/shard_map/clus_exchange/ppermute | solution.py:8
  58.9 11.3 %collective-permute-start.10 = (f32[4,128]{1,0:T(4,128)S(1)}, f32[4,128]{1,0:T(4,128)S(1)}, u32[]{:S(2)}, u32[]{:S(2)}) collective-permute-start(f32[4,128]{1,0:T(4,128)S(1)} %get-tuple-element.30), channel_id=1, source_target_pairs={{0,8},{4,12},{8,0},{12,4},{1,9},{5,13},{9,1},{13,5},{2,10},{6,14},... | collective-permute-start | bytes 6152 | tf_op jit(solution)/shard_map/clus_exchange/ppermute | solution.py:8
  61.8 6.8 %collective-permute-start.8 = (f32[4,2176]{1,0:T(4,128)S(1)}, f32[4,2176]{1,0:T(4,128)S(1)}, u32[]{:S(2)}, u32[]{:S(2)}) collective-permute-start(f32[4,2176]{1,0:T(4,128)S(1)} %get-tuple-element.18), channel_id=1, source_target_pairs={{0,12},{4,0},{8,4},{12,8},{1,13},{5,1},{9,5},{13,9},{2,14},{6,2},{... | collective-permute-start | bytes 104456 | tf_op jit(solution)/shard_map/clus_exchange/ppermute | solution.py:8
  62.9 5.7 %collective-permute-start.9 = (f32[4,2176]{1,0:T(4,128)S(1)}, f32[4,2176]{1,0:T(4,128)S(1)}, u32[]{:S(2)}, u32[]{:S(2)}) collective-permute-start(f32[4,2176]{1,0:T(4,128)S(1)} %get-tuple-element.17), channel_id=1, source_target_pairs={{0,4},{4,8},{8,12},{12,0},{1,5},{5,9},{9,13},{13,1},{2,6},{6,10},{... | collective-permute-start | bytes 104456 | tf_op jit(solution)/shard_map/clus_exchange/ppermute | solution.py:8
  65.5 6.0 %collective-permute-start.23 = (f32[4,2176]{1,0:T(4,128)S(1)}, f32[4,2176]{1,0:T(4,128)S(1)}, u32[]{:S(2)}, u32[]{:S(2)}) collective-permute-start(f32[4,2176]{1,0:T(4,128)S(1)} %pad_maximum_fusion.24), channel_id=1, source_target_pairs={{0,2},{2,0},{1,3},{3,1},{4,6},{6,4},{5,7},{7,5},{8,10},{10,8},{9,1... | collective-permute-start | bytes 104456 | tf_op jit(solution)/shard_map/pair_sums/ppermute | solution.py:8
  70.2 4.0 %collective-permute-start.11 = (f32[4,2176]{1,0:T(4,128)S(1)}, f32[4,2176]{1,0:T(4,128)S(1)}, u32[]{:S(2)}, u32[]{:S(2)}) collective-permute-start(f32[4,2176]{1,0:T(4,128)S(1)} %pad_maximum_fusion.15), channel_id=1, source_target_pairs={{0,2},{2,0},{1,3},{3,1},{4,6},{6,4},{5,7},{7,5},{8,10},{10,8},{9,1... | collective-permute-start | bytes 104456 | tf_op jit(solution)/shard_map/pair_sums/ppermute | solution.py:8

commit v4 on v2

--- a/solution.py
+++ b/solution.py
@@ -44,9 +44,11 @@
     relative = (near_src // clusters_here - my_index) % peer_count
     slot = jnp.where(relative == 0, 0, jnp.where(relative == 1, 1, 2))
     near_index = slot * clusters_here + near_src % clusters_here
+    near_pick = (near_index[:, None] == jnp.arange(3 * clusters_here)[None, :]).astype(jnp.bfloat16)
 
     far_local = far_src - my_base
     far_hot = (far_tgt[:, None] == jnp.arange(cluster_count)[None, :]).astype(jnp.float32)
+    far_pick = (far_local[:, None] == jnp.arange(clusters_here)[None, :]).astype(jnp.bfloat16)
     row_f32 = row_basis.astype(jnp.float32)
 
     iterate = (coefficients[degree_top] * source).astype(jnp.bfloat16)
@@ -54,7 +56,9 @@
     for step in range(degree_top):
         degree = degree_top - 1 - step
         with jax.named_scope("far_partial"):
-            far_input = iterate[:, far_local, :]
+            far_input = jnp.einsum(
+                "jc,rcl->rjl", far_pick, iterate, preferred_element_type=jnp.bfloat16
+            )
             coef = jnp.einsum(
                 "rjl,jkl->jrk", far_input, col_basis, preferred_element_type=jnp.float32
             )
@@ -87,7 +91,9 @@
                 far_mine = far_mine + incoming
         with jax.named_scope("near_partial"):
             extended = jnp.concatenate([iterate, from_plus, from_minus], axis=1)
-            gathered = extended[:, near_index, :]
+            gathered = jnp.einsum(
+                "jc,rcs->rjs", near_pick, extended, preferred_element_type=jnp.bfloat16
+            )
             contrib = jnp.einsum(
                 "rjs,jts->rjt", gathered, near_blocks, preferred_element_type=jnp.float32
             )
@@ -108,7 +114,8 @@
             far_field = jnp.einsum(
                 "rck,ckl->rcl", coef_sum, row_f32, precision=lax.Precision.HIGHEST
             )
-        result = near_sum + far_field + coefficients[degree] * source
+        source_late, near_sum = lax.optimization_barrier((source, near_sum))
+        result = near_sum + far_field + coefficients[degree] * source_late
         iterate = result.astype(jnp.bfloat16)
     return result.reshape(rhs_here, clusters_here * leaf_size)
 

time: 56 us -> 55.8 us (level)
  matrix products: 6.06 us -> 11.4 us
  local copies, waits for them, and re-layouts: 6.13 us -> 3.23 us
  waiting for transfers between devices: 19.5 us -> 17.2 us
  other arithmetic: 4.99 us -> 2.87 us
  starting transfers between devices: 18.5 us -> 20.4 us
    gather x6 -> x0, local copies, waits for them, and re-layouts: 3.46 us -> none  [the longest x3 1.79 us: shards(): far_input = iterate[:, far_local, :]]
    convert_element_type x3, other arithmetic: 3.45 us -> 0.59 us  [shards(): iterate.reshape(rhs_here, clusters_here * leaf_size).astype(jnp.float32)]
    dot_general x3, matrix products: 0.48 us -> 3.12 us  [shards(): jnp.einsum('rck,ckl->rcl', coef_sum, row_f32, precision=lax.Precision.HIG...]
    ppermute x12, waiting for transfers between devices: 19.5 us -> 17.2 us  [shift(): lax.ppermute(value, axis, [(i, (i + step) % count) for i in range(count)])]
    ppermute x12, starting transfers between devices: 18.5 us -> 20.4 us  [shift(): lax.ppermute(value, axis, [(i, (i + step) % count) for i in range(count)])]
    dot_general x0 -> x6, matrix products: none -> 1.89 us  [the longest x3 1.08 us: shards(): jnp.einsum('jc,rcs->rjs', near_pick, extended, preferred_element_type=jnp...]
    convert_element_type x2 -> x1, other arithmetic: 0.03 us -> 1.42 us  [shards(): iterate = (coefficients[degree_top] * source).astype(jnp.bfloat16)]
    select_n x2 -> x0, other arithmetic: 0.68 us -> none  [the longest x1 0.66 us: shards(): far_input = iterate[:, far_local, :]]
  transfers between devices with their start and end apart: 12 -> 12, of which waited for: 8 -> 9; matrix products, arithmetic and copies ran while one was open for 8% -> 9% of each run, Pallas kernels for 0% -> 0%
where the time goes in v4:
time: 55.8 us; the launch traced here: 55.6 us
  starting transfers between devices  20.4 us (37%)
  waiting for transfers between devices  17.2 us (31%)
  matrix products  11.4 us (20%)
  local copies, waits for them, and re-layouts  3.23 us (6%)
  other arithmetic  2.87 us (5%)
    ppermute x12, starting transfers between devices, shift(): lax.ppermute(value, axis, [(i, (i + step) % count) for i in range(count)])  20.4 us
    ppermute x12, waiting for transfers between devices, shift(): lax.ppermute(value, axis, [(i, (i + step) % count) for i in range(count)])  17.2 us
    dot_general x3, matrix products, shards(): jnp.einsum('rck,ckl->rcl', coef_sum, row_f32, precision=lax.Precision.HIG...  3.12 us
    dot_general x3, matrix products, shards(): jnp.einsum('jc,jm->cm', far_hot, coef, precision=lax.Precision.HIGHEST)  1.94 us
    dot_general x3, matrix products, shards(): jnp.einsum('rjs,jts->rjt', gathered, near_blocks, preferred_element_type=...  1.91 us
    dot_general x3, matrix products, shards(): jnp.einsum('rjl,jkl->jrk', far_input, col_basis, preferred_element_type=j...  1.87 us
    slice x1, local copies, waits for them, and re-layouts, shards(): result = near_sum + far_field + coefficients[degree] * source_late  1.5 us
    convert_element_type x1, other arithmetic, shards(): iterate = (coefficients[degree_top] * source).astype(jnp.bfloat16)  1.42 us
  transfers between devices with their start and end apart: 12, of which 9 were waited for; matrix products, arithmetic and copies ran while one was open for 9% of the time, Pallas kernels for 0%

profile of v4, /device:TPU:0, one launch (start us, length us, event | category | flops | bytes accessed | tf_op | source)
XLA Modules:
  0.0 55.6 jit_solution(1348172934411154995)
XLA Ops:
  0.1 1.5 %fusion.81 = (f32[1]{0:T(128)}, f32[1]{0:T(128)}, f32[1]{0:T(128)}, f32[1]{0:T(128)}) fusion(f32[4]{0:T(128)} %param.10), kind=kLoop, calls=%fused_computation.135 | loop fusion | bytes 32 | tf_op jit(solution)/shard_map/slice | solution.py:118
  1.6 0.7 %broadcast_subtract_fusion = s32[64]{0:T(128)S(1)} fusion(s32[64]{0:T(128)} %param.16, s32[]{:T(128)S(6)} %mul.35), kind=kLoop, calls=%fused_computation.130 | loop fusion | flops 64 | bytes 516 | tf_op jit(solution)/shard_map/sub | solution.py:49
  2.2 1.4 %multiply_convert_fusion.1 = bf16[8,8,256]{2,0,1:T(8,128)(2,1)S(1)} fusion(f32[8,8,256]{2,0,1:T(8,128)} %bitcast.176, f32[]{:T(128)} %bitcast.2), kind=kLoop, calls=%fused_computation.60 | loop fusion | flops 32768 | bytes 98308 | tf_op jit(solution)/shard_map/convert_element_type | solution.py:54
  3.9 1.3 %fusion.12 = f32[64,8,16]{2,1,0:T(8,128)S(1)} fusion(bf16[64,16,256]{2,1,0:T(8,128)(2,1)} %param.15, bf16[8,256,64]{1,2,0:T(8,128)(2,1)S(1)} %fusion.34), kind=kOutput, calls=%fused_computation.24 | convolution fusion | flops 4194304 | bytes 819200 | tf_op jit(solution)/shard_map/far_partial/rjl,jkl->jrk/dot_general | solution.py:62
  5.4 1.1 %convolution_bitcast_fusion.5 = f32[4,8,8,16]{3,2,1,0:T(8,128)S(1)} fusion(f32[64,8,16]{0,2,1:T(8,128)S(1)} %copy.13, s32[4,8]{1,0:T(4,128)S(1)} %multiply_add_fusion, s32[64]{0:T(128)} %param.17), kind=kOutput, calls=%fused_computation.5 | convolution fusion | flops 3147776 | bytes 49536 | tf_op jit(solution)/shard_map/far_partial/jc,jm->cm/dot_general | solution.py:66
  6.6 4.1 %collective-permute-start.2 = (f32[8,128]{1,0:T(8,128)S(1)}, f32[8,128]{1,0:T(8,128)S(1)}, u32[]{:S(2)}, u32[]{:S(2)}) collective-permute-start(f32[8,128]{1,0:T(8,128)S(1)} %get-tuple-element.30), channel_id=1, source_target_pairs={{0,8},{4,12},{8,0},{12,4},{1,9},{5,13},{9,1},{13,5},{2,10},{6,14},... | collective-permute-start | bytes 12296 | tf_op jit(solution)/shard_map/clus_exchange/ppermute | solution.py:8
  10.7 0.6 %fusion.29 = f32[8,2048]{1,0:T(8,128)S(1)} fusion(f32[8,2048]{1,0:T(8,128)S(1)} %copy-done.2, f32[]{:T(128)} %bitcast.2), kind=kLoop, calls=%fused_computation.61 | loop fusion | flops 49152 | bytes 131076 | tf_op jit(solution)/shard_map/clus_exchange/convert_element_type | solution.py:73
  11.3 1.6 %collective-permute-start.1 = (f32[8,2176]{1,0:T(8,128)S(1)}, f32[8,2176]{1,0:T(8,128)S(1)}, u32[]{:S(2)}, u32[]{:S(2)}) collective-permute-start(f32[8,2176]{1,0:T(8,128)S(1)} %get-tuple-element.21), channel_id=1, source_target_pairs={{0,4},{4,8},{8,12},{12,0},{1,5},{5,9},{9,13},{13,1},{2,6},{6,10},{... | collective-permute-start | bytes 208904 | tf_op jit(solution)/shard_map/clus_exchange/ppermute | solution.py:8
  12.9 2.2 %collective-permute-start = (f32[8,2176]{1,0:T(8,128)S(1)}, f32[8,2176]{1,0:T(8,128)S(1)}, u32[]{:S(2)}, u32[]{:S(2)}) collective-permute-start(f32[8,2176]{1,0:T(8,128)S(1)} %get-tuple-element.22), channel_id=1, source_target_pairs={{0,12},{4,0},{8,4},{12,8},{1,13},{5,1},{9,5},{13,9},{2,14},{6,2},{... | collective-permute-start | bytes 208904 | tf_op jit(solution)/shard_map/clus_exchange/ppermute | solution.py:8
  15.2 2.4 %collective-permute-done.1 = f32[8,2176]{1,0:T(8,128)S(1)} collective-permute-done((f32[8,2176]{1,0:T(8,128)S(1)}, f32[8,2176]{1,0:T(8,128)S(1)}, u32[]{:S(2)}, u32[]{:S(2)}) %collective-permute-start.1) | collective-permute-done | bytes 69664 | tf_op jit(solution)/shard_map/clus_exchange/ppermute | solution.py:8
  18.0 0.4 convolution_bitcast_fusion.2
  18.6 0.6 %fusion.82 = f32[16,8,256]{2,1,0:T(8,128)S(1)} fusion(bf16[8,16,256]{2,0,1:T(8,128)(2,1)S(1)} %copy.23, bf16[16,256,256]{2,1,0:T(8,128)(2,1)S(1)} %copy-done), kind=kOutput, calls=%fused_computation.136 | convolution fusion | flops 16777216 | bytes 2293760 | tf_op jit(solution)/shard_map/near_partial/rjs,jts->rjt/dot_general | solution.py:97
  19.6 1.6 %collective-permute-start.3 = (f32[8,2176]{1,0:T(8,128)S(1)}, f32[8,2176]{1,0:T(8,128)S(1)}, u32[]{:S(2)}, u32[]{:S(2)}) collective-permute-start(f32[8,2176]{1,0:T(8,128)S(1)} %pad_maximum_fusion.5), channel_id=1, source_target_pairs={{0,2},{2,0},{1,3},{3,1},{4,6},{6,4},{5,7},{7,5},{8,10},{10,8},{9,1... | collective-permute-start | bytes 208904 | tf_op jit(solution)/shard_map/pair_sums/ppermute | solution.py:8
  21.1 2.8 %collective-permute-done.3 = f32[8,2176]{1,0:T(8,128)S(1)} collective-permute-done((f32[8,2176]{1,0:T(8,128)S(1)}, f32[8,2176]{1,0:T(8,128)S(1)}, u32[]{:S(2)}, u32[]{:S(2)}) %collective-permute-start.3) | collective-permute-done | bytes 69664 | tf_op jit(solution)/shard_map/pair_sums/ppermute | solution.py:8
  24.1 0.8 %fusion.6 = bf16[8,8,256]{2,0,1:T(8,128)(2,1)S(1)} fusion(f32[8,8,256]{2,0,1:T(8,128)S(1)} %bitcast.189, bf16[8,16,256]{2,1,0:T(8,128)(2,1)S(1)} %copy-done.3, f32[8,8,256]{2,0,1:T(8,128)S(1)} %bitcast.177, f32[8,8,16]{2,1,0:T(8,128)S(1)} %reshape.114, f32[]{:T(128)} %bitcast.24), kind=kOutput, calls=%fused_computation.18 | convolution fusion | flops 3211264 | bytes 233476 | tf_op jit(solution)/shard_map/far_field/rck,ckl->rcl/dot_general | solution.py:114
  25.6 0.4 convolution_bitcast_fusion.4
  26.2 3.8 %collective-permute-start.4 = (f32[8,2176]{1,0:T(8,128)S(1)}, f32[8,2176]{1,0:T(8,128)S(1)}, u32[]{:S(2)}, u32[]{:S(2)}) collective-permute-start(f32[8,2176]{1,0:T(8,128)S(1)} %get-tuple-element.20), channel_id=1, source_target_pairs={{0,12},{4,0},{8,4},{12,8},{1,13},{5,1},{9,5},{13,9},{2,14},{6,2},{... | collective-permute-start | bytes 208904 | tf_op jit(solution)/shard_map/clus_exchange/ppermute | solution.py:8
  30.1 2.3 %collective-permute-done.5 = f32[8,2176]{1,0:T(8,128)S(1)} collective-permute-done((f32[8,2176]{1,0:T(8,128)S(1)}, f32[8,2176]{1,0:T(8,128)S(1)}, u32[]{:S(2)}, u32[]{:S(2)}) %collective-permute-start.5) | collective-permute-done | bytes 69664 | tf_op jit(solution)/shard_map/clus_exchange/ppermute | solution.py:8
  33.0 0.6 %fusion.83 = f32[16,8,256]{2,1,0:T(8,128)S(1)} fusion(bf16[8,16,256]{2,0,1:T(8,128)(2,1)S(1)} %copy.28, bf16[16,256,256]{2,1,0:T(8,128)(2,1)S(1)} %copy-done), kind=kOutput, calls=%fused_computation.137 | convolution fusion | flops 16777216 | bytes 2293760 | tf_op jit(solution)/shard_map/near_partial/rjs,jts->rjt/dot_general | solution.py:97
  33.9 0.6 %collective-permute-done.6 = f32[8,128]{1,0:T(8,128)S(1)} collective-permute-done((f32[8,128]{1,0:T(8,128)S(1)}, f32[8,128]{1,0:T(8,128)S(1)}, u32[]{:S(2)}, u32[]{:S(2)}) %collective-permute-start.6) | collective-permute-done | bytes 4128 | tf_op jit(solution)/shard_map/clus_exchange/ppermute | solution.py:8
  34.6 1.6 %collective-permute-start.7 = (f32[8,2176]{1,0:T(8,128)S(1)}, f32[8,2176]{1,0:T(8,128)S(1)}, u32[]{:S(2)}, u32[]{:S(2)}) collective-permute-start(f32[8,2176]{1,0:T(8,128)S(1)} %pad_maximum_fusion.8), channel_id=1, source_target_pairs={{0,2},{2,0},{1,3},{3,1},{4,6},{6,4},{5,7},{7,5},{8,10},{10,8},{9,1... | collective-permute-start | bytes 208904 | tf_op jit(solution)/shard_map/pair_sums/ppermute | solution.py:8
  36.1 2.8 %collective-permute-done.7 = f32[8,2176]{1,0:T(8,128)S(1)} collective-permute-done((f32[8,2176]{1,0:T(8,128)S(1)}, f32[8,2176]{1,0:T(8,128)S(1)}, u32[]{:S(2)}, u32[]{:S(2)}) %collective-permute-start.7) | collective-permute-done | bytes 69664 | tf_op jit(solution)/shard_map/pair_sums/ppermute | solution.py:8
  39.1 0.8 %fusion.7 = bf16[8,8,256]{2,0,1:T(8,128)(2,1)S(1)} fusion(f32[8,8,256]{2,0,1:T(8,128)S(1)} %bitcast.190, bf16[8,16,256]{2,1,0:T(8,128)(2,1)S(1)} %copy-done.3, f32[8,8,256]{2,0,1:T(8,128)S(1)} %bitcast.178, f32[8,8,16]{2,1,0:T(8,128)S(1)} %reshape.121, f32[]{:T(128)} %bitcast.45), kind=kOutput, calls=%fused_computation.19 | convolution fusion | flops 3211264 | bytes 233476 | tf_op jit(solution)/shard_map/far_field/rck,ckl->rcl/dot_general | solution.py:114
  40.6 0.4 convolution_bitcast_fusion.3
  41.2 0.7 %collective-permute-start.9 = (f32[8,2176]{1,0:T(8,128)S(1)}, f32[8,2176]{1,0:T(8,128)S(1)}, u32[]{:S(2)}, u32[]{:S(2)}) collective-permute-start(f32[8,2176]{1,0:T(8,128)S(1)} %get-tuple-element.17), channel_id=1, source_target_pairs={{0,4},{4,8},{8,12},{12,0},{1,5},{5,9},{9,13},{13,1},{2,6},{6,10},{... | collective-permute-start | bytes 208904 | tf_op jit(solution)/shard_map/clus_exchange/ppermute | solution.py:8
  41.8 3.2 %collective-permute-start.8 = (f32[8,2176]{1,0:T(8,128)S(1)}, f32[8,2176]{1,0:T(8,128)S(1)}, u32[]{:S(2)}, u32[]{:S(2)}) collective-permute-start(f32[8,2176]{1,0:T(8,128)S(1)} %get-tuple-element.18), channel_id=1, source_target_pairs={{0,12},{4,0},{8,4},{12,8},{1,13},{5,1},{9,5},{13,9},{2,14},{6,2},{... | collective-permute-start | bytes 208904 | tf_op jit(solution)/shard_map/clus_exchange/ppermute | solution.py:8
  45.1 2.4 %collective-permute-done.9 = f32[8,2176]{1,0:T(8,128)S(1)} collective-permute-done((f32[8,2176]{1,0:T(8,128)S(1)}, f32[8,2176]{1,0:T(8,128)S(1)}, u32[]{:S(2)}, u32[]{:S(2)}) %collective-permute-start.9) | collective-permute-done | bytes 69664 | tf_op jit(solution)/shard_map/clus_exchange/ppermute | solution.py:8
  48.1 0.6 %fusion.84 = f32[16,8,256]{2,1,0:T(8,128)S(1)} fusion(bf16[8,16,256]{2,0,1:T(8,128)(2,1)S(1)} %copy.33, bf16[16,256,256]{2,1,0:T(8,128)(2,1)S(1)} %copy-done), kind=kOutput, calls=%fused_computation.138 | convolution fusion | flops 16777216 | bytes 2293760 | tf_op jit(solution)/shard_map/near_partial/rjs,jts->rjt/dot_general | solution.py:97
  49.0 0.6 %collective-permute-done.10 = f32[8,128]{1,0:T(8,128)S(1)} collective-permute-done((f32[8,128]{1,0:T(8,128)S(1)}, f32[8,128]{1,0:T(8,128)S(1)}, u32[]{:S(2)}, u32[]{:S(2)}) %collective-permute-start.10) | collective-permute-done | bytes 4128 | tf_op jit(solution)/shard_map/clus_exchange/ppermute | solution.py:8
  49.6 1.6 %collective-permute-start.11 = (f32[8,2176]{1,0:T(8,128)S(1)}, f32[8,2176]{1,0:T(8,128)S(1)}, u32[]{:S(2)}, u32[]{:S(2)}) collective-permute-start(f32[8,2176]{1,0:T(8,128)S(1)} %pad_maximum_fusion.11), channel_id=1, source_target_pairs={{0,2},{2,0},{1,3},{3,1},{4,6},{6,4},{5,7},{7,5},{8,10},{10,8},{9,1... | collective-permute-start | bytes 208904 | tf_op jit(solution)/shard_map/pair_sums/ppermute | solution.py:8
  51.1 2.8 %collective-permute-done.11 = f32[8,2176]{1,0:T(8,128)S(1)} collective-permute-done((f32[8,2176]{1,0:T(8,128)S(1)}, f32[8,2176]{1,0:T(8,128)S(1)}, u32[]{:S(2)}, u32[]{:S(2)}) %collective-permute-start.11) | collective-permute-done | bytes 69664 | tf_op jit(solution)/shard_map/pair_sums/ppermute | solution.py:8
  54.1 1.5 %fusion.1 = f32[8,8,256]{2,0,1:T(8,128)} fusion(f32[8,8,256]{2,0,1:T(8,128)S(1)} %bitcast.188, bf16[8,16,256]{2,1,0:T(8,128)(2,1)S(1)} %copy-done.3, f32[8,8,256]{2,0,1:T(8,128)S(1)} %bitcast.179, f32[8,8,16]{2,1,0:T(8,128)S(1)} %reshape.128, f32[]{:T(128)} %bitcast.65), kind=kOutput, calls=%fused_computation.8 | convolution fusion | flops 3194880 | bytes 266244 | tf_op jit(solution)/shard_map/far_field/rck,ckl->rcl/dot_general | solution.py:114
  (81 shorter events, 5.1 us)
Async XLA Ops:
  0.0 18.6 %copy-start = (bf16[16,256,256]{2,1,0:T(8,128)(2,1)S(1)}, bf16[16,256,256]{2,1,0:T(8,128)(2,1)}, u32[]{:S(2)}) copy-start(bf16[16,256,256]{2,1,0:T(8,128)(2,1)} %param.11) | copy-start | bytes 6291460
  0.0 10.7 %copy-start.2 = (f32[8,2048]{1,0:T(8,128)S(1)}, f32[8,2048]{1,0:T(8,128)}, u32[]{:S(2)}) copy-start(f32[8,2048]{1,0:T(8,128)} %param.9) | copy-start | bytes 196612
  0.0 15.2 %copy-start.5 = (s32[16]{0:T(128)S(1)}, s32[16]{0:T(128)}, u32[]{:S(2)}) copy-start(s32[16]{0:T(128)} %param.13) | copy-start | bytes 196
  0.0 15.2 %copy-start.6 = (s32[16]{0:T(128)S(1)}, s32[16]{0:T(128)}, u32[]{:S(2)}) copy-start(s32[16]{0:T(128)} %param.12) | copy-start | bytes 196
  6.6 12.9 %collective-permute-start.2 = (f32[8,128]{1,0:T(8,128)S(1)}, f32[8,128]{1,0:T(8,128)S(1)}, u32[]{:S(2)}, u32[]{:S(2)}) collective-permute-start(f32[8,128]{1,0:T(8,128)S(1)} %get-tuple-element.30), channel_id=1, source_target_pairs={{0,8},{4,12},{8,0},{12,4},{1,9},{5,13},{9,1},{13,5},{2,10},{6,14},... | collective-permute-start | bytes 12296 | tf_op jit(solution)/shard_map/clus_exchange/ppermute | solution.py:8
  11.3 6.3 %collective-permute-start.1 = (f32[8,2176]{1,0:T(8,128)S(1)}, f32[8,2176]{1,0:T(8,128)S(1)}, u32[]{:S(2)}, u32[]{:S(2)}) collective-permute-start(f32[8,2176]{1,0:T(8,128)S(1)} %get-tuple-element.21), channel_id=1, source_target_pairs={{0,4},{4,8},{8,12},{12,0},{1,5},{5,9},{9,13},{13,1},{2,6},{6,10},{... | collective-permute-start | bytes 208904 | tf_op jit(solution)/shard_map/clus_exchange/ppermute | solution.py:8
  12.9 5.1 %collective-permute-start = (f32[8,2176]{1,0:T(8,128)S(1)}, f32[8,2176]{1,0:T(8,128)S(1)}, u32[]{:S(2)}, u32[]{:S(2)}) collective-permute-start(f32[8,2176]{1,0:T(8,128)S(1)} %get-tuple-element.22), channel_id=1, source_target_pairs={{0,12},{4,0},{8,4},{12,8},{1,13},{5,1},{9,5},{13,9},{2,14},{6,2},{... | collective-permute-start | bytes 208904 | tf_op jit(solution)/shard_map/clus_exchange/ppermute | solution.py:8
  18.0 6.0 %copy-start.3 = (bf16[8,16,256]{2,1,0:T(8,128)(2,1)S(1)}, bf16[8,16,256]{2,1,0:T(8,128)(2,1)}, u32[]{:S(2)}) copy-start(bf16[8,16,256]{2,1,0:T(8,128)(2,1)} %param.14) | copy-start | bytes 196612
  18.4 6.8 %copy-start.1 = (bf16[64,16,256]{2,1,0:T(8,128)(2,1)S(1)}, bf16[64,16,256]{2,1,0:T(8,128)(2,1)}, u32[]{:S(2)}) copy-start(bf16[64,16,256]{2,1,0:T(8,128)(2,1)} %param.15) | copy-start | bytes 1572868
  18.6 7.0 %copy-start.4 = (s32[64]{0:T(128)S(1)}, s32[64]{0:T(128)}, u32[]{:S(2)}) copy-start(s32[64]{0:T(128)} %param.17) | copy-start | bytes 772
  19.6 4.4 %collective-permute-start.3 = (f32[8,2176]{1,0:T(8,128)S(1)}, f32[8,2176]{1,0:T(8,128)S(1)}, u32[]{:S(2)}, u32[]{:S(2)}) collective-permute-start(f32[8,2176]{1,0:T(8,128)S(1)} %pad_maximum_fusion.5), channel_id=1, source_target_pairs={{0,2},{2,0},{1,3},{3,1},{4,6},{6,4},{5,7},{7,5},{8,10},{10,8},{9,1... | collective-permute-start | bytes 208904 | tf_op jit(solution)/shard_map/pair_sums/ppermute | solution.py:8
  26.2 6.2 %collective-permute-start.5 = (f32[8,2176]{1,0:T(8,128)S(1)}, f32[8,2176]{1,0:T(8,128)S(1)}, u32[]{:S(2)}, u32[]{:S(2)}) collective-permute-start(f32[8,2176]{1,0:T(8,128)S(1)} %get-tuple-element.19), channel_id=1, source_target_pairs={{0,4},{4,8},{8,12},{12,0},{1,5},{5,9},{9,13},{13,1},{2,6},{6,10},{... | collective-permute-start | bytes 208904 | tf_op jit(solution)/shard_map/clus_exchange/ppermute | solution.py:8
  26.2 6.2 %collective-permute-start.4 = (f32[8,2176]{1,0:T(8,128)S(1)}, f32[8,2176]{1,0:T(8,128)S(1)}, u32[]{:S(2)}, u32[]{:S(2)}) collective-permute-start(f32[8,2176]{1,0:T(8,128)S(1)} %get-tuple-element.20), channel_id=1, source_target_pairs={{0,12},{4,0},{8,4},{12,8},{1,13},{5,1},{9,5},{13,9},{2,14},{6,2},{... | collective-permute-start | bytes 208904 | tf_op jit(solution)/shard_map/clus_exchange/ppermute | solution.py:8
  30.1 4.5 %collective-permute-start.6 = (f32[8,128]{1,0:T(8,128)S(1)}, f32[8,128]{1,0:T(8,128)S(1)}, u32[]{:S(2)}, u32[]{:S(2)}) collective-permute-start(f32[8,128]{1,0:T(8,128)S(1)} %get-tuple-element.27), channel_id=1, source_target_pairs={{0,8},{4,12},{8,0},{12,4},{1,9},{5,13},{9,1},{13,5},{2,10},{6,14},... | collective-permute-start | bytes 12296 | tf_op jit(solution)/shard_map/clus_exchange/ppermute | solution.py:8
  34.6 4.4 %collective-permute-start.7 = (f32[8,2176]{1,0:T(8,128)S(1)}, f32[8,2176]{1,0:T(8,128)S(1)}, u32[]{:S(2)}, u32[]{:S(2)}) collective-permute-start(f32[8,2176]{1,0:T(8,128)S(1)} %pad_maximum_fusion.8), channel_id=1, source_target_pairs={{0,2},{2,0},{1,3},{3,1},{4,6},{6,4},{5,7},{7,5},{8,10},{10,8},{9,1... | collective-permute-start | bytes 208904 | tf_op jit(solution)/shard_map/pair_sums/ppermute | solution.py:8
  41.2 6.3 %collective-permute-start.9 = (f32[8,2176]{1,0:T(8,128)S(1)}, f32[8,2176]{1,0:T(8,128)S(1)}, u32[]{:S(2)}, u32[]{:S(2)}) collective-permute-start(f32[8,2176]{1,0:T(8,128)S(1)} %get-tuple-element.17), channel_id=1, source_target_pairs={{0,4},{4,8},{8,12},{12,0},{1,5},{5,9},{9,13},{13,1},{2,6},{6,10},{... | collective-permute-start | bytes 208904 | tf_op jit(solution)/shard_map/clus_exchange/ppermute | solution.py:8
  41.8 5.6 %collective-permute-start.8 = (f32[8,2176]{1,0:T(8,128)S(1)}, f32[8,2176]{1,0:T(8,128)S(1)}, u32[]{:S(2)}, u32[]{:S(2)}) collective-permute-start(f32[8,2176]{1,0:T(8,128)S(1)} %get-tuple-element.18), channel_id=1, source_target_pairs={{0,12},{4,0},{8,4},{12,8},{1,13},{5,1},{9,5},{13,9},{2,14},{6,2},{... | collective-permute-start | bytes 208904 | tf_op jit(solution)/shard_map/clus_exchange/ppermute | solution.py:8
  45.1 4.5 %collective-permute-start.10 = (f32[8,128]{1,0:T(8,128)S(1)}, f32[8,128]{1,0:T(8,128)S(1)}, u32[]{:S(2)}, u32[]{:S(2)}) collective-permute-start(f32[8,128]{1,0:T(8,128)S(1)} %get-tuple-element.24), channel_id=1, source_target_pairs={{0,8},{4,12},{8,0},{12,4},{1,9},{5,13},{9,1},{13,5},{2,10},{6,14},... | collective-permute-start | bytes 12296 | tf_op jit(solution)/shard_map/clus_exchange/ppermute | solution.py:8
  49.6 4.4 %collective-permute-start.11 = (f32[8,2176]{1,0:T(8,128)S(1)}, f32[8,2176]{1,0:T(8,128)S(1)}, u32[]{:S(2)}, u32[]{:S(2)}) collective-permute-start(f32[8,2176]{1,0:T(8,128)S(1)} %pad_maximum_fusion.11), channel_id=1, source_target_pairs={{0,2},{2,0},{1,3},{3,1},{4,6},{6,4},{5,7},{7,5},{8,10},{10,8},{9,1... | collective-permute-start | bytes 208904 | tf_op jit(solution)/shard_map/pair_sums/ppermute | solution.py:8

commit v5 on v4

--- a/solution.py
+++ b/solution.py
@@ -53,6 +53,7 @@
 
     iterate = (coefficients[degree_top] * source).astype(jnp.bfloat16)
     result = source
+    scaled = None
     for step in range(degree_top):
         degree = degree_top - 1 - step
         with jax.named_scope("far_partial"):
@@ -63,7 +64,7 @@
                 "rjl,jkl->jrk", far_input, col_basis, preferred_element_type=jnp.float32
             )
             coef = coef.reshape(coef.shape[0], rhs_here * rank_size)
-            partial_value = jnp.einsum("jc,jm->cm", far_hot, coef, precision=lax.Precision.HIGHEST)
+            partial_value = jnp.einsum("jc,jm->cm", far_hot, coef, precision=lax.Precision.HIGH)
             partial_value = partial_value.reshape(peer_count, clusters_here, rhs_here, rank_size)
             partial_value = partial_value.transpose(0, 2, 1, 3).reshape(
                 peer_count, rhs_here, clusters_here * rank_size
@@ -79,6 +80,9 @@
                 carries_iterate = s == 1 or s == peer_count - 1
                 if carries_iterate:
                     outgoing = jnp.concatenate([iterate_wide, outgoing], axis=1)
+                if scaled is None:
+                    source_late, outgoing = lax.optimization_barrier((source, outgoing))
+                    scaled = [coefficients[d] * source_late for d in range(degree_top)]
                 incoming = shift(outgoing, "clus", peer_count, s)
                 if carries_iterate:
                     neighbour = incoming[:, :iterate_size].astype(jnp.bfloat16)
@@ -98,7 +102,7 @@
                 "rjs,jts->rjt", gathered, near_blocks, preferred_element_type=jnp.float32
             )
             near_part = jnp.einsum(
-                "rjt,jc->rct", contrib, target_hot, precision=lax.Precision.HIGHEST
+                "rjt,jc->rct", contrib, target_hot, precision=lax.Precision.HIGH
             )
         with jax.named_scope("pair_sums"):
             near_flat = near_part.reshape(rhs_here, clusters_here * leaf_size)
@@ -112,10 +116,11 @@
             )
         with jax.named_scope("far_field"):
             far_field = jnp.einsum(
-                "rck,ckl->rcl", coef_sum, row_f32, precision=lax.Precision.HIGHEST
+                "rck,ckl->rcl", coef_sum, row_f32, precision=lax.Precision.HIGH
             )
-        source_late, near_sum = lax.optimization_barrier((source, near_sum))
-        result = near_sum + far_field + coefficients[degree] * source_late
+        if scaled is None:
+            scaled = [coefficients[d] * source for d in range(degree_top)]
+        result = near_sum + far_field + scaled[degree]
         iterate = result.astype(jnp.bfloat16)
     return result.reshape(rhs_here, clusters_here * leaf_size)
 

time: 55.8 us -> 55.6 us (level)
  matrix products: 11.4 us -> 8.35 us
  other arithmetic: 2.87 us -> 5.55 us
    dot_general x9, matrix products: 5.72 us -> 2.68 us  [the longest x3 1.68 us: shards(): jnp.einsum('jc,jm->cm', far_hot, coef, precision=lax.Precision.HIGH)]
    convert_element_type x0 -> x2, other arithmetic: none -> 1.35 us  [shards(): iterate = result.astype(jnp.bfloat16)]
    add x0 -> x1, other arithmetic: none -> 1.34 us  [shards(): result = near_sum + far_field + scaled[degree]]
where the time goes in v5:
time: 55.6 us; the launch traced here: 55.3 us
  starting transfers between devices  20.4 us (37%)
  waiting for transfers between devices  17.2 us (31%)
  matrix products  8.35 us (15%)
  other arithmetic  5.55 us (10%)
  local copies, waits for them, and re-layouts  3.23 us (6%)
    ppermute x12, starting transfers between devices, shift(): lax.ppermute(value, axis, [(i, (i + step) % count) for i in range(count)])  20.4 us
    ppermute x12, waiting for transfers between devices, shift(): lax.ppermute(value, axis, [(i, (i + step) % count) for i in range(count)])  17.2 us
    dot_general x3, matrix products, shards(): jnp.einsum('rjs,jts->rjt', gathered, near_blocks, preferred_element_type=...  1.91 us
    dot_general x3, matrix products, shards(): jnp.einsum('rjl,jkl->jrk', far_input, col_basis, preferred_element_type=j...  1.87 us
    dot_general x3, matrix products, shards(): jnp.einsum('jc,jm->cm', far_hot, coef, precision=lax.Precision.HIGH)  1.68 us
    slice x1, local copies, waits for them, and re-layouts, shards(): scaled = [coefficients[d] * source_late for d in range(degree_top)]  1.5 us
    convert_element_type x1, other arithmetic, shards(): iterate = (coefficients[degree_top] * source).astype(jnp.bfloat16)  1.42 us
    convert_element_type x2, other arithmetic, shards(): iterate = result.astype(jnp.bfloat16)  1.35 us
  transfers between devices with their start and end apart: 12, of which 9 were waited for; matrix products, arithmetic and copies ran while one was open for 9% of the time, Pallas kernels for 0%

profile of v5, /device:TPU:0, one launch (start us, length us, event | category | flops | bytes accessed | tf_op | source)
XLA Modules:
  0.0 55.3 jit_solution(2379666265957013333)
XLA Ops:
  0.1 1.5 %fusion.73 = (f32[1]{0:T(128)}, f32[1]{0:T(128)}, f32[1]{0:T(128)}, f32[1]{0:T(128)}) fusion(f32[4]{0:T(128)} %param.10), kind=kLoop, calls=%fused_computation.130 | loop fusion | bytes 32 | tf_op jit(solution)/shard_map/clus_exchange/slice | solution.py:85
  1.6 0.7 %broadcast_subtract_fusion = s32[64]{0:T(128)S(1)} fusion(s32[64]{0:T(128)} %param.16, s32[]{:T(128)S(6)} %mul.35), kind=kLoop, calls=%fused_computation.125 | loop fusion | flops 64 | bytes 516 | tf_op jit(solution)/shard_map/sub | solution.py:49
  2.2 1.4 %multiply_convert_fusion.1 = bf16[8,8,256]{2,0,1:T(8,128)(2,1)S(1)} fusion(f32[8,8,256]{2,0,1:T(8,128)} %bitcast.160, f32[]{:T(128)} %bitcast.1), kind=kLoop, calls=%fused_computation.55 | loop fusion | flops 32768 | bytes 98308 | tf_op jit(solution)/shard_map/convert_element_type | solution.py:54
  3.9 1.3 %fusion.4 = f32[64,8,16]{2,1,0:T(8,128)S(1)} fusion(bf16[64,16,256]{2,1,0:T(8,128)(2,1)} %param.15, bf16[8,256,64]{1,2,0:T(8,128)(2,1)S(1)} %fusion.26), kind=kOutput, calls=%fused_computation.16 | convolution fusion | flops 4194304 | bytes 819200 | tf_op jit(solution)/shard_map/far_partial/rjl,jkl->jrk/dot_general | solution.py:63
  5.4 1.0 %convolution_bitcast_fusion.5 = f32[4,8,8,16]{3,2,1,0:T(8,128)S(1)} fusion(f32[64,8,16]{0,2,1:T(8,128)S(1)} %copy.13, s32[4,8]{1,0:T(4,128)S(1)} %multiply_add_fusion.1, s32[64]{0:T(128)} %param.17), kind=kOutput, calls=%fused_computation.5 | convolution fusion | flops 1574912 | bytes 49536 | tf_op jit(solution)/shard_map/far_partial/jc,jm->cm/dot_general | solution.py:67
  6.5 4.1 %collective-permute-start.2 = (f32[8,128]{1,0:T(8,128)S(1)}, f32[8,128]{1,0:T(8,128)S(1)}, u32[]{:S(2)}, u32[]{:S(2)}) collective-permute-start(f32[8,128]{1,0:T(8,128)S(1)} %get-tuple-element.21), channel_id=1, source_target_pairs={{0,8},{4,12},{8,0},{12,4},{1,9},{5,13},{9,1},{13,5},{2,10},{6,14},... | collective-permute-start | bytes 12296 | tf_op jit(solution)/shard_map/clus_exchange/ppermute | solution.py:8
  10.6 0.6 %fusion.21 = f32[8,2048]{1,0:T(8,128)S(1)} fusion(f32[8,2048]{1,0:T(8,128)S(1)} %copy-done.2, f32[]{:T(128)} %bitcast.1), kind=kLoop, calls=%fused_computation.56 | loop fusion | flops 49152 | bytes 131076 | tf_op jit(solution)/shard_map/clus_exchange/convert_element_type | solution.py:74
  11.2 1.6 %collective-permute-start.1 = (f32[8,2176]{1,0:T(8,128)S(1)}, f32[8,2176]{1,0:T(8,128)S(1)}, u32[]{:S(2)}, u32[]{:S(2)}) collective-permute-start(f32[8,2176]{1,0:T(8,128)S(1)} %get-tuple-element.7), channel_id=1, source_target_pairs={{0,4},{4,8},{8,12},{12,0},{1,5},{5,9},{9,13},{13,1},{2,6},{6,10},{... | collective-permute-start | bytes 208904 | tf_op jit(solution)/shard_map/clus_exchange/ppermute | solution.py:8
  12.9 2.2 %collective-permute-start = (f32[8,2176]{1,0:T(8,128)S(1)}, f32[8,2176]{1,0:T(8,128)S(1)}, u32[]{:S(2)}, u32[]{:S(2)}) collective-permute-start(f32[8,2176]{1,0:T(8,128)S(1)} %get-tuple-element.13), channel_id=1, source_target_pairs={{0,12},{4,0},{8,4},{12,8},{1,13},{5,1},{9,5},{13,9},{2,14},{6,2},{... | collective-permute-start | bytes 208904 | tf_op jit(solution)/shard_map/clus_exchange/ppermute | solution.py:8
  15.1 2.4 %collective-permute-done.1 = f32[8,2176]{1,0:T(8,128)S(1)} collective-permute-done((f32[8,2176]{1,0:T(8,128)S(1)}, f32[8,2176]{1,0:T(8,128)S(1)}, u32[]{:S(2)}, u32[]{:S(2)}) %collective-permute-start.1) | collective-permute-done | bytes 69664 | tf_op jit(solution)/shard_map/clus_exchange/ppermute | solution.py:8
  17.9 0.4 convolution_bitcast_fusion.2
  18.6 0.6 %fusion.74 = f32[16,8,256]{2,1,0:T(8,128)S(1)} fusion(bf16[8,16,256]{2,0,1:T(8,128)(2,1)S(1)} %copy.23, bf16[16,256,256]{2,1,0:T(8,128)(2,1)S(1)} %copy-done), kind=kOutput, calls=%fused_computation.131 | convolution fusion | flops 16777216 | bytes 2293760 | tf_op jit(solution)/shard_map/near_partial/rjs,jts->rjt/dot_general | solution.py:101
  19.5 1.6 %collective-permute-start.3 = (f32[8,2176]{1,0:T(8,128)S(1)}, f32[8,2176]{1,0:T(8,128)S(1)}, u32[]{:S(2)}, u32[]{:S(2)}) collective-permute-start(f32[8,2176]{1,0:T(8,128)S(1)} %pad_maximum_fusion.5), channel_id=1, source_target_pairs={{0,2},{2,0},{1,3},{3,1},{4,6},{6,4},{5,7},{7,5},{8,10},{10,8},{9,1... | collective-permute-start | bytes 208904 | tf_op jit(solution)/shard_map/pair_sums/ppermute | solution.py:8
  21.0 2.8 %collective-permute-done.3 = f32[8,2176]{1,0:T(8,128)S(1)} collective-permute-done((f32[8,2176]{1,0:T(8,128)S(1)}, f32[8,2176]{1,0:T(8,128)S(1)}, u32[]{:S(2)}, u32[]{:S(2)}) %collective-permute-start.3) | collective-permute-done | bytes 69664 | tf_op jit(solution)/shard_map/pair_sums/ppermute | solution.py:8
  24.1 0.7 %add_convert_fusion.1 = bf16[8,8,256]{2,0,1:T(8,128)(2,1)S(1)} fusion(f32[8,8,256]{2,0,1:T(8,128)S(1)} %bitcast.161, f32[8,8,256]{2,0,1:T(8,128)S(1)} %bitcast.172, f32[8,8,256]{2,0,1:T(8,128)S(1)} %convolution_bitcast_fusion.10, f32[]{:T(128)} %bitcast.24), kind=kLoop, calls=%fused_computation.53 | loop fusion | flops 65536 | bytes 229380 | tf_op jit(solution)/shard_map/convert_element_type | solution.py:124
  26.0 3.8 %collective-permute-start.4 = (f32[8,2176]{1,0:T(8,128)S(1)}, f32[8,2176]{1,0:T(8,128)S(1)}, u32[]{:S(2)}, u32[]{:S(2)}) collective-permute-start(f32[8,2176]{1,0:T(8,128)S(1)} %get-tuple-element.12), channel_id=1, source_target_pairs={{0,12},{4,0},{8,4},{12,8},{1,13},{5,1},{9,5},{13,9},{2,14},{6,2},{... | collective-permute-start | bytes 208904 | tf_op jit(solution)/shard_map/clus_exchange/ppermute | solution.py:8
  29.9 2.3 %collective-permute-done.5 = f32[8,2176]{1,0:T(8,128)S(1)} collective-permute-done((f32[8,2176]{1,0:T(8,128)S(1)}, f32[8,2176]{1,0:T(8,128)S(1)}, u32[]{:S(2)}, u32[]{:S(2)}) %collective-permute-start.5) | collective-permute-done | bytes 69664 | tf_op jit(solution)/shard_map/clus_exchange/ppermute | solution.py:8
  32.3 0.4 convolution_bitcast_fusion.1
  32.8 0.6 %fusion.75 = f32[16,8,256]{2,1,0:T(8,128)S(1)} fusion(bf16[8,16,256]{2,0,1:T(8,128)(2,1)S(1)} %copy.28, bf16[16,256,256]{2,1,0:T(8,128)(2,1)S(1)} %copy-done), kind=kOutput, calls=%fused_computation.132 | convolution fusion | flops 16777216 | bytes 2293760 | tf_op jit(solution)/shard_map/near_partial/rjs,jts->rjt/dot_general | solution.py:101
  33.7 0.7 %collective-permute-done.6 = f32[8,128]{1,0:T(8,128)S(1)} collective-permute-done((f32[8,128]{1,0:T(8,128)S(1)}, f32[8,128]{1,0:T(8,128)S(1)}, u32[]{:S(2)}, u32[]{:S(2)}) %collective-permute-start.6) | collective-permute-done | bytes 4128 | tf_op jit(solution)/shard_map/clus_exchange/ppermute | solution.py:8
  34.4 1.6 %collective-permute-start.7 = (f32[8,2176]{1,0:T(8,128)S(1)}, f32[8,2176]{1,0:T(8,128)S(1)}, u32[]{:S(2)}, u32[]{:S(2)}) collective-permute-start(f32[8,2176]{1,0:T(8,128)S(1)} %pad_maximum_fusion.8), channel_id=1, source_target_pairs={{0,2},{2,0},{1,3},{3,1},{4,6},{6,4},{5,7},{7,5},{8,10},{10,8},{9,1... | collective-permute-start | bytes 208904 | tf_op jit(solution)/shard_map/pair_sums/ppermute | solution.py:8
  35.9 2.8 %collective-permute-done.7 = f32[8,2176]{1,0:T(8,128)S(1)} collective-permute-done((f32[8,2176]{1,0:T(8,128)S(1)}, f32[8,2176]{1,0:T(8,128)S(1)}, u32[]{:S(2)}, u32[]{:S(2)}) %collective-permute-start.7) | collective-permute-done | bytes 69664 | tf_op jit(solution)/shard_map/pair_sums/ppermute | solution.py:8
  39.0 0.7 %add_convert_fusion = bf16[8,8,256]{2,0,1:T(8,128)(2,1)S(1)} fusion(f32[8,8,256]{2,0,1:T(8,128)S(1)} %bitcast.162, f32[8,8,256]{2,0,1:T(8,128)S(1)} %bitcast.173, f32[8,8,256]{2,0,1:T(8,128)S(1)} %convolution_bitcast_fusion.8, f32[]{:T(128)} %bitcast.45), kind=kLoop, calls=%fused_computation.52 | loop fusion | flops 65536 | bytes 229380 | tf_op jit(solution)/shard_map/convert_element_type | solution.py:124
  40.9 0.6 %collective-permute-start.9 = (f32[8,2176]{1,0:T(8,128)S(1)}, f32[8,2176]{1,0:T(8,128)S(1)}, u32[]{:S(2)}, u32[]{:S(2)}) collective-permute-start(f32[8,2176]{1,0:T(8,128)S(1)} %get-tuple-element.9), channel_id=1, source_target_pairs={{0,4},{4,8},{8,12},{12,0},{1,5},{5,9},{9,13},{13,1},{2,6},{6,10},{... | collective-permute-start | bytes 208904 | tf_op jit(solution)/shard_map/clus_exchange/ppermute | solution.py:8
  41.5 3.2 %collective-permute-start.8 = (f32[8,2176]{1,0:T(8,128)S(1)}, f32[8,2176]{1,0:T(8,128)S(1)}, u32[]{:S(2)}, u32[]{:S(2)}) collective-permute-start(f32[8,2176]{1,0:T(8,128)S(1)} %get-tuple-element.10), channel_id=1, source_target_pairs={{0,12},{4,0},{8,4},{12,8},{1,13},{5,1},{9,5},{13,9},{2,14},{6,2},{... | collective-permute-start | bytes 208904 | tf_op jit(solution)/shard_map/clus_exchange/ppermute | solution.py:8
  44.8 2.4 %collective-permute-done.9 = f32[8,2176]{1,0:T(8,128)S(1)} collective-permute-done((f32[8,2176]{1,0:T(8,128)S(1)}, f32[8,2176]{1,0:T(8,128)S(1)}, u32[]{:S(2)}, u32[]{:S(2)}) %collective-permute-start.9) | collective-permute-done | bytes 69664 | tf_op jit(solution)/shard_map/clus_exchange/ppermute | solution.py:8
  47.2 0.4 convolution_bitcast_fusion
  47.8 0.6 %fusion.76 = f32[16,8,256]{2,1,0:T(8,128)S(1)} fusion(bf16[8,16,256]{2,0,1:T(8,128)(2,1)S(1)} %copy.33, bf16[16,256,256]{2,1,0:T(8,128)(2,1)S(1)} %copy-done), kind=kOutput, calls=%fused_computation.133 | convolution fusion | flops 16777216 | bytes 2293760 | tf_op jit(solution)/shard_map/near_partial/rjs,jts->rjt/dot_general | solution.py:101
  48.7 0.6 %collective-permute-done.10 = f32[8,128]{1,0:T(8,128)S(1)} collective-permute-done((f32[8,128]{1,0:T(8,128)S(1)}, f32[8,128]{1,0:T(8,128)S(1)}, u32[]{:S(2)}, u32[]{:S(2)}) %collective-permute-start.10) | collective-permute-done | bytes 4128 | tf_op jit(solution)/shard_map/clus_exchange/ppermute | solution.py:8
  49.3 1.6 %collective-permute-start.11 = (f32[8,2176]{1,0:T(8,128)S(1)}, f32[8,2176]{1,0:T(8,128)S(1)}, u32[]{:S(2)}, u32[]{:S(2)}) collective-permute-start(f32[8,2176]{1,0:T(8,128)S(1)} %pad_maximum_fusion.11), channel_id=1, source_target_pairs={{0,2},{2,0},{1,3},{3,1},{4,6},{6,4},{5,7},{7,5},{8,10},{10,8},{9,1... | collective-permute-start | bytes 208904 | tf_op jit(solution)/shard_map/pair_sums/ppermute | solution.py:8
  50.9 2.8 %collective-permute-done.11 = f32[8,2176]{1,0:T(8,128)S(1)} collective-permute-done((f32[8,2176]{1,0:T(8,128)S(1)}, f32[8,2176]{1,0:T(8,128)S(1)}, u32[]{:S(2)}, u32[]{:S(2)}) %collective-permute-start.11) | collective-permute-done | bytes 69664 | tf_op jit(solution)/shard_map/pair_sums/ppermute | solution.py:8
  53.9 1.3 %multiply_add_fusion = f32[8,8,256]{2,0,1:T(8,128)} fusion(f32[8,8,256]{2,0,1:T(8,128)S(1)} %bitcast.163, f32[8,8,256]{2,0,1:T(8,128)S(1)} %bitcast.174, f32[8,8,256]{2,0,1:T(8,128)S(1)} %convolution_bitcast_fusion.6, f32[]{:T(128)} %bitcast.65), kind=kLoop, calls=%fused_computation.51 | loop fusion | flops 49152 | bytes 262148 | tf_op jit(solution)/shard_map/add | solution.py:123
  (84 shorter events, 5.4 us)
Async XLA Ops:
  0.0 18.5 %copy-start = (bf16[16,256,256]{2,1,0:T(8,128)(2,1)S(1)}, bf16[16,256,256]{2,1,0:T(8,128)(2,1)}, u32[]{:S(2)}) copy-start(bf16[16,256,256]{2,1,0:T(8,128)(2,1)} %param.11) | copy-start | bytes 6291460
  0.0 10.6 %copy-start.2 = (f32[8,2048]{1,0:T(8,128)S(1)}, f32[8,2048]{1,0:T(8,128)}, u32[]{:S(2)}) copy-start(f32[8,2048]{1,0:T(8,128)} %param.9) | copy-start | bytes 196612
  0.0 15.1 %copy-start.5 = (s32[16]{0:T(128)S(1)}, s32[16]{0:T(128)}, u32[]{:S(2)}) copy-start(s32[16]{0:T(128)} %param.13) | copy-start | bytes 196
  0.0 15.1 %copy-start.6 = (s32[16]{0:T(128)S(1)}, s32[16]{0:T(128)}, u32[]{:S(2)}) copy-start(s32[16]{0:T(128)} %param.12) | copy-start | bytes 196
  6.5 12.9 %collective-permute-start.2 = (f32[8,128]{1,0:T(8,128)S(1)}, f32[8,128]{1,0:T(8,128)S(1)}, u32[]{:S(2)}, u32[]{:S(2)}) collective-permute-start(f32[8,128]{1,0:T(8,128)S(1)} %get-tuple-element.21), channel_id=1, source_target_pairs={{0,8},{4,12},{8,0},{12,4},{1,9},{5,13},{9,1},{13,5},{2,10},{6,14},... | collective-permute-start | bytes 12296 | tf_op jit(solution)/shard_map/clus_exchange/ppermute | solution.py:8
  11.2 6.3 %collective-permute-start.1 = (f32[8,2176]{1,0:T(8,128)S(1)}, f32[8,2176]{1,0:T(8,128)S(1)}, u32[]{:S(2)}, u32[]{:S(2)}) collective-permute-start(f32[8,2176]{1,0:T(8,128)S(1)} %get-tuple-element.7), channel_id=1, source_target_pairs={{0,4},{4,8},{8,12},{12,0},{1,5},{5,9},{9,13},{13,1},{2,6},{6,10},{... | collective-permute-start | bytes 208904 | tf_op jit(solution)/shard_map/clus_exchange/ppermute | solution.py:8
  12.9 5.1 %collective-permute-start = (f32[8,2176]{1,0:T(8,128)S(1)}, f32[8,2176]{1,0:T(8,128)S(1)}, u32[]{:S(2)}, u32[]{:S(2)}) collective-permute-start(f32[8,2176]{1,0:T(8,128)S(1)} %get-tuple-element.13), channel_id=1, source_target_pairs={{0,12},{4,0},{8,4},{12,8},{1,13},{5,1},{9,5},{13,9},{2,14},{6,2},{... | collective-permute-start | bytes 208904 | tf_op jit(solution)/shard_map/clus_exchange/ppermute | solution.py:8
  17.9 6.0 %copy-start.3 = (bf16[8,16,256]{2,1,0:T(8,128)(2,1)S(1)}, bf16[8,16,256]{2,1,0:T(8,128)(2,1)}, u32[]{:S(2)}) copy-start(bf16[8,16,256]{2,1,0:T(8,128)(2,1)} %param.14) | copy-start | bytes 196612
  18.5 6.5 %copy-start.1 = (bf16[64,16,256]{2,1,0:T(8,128)(2,1)S(1)}, bf16[64,16,256]{2,1,0:T(8,128)(2,1)}, u32[]{:S(2)}) copy-start(bf16[64,16,256]{2,1,0:T(8,128)(2,1)} %param.15) | copy-start | bytes 1572868
  18.5 6.9 %copy-start.4 = (s32[64]{0:T(128)S(1)}, s32[64]{0:T(128)}, u32[]{:S(2)}) copy-start(s32[64]{0:T(128)} %param.17) | copy-start | bytes 772
  19.5 4.4 %collective-permute-start.3 = (f32[8,2176]{1,0:T(8,128)S(1)}, f32[8,2176]{1,0:T(8,128)S(1)}, u32[]{:S(2)}, u32[]{:S(2)}) collective-permute-start(f32[8,2176]{1,0:T(8,128)S(1)} %pad_maximum_fusion.5), channel_id=1, source_target_pairs={{0,2},{2,0},{1,3},{3,1},{4,6},{6,4},{5,7},{7,5},{8,10},{10,8},{9,1... | collective-permute-start | bytes 208904 | tf_op jit(solution)/shard_map/pair_sums/ppermute | solution.py:8
  26.0 6.2 %collective-permute-start.5 = (f32[8,2176]{1,0:T(8,128)S(1)}, f32[8,2176]{1,0:T(8,128)S(1)}, u32[]{:S(2)}, u32[]{:S(2)}) collective-permute-start(f32[8,2176]{1,0:T(8,128)S(1)} %get-tuple-element.11), channel_id=1, source_target_pairs={{0,4},{4,8},{8,12},{12,0},{1,5},{5,9},{9,13},{13,1},{2,6},{6,10},{... | collective-permute-start | bytes 208904 | tf_op jit(solution)/shard_map/clus_exchange/ppermute | solution.py:8
  26.0 6.2 %collective-permute-start.4 = (f32[8,2176]{1,0:T(8,128)S(1)}, f32[8,2176]{1,0:T(8,128)S(1)}, u32[]{:S(2)}, u32[]{:S(2)}) collective-permute-start(f32[8,2176]{1,0:T(8,128)S(1)} %get-tuple-element.12), channel_id=1, source_target_pairs={{0,12},{4,0},{8,4},{12,8},{1,13},{5,1},{9,5},{13,9},{2,14},{6,2},{... | collective-permute-start | bytes 208904 | tf_op jit(solution)/shard_map/clus_exchange/ppermute | solution.py:8
  29.9 4.5 %collective-permute-start.6 = (f32[8,128]{1,0:T(8,128)S(1)}, f32[8,128]{1,0:T(8,128)S(1)}, u32[]{:S(2)}, u32[]{:S(2)}) collective-permute-start(f32[8,128]{1,0:T(8,128)S(1)} %get-tuple-element.19), channel_id=1, source_target_pairs={{0,8},{4,12},{8,0},{12,4},{1,9},{5,13},{9,1},{13,5},{2,10},{6,14},... | collective-permute-start | bytes 12296 | tf_op jit(solution)/shard_map/clus_exchange/ppermute | solution.py:8
  34.4 4.4 %collective-permute-start.7 = (f32[8,2176]{1,0:T(8,128)S(1)}, f32[8,2176]{1,0:T(8,128)S(1)}, u32[]{:S(2)}, u32[]{:S(2)}) collective-permute-start(f32[8,2176]{1,0:T(8,128)S(1)} %pad_maximum_fusion.8), channel_id=1, source_target_pairs={{0,2},{2,0},{1,3},{3,1},{4,6},{6,4},{5,7},{7,5},{8,10},{10,8},{9,1... | collective-permute-start | bytes 208904 | tf_op jit(solution)/shard_map/pair_sums/ppermute | solution.py:8
  40.9 6.3 %collective-permute-start.9 = (f32[8,2176]{1,0:T(8,128)S(1)}, f32[8,2176]{1,0:T(8,128)S(1)}, u32[]{:S(2)}, u32[]{:S(2)}) collective-permute-start(f32[8,2176]{1,0:T(8,128)S(1)} %get-tuple-element.9), channel_id=1, source_target_pairs={{0,4},{4,8},{8,12},{12,0},{1,5},{5,9},{9,13},{13,1},{2,6},{6,10},{... | collective-permute-start | bytes 208904 | tf_op jit(solution)/shard_map/clus_exchange/ppermute | solution.py:8
  41.5 5.6 %collective-permute-start.8 = (f32[8,2176]{1,0:T(8,128)S(1)}, f32[8,2176]{1,0:T(8,128)S(1)}, u32[]{:S(2)}, u32[]{:S(2)}) collective-permute-start(f32[8,2176]{1,0:T(8,128)S(1)} %get-tuple-element.10), channel_id=1, source_target_pairs={{0,12},{4,0},{8,4},{12,8},{1,13},{5,1},{9,5},{13,9},{2,14},{6,2},{... | collective-permute-start | bytes 208904 | tf_op jit(solution)/shard_map/clus_exchange/ppermute | solution.py:8
  44.8 4.5 %collective-permute-start.10 = (f32[8,128]{1,0:T(8,128)S(1)}, f32[8,128]{1,0:T(8,128)S(1)}, u32[]{:S(2)}, u32[]{:S(2)}) collective-permute-start(f32[8,128]{1,0:T(8,128)S(1)} %get-tuple-element.16), channel_id=1, source_target_pairs={{0,8},{4,12},{8,0},{12,4},{1,9},{5,13},{9,1},{13,5},{2,10},{6,14},... | collective-permute-start | bytes 12296 | tf_op jit(solution)/shard_map/clus_exchange/ppermute | solution.py:8
  49.3 4.4 %collective-permute-start.11 = (f32[8,2176]{1,0:T(8,128)S(1)}, f32[8,2176]{1,0:T(8,128)S(1)}, u32[]{:S(2)}, u32[]{:S(2)}) collective-permute-start(f32[8,2176]{1,0:T(8,128)S(1)} %pad_maximum_fusion.11), channel_id=1, source_target_pairs={{0,2},{2,0},{1,3},{3,1},{4,6},{6,4},{5,7},{7,5},{8,10},{10,8},{9,1... | collective-permute-start | bytes 208904 | tf_op jit(solution)/shard_map/pair_sums/ppermute | solution.py:8

commit v6 on v2

--- a/solution.py
+++ b/solution.py
@@ -44,6 +44,14 @@
     relative = (near_src // clusters_here - my_index) % peer_count
     slot = jnp.where(relative == 0, 0, jnp.where(relative == 1, 1, 2))
     near_index = slot * clusters_here + near_src % clusters_here
+    is_local = relative == 0
+    local_index = jnp.where(is_local, near_src - my_base, 0)
+    local_hot = target_hot * is_local[:, None].astype(jnp.float32)
+    remote_count = min(4, near_tgt.shape[0]) if peer_count > 1 else 0
+    remote_rows = jnp.argsort(is_local.astype(jnp.int32), stable=True)[:remote_count]
+    remote_blocks = near_blocks[remote_rows]
+    remote_index = near_index[remote_rows] - clusters_here
+    remote_hot = target_hot[remote_rows]
 
     far_local = far_src - my_base
     far_hot = (far_tgt[:, None] == jnp.arange(cluster_count)[None, :]).astype(jnp.float32)
@@ -85,15 +93,24 @@
                         from_plus = neighbour
                     incoming = incoming[:, iterate_size:]
                 far_mine = far_mine + incoming
-        with jax.named_scope("near_partial"):
-            extended = jnp.concatenate([iterate, from_plus, from_minus], axis=1)
-            gathered = extended[:, near_index, :]
+        with jax.named_scope("near_local"):
+            gathered = iterate[:, local_index, :]
             contrib = jnp.einsum(
                 "rjs,jts->rjt", gathered, near_blocks, preferred_element_type=jnp.float32
             )
             near_part = jnp.einsum(
-                "rjt,jc->rct", contrib, target_hot, precision=lax.Precision.HIGHEST
+                "rjt,jc->rct", contrib, local_hot, precision=lax.Precision.HIGHEST
             )
+        with jax.named_scope("near_remote"):
+            if remote_count:
+                neighbours = jnp.concatenate([from_plus, from_minus], axis=1)
+                gathered = neighbours[:, remote_index, :]
+                contrib = jnp.einsum(
+                    "rjs,jts->rjt", gathered, remote_blocks, preferred_element_type=jnp.float32
+                )
+                near_part = near_part + jnp.einsum(
+                    "rjt,jc->rct", contrib, remote_hot, precision=lax.Precision.HIGHEST
+                )
         with jax.named_scope("pair_sums"):
             near_flat = near_part.reshape(rhs_here, clusters_here * leaf_size)
             packed = jnp.concatenate([near_flat, far_mine], axis=1)

time: 56 us -> 75.3 us (1.34)
  local copies, waits for them, and re-layouts: 6.13 us -> 17.4 us
  matrix products: 6.06 us -> 13.6 us
  other arithmetic: 4.99 us -> 10.7 us
  waiting for transfers between devices: 19.5 us -> 15.6 us
  starting transfers between devices: 18.5 us -> 16.8 us
    gather x3 -> x9, local copies, waits for them, and re-layouts: 1.67 us -> 7.41 us  [the longest x3 3.15 us: shards(): gathered = iterate[:, local_index, :]]
    ppermute x12, waiting for transfers between devices: 19.5 us -> 15.6 us  [shift(): lax.ppermute(value, axis, [(i, (i + step) % count) for i in range(count)])]
    dot_general x3 -> x9, matrix products: 0.65 us -> 3.72 us  [the longest x3 1.64 us: shards(): jnp.einsum('rjt,jc->rct', contrib, local_hot, precision=lax.Precision.HIG...]
    dot_general x3, local copies, waits for them, and re-layouts: 0.43 us -> 2.27 us  [shards(): jnp.einsum('rjl,jkl->jrk', far_input, col_basis, preferred_element_type=j...]
    ppermute x12, starting transfers between devices: 18.5 us -> 16.8 us  [shift(): lax.ppermute(value, axis, [(i, (i + step) % count) for i in range(count)])]
    dot_general x3, matrix products: 1.91 us -> 3.62 us  [shards(): jnp.einsum('rjs,jts->rjt', gathered, near_blocks, preferred_element_type=...]
    slice x6, local copies, waits for them, and re-layouts: 0.03 us -> 1.71 us  [shards(): neighbour = incoming[:, :iterate_size].astype(jnp.bfloat16)]
    dot_general x3, matrix products: 1.73 us -> 3.17 us  [shards(): jnp.einsum('rjl,jkl->jrk', far_input, col_basis, preferred_element_type=j...]
  transfers between devices with their start and end apart: 12 -> 12, of which waited for: 8 -> 5; matrix products, arithmetic and copies ran while one was open for 8% -> 23% of each run, Pallas kernels for 0% -> 0%
where the time goes in v6:
time: 75.3 us; the launch traced here: 74.6 us
  local copies, waits for them, and re-layouts  17.4 us (23%)
  starting transfers between devices  16.8 us (22%)
  waiting for transfers between devices  15.6 us (21%)
  matrix products  13.6 us (18%)
  other arithmetic  10.7 us (14%)
    ppermute x12, starting transfers between devices, shift(): lax.ppermute(value, axis, [(i, (i + step) % count) for i in range(count)])  16.8 us
    ppermute x12, waiting for transfers between devices, shift(): lax.ppermute(value, axis, [(i, (i + step) % count) for i in range(count)])  15.6 us
    convert_element_type x3, other arithmetic, shards(): iterate.reshape(rhs_here, clusters_here * leaf_size).astype(jnp.float32)  3.99 us
    dot_general x3, matrix products, shards(): jnp.einsum('rjs,jts->rjt', gathered, near_blocks, preferred_element_type=...  3.62 us
    dot_general x3, matrix products, shards(): jnp.einsum('rjl,jkl->jrk', far_input, col_basis, preferred_element_type=j...  3.17 us
    gather x3, local copies, waits for them, and re-layouts, shards(): gathered = iterate[:, local_index, :]  3.15 us
    dot_general x3, matrix products, shards(): jnp.einsum('jc,jm->cm', far_hot, coef, precision=lax.Precision.HIGHEST)  2.58 us
    dot_general x3, local copies, waits for them, and re-layouts, shards(): jnp.einsum('rjl,jkl->jrk', far_input, col_basis, preferred_element_type=j...  2.27 us
  transfers between devices with their start and end apart: 12, of which 5 were waited for; matrix products, arithmetic and copies ran while one was open for 23% of the time, Pallas kernels for 0%

profile of v6, /device:TPU:0, one launch (start us, length us, event | category | flops | bytes accessed | tf_op | source)
XLA Modules:
  0.0 74.6 jit_solution(15746227194796228663)
XLA Ops:
  0.1 1.5 %fusion.88 = (f32[1]{0:T(128)}, f32[1]{0:T(128)}, f32[1]{0:T(128)}, f32[1]{0:T(128)}) fusion(f32[4]{0:T(128)} %param.10), kind=kLoop, calls=%fused_computation.170 | loop fusion | bytes 32 | tf_op jit(solution)/shard_map/slice | solution.py:60
  2.2 4.0 %fusion.87 = (f32[8,2048]{1,0:T(8,128)S(1)}, bf16[8,2048]{1,0:T(8,128)(2,1)S(1)}, f32[8,2048]{1,0:T(8,128)S(1)}, f32[8,2048]{1,0:T(8,128)}, f32[8,2048]{1,0:T(8,128)}) fusion(f32[8,2048]{1,0:T(8,128)} %param.9, f32[]{:T(128)} %bitcast.3, f32[]{:T(128)} %bitcast.30, f32[]{:T(128)} %bitcast.77, f32[]{:T(128)} %bitcast.54), kind=kLoop, calls=%fused_computation.169 | loop fusion | flops 98304 | bytes 360464 | tf_op jit(solution)/shard_map/clus_exchange/convert_element_type | solution.py:77
  6.8 1.3 %fusion.7 = f32[64,8,16]{2,1,0:T(8,128)S(1)} fusion(bf16[64,16,256]{2,1,0:T(8,128)(2,1)} %param.15, bf16[64,8,256]{2,1,0:T(8,128)(2,1)S(1)} %gather_fusion.3), kind=kOutput, calls=%fused_computation.28 | convolution fusion | flops 4194304 | bytes 819200 | tf_op jit(solution)/shard_map/far_partial/rjl,jkl->jrk/dot_general | solution.py:66
  10.0 5.1 %collective-permute-start = (f32[8,2176]{1,0:T(8,128)S(1)}, f32[8,2176]{1,0:T(8,128)}, u32[]{:S(2)}, u32[]{:S(2)}) collective-permute-start(f32[8,2176]{1,0:T(8,128)S(1)} %get-tuple-element.16), channel_id=1, source_target_pairs={{0,12},{4,0},{8,4},{12,8},{1,13},{5,1},{9,5},{13,9},{2,14},{6,2},{... | collective-permute-start | bytes 208904 | tf_op jit(solution)/shard_map/clus_exchange/ppermute | solution.py:8
  15.1 1.0 %collective-permute-start.1 = (f32[8,2176]{1,0:T(8,128)}, f32[8,2176]{1,0:T(8,128)}, u32[]{:S(2)}, u32[]{:S(2)}) collective-permute-start(f32[8,2176]{1,0:T(8,128)} %get-tuple-element.15), channel_id=1, source_target_pairs={{0,4},{4,8},{8,12},{12,0},{1,5},{5,9},{9,13},{13,1},{2,6},{6,10},{... | collective-permute-start | bytes 208904 | tf_op jit(solution)/shard_map/clus_exchange/ppermute | solution.py:8
  17.3 1.3 %sort.17 = (s32[16]{0:T(128)}, s32[16]{0:T(128)S(1)}) sort(s32[16]{0:T(128)S(1)} %get-tuple-element.29, s32[16]{0:T(128)S(1)} %iota.18), dimensions={0}, to_apply=%region_0.1 | sort | flops 64 | bytes 256 | tf_op jit(solution)/shard_map/jit(argsort)/sort | solution.py:51
  21.2 1.1 %gather_fusion.1 = pred[4,8]{1,0:T(4,128)(4,1)} fusion(pred[16,8]{1,0:T(8,128)(4,1)S(1)} %iota_compare_fusion, s32[1024]{0:T(1024)S(1)} %pad_clamp_fusion.2), kind=kCustom, calls=%fused_computation.1 | custom fusion | bytes 80 | tf_op jit(solution)/shard_map/gather | solution.py:54
  22.3 1.0 %fusion.13 = f32[8,8,256]{2,0,1:T(8,128)S(1)} fusion(f32[16,8,256]{2,1,0:T(8,128)S(1)} %fusion.25, f32[16]{0:T(128)} %get-tuple-element.30, s32[16]{0:T(128)S(1)} %get-tuple-element.36), kind=kOutput, calls=%fused_computation.34 | convolution fusion | flops 3145984 | bytes 196736 | tf_op jit(solution)/shard_map/near_local/rjt,jc->rct/dot_general | solution.py:101
  23.9 0.8 %slice.169 = bf16[8,2048]{1,0:T(8,128)(2,1)S(1)} slice(f32[8,2176]{1,0:T(8,128)} %collective-permute-done.1), slice={[0:8], [0:2048]} | slice | bytes 65536 | tf_op jit(solution)/shard_map/clus_exchange/slice | solution.py:88
  24.8 0.8 %slice.170 = bf16[8,2048]{1,0:T(8,128)(2,1)S(1)} slice(f32[8,2176]{1,0:T(8,128)} %collective-permute-done), slice={[0:8], [0:2048]} | slice | bytes 65536 | tf_op jit(solution)/shard_map/clus_exchange/slice | solution.py:88
  26.4 0.9 %fusion.2 = f32[1,8,8,256]{3,2,1,0:T(8,128)S(1)} fusion(f32[8,8,256]{2,0,1:T(8,128)S(1)} %fusion.13, f32[4,256,8]{1,2,0:T(8,128)S(1)} %fusion.40, pred[4,8]{1,0:T(4,128)(4,1)} %gather_fusion.1), kind=kOutput, calls=%fused_computation.23 | convolution fusion | flops 802816 | bytes 163872 | tf_op jit(solution)/shard_map/near_remote/rjt,jc->rct/dot_general | solution.py:111
  28.1 1.6 %collective-permute-start.3 = (f32[8,2176]{1,0:T(8,128)S(1)}, f32[8,2176]{1,0:T(8,128)S(1)}, u32[]{:S(2)}, u32[]{:S(2)}) collective-permute-start(f32[8,2176]{1,0:T(8,128)S(1)} %pad_maximum_fusion.2), channel_id=1, source_target_pairs={{0,2},{2,0},{1,3},{3,1},{4,6},{6,4},{5,7},{7,5},{8,10},{10,8},{9,1... | collective-permute-start | bytes 208904 | tf_op jit(solution)/shard_map/pair_sums/ppermute | solution.py:8
  29.7 2.8 %collective-permute-done.3 = f32[8,2176]{1,0:T(8,128)S(1)} collective-permute-done((f32[8,2176]{1,0:T(8,128)S(1)}, f32[8,2176]{1,0:T(8,128)S(1)}, u32[]{:S(2)}, u32[]{:S(2)}) %collective-permute-start.3) | collective-permute-done | bytes 69664 | tf_op jit(solution)/shard_map/pair_sums/ppermute | solution.py:8
  33.5 1.3 %gather_fusion.6 = bf16[16,8,256]{2,1,0:T(8,128)(2,1)} fusion(bf16[8,8,256]{2,0,1:T(8,128)(2,1)S(1)} %add_convert_fusion.1, s32[1024]{0:T(1024)} %copy-done.10), kind=kCustom, calls=%fused_computation.6 | custom fusion | bytes 131136 | tf_op jit(solution)/shard_map/near_local/gather | solution.py:97
  34.8 1.0 %fusion.5 = f32[64,8,16]{2,1,0:T(8,128)} fusion(bf16[64,16,256]{2,1,0:T(8,128)(2,1)S(1)} %copy-done.1, bf16[64,8,256]{2,1,0:T(8,128)(2,1)S(1)} %gather_fusion.7), kind=kOutput, calls=%fused_computation.26 | convolution fusion | flops 4194304 | bytes 819200 | tf_op jit(solution)/shard_map/far_partial/rjl,jkl->jrk/dot_general | solution.py:66
  35.8 1.1 %copy.20 = f32[64,8,16]{0,2,1:T(8,128)S(1)} copy(f32[64,8,16]{2,1,0:T(8,128)} %fusion.5) | data formatting | bytes 65536 | tf_op jit(solution)/shard_map/far_partial/rjl,jkl->jrk/dot_general | solution.py:66
  36.9 1.1 %convolution_bitcast_fusion.1 = f32[4,8,8,16]{3,2,1,0:T(8,128)S(1)} fusion(f32[64,8,16]{0,2,1:T(8,128)S(1)} %copy.20, s32[4,8]{1,0:T(4,128)S(1)} %multiply_add_fusion, s32[64]{0:T(128)} %param.17), kind=kOutput, calls=%fused_computation.13 | convolution fusion | flops 3147776 | bytes 49536 | tf_op jit(solution)/shard_map/far_partial/jc,jm->cm/dot_general | solution.py:70
  38.7 2.9 %collective-permute-start.4 = (f32[8,2176]{1,0:T(8,128)S(1)}, f32[8,2176]{1,0:T(8,128)S(1)}, u32[]{:S(2)}, u32[]{:S(2)}) collective-permute-start(f32[8,2176]{1,0:T(8,128)S(1)} %get-tuple-element.14), channel_id=1, source_target_pairs={{0,12},{4,0},{8,4},{12,8},{1,13},{5,1},{9,5},{13,9},{2,14},{6,2},{... | collective-permute-start | bytes 208904 | tf_op jit(solution)/shard_map/clus_exchange/ppermute | solution.py:8
  41.5 1.1 %collective-permute-start.6 = (f32[8,128]{1,0:T(8,128)}, f32[8,128]{1,0:T(8,128)}, u32[]{:S(2)}, u32[]{:S(2)}) collective-permute-start(f32[8,128]{1,0:T(8,128)} %get-tuple-element.24), channel_id=1, source_target_pairs={{0,8},{4,12},{8,0},{12,4},{1,9},{5,13},{9,1},{13,5},{2,10},{6,14},... | collective-permute-start | bytes 12296 | tf_op jit(solution)/shard_map/clus_exchange/ppermute | solution.py:8
  42.7 1.5 %fusion.23 = f32[16,8,256]{2,1,0:T(8,128)S(1)} fusion(bf16[16,256,256]{2,1,0:T(8,128)(2,1)S(1)} %copy-done, bf16[16,8,256]{2,1,0:T(8,128)(2,1)} %gather_fusion.6), kind=kOutput, calls=%fused_computation.62 | convolution fusion | flops 16777216 | bytes 2293760 | tf_op jit(solution)/shard_map/near_local/rjs,jts->rjt/dot_general | solution.py:98
  44.5 4.2 %collective-permute-done.5 = f32[8,2176]{1,0:T(8,128)S(1)} collective-permute-done((f32[8,2176]{1,0:T(8,128)S(1)}, f32[8,2176]{1,0:T(8,128)S(1)}, u32[]{:S(2)}, u32[]{:S(2)}) %collective-permute-start.5) | collective-permute-done | bytes 69664 | tf_op jit(solution)/shard_map/clus_exchange/ppermute | solution.py:8
  51.3 1.6 %collective-permute-start.7 = (f32[8,2176]{1,0:T(8,128)S(1)}, f32[8,2176]{1,0:T(8,128)S(1)}, u32[]{:S(2)}, u32[]{:S(2)}) collective-permute-start(f32[8,2176]{1,0:T(8,128)S(1)} %pad_maximum_fusion.5), channel_id=1, source_target_pairs={{0,2},{2,0},{1,3},{3,1},{4,6},{6,4},{5,7},{7,5},{8,10},{10,8},{9,1... | collective-permute-start | bytes 208904 | tf_op jit(solution)/shard_map/pair_sums/ppermute | solution.py:8
  52.9 2.8 %collective-permute-done.7 = f32[8,2176]{1,0:T(8,128)S(1)} collective-permute-done((f32[8,2176]{1,0:T(8,128)S(1)}, f32[8,2176]{1,0:T(8,128)S(1)}, u32[]{:S(2)}, u32[]{:S(2)}) %collective-permute-start.7) | collective-permute-done | bytes 69664 | tf_op jit(solution)/shard_map/pair_sums/ppermute | solution.py:8
  56.7 1.3 %gather_fusion.9 = bf16[16,8,256]{2,1,0:T(8,128)(2,1)} fusion(bf16[8,8,256]{2,0,1:T(8,128)(2,1)S(1)} %add_convert_fusion, s32[1024]{0:T(1024)} %copy-done.10), kind=kCustom, calls=%fused_computation.9 | custom fusion | bytes 131136 | tf_op jit(solution)/shard_map/near_local/gather | solution.py:97
  58.0 1.0 %fusion.3 = f32[64,8,16]{2,1,0:T(8,128)} fusion(bf16[64,16,256]{2,1,0:T(8,128)(2,1)S(1)} %copy-done.1, bf16[64,8,256]{2,1,0:T(8,128)(2,1)S(1)} %gather_fusion.10), kind=kOutput, calls=%fused_computation.24 | convolution fusion | flops 4194304 | bytes 819200 | tf_op jit(solution)/shard_map/far_partial/rjl,jkl->jrk/dot_general | solution.py:66
  59.0 1.1 %copy.23 = f32[64,8,16]{0,2,1:T(8,128)S(1)} copy(f32[64,8,16]{2,1,0:T(8,128)} %fusion.3) | data formatting | bytes 65536 | tf_op jit(solution)/shard_map/far_partial/rjl,jkl->jrk/dot_general | solution.py:66
  60.0 1.1 %convolution_bitcast_fusion = f32[4,8,8,16]{3,2,1,0:T(8,128)S(1)} fusion(f32[64,8,16]{0,2,1:T(8,128)S(1)} %copy.23, s32[4,8]{1,0:T(4,128)S(1)} %multiply_add_fusion, s32[64]{0:T(128)} %param.17), kind=kOutput, calls=%fused_computation.12 | convolution fusion | flops 3147776 | bytes 49536 | tf_op jit(solution)/shard_map/far_partial/jc,jm->cm/dot_general | solution.py:70
  61.4 1.9 %collective-permute-start.9 = (f32[8,2176]{1,0:T(8,128)S(1)}, f32[8,2176]{1,0:T(8,128)S(1)}, u32[]{:S(2)}, u32[]{:S(2)}) collective-permute-start(f32[8,2176]{1,0:T(8,128)S(1)} %get-tuple-element.11), channel_id=1, source_target_pairs={{0,4},{4,8},{8,12},{12,0},{1,5},{5,9},{9,13},{13,1},{2,6},{6,10},{... | collective-permute-start | bytes 208904 | tf_op jit(solution)/shard_map/clus_exchange/ppermute | solution.py:8
  63.4 1.5 %fusion.21 = f32[16,8,256]{2,1,0:T(8,128)S(1)} fusion(bf16[16,256,256]{2,1,0:T(8,128)(2,1)S(1)} %copy-done, bf16[16,8,256]{2,1,0:T(8,128)(2,1)} %gather_fusion.9), kind=kOutput, calls=%fused_computation.60 | convolution fusion | flops 16777216 | bytes 2293760 | tf_op jit(solution)/shard_map/near_local/rjs,jts->rjt/dot_general | solution.py:98
  65.2 2.9 %collective-permute-done.9 = f32[8,2176]{1,0:T(8,128)S(1)} collective-permute-done((f32[8,2176]{1,0:T(8,128)S(1)}, f32[8,2176]{1,0:T(8,128)S(1)}, u32[]{:S(2)}, u32[]{:S(2)}) %collective-permute-start.9) | collective-permute-done | bytes 69664 | tf_op jit(solution)/shard_map/clus_exchange/ppermute | solution.py:8
  69.3 1.6 %collective-permute-start.11 = (f32[8,2176]{1,0:T(8,128)S(1)}, f32[8,2176]{1,0:T(8,128)S(1)}, u32[]{:S(2)}, u32[]{:S(2)}) collective-permute-start(f32[8,2176]{1,0:T(8,128)S(1)} %pad_maximum_fusion.8), channel_id=1, source_target_pairs={{0,2},{2,0},{1,3},{3,1},{4,6},{6,4},{5,7},{7,5},{8,10},{10,8},{9,1... | collective-permute-start | bytes 208904 | tf_op jit(solution)/shard_map/pair_sums/ppermute | solution.py:8
  70.9 2.8 %collective-permute-done.11 = f32[8,2176]{1,0:T(8,128)S(1)} collective-permute-done((f32[8,2176]{1,0:T(8,128)S(1)}, f32[8,2176]{1,0:T(8,128)S(1)}, u32[]{:S(2)}, u32[]{:S(2)}) %collective-permute-start.11) | collective-permute-done | bytes 69664 | tf_op jit(solution)/shard_map/pair_sums/ppermute | solution.py:8
  (120 shorter events, 17.4 us)
Async XLA Ops:
  0.0 18.6 %copy-start = (bf16[16,256,256]{2,1,0:T(8,128)(2,1)S(1)}, bf16[16,256,256]{2,1,0:T(8,128)(2,1)}, u32[]{:S(2)}) copy-start(bf16[16,256,256]{2,1,0:T(8,128)(2,1)} %param.11) | copy-start | bytes 6291460
  0.0 8.2 %copy-start.11 = (s32[64]{0:T(128)S(1)}, s32[64]{0:T(128)}, u32[]{:S(2)}) copy-start(s32[64]{0:T(128)} %param.17) | copy-start | bytes 772
  0.0 16.1 %copy-start.14 = (s32[16]{0:T(128)S(1)}, s32[16]{0:T(128)}, u32[]{:S(2)}) copy-start(s32[16]{0:T(128)} %param.13) | copy-start | bytes 196
  0.0 16.7 %copy-start.15 = (s32[16]{0:T(128)S(1)}, s32[16]{0:T(128)}, u32[]{:S(2)}) copy-start(s32[16]{0:T(128)} %param.12) | copy-start | bytes 196
  2.2 7.2 %copy-start.8 = (s32[1024]{0:T(1024)}, s32[1024]{0:T(1024)S(1)}, u32[]{:S(2)}) copy-start(s32[1024]{0:T(1024)S(1)} %pad_clamp_fusion.1) | copy-start | bytes 12292
  8.8 9.8 %copy-start.5 = (f32[4,8,128]{2,1,0:T(8,128)}, f32[4,8,128]{2,1,0:T(8,128)S(1)}, u32[]{:S(2)}) copy-start(f32[4,8,128]{2,1,0:T(8,128)S(1)} %reshape.135) | copy-start | bytes 49156
  10.0 14.7 %collective-permute-start = (f32[8,2176]{1,0:T(8,128)S(1)}, f32[8,2176]{1,0:T(8,128)}, u32[]{:S(2)}, u32[]{:S(2)}) collective-permute-start(f32[8,2176]{1,0:T(8,128)S(1)} %get-tuple-element.16), channel_id=1, source_target_pairs={{0,12},{4,0},{8,4},{12,8},{1,13},{5,1},{9,5},{13,9},{2,14},{6,2},{... | collective-permute-start | bytes 208904 | tf_op jit(solution)/shard_map/clus_exchange/ppermute | solution.py:8
  15.1 12.3 %collective-permute-start.2 = (f32[8,128]{1,0:T(8,128)}, f32[8,128]{1,0:T(8,128)}, u32[]{:S(2)}, u32[]{:S(2)}) collective-permute-start(f32[8,128]{1,0:T(8,128)} %get-tuple-element.27), channel_id=1, source_target_pairs={{0,8},{4,12},{8,0},{12,4},{1,9},{5,13},{9,1},{13,5},{2,10},{6,14},... | collective-permute-start | bytes 12296 | tf_op jit(solution)/shard_map/clus_exchange/ppermute | solution.py:8
  15.1 8.8 %collective-permute-start.1 = (f32[8,2176]{1,0:T(8,128)}, f32[8,2176]{1,0:T(8,128)}, u32[]{:S(2)}, u32[]{:S(2)}) collective-permute-start(f32[8,2176]{1,0:T(8,128)} %get-tuple-element.15), channel_id=1, source_target_pairs={{0,4},{4,8},{8,12},{12,0},{1,5},{5,9},{9,13},{13,1},{2,6},{6,10},{... | collective-permute-start | bytes 208904 | tf_op jit(solution)/shard_map/clus_exchange/ppermute | solution.py:8
  16.7 1.9 %copy-start.10 = (s32[1024]{0:T(1024)}, s32[1024]{0:T(1024)S(1)}, u32[]{:S(2)}) copy-start(s32[1024]{0:T(1024)S(1)} %pad_clamp_fusion.3) | copy-start | bytes 12292
  19.3 13.4 %copy-start.2 = (bf16[8,16,256]{2,1,0:T(8,128)(2,1)S(1)}, bf16[8,16,256]{2,1,0:T(8,128)(2,1)}, u32[]{:S(2)}) copy-start(bf16[8,16,256]{2,1,0:T(8,128)(2,1)} %param.14) | copy-start | bytes 196612
  19.3 15.6 %copy-start.1 = (bf16[64,16,256]{2,1,0:T(8,128)(2,1)S(1)}, bf16[64,16,256]{2,1,0:T(8,128)(2,1)}, u32[]{:S(2)}) copy-start(bf16[64,16,256]{2,1,0:T(8,128)(2,1)} %param.15) | copy-start | bytes 1572868
  23.9 4.2 %copy-start.9 = (s32[1024]{0:T(1024)}, s32[1024]{0:T(1024)S(1)}, u32[]{:S(2)}) copy-start(s32[1024]{0:T(1024)S(1)} %pad_clamp_fusion) | copy-start | bytes 12292
  28.1 4.4 %collective-permute-start.3 = (f32[8,2176]{1,0:T(8,128)S(1)}, f32[8,2176]{1,0:T(8,128)S(1)}, u32[]{:S(2)}, u32[]{:S(2)}) collective-permute-start(f32[8,2176]{1,0:T(8,128)S(1)} %pad_maximum_fusion.2), channel_id=1, source_target_pairs={{0,2},{2,0},{1,3},{3,1},{4,6},{6,4},{5,7},{7,5},{8,10},{10,8},{9,1... | collective-permute-start | bytes 208904 | tf_op jit(solution)/shard_map/pair_sums/ppermute | solution.py:8
  35.8 8.4 %copy-start.12 = (f32[16]{0:T(128)S(1)}, f32[16]{0:T(128)}, u32[]{:S(2)}) copy-start(f32[16]{0:T(128)} %get-tuple-element.30) | copy-start | bytes 196
  36.8 13.5 %copy-start.7 = (pred[4,8]{1,0:T(4,128)(4,1)S(1)}, pred[4,8]{1,0:T(4,128)(4,1)}, u32[]{:S(2)}) copy-start(pred[4,8]{1,0:T(4,128)(4,1)} %gather_fusion.1) | copy-start | bytes 100
  38.7 10.1 %collective-permute-start.4 = (f32[8,2176]{1,0:T(8,128)S(1)}, f32[8,2176]{1,0:T(8,128)S(1)}, u32[]{:S(2)}, u32[]{:S(2)}) collective-permute-start(f32[8,2176]{1,0:T(8,128)S(1)} %get-tuple-element.14), channel_id=1, source_target_pairs={{0,12},{4,0},{8,4},{12,8},{1,13},{5,1},{9,5},{13,9},{2,14},{6,2},{... | collective-permute-start | bytes 208904 | tf_op jit(solution)/shard_map/clus_exchange/ppermute | solution.py:8
  41.5 9.1 %collective-permute-start.6 = (f32[8,128]{1,0:T(8,128)}, f32[8,128]{1,0:T(8,128)}, u32[]{:S(2)}, u32[]{:S(2)}) collective-permute-start(f32[8,128]{1,0:T(8,128)} %get-tuple-element.24), channel_id=1, source_target_pairs={{0,8},{4,12},{8,0},{12,4},{1,9},{5,13},{9,1},{13,5},{2,10},{6,14},... | collective-permute-start | bytes 12296 | tf_op jit(solution)/shard_map/clus_exchange/ppermute | solution.py:8
  42.7 13.3 %copy-start.3 = (f32[8,2048]{1,0:T(8,128)S(1)}, f32[8,2048]{1,0:T(8,128)}, u32[]{:S(2)}) copy-start(f32[8,2048]{1,0:T(8,128)} %get-tuple-element.19) | copy-start | bytes 196612
  42.7 6.1 %collective-permute-start.5 = (f32[8,2176]{1,0:T(8,128)S(1)}, f32[8,2176]{1,0:T(8,128)S(1)}, u32[]{:S(2)}, u32[]{:S(2)}) collective-permute-start(f32[8,2176]{1,0:T(8,128)S(1)} %get-tuple-element.13), channel_id=1, source_target_pairs={{0,4},{4,8},{8,12},{12,0},{1,5},{5,9},{9,13},{13,1},{2,6},{6,10},{... | collective-permute-start | bytes 208904 | tf_op jit(solution)/shard_map/clus_exchange/ppermute | solution.py:8
  48.8 0.6 copy-start.6
  51.3 4.4 %collective-permute-start.7 = (f32[8,2176]{1,0:T(8,128)S(1)}, f32[8,2176]{1,0:T(8,128)S(1)}, u32[]{:S(2)}, u32[]{:S(2)}) collective-permute-start(f32[8,2176]{1,0:T(8,128)S(1)} %pad_maximum_fusion.5), channel_id=1, source_target_pairs={{0,2},{2,0},{1,3},{3,1},{4,6},{6,4},{5,7},{7,5},{8,10},{10,8},{9,1... | collective-permute-start | bytes 208904 | tf_op jit(solution)/shard_map/pair_sums/ppermute | solution.py:8
  58.0 6.8 %copy-start.13 = (f32[16]{0:T(128)S(1)}, f32[16]{0:T(128)}, u32[]{:S(2)}) copy-start(f32[16]{0:T(128)} %get-tuple-element.30) | copy-start | bytes 196
  61.3 6.8 %collective-permute-start.8 = (f32[8,2176]{1,0:T(8,128)S(1)}, f32[8,2176]{1,0:T(8,128)S(1)}, u32[]{:S(2)}, u32[]{:S(2)}) collective-permute-start(f32[8,2176]{1,0:T(8,128)S(1)} %get-tuple-element.12), channel_id=1, source_target_pairs={{0,12},{4,0},{8,4},{12,8},{1,13},{5,1},{9,5},{13,9},{2,14},{6,2},{... | collective-permute-start | bytes 208904 | tf_op jit(solution)/shard_map/clus_exchange/ppermute | solution.py:8
  61.4 7.9 %collective-permute-start.10 = (f32[8,128]{1,0:T(8,128)S(1)}, f32[8,128]{1,0:T(8,128)S(1)}, u32[]{:S(2)}, u32[]{:S(2)}) collective-permute-start(f32[8,128]{1,0:T(8,128)S(1)} %get-tuple-element.21), channel_id=1, source_target_pairs={{0,8},{4,12},{8,0},{12,4},{1,9},{5,13},{9,1},{13,5},{2,10},{6,14},... | collective-permute-start | bytes 12296 | tf_op jit(solution)/shard_map/clus_exchange/ppermute | solution.py:8
  61.4 12.6 %copy-start.4 = (f32[8,2048]{1,0:T(8,128)S(1)}, f32[8,2048]{1,0:T(8,128)}, u32[]{:S(2)}) copy-start(f32[8,2048]{1,0:T(8,128)} %get-tuple-element.18) | copy-start | bytes 196612
  61.4 6.6 %collective-permute-start.9 = (f32[8,2176]{1,0:T(8,128)S(1)}, f32[8,2176]{1,0:T(8,128)S(1)}, u32[]{:S(2)}, u32[]{:S(2)}) collective-permute-start(f32[8,2176]{1,0:T(8,128)S(1)} %get-tuple-element.11), channel_id=1, source_target_pairs={{0,4},{4,8},{8,12},{12,0},{1,5},{5,9},{9,13},{13,1},{2,6},{6,10},{... | collective-permute-start | bytes 208904 | tf_op jit(solution)/shard_map/clus_exchange/ppermute | solution.py:8
  69.3 4.4 %collective-permute-start.11 = (f32[8,2176]{1,0:T(8,128)S(1)}, f32[8,2176]{1,0:T(8,128)S(1)}, u32[]{:S(2)}, u32[]{:S(2)}) collective-permute-start(f32[8,2176]{1,0:T(8,128)S(1)} %pad_maximum_fusion.8), channel_id=1, source_target_pairs={{0,2},{2,0},{1,3},{3,1},{4,6},{6,4},{5,7},{7,5},{8,10},{10,8},{9,1... | collective-permute-start | bytes 208904 | tf_op jit(solution)/shard_map/pair_sums/ppermute | solution.py:8

commit v7 on v2

--- a/solution.py
+++ b/solution.py
@@ -51,6 +51,7 @@
 
     iterate = (coefficients[degree_top] * source).astype(jnp.bfloat16)
     result = source
+    scaled = None
     for step in range(degree_top):
         degree = degree_top - 1 - step
         with jax.named_scope("far_partial"):
@@ -75,6 +76,9 @@
                 carries_iterate = s == 1 or s == peer_count - 1
                 if carries_iterate:
                     outgoing = jnp.concatenate([iterate_wide, outgoing], axis=1)
+                if scaled is None:
+                    source_late, outgoing = lax.optimization_barrier((source, outgoing))
+                    scaled = [coefficients[d] * source_late for d in range(degree_top)]
                 incoming = shift(outgoing, "clus", peer_count, s)
                 if carries_iterate:
                     neighbour = incoming[:, :iterate_size].astype(jnp.bfloat16)
@@ -108,7 +112,9 @@
             far_field = jnp.einsum(
                 "rck,ckl->rcl", coef_sum, row_f32, precision=lax.Precision.HIGHEST
             )
-        result = near_sum + far_field + coefficients[degree] * source
+        if scaled is None:
+            scaled = [coefficients[d] * source for d in range(degree_top)]
+        result = near_sum + far_field + scaled[degree]
         iterate = result.astype(jnp.bfloat16)
     return result.reshape(rhs_here, clusters_here * leaf_size)
 

time: 56 us -> 56.9 us (1.016)
  other arithmetic: 4.99 us -> 6.54 us
  starting transfers between devices: 18.5 us -> 17.1 us
  waiting for transfers between devices: 19.5 us -> 20.3 us
    convert_element_type x3, other arithmetic: 3.45 us -> 1.43 us  [shards(): iterate.reshape(rhs_here, clusters_here * leaf_size).astype(jnp.float32)]
    convert_element_type x0 -> x1, other arithmetic: none -> 1.42 us  [shards(): iterate = (coefficients[degree_top] * source).astype(jnp.bfloat16)]
    ppermute x12, starting transfers between devices: 18.5 us -> 17.1 us  [shift(): lax.ppermute(value, axis, [(i, (i + step) % count) for i in range(count)])]
    convert_element_type x2, other arithmetic: 0.03 us -> 1.35 us  [shards(): iterate = result.astype(jnp.bfloat16)]
    ppermute x12, waiting for transfers between devices: 19.5 us -> 20.3 us  [shift(): lax.ppermute(value, axis, [(i, (i + step) % count) for i in range(count)])]
    add x1, other arithmetic: 0.64 us -> 1.33 us  [shards(): result = near_sum + far_field + scaled[degree]]
  transfers between devices with their start and end apart: 12 -> 12, of which waited for: 8 -> 9; matrix products, arithmetic and copies ran while one was open for 8% -> 8% of each run, Pallas kernels for 0% -> 0%
where the time goes in v7:
time: 56.9 us; the launch traced here: 56.6 us
  waiting for transfers between devices  20.3 us (36%)
  starting transfers between devices  17.1 us (30%)
  other arithmetic  6.54 us (11%)
  local copies, waits for them, and re-layouts  6.07 us (11%)
  matrix products  6.06 us (11%)
    ppermute x12, waiting for transfers between devices, shift(): lax.ppermute(value, axis, [(i, (i + step) % count) for i in range(count)])  20.3 us
    ppermute x12, starting transfers between devices, shift(): lax.ppermute(value, axis, [(i, (i + step) % count) for i in range(count)])  17.1 us
    dot_general x3, matrix products, shards(): jnp.einsum('rjs,jts->rjt', gathered, near_blocks, preferred_element_type=...  1.91 us
    gather x3, local copies, waits for them, and re-layouts, shards(): far_input = iterate[:, far_local, :]  1.79 us
    dot_general x3, matrix products, shards(): jnp.einsum('rjl,jkl->jrk', far_input, col_basis, preferred_element_type=j...  1.73 us
    gather x3, local copies, waits for them, and re-layouts, shards(): gathered = extended[:, near_index, :]  1.67 us
    slice x1, local copies, waits for them, and re-layouts, shards(): scaled = [coefficients[d] * source_late for d in range(degree_top)]  1.45 us
    convert_element_type x3, other arithmetic, shards(): iterate.reshape(rhs_here, clusters_here * leaf_size).astype(jnp.float32)  1.43 us
  transfers between devices with their start and end apart: 12, of which 9 were waited for; matrix products, arithmetic and copies ran while one was open for 8% of the time, Pallas kernels for 0%

profile of v7, /device:TPU:0, one launch (start us, length us, event | category | flops | bytes accessed | tf_op | source)
XLA Modules:
  0.0 56.6 jit_solution(16364388214614796085)
XLA Ops:
  0.1 0.8 %compare_select_fusion.1 = s32[64]{0:T(128)S(1)} fusion(s32[64]{0:T(128)} %param.16, s32[]{:T(128)S(6)} %mul.35), kind=kLoop, calls=%fused_computation.98 | loop fusion | flops 256 | bytes 516 | tf_op jit(solution)/shard_map/far_partial/select_n | solution.py:58
  0.9 1.5 %fusion.53 = (f32[1]{0:T(128)}, f32[1]{0:T(128)}, f32[1]{0:T(128)}, f32[1]{0:T(128)}) fusion(f32[4]{0:T(128)} %param.10), kind=kLoop, calls=%fused_computation.120 | loop fusion | bytes 32 | tf_op jit(solution)/shard_map/clus_exchange/slice | solution.py:81
  2.3 1.4 %fusion.21 = f32[8,2048]{1,0:T(8,128)S(1)} fusion(f32[8,2048]{1,0:T(8,128)} %param.9, f32[]{:T(128)} %bitcast.1), kind=kLoop, calls=%fused_computation.59 | loop fusion | flops 49152 | bytes 131076 | tf_op jit(solution)/shard_map/clus_exchange/convert_element_type | solution.py:70
  3.7 1.4 %multiply_convert_fusion.1 = bf16[8,8,256]{2,0,1:T(8,128)(2,1)S(1)} fusion(f32[8,8,256]{2,0,1:T(8,128)} %bitcast.152, f32[]{:T(128)} %bitcast.1), kind=kLoop, calls=%fused_computation.58 | loop fusion | flops 32768 | bytes 98308 | tf_op jit(solution)/shard_map/convert_element_type | solution.py:52
  5.8 1.3 %fusion.4 = f32[64,8,16]{2,1,0:T(8,128)S(1)} fusion(bf16[64,16,256]{2,1,0:T(8,128)(2,1)} %param.15, bf16[64,8,256]{2,1,0:T(8,128)(2,1)S(1)} %gather_fusion), kind=kOutput, calls=%fused_computation.19 | convolution fusion | flops 4194304 | bytes 819200 | tf_op jit(solution)/shard_map/far_partial/rjl,jkl->jrk/dot_general | solution.py:59
  7.8 3.1 %collective-permute-start.1 = (f32[8,2176]{1,0:T(8,128)S(1)}, f32[8,2176]{1,0:T(8,128)S(1)}, u32[]{:S(2)}, u32[]{:S(2)}) collective-permute-start(f32[8,2176]{1,0:T(8,128)S(1)} %get-tuple-element.7), channel_id=1, source_target_pairs={{0,4},{4,8},{8,12},{12,0},{1,5},{5,9},{9,13},{13,1},{2,6},{6,10},{... | collective-permute-start | bytes 208904 | tf_op jit(solution)/shard_map/clus_exchange/ppermute | solution.py:8
  10.9 2.1 %collective-permute-start = (f32[8,2176]{1,0:T(8,128)S(1)}, f32[8,2176]{1,0:T(8,128)S(1)}, u32[]{:S(2)}, u32[]{:S(2)}) collective-permute-start(f32[8,2176]{1,0:T(8,128)S(1)} %get-tuple-element.13), channel_id=1, source_target_pairs={{0,12},{4,0},{8,4},{12,8},{1,13},{5,1},{9,5},{13,9},{2,14},{6,2},{... | collective-permute-start | bytes 208904 | tf_op jit(solution)/shard_map/clus_exchange/ppermute | solution.py:8
  13.0 0.9 %collective-permute-start.2 = (f32[8,128]{1,0:T(8,128)S(1)}, f32[8,128]{1,0:T(8,128)S(1)}, u32[]{:S(2)}, u32[]{:S(2)}) collective-permute-start(f32[8,128]{1,0:T(8,128)S(1)} %get-tuple-element.21), channel_id=1, source_target_pairs={{0,8},{4,12},{8,0},{12,4},{1,9},{5,13},{9,1},{13,5},{2,10},{6,14},... | collective-permute-start | bytes 12296 | tf_op jit(solution)/shard_map/clus_exchange/ppermute | solution.py:8
  14.0 1.4 %collective-permute-done.1 = f32[8,2176]{1,0:T(8,128)S(1)} collective-permute-done((f32[8,2176]{1,0:T(8,128)S(1)}, f32[8,2176]{1,0:T(8,128)S(1)}, u32[]{:S(2)}, u32[]{:S(2)}) %collective-permute-start.1) | collective-permute-done | bytes 69664 | tf_op jit(solution)/shard_map/clus_exchange/ppermute | solution.py:8
  15.4 0.6 %collective-permute-done = f32[8,2176]{1,0:T(8,128)S(1)} collective-permute-done((f32[8,2176]{1,0:T(8,128)S(1)}, f32[8,2176]{1,0:T(8,128)S(1)}, u32[]{:S(2)}, u32[]{:S(2)}) %collective-permute-start) | collective-permute-done | bytes 69664 | tf_op jit(solution)/shard_map/clus_exchange/ppermute | solution.py:8
  16.6 0.6 %fusion.19 = f32[16,8,256]{2,1,0:T(8,128)S(1)} fusion(bf16[16,256,256]{2,1,0:T(8,128)(2,1)S(1)} %copy-done, bf16[16,8,256]{2,1,0:T(8,128)(2,1)S(1)} %gather_fusion.1), kind=kOutput, calls=%fused_computation.52 | convolution fusion | flops 16777216 | bytes 2293760 | tf_op jit(solution)/shard_map/near_partial/rjs,jts->rjt/dot_general | solution.py:95
  17.5 1.7 %collective-permute-start.3 = (f32[8,2176]{1,0:T(8,128)S(1)}, f32[8,2176]{1,0:T(8,128)S(1)}, u32[]{:S(2)}, u32[]{:S(2)}) collective-permute-start(f32[8,2176]{1,0:T(8,128)S(1)} %pad_maximum_fusion.5), channel_id=1, source_target_pairs={{0,2},{2,0},{1,3},{3,1},{4,6},{6,4},{5,7},{7,5},{8,10},{10,8},{9,1... | collective-permute-start | bytes 208904 | tf_op jit(solution)/shard_map/pair_sums/ppermute | solution.py:8
  19.2 2.7 %collective-permute-done.3 = f32[8,2176]{1,0:T(8,128)S(1)} collective-permute-done((f32[8,2176]{1,0:T(8,128)S(1)}, f32[8,2176]{1,0:T(8,128)S(1)}, u32[]{:S(2)}, u32[]{:S(2)}) %collective-permute-start.3) | collective-permute-done | bytes 69664 | tf_op jit(solution)/shard_map/pair_sums/ppermute | solution.py:8
  22.2 0.7 %add_convert_fusion.1 = bf16[8,8,256]{2,0,1:T(8,128)(2,1)S(1)} fusion(f32[8,8,256]{2,0,1:T(8,128)S(1)} %bitcast.153, f32[8,8,256]{2,0,1:T(8,128)S(1)} %bitcast.162, f32[8,8,256]{2,0,1:T(8,128)S(1)} %convolution_bitcast_fusion.7, f32[]{:T(128)} %bitcast.22), kind=kLoop, calls=%fused_computation.56 | loop fusion | flops 65536 | bytes 229380 | tf_op jit(solution)/shard_map/convert_element_type | solution.py:118
  22.9 0.6 %gather_fusion.2 = bf16[64,8,256]{2,1,0:T(8,128)(2,1)S(1)} fusion(bf16[8,8,256]{2,0,1:T(8,128)(2,1)S(1)} %add_convert_fusion.1, s32[1024]{0:T(1024)S(1)} %pad_clamp_fusion.1), kind=kCustom, calls=%fused_computation.2 | custom fusion | bytes 524544 | tf_op jit(solution)/shard_map/far_partial/gather | solution.py:58
  24.5 3.1 %collective-permute-start.4 = (f32[8,2176]{1,0:T(8,128)S(1)}, f32[8,2176]{1,0:T(8,128)S(1)}, u32[]{:S(2)}, u32[]{:S(2)}) collective-permute-start(f32[8,2176]{1,0:T(8,128)S(1)} %get-tuple-element.12), channel_id=1, source_target_pairs={{0,12},{4,0},{8,4},{12,8},{1,13},{5,1},{9,5},{13,9},{2,14},{6,2},{... | collective-permute-start | bytes 208904 | tf_op jit(solution)/shard_map/clus_exchange/ppermute | solution.py:8
  27.6 0.7 %collective-permute-start.6 = (f32[8,128]{1,0:T(8,128)S(1)}, f32[8,128]{1,0:T(8,128)S(1)}, u32[]{:S(2)}, u32[]{:S(2)}) collective-permute-start(f32[8,128]{1,0:T(8,128)S(1)} %get-tuple-element.19), channel_id=1, source_target_pairs={{0,8},{4,12},{8,0},{12,4},{1,9},{5,13},{9,1},{13,5},{2,10},{6,14},... | collective-permute-start | bytes 12296 | tf_op jit(solution)/shard_map/clus_exchange/ppermute | solution.py:8
  28.3 1.2 %collective-permute-done.4 = f32[8,2176]{1,0:T(8,128)S(1)} collective-permute-done((f32[8,2176]{1,0:T(8,128)S(1)}, f32[8,2176]{1,0:T(8,128)S(1)}, u32[]{:S(2)}, u32[]{:S(2)}) %collective-permute-start.4) | collective-permute-done | bytes 69664 | tf_op jit(solution)/shard_map/clus_exchange/ppermute | solution.py:8
  29.5 4.2 %collective-permute-done.5 = f32[8,2176]{1,0:T(8,128)S(1)} collective-permute-done((f32[8,2176]{1,0:T(8,128)S(1)}, f32[8,2176]{1,0:T(8,128)S(1)}, u32[]{:S(2)}, u32[]{:S(2)}) %collective-permute-start.5) | collective-permute-done | bytes 69664 | tf_op jit(solution)/shard_map/clus_exchange/ppermute | solution.py:8
  34.3 0.6 %fusion.17 = f32[16,8,256]{2,1,0:T(8,128)S(1)} fusion(bf16[16,256,256]{2,1,0:T(8,128)(2,1)S(1)} %copy-done, bf16[16,8,256]{2,1,0:T(8,128)(2,1)S(1)} %gather_fusion.3), kind=kOutput, calls=%fused_computation.50 | convolution fusion | flops 16777216 | bytes 2293760 | tf_op jit(solution)/shard_map/near_partial/rjs,jts->rjt/dot_general | solution.py:95
  35.2 1.7 %collective-permute-start.7 = (f32[8,2176]{1,0:T(8,128)S(1)}, f32[8,2176]{1,0:T(8,128)S(1)}, u32[]{:S(2)}, u32[]{:S(2)}) collective-permute-start(f32[8,2176]{1,0:T(8,128)S(1)} %pad_maximum_fusion.8), channel_id=1, source_target_pairs={{0,2},{2,0},{1,3},{3,1},{4,6},{6,4},{5,7},{7,5},{8,10},{10,8},{9,1... | collective-permute-start | bytes 208904 | tf_op jit(solution)/shard_map/pair_sums/ppermute | solution.py:8
  36.9 2.7 %collective-permute-done.7 = f32[8,2176]{1,0:T(8,128)S(1)} collective-permute-done((f32[8,2176]{1,0:T(8,128)S(1)}, f32[8,2176]{1,0:T(8,128)S(1)}, u32[]{:S(2)}, u32[]{:S(2)}) %collective-permute-start.7) | collective-permute-done | bytes 69664 | tf_op jit(solution)/shard_map/pair_sums/ppermute | solution.py:8
  39.9 0.7 %add_convert_fusion = bf16[8,8,256]{2,0,1:T(8,128)(2,1)S(1)} fusion(f32[8,8,256]{2,0,1:T(8,128)S(1)} %bitcast.154, f32[8,8,256]{2,0,1:T(8,128)S(1)} %bitcast.163, f32[8,8,256]{2,0,1:T(8,128)S(1)} %convolution_bitcast_fusion.5, f32[]{:T(128)} %bitcast.43), kind=kLoop, calls=%fused_computation.55 | loop fusion | flops 65536 | bytes 229380 | tf_op jit(solution)/shard_map/convert_element_type | solution.py:118
  40.6 0.6 %gather_fusion.4 = bf16[64,8,256]{2,1,0:T(8,128)(2,1)S(1)} fusion(bf16[8,8,256]{2,0,1:T(8,128)(2,1)S(1)} %add_convert_fusion, s32[1024]{0:T(1024)S(1)} %pad_clamp_fusion.1), kind=kCustom, calls=%fused_computation.4 | custom fusion | bytes 524544 | tf_op jit(solution)/shard_map/far_partial/gather | solution.py:58
  42.1 0.8 %collective-permute-start.8 = (f32[8,2176]{1,0:T(8,128)S(1)}, f32[8,2176]{1,0:T(8,128)S(1)}, u32[]{:S(2)}, u32[]{:S(2)}) collective-permute-start(f32[8,2176]{1,0:T(8,128)S(1)} %get-tuple-element.10), channel_id=1, source_target_pairs={{0,12},{4,0},{8,4},{12,8},{1,13},{5,1},{9,5},{13,9},{2,14},{6,2},{... | collective-permute-start | bytes 208904 | tf_op jit(solution)/shard_map/clus_exchange/ppermute | solution.py:8
  42.9 1.3 %collective-permute-start.9 = (f32[8,2176]{1,0:T(8,128)S(1)}, f32[8,2176]{1,0:T(8,128)S(1)}, u32[]{:S(2)}, u32[]{:S(2)}) collective-permute-start(f32[8,2176]{1,0:T(8,128)S(1)} %get-tuple-element.9), channel_id=1, source_target_pairs={{0,4},{4,8},{8,12},{12,0},{1,5},{5,9},{9,13},{13,1},{2,6},{6,10},{... | collective-permute-start | bytes 208904 | tf_op jit(solution)/shard_map/clus_exchange/ppermute | solution.py:8
  44.2 2.3 %collective-permute-done.8 = f32[8,2176]{1,0:T(8,128)S(1)} collective-permute-done((f32[8,2176]{1,0:T(8,128)S(1)}, f32[8,2176]{1,0:T(8,128)S(1)}, u32[]{:S(2)}, u32[]{:S(2)}) %collective-permute-start.8) | collective-permute-done | bytes 69664 | tf_op jit(solution)/shard_map/clus_exchange/ppermute | solution.py:8
  46.5 2.5 %collective-permute-done.9 = f32[8,2176]{1,0:T(8,128)S(1)} collective-permute-done((f32[8,2176]{1,0:T(8,128)S(1)}, f32[8,2176]{1,0:T(8,128)S(1)}, u32[]{:S(2)}, u32[]{:S(2)}) %collective-permute-start.9) | collective-permute-done | bytes 69664 | tf_op jit(solution)/shard_map/clus_exchange/ppermute | solution.py:8
  49.6 0.6 %fusion.15 = f32[16,8,256]{2,1,0:T(8,128)S(1)} fusion(bf16[16,256,256]{2,1,0:T(8,128)(2,1)S(1)} %copy-done, bf16[16,8,256]{2,1,0:T(8,128)(2,1)S(1)} %gather_fusion.5), kind=kOutput, calls=%fused_computation.48 | convolution fusion | flops 16777216 | bytes 2293760 | tf_op jit(solution)/shard_map/near_partial/rjs,jts->rjt/dot_general | solution.py:95
  50.6 1.7 %collective-permute-start.11 = (f32[8,2176]{1,0:T(8,128)S(1)}, f32[8,2176]{1,0:T(8,128)S(1)}, u32[]{:S(2)}, u32[]{:S(2)}) collective-permute-start(f32[8,2176]{1,0:T(8,128)S(1)} %pad_maximum_fusion.11), channel_id=1, source_target_pairs={{0,2},{2,0},{1,3},{3,1},{4,6},{6,4},{5,7},{7,5},{8,10},{10,8},{9,1... | collective-permute-start | bytes 208904 | tf_op jit(solution)/shard_map/pair_sums/ppermute | solution.py:8
  52.3 2.7 %collective-permute-done.11 = f32[8,2176]{1,0:T(8,128)S(1)} collective-permute-done((f32[8,2176]{1,0:T(8,128)S(1)}, f32[8,2176]{1,0:T(8,128)S(1)}, u32[]{:S(2)}, u32[]{:S(2)}) %collective-permute-start.11) | collective-permute-done | bytes 69664 | tf_op jit(solution)/shard_map/pair_sums/ppermute | solution.py:8
  55.2 1.3 %multiply_add_fusion = f32[8,8,256]{2,0,1:T(8,128)} fusion(f32[8,8,256]{2,0,1:T(8,128)S(1)} %bitcast.155, f32[8,8,256]{2,0,1:T(8,128)S(1)} %bitcast.164, f32[8,8,256]{2,0,1:T(8,128)S(1)} %convolution_bitcast_fusion.3, f32[]{:T(128)} %bitcast.63), kind=kLoop, calls=%fused_computation.54 | loop fusion | flops 49152 | bytes 262148 | tf_op jit(solution)/shard_map/add | solution.py:117
  (83 shorter events, 6.5 us)
Async XLA Ops:
  0.0 16.6 %copy-start = (bf16[16,256,256]{2,1,0:T(8,128)(2,1)S(1)}, bf16[16,256,256]{2,1,0:T(8,128)(2,1)}, u32[]{:S(2)}) copy-start(bf16[16,256,256]{2,1,0:T(8,128)(2,1)} %param.11) | copy-start | bytes 6291460
  0.0 7.2 %copy-start.4 = (s32[64]{0:T(128)S(1)}, s32[64]{0:T(128)}, u32[]{:S(2)}) copy-start(s32[64]{0:T(128)} %param.17) | copy-start | bytes 772
  0.0 13.9 %copy-start.5 = (s32[16]{0:T(128)S(1)}, s32[16]{0:T(128)}, u32[]{:S(2)}) copy-start(s32[16]{0:T(128)} %param.13) | copy-start | bytes 196
  0.0 13.9 %copy-start.6 = (s32[16]{0:T(128)S(1)}, s32[16]{0:T(128)}, u32[]{:S(2)}) copy-start(s32[16]{0:T(128)} %param.12) | copy-start | bytes 196
  7.2 14.9 %copy-start.3 = (bf16[8,16,256]{2,1,0:T(8,128)(2,1)S(1)}, bf16[8,16,256]{2,1,0:T(8,128)(2,1)}, u32[]{:S(2)}) copy-start(bf16[8,16,256]{2,1,0:T(8,128)(2,1)} %param.14) | copy-start | bytes 196612
  7.6 14.6 %copy-start.2 = (f32[8,2048]{1,0:T(8,128)S(1)}, f32[8,2048]{1,0:T(8,128)}, u32[]{:S(2)}) copy-start(f32[8,2048]{1,0:T(8,128)} %param.9) | copy-start | bytes 196612
  7.8 7.6 %collective-permute-start.1 = (f32[8,2176]{1,0:T(8,128)S(1)}, f32[8,2176]{1,0:T(8,128)S(1)}, u32[]{:S(2)}, u32[]{:S(2)}) collective-permute-start(f32[8,2176]{1,0:T(8,128)S(1)} %get-tuple-element.7), channel_id=1, source_target_pairs={{0,4},{4,8},{8,12},{12,0},{1,5},{5,9},{9,13},{13,1},{2,6},{6,10},{... | collective-permute-start | bytes 208904 | tf_op jit(solution)/shard_map/clus_exchange/ppermute | solution.py:8
  10.9 5.1 %collective-permute-start = (f32[8,2176]{1,0:T(8,128)S(1)}, f32[8,2176]{1,0:T(8,128)S(1)}, u32[]{:S(2)}, u32[]{:S(2)}) collective-permute-start(f32[8,2176]{1,0:T(8,128)S(1)} %get-tuple-element.13), channel_id=1, source_target_pairs={{0,12},{4,0},{8,4},{12,8},{1,13},{5,1},{9,5},{13,9},{2,14},{6,2},{... | collective-permute-start | bytes 208904 | tf_op jit(solution)/shard_map/clus_exchange/ppermute | solution.py:8
  13.0 4.5 %collective-permute-start.2 = (f32[8,128]{1,0:T(8,128)S(1)}, f32[8,128]{1,0:T(8,128)S(1)}, u32[]{:S(2)}, u32[]{:S(2)}) collective-permute-start(f32[8,128]{1,0:T(8,128)S(1)} %get-tuple-element.21), channel_id=1, source_target_pairs={{0,8},{4,12},{8,0},{12,4},{1,9},{5,13},{9,1},{13,5},{2,10},{6,14},... | collective-permute-start | bytes 12296 | tf_op jit(solution)/shard_map/clus_exchange/ppermute | solution.py:8
  16.0 7.5 %copy-start.1 = (bf16[64,16,256]{2,1,0:T(8,128)(2,1)S(1)}, bf16[64,16,256]{2,1,0:T(8,128)(2,1)}, u32[]{:S(2)}) copy-start(bf16[64,16,256]{2,1,0:T(8,128)(2,1)} %param.15) | copy-start | bytes 1572868
  17.5 4.4 %collective-permute-start.3 = (f32[8,2176]{1,0:T(8,128)S(1)}, f32[8,2176]{1,0:T(8,128)S(1)}, u32[]{:S(2)}, u32[]{:S(2)}) collective-permute-start(f32[8,2176]{1,0:T(8,128)S(1)} %pad_maximum_fusion.5), channel_id=1, source_target_pairs={{0,2},{2,0},{1,3},{3,1},{4,6},{6,4},{5,7},{7,5},{8,10},{10,8},{9,1... | collective-permute-start | bytes 208904 | tf_op jit(solution)/shard_map/pair_sums/ppermute | solution.py:8
  24.5 5.1 %collective-permute-start.4 = (f32[8,2176]{1,0:T(8,128)S(1)}, f32[8,2176]{1,0:T(8,128)S(1)}, u32[]{:S(2)}, u32[]{:S(2)}) collective-permute-start(f32[8,2176]{1,0:T(8,128)S(1)} %get-tuple-element.12), channel_id=1, source_target_pairs={{0,12},{4,0},{8,4},{12,8},{1,13},{5,1},{9,5},{13,9},{2,14},{6,2},{... | collective-permute-start | bytes 208904 | tf_op jit(solution)/shard_map/clus_exchange/ppermute | solution.py:8
  27.6 6.1 %collective-permute-start.5 = (f32[8,2176]{1,0:T(8,128)S(1)}, f32[8,2176]{1,0:T(8,128)S(1)}, u32[]{:S(2)}, u32[]{:S(2)}) collective-permute-start(f32[8,2176]{1,0:T(8,128)S(1)} %get-tuple-element.11), channel_id=1, source_target_pairs={{0,4},{4,8},{8,12},{12,0},{1,5},{5,9},{9,13},{13,1},{2,6},{6,10},{... | collective-permute-start | bytes 208904 | tf_op jit(solution)/shard_map/clus_exchange/ppermute | solution.py:8
  27.6 7.6 %collective-permute-start.6 = (f32[8,128]{1,0:T(8,128)S(1)}, f32[8,128]{1,0:T(8,128)S(1)}, u32[]{:S(2)}, u32[]{:S(2)}) collective-permute-start(f32[8,128]{1,0:T(8,128)S(1)} %get-tuple-element.19), channel_id=1, source_target_pairs={{0,8},{4,12},{8,0},{12,4},{1,9},{5,13},{9,1},{13,5},{2,10},{6,14},... | collective-permute-start | bytes 12296 | tf_op jit(solution)/shard_map/clus_exchange/ppermute | solution.py:8
  35.2 4.4 %collective-permute-start.7 = (f32[8,2176]{1,0:T(8,128)S(1)}, f32[8,2176]{1,0:T(8,128)S(1)}, u32[]{:S(2)}, u32[]{:S(2)}) collective-permute-start(f32[8,2176]{1,0:T(8,128)S(1)} %pad_maximum_fusion.8), channel_id=1, source_target_pairs={{0,2},{2,0},{1,3},{3,1},{4,6},{6,4},{5,7},{7,5},{8,10},{10,8},{9,1... | collective-permute-start | bytes 208904 | tf_op jit(solution)/shard_map/pair_sums/ppermute | solution.py:8
  42.1 4.4 %collective-permute-start.8 = (f32[8,2176]{1,0:T(8,128)S(1)}, f32[8,2176]{1,0:T(8,128)S(1)}, u32[]{:S(2)}, u32[]{:S(2)}) collective-permute-start(f32[8,2176]{1,0:T(8,128)S(1)} %get-tuple-element.10), channel_id=1, source_target_pairs={{0,12},{4,0},{8,4},{12,8},{1,13},{5,1},{9,5},{13,9},{2,14},{6,2},{... | collective-permute-start | bytes 208904 | tf_op jit(solution)/shard_map/clus_exchange/ppermute | solution.py:8
  42.9 6.1 %collective-permute-start.9 = (f32[8,2176]{1,0:T(8,128)S(1)}, f32[8,2176]{1,0:T(8,128)S(1)}, u32[]{:S(2)}, u32[]{:S(2)}) collective-permute-start(f32[8,2176]{1,0:T(8,128)S(1)} %get-tuple-element.9), channel_id=1, source_target_pairs={{0,4},{4,8},{8,12},{12,0},{1,5},{5,9},{9,13},{13,1},{2,6},{6,10},{... | collective-permute-start | bytes 208904 | tf_op jit(solution)/shard_map/clus_exchange/ppermute | solution.py:8
  44.2 6.3 %collective-permute-start.10 = (f32[8,128]{1,0:T(8,128)S(1)}, f32[8,128]{1,0:T(8,128)S(1)}, u32[]{:S(2)}, u32[]{:S(2)}) collective-permute-start(f32[8,128]{1,0:T(8,128)S(1)} %get-tuple-element.16), channel_id=1, source_target_pairs={{0,8},{4,12},{8,0},{12,4},{1,9},{5,13},{9,1},{13,5},{2,10},{6,14},... | collective-permute-start | bytes 12296 | tf_op jit(solution)/shard_map/clus_exchange/ppermute | solution.py:8
  50.6 4.4 %collective-permute-start.11 = (f32[8,2176]{1,0:T(8,128)S(1)}, f32[8,2176]{1,0:T(8,128)S(1)}, u32[]{:S(2)}, u32[]{:S(2)}) collective-permute-start(f32[8,2176]{1,0:T(8,128)S(1)} %pad_maximum_fusion.11), channel_id=1, source_target_pairs={{0,2},{2,0},{1,3},{3,1},{4,6},{6,4},{5,7},{7,5},{8,10},{10,8},{9,1... | collective-permute-start | bytes 208904 | tf_op jit(solution)/shard_map/pair_sums/ppermute | solution.py:8

commit v8 on v2

--- a/solution.py
+++ b/solution.py
@@ -6,6 +6,23 @@
 
 def shift(value, axis, count, step):
     return lax.ppermute(value, axis, [(i, (i + step) % count) for i in range(count)])
+
+
+def split_three(value):
+    high = lax.reduce_precision(value, exponent_bits=8, mantissa_bits=7)
+    rest = value - high
+    middle = lax.reduce_precision(rest, exponent_bits=8, mantissa_bits=7)
+    low = rest - middle
+    parts = [high, middle, low]
+    return jnp.concatenate([part.astype(jnp.bfloat16) for part in parts], axis=-1)
+
+
+def join_three(parts):
+    width = parts.shape[-1] // 3
+    high, middle, low = (
+        parts[..., k * width : (k + 1) * width].astype(jnp.float32) for k in range(3)
+    )
+    return (high + middle) + low
 
 
 def pair_total(value, pair_count, pair_index):
@@ -66,25 +83,25 @@
             )
         with jax.named_scope("clus_exchange"):
             far_mine = partial_value[my_index]
-            iterate_wide = iterate.reshape(rhs_here, clusters_here * leaf_size).astype(jnp.float32)
+            iterate_flat = iterate.reshape(rhs_here, clusters_here * leaf_size)
             iterate_size = clusters_here * leaf_size
             from_minus = iterate
             from_plus = iterate
             for s in range(1, peer_count):
-                outgoing = partial_value[(my_index + s) % peer_count]
+                outgoing = split_three(partial_value[(my_index + s) % peer_count])
                 carries_iterate = s == 1 or s == peer_count - 1
                 if carries_iterate:
-                    outgoing = jnp.concatenate([iterate_wide, outgoing], axis=1)
+                    outgoing = jnp.concatenate([iterate_flat, outgoing], axis=1)
                 incoming = shift(outgoing, "clus", peer_count, s)
                 if carries_iterate:
-                    neighbour = incoming[:, :iterate_size].astype(jnp.bfloat16)
+                    neighbour = incoming[:, :iterate_size]
                     neighbour = neighbour.reshape(rhs_here, clusters_here, leaf_size)
                     if s == 1:
                         from_minus = neighbour
                     if s == peer_count - 1:
                         from_plus = neighbour
                     incoming = incoming[:, iterate_size:]
-                far_mine = far_mine + incoming
+                far_mine = far_mine + join_three(incoming)
         with jax.named_scope("near_partial"):
             extended = jnp.concatenate([iterate, from_plus, from_minus], axis=1)
             gathered = extended[:, near_index, :]

time: 56 us -> 55.2 us (0.986)
  starting transfers between devices: 18.5 us -> 16.1 us
  waiting for transfers between devices: 19.5 us -> 21.2 us
    ppermute x12, starting transfers between devices: 18.5 us -> 16.1 us  [shift(): lax.ppermute(value, axis, [(i, (i + step) % count) for i in range(count)])]
    ppermute x12, waiting for transfers between devices: 19.5 us -> 21.2 us  [shift(): lax.ppermute(value, axis, [(i, (i + step) % count) for i in range(count)])]
    convert_element_type x3 -> x4, other arithmetic: 3.45 us -> 3.49 us  [the longest x1 3.43 us: shards(): iterate = (coefficients[degree_top] * source).astype(jnp.bfloat16)]
  transfers between devices with their start and end apart: 12 -> 12, of which waited for: 8 -> 6; matrix products, arithmetic and copies ran while one was open for 8% -> 8% of each run, Pallas kernels for 0% -> 0%
where the time goes in v8:
time: 55.2 us; the launch traced here: 54.9 us
  waiting for transfers between devices  21.2 us (38%)
  starting transfers between devices  16.1 us (29%)
  local copies, waits for them, and re-layouts  6.07 us (11%)
  matrix products  6.05 us (11%)
  other arithmetic  5.04 us (9%)
    ppermute x12, waiting for transfers between devices, shift(): lax.ppermute(value, axis, [(i, (i + step) % count) for i in range(count)])  21.2 us
    ppermute x12, starting transfers between devices, shift(): lax.ppermute(value, axis, [(i, (i + step) % count) for i in range(count)])  16.1 us
    convert_element_type x1, other arithmetic, shards(): iterate = (coefficients[degree_top] * source).astype(jnp.bfloat16)  3.43 us
    dot_general x3, matrix products, shards(): jnp.einsum('rjs,jts->rjt', gathered, near_blocks, preferred_element_type=...  1.91 us
    gather x3, local copies, waits for them, and re-layouts, shards(): far_input = iterate[:, far_local, :]  1.79 us
    dot_general x3, matrix products, shards(): jnp.einsum('rjl,jkl->jrk', far_input, col_basis, preferred_element_type=j...  1.73 us
    gather x3, local copies, waits for them, and re-layouts, shards(): gathered = extended[:, near_index, :]  1.67 us
    slice x1, local copies, waits for them, and re-layouts, shards(): iterate = (coefficients[degree_top] * source).astype(jnp.bfloat16)  1.51 us
  transfers between devices with their start and end apart: 12, of which 6 were waited for; matrix products, arithmetic and copies ran while one was open for 8% of the time, Pallas kernels for 0%

profile of v8, /device:TPU:0, one launch (start us, length us, event | category | flops | bytes accessed | tf_op | source)
XLA Modules:
  0.0 54.9 jit_solution(11141702502110791763)
XLA Ops:
  0.1 1.5 %fusion.64 = (f32[1]{0:T(128)}, f32[1]{0:T(128)}, f32[1]{0:T(128)}, f32[1]{0:T(128)}) fusion(f32[4]{0:T(128)} %param.10), kind=kLoop, calls=%fused_computation.154 | loop fusion | bytes 32 | tf_op jit(solution)/shard_map/slice | solution.py:69
  1.6 0.7 %compare_select_fusion.1 = s32[64]{0:T(128)S(1)} fusion(s32[64]{0:T(128)} %param.16, s32[]{:T(128)S(6)} %mul.41), kind=kLoop, calls=%fused_computation.132 | loop fusion | flops 256 | bytes 516 | tf_op jit(solution)/shard_map/far_partial/select_n | solution.py:74
  2.2 3.4 %multiply_convert_fusion = (bf16[8,2048]{1,0:T(8,128)(2,1)S(1)}, f32[8,2048]{1,0:T(8,128)S(1)}, f32[8,2048]{1,0:T(8,128)S(1)}, f32[8,2048]{1,0:T(8,128)S(1)}) fusion(f32[8,2048]{1,0:T(8,128)} %param.9, f32[]{:T(128)} %bitcast.1, f32[]{:T(128)} %bitcast.22, f32[]{:T(128)} %bitcast.63, f32[]{:T(128)} %bitcast.43), kind=kLoop, calls=%fused_computation.45 | loop fusion | flops 81920 | bytes 294928 | tf_op jit(solution)/shard_map/convert_element_type | solution.py:69
  5.7 0.6 %gather_fusion = bf16[64,8,256]{2,1,0:T(8,128)(2,1)S(1)} fusion(bf16[8,8,256]{2,0,1:T(8,128)(2,1)S(1)} %bitcast.208, s32[1024]{0:T(1024)S(1)} %pad_clamp_fusion.1), kind=kCustom, calls=%fused_computation | custom fusion | bytes 524544 | tf_op jit(solution)/shard_map/far_partial/gather | solution.py:74
  6.3 1.3 %fusion.4 = f32[64,8,16]{2,1,0:T(8,128)S(1)} fusion(bf16[64,16,256]{2,1,0:T(8,128)(2,1)} %param.15, bf16[64,8,256]{2,1,0:T(8,128)(2,1)S(1)} %gather_fusion), kind=kOutput, calls=%fused_computation.19 | convolution fusion | flops 4194304 | bytes 819200 | tf_op jit(solution)/shard_map/far_partial/rjl,jkl->jrk/dot_general | solution.py:75
  8.3 5.1 %collective-permute-start = (bf16[8,2432]{1,0:T(8,128)(2,1)S(1)}, bf16[8,2432]{1,0:T(8,128)(2,1)S(1)}, u32[]{:S(2)}, u32[]{:S(2)}) collective-permute-start(bf16[8,2432]{1,0:T(8,128)(2,1)S(1)} %get-tuple-element.14), channel_id=1, source_target_pairs={{0,12},{4,0},{8,4},{12,8},{1,13},{5,1},{9,5},{13,9},{2,14},{6,2},{... | collective-permute-start | bytes 116744 | tf_op jit(solution)/shard_map/clus_exchange/ppermute | solution.py:8
  13.4 1.0 %collective-permute-start.1 = (bf16[8,2432]{1,0:T(8,128)(2,1)S(1)}, bf16[8,2432]{1,0:T(8,128)(2,1)S(1)}, u32[]{:S(2)}, u32[]{:S(2)}) collective-permute-start(bf16[8,2432]{1,0:T(8,128)(2,1)S(1)} %get-tuple-element.13), channel_id=1, source_target_pairs={{0,4},{4,8},{8,12},{12,0},{1,5},{5,9},{9,13},{13,1},{2,6},{6,10},{... | collective-permute-start | bytes 116744 | tf_op jit(solution)/shard_map/clus_exchange/ppermute | solution.py:8
  14.5 4.7 %collective-permute-done.1 = bf16[8,2432]{1,0:T(8,128)(2,1)S(1)} collective-permute-done((bf16[8,2432]{1,0:T(8,128)(2,1)S(1)}, bf16[8,2432]{1,0:T(8,128)(2,1)S(1)}, u32[]{:S(2)}, u32[]{:S(2)}) %collective-permute-start.1) | collective-permute-done | bytes 38944 | tf_op jit(solution)/shard_map/clus_exchange/ppermute | solution.py:8
  19.2 0.6 %gather_fusion.1 = bf16[16,8,256]{2,1,0:T(8,128)(2,1)S(1)} fusion(bf16[8,24,256]{2,0,1:T(8,128)(2,1)S(1)} %pad_maximum_fusion, s32[1024]{0:T(1024)S(1)} %pad_clamp_fusion), kind=kCustom, calls=%fused_computation.1 | custom fusion | bytes 131136 | tf_op jit(solution)/shard_map/near_partial/gather | solution.py:107
  19.8 0.6 %fusion.19 = f32[16,8,256]{2,1,0:T(8,128)S(1)} fusion(bf16[16,256,256]{2,1,0:T(8,128)(2,1)S(1)} %copy-done, bf16[16,8,256]{2,1,0:T(8,128)(2,1)S(1)} %gather_fusion.1), kind=kOutput, calls=%fused_computation.40 | convolution fusion | flops 16777216 | bytes 2293760 | tf_op jit(solution)/shard_map/near_partial/rjs,jts->rjt/dot_general | solution.py:108
  20.8 1.6 %collective-permute-start.3 = (f32[8,2176]{1,0:T(8,128)S(1)}, f32[8,2176]{1,0:T(8,128)S(1)}, u32[]{:S(2)}, u32[]{:S(2)}) collective-permute-start(f32[8,2176]{1,0:T(8,128)S(1)} %pad_maximum_fusion.3), channel_id=1, source_target_pairs={{0,2},{2,0},{1,3},{3,1},{4,6},{6,4},{5,7},{7,5},{8,10},{10,8},{9,1... | collective-permute-start | bytes 208904 | tf_op jit(solution)/shard_map/pair_sums/ppermute | solution.py:8
  22.3 2.8 %collective-permute-done.3 = f32[8,2176]{1,0:T(8,128)S(1)} collective-permute-done((f32[8,2176]{1,0:T(8,128)S(1)}, f32[8,2176]{1,0:T(8,128)S(1)}, u32[]{:S(2)}, u32[]{:S(2)}) %collective-permute-start.3) | collective-permute-done | bytes 69664 | tf_op jit(solution)/shard_map/pair_sums/ppermute | solution.py:8
  25.4 0.6 %gather_fusion.2 = bf16[64,8,256]{2,1,0:T(8,128)(2,1)S(1)} fusion(bf16[8,8,256]{2,0,1:T(8,128)(2,1)S(1)} %add_convert_fusion.1, s32[1024]{0:T(1024)S(1)} %pad_clamp_fusion.1), kind=kCustom, calls=%fused_computation.2 | custom fusion | bytes 524544 | tf_op jit(solution)/shard_map/far_partial/gather | solution.py:74
  26.4 0.4 convolution_bitcast_fusion.1
  27.0 0.6 %collective-permute-start.4 = (bf16[8,2432]{1,0:T(8,128)(2,1)S(1)}, bf16[8,2432]{1,0:T(8,128)(2,1)S(1)}, u32[]{:S(2)}, u32[]{:S(2)}) collective-permute-start(bf16[8,2432]{1,0:T(8,128)(2,1)S(1)} %get-tuple-element.12), channel_id=1, source_target_pairs={{0,12},{4,0},{8,4},{12,8},{1,13},{5,1},{9,5},{13,9},{2,14},{6,2},{... | collective-permute-start | bytes 116744 | tf_op jit(solution)/shard_map/clus_exchange/ppermute | solution.py:8
  27.6 1.5 %collective-permute-start.5 = (bf16[8,2432]{1,0:T(8,128)(2,1)S(1)}, bf16[8,2432]{1,0:T(8,128)(2,1)S(1)}, u32[]{:S(2)}, u32[]{:S(2)}) collective-permute-start(bf16[8,2432]{1,0:T(8,128)(2,1)S(1)} %get-tuple-element.11), channel_id=1, source_target_pairs={{0,4},{4,8},{8,12},{12,0},{1,5},{5,9},{9,13},{13,1},{2,6},{6,10},{... | collective-permute-start | bytes 116744 | tf_op jit(solution)/shard_map/clus_exchange/ppermute | solution.py:8
  29.1 1.1 %collective-permute-start.6 = (bf16[8,384]{1,0:T(8,128)(2,1)S(1)}, bf16[8,384]{1,0:T(8,128)(2,1)S(1)}, u32[]{:S(2)}, u32[]{:S(2)}) collective-permute-start(bf16[8,384]{1,0:T(8,128)(2,1)S(1)} %pad_maximum_fusion.13), channel_id=1, source_target_pairs={{0,8},{4,12},{8,0},{12,4},{1,9},{5,13},{9,1},{13,5},{2,10},{6,14},... | collective-permute-start | bytes 18440 | tf_op jit(solution)/shard_map/clus_exchange/ppermute | solution.py:8
  30.2 3.2 %collective-permute-done.5 = bf16[8,2432]{1,0:T(8,128)(2,1)S(1)} collective-permute-done((bf16[8,2432]{1,0:T(8,128)(2,1)S(1)}, bf16[8,2432]{1,0:T(8,128)(2,1)S(1)}, u32[]{:S(2)}, u32[]{:S(2)}) %collective-permute-start.5) | collective-permute-done | bytes 38944 | tf_op jit(solution)/shard_map/clus_exchange/ppermute | solution.py:8
  33.4 0.6 %gather_fusion.3 = bf16[16,8,256]{2,1,0:T(8,128)(2,1)S(1)} fusion(bf16[8,24,256]{2,0,1:T(8,128)(2,1)S(1)} %pad_maximum_fusion.1, s32[1024]{0:T(1024)S(1)} %pad_clamp_fusion), kind=kCustom, calls=%fused_computation.3 | custom fusion | bytes 131136 | tf_op jit(solution)/shard_map/near_partial/gather | solution.py:107
  34.0 0.6 %fusion.17 = f32[16,8,256]{2,1,0:T(8,128)S(1)} fusion(bf16[16,256,256]{2,1,0:T(8,128)(2,1)S(1)} %copy-done, bf16[16,8,256]{2,1,0:T(8,128)(2,1)S(1)} %gather_fusion.3), kind=kOutput, calls=%fused_computation.38 | convolution fusion | flops 16777216 | bytes 2293760 | tf_op jit(solution)/shard_map/near_partial/rjs,jts->rjt/dot_general | solution.py:108
  34.9 1.6 %collective-permute-start.7 = (f32[8,2176]{1,0:T(8,128)S(1)}, f32[8,2176]{1,0:T(8,128)S(1)}, u32[]{:S(2)}, u32[]{:S(2)}) collective-permute-start(f32[8,2176]{1,0:T(8,128)S(1)} %pad_maximum_fusion.4), channel_id=1, source_target_pairs={{0,2},{2,0},{1,3},{3,1},{4,6},{6,4},{5,7},{7,5},{8,10},{10,8},{9,1... | collective-permute-start | bytes 208904 | tf_op jit(solution)/shard_map/pair_sums/ppermute | solution.py:8
  36.5 2.8 %collective-permute-done.7 = f32[8,2176]{1,0:T(8,128)S(1)} collective-permute-done((f32[8,2176]{1,0:T(8,128)S(1)}, f32[8,2176]{1,0:T(8,128)S(1)}, u32[]{:S(2)}, u32[]{:S(2)}) %collective-permute-start.7) | collective-permute-done | bytes 69664 | tf_op jit(solution)/shard_map/pair_sums/ppermute | solution.py:8
  39.6 0.6 %gather_fusion.4 = bf16[64,8,256]{2,1,0:T(8,128)(2,1)S(1)} fusion(bf16[8,8,256]{2,0,1:T(8,128)(2,1)S(1)} %add_convert_fusion, s32[1024]{0:T(1024)S(1)} %pad_clamp_fusion.1), kind=kCustom, calls=%fused_computation.4 | custom fusion | bytes 524544 | tf_op jit(solution)/shard_map/far_partial/gather | solution.py:74
  40.6 0.4 convolution_bitcast_fusion
  41.2 1.1 %collective-permute-start.8 = (bf16[8,2432]{1,0:T(8,128)(2,1)S(1)}, bf16[8,2432]{1,0:T(8,128)(2,1)S(1)}, u32[]{:S(2)}, u32[]{:S(2)}) collective-permute-start(bf16[8,2432]{1,0:T(8,128)(2,1)S(1)} %get-tuple-element.10), channel_id=1, source_target_pairs={{0,12},{4,0},{8,4},{12,8},{1,13},{5,1},{9,5},{13,9},{2,14},{6,2},{... | collective-permute-start | bytes 116744 | tf_op jit(solution)/shard_map/clus_exchange/ppermute | solution.py:8
  42.3 1.0 %collective-permute-start.9 = (bf16[8,2432]{1,0:T(8,128)(2,1)S(1)}, bf16[8,2432]{1,0:T(8,128)(2,1)S(1)}, u32[]{:S(2)}, u32[]{:S(2)}) collective-permute-start(bf16[8,2432]{1,0:T(8,128)(2,1)S(1)} %get-tuple-element.9), channel_id=1, source_target_pairs={{0,4},{4,8},{8,12},{12,0},{1,5},{5,9},{9,13},{13,1},{2,6},{6,10},{... | collective-permute-start | bytes 116744 | tf_op jit(solution)/shard_map/clus_exchange/ppermute | solution.py:8
  43.3 4.8 %collective-permute-done.9 = bf16[8,2432]{1,0:T(8,128)(2,1)S(1)} collective-permute-done((bf16[8,2432]{1,0:T(8,128)(2,1)S(1)}, bf16[8,2432]{1,0:T(8,128)(2,1)S(1)}, u32[]{:S(2)}, u32[]{:S(2)}) %collective-permute-start.9) | collective-permute-done | bytes 38944 | tf_op jit(solution)/shard_map/clus_exchange/ppermute | solution.py:8
  48.1 0.6 %gather_fusion.5 = bf16[16,8,256]{2,1,0:T(8,128)(2,1)S(1)} fusion(bf16[8,24,256]{2,0,1:T(8,128)(2,1)S(1)} %pad_maximum_fusion.2, s32[1024]{0:T(1024)S(1)} %pad_clamp_fusion), kind=kCustom, calls=%fused_computation.5 | custom fusion | bytes 131136 | tf_op jit(solution)/shard_map/near_partial/gather | solution.py:107
  48.7 0.6 %fusion.15 = f32[16,8,256]{2,1,0:T(8,128)S(1)} fusion(bf16[16,256,256]{2,1,0:T(8,128)(2,1)S(1)} %copy-done, bf16[16,8,256]{2,1,0:T(8,128)(2,1)S(1)} %gather_fusion.5), kind=kOutput, calls=%fused_computation.36 | convolution fusion | flops 16777216 | bytes 2293760 | tf_op jit(solution)/shard_map/near_partial/rjs,jts->rjt/dot_general | solution.py:108
  49.6 1.6 %collective-permute-start.11 = (f32[8,2176]{1,0:T(8,128)S(1)}, f32[8,2176]{1,0:T(8,128)S(1)}, u32[]{:S(2)}, u32[]{:S(2)}) collective-permute-start(f32[8,2176]{1,0:T(8,128)S(1)} %pad_maximum_fusion.5), channel_id=1, source_target_pairs={{0,2},{2,0},{1,3},{3,1},{4,6},{6,4},{5,7},{7,5},{8,10},{10,8},{9,1... | collective-permute-start | bytes 208904 | tf_op jit(solution)/shard_map/pair_sums/ppermute | solution.py:8
  51.2 2.8 %collective-permute-done.11 = f32[8,2176]{1,0:T(8,128)S(1)} collective-permute-done((f32[8,2176]{1,0:T(8,128)S(1)}, f32[8,2176]{1,0:T(8,128)S(1)}, u32[]{:S(2)}, u32[]{:S(2)}) %collective-permute-start.11) | collective-permute-done | bytes 69664 | tf_op jit(solution)/shard_map/pair_sums/ppermute | solution.py:8
  54.3 0.6 %add_add_fusion = f32[8,8,256]{2,0,1:T(8,128)} fusion(f32[8,8,256]{2,0,1:T(8,128)S(1)} %bitcast.223, f32[8,8,256]{2,0,1:T(8,128)S(1)} %bitcast.222, f32[8,8,256]{2,0,1:T(8,128)S(1)} %convolution_bitcast_fusion.3), kind=kLoop, calls=%fused_computation.42 | loop fusion | flops 32768 | bytes 262144 | tf_op jit(solution)/shard_map/add | solution.py:128
  (81 shorter events, 3.4 us)
Async XLA Ops:
  0.0 19.8 %copy-start = (bf16[16,256,256]{2,1,0:T(8,128)(2,1)S(1)}, bf16[16,256,256]{2,1,0:T(8,128)(2,1)}, u32[]{:S(2)}) copy-start(bf16[16,256,256]{2,1,0:T(8,128)(2,1)} %param.11) | copy-start | bytes 6291460
  0.0 7.7 %copy-start.3 = (s32[64]{0:T(128)S(1)}, s32[64]{0:T(128)}, u32[]{:S(2)}) copy-start(s32[64]{0:T(128)} %param.17) | copy-start | bytes 772
  0.0 14.4 %copy-start.4 = (s32[16]{0:T(128)S(1)}, s32[16]{0:T(128)}, u32[]{:S(2)}) copy-start(s32[16]{0:T(128)} %param.13) | copy-start | bytes 196
  0.0 14.5 %copy-start.5 = (s32[16]{0:T(128)S(1)}, s32[16]{0:T(128)}, u32[]{:S(2)}) copy-start(s32[16]{0:T(128)} %param.12) | copy-start | bytes 196
  7.7 17.5 %copy-start.2 = (bf16[8,16,256]{2,1,0:T(8,128)(2,1)S(1)}, bf16[8,16,256]{2,1,0:T(8,128)(2,1)}, u32[]{:S(2)}) copy-start(bf16[8,16,256]{2,1,0:T(8,128)(2,1)} %param.14) | copy-start | bytes 196612
  8.3 10.9 %collective-permute-start = (bf16[8,2432]{1,0:T(8,128)(2,1)S(1)}, bf16[8,2432]{1,0:T(8,128)(2,1)S(1)}, u32[]{:S(2)}, u32[]{:S(2)}) collective-permute-start(bf16[8,2432]{1,0:T(8,128)(2,1)S(1)} %get-tuple-element.14), channel_id=1, source_target_pairs={{0,12},{4,0},{8,4},{12,8},{1,13},{5,1},{9,5},{13,9},{2,14},{6,2},{... | collective-permute-start | bytes 116744 | tf_op jit(solution)/shard_map/clus_exchange/ppermute | solution.py:8
  13.4 7.3 %collective-permute-start.2 = (bf16[8,384]{1,0:T(8,128)(2,1)S(1)}, bf16[8,384]{1,0:T(8,128)(2,1)S(1)}, u32[]{:S(2)}, u32[]{:S(2)}) collective-permute-start(bf16[8,384]{1,0:T(8,128)(2,1)S(1)} %pad_maximum_fusion.12), channel_id=1, source_target_pairs={{0,8},{4,12},{8,0},{12,4},{1,9},{5,13},{9,1},{13,5},{2,10},{6,14},... | collective-permute-start | bytes 18440 | tf_op jit(solution)/shard_map/clus_exchange/ppermute | solution.py:8
  13.4 5.8 %collective-permute-start.1 = (bf16[8,2432]{1,0:T(8,128)(2,1)S(1)}, bf16[8,2432]{1,0:T(8,128)(2,1)S(1)}, u32[]{:S(2)}, u32[]{:S(2)}) collective-permute-start(bf16[8,2432]{1,0:T(8,128)(2,1)S(1)} %get-tuple-element.13), channel_id=1, source_target_pairs={{0,4},{4,8},{8,12},{12,0},{1,5},{5,9},{9,13},{13,1},{2,6},{6,10},{... | collective-permute-start | bytes 116744 | tf_op jit(solution)/shard_map/clus_exchange/ppermute | solution.py:8
  19.2 6.8 %copy-start.1 = (bf16[64,16,256]{2,1,0:T(8,128)(2,1)S(1)}, bf16[64,16,256]{2,1,0:T(8,128)(2,1)}, u32[]{:S(2)}) copy-start(bf16[64,16,256]{2,1,0:T(8,128)(2,1)} %param.15) | copy-start | bytes 1572868
  20.8 4.4 %collective-permute-start.3 = (f32[8,2176]{1,0:T(8,128)S(1)}, f32[8,2176]{1,0:T(8,128)S(1)}, u32[]{:S(2)}, u32[]{:S(2)}) collective-permute-start(f32[8,2176]{1,0:T(8,128)S(1)} %pad_maximum_fusion.3), channel_id=1, source_target_pairs={{0,2},{2,0},{1,3},{3,1},{4,6},{6,4},{5,7},{7,5},{8,10},{10,8},{9,1... | collective-permute-start | bytes 208904 | tf_op jit(solution)/shard_map/pair_sums/ppermute | solution.py:8
  27.0 6.4 %collective-permute-start.4 = (bf16[8,2432]{1,0:T(8,128)(2,1)S(1)}, bf16[8,2432]{1,0:T(8,128)(2,1)S(1)}, u32[]{:S(2)}, u32[]{:S(2)}) collective-permute-start(bf16[8,2432]{1,0:T(8,128)(2,1)S(1)} %get-tuple-element.12), channel_id=1, source_target_pairs={{0,12},{4,0},{8,4},{12,8},{1,13},{5,1},{9,5},{13,9},{2,14},{6,2},{... | collective-permute-start | bytes 116744 | tf_op jit(solution)/shard_map/clus_exchange/ppermute | solution.py:8
  27.6 5.8 %collective-permute-start.5 = (bf16[8,2432]{1,0:T(8,128)(2,1)S(1)}, bf16[8,2432]{1,0:T(8,128)(2,1)S(1)}, u32[]{:S(2)}, u32[]{:S(2)}) collective-permute-start(bf16[8,2432]{1,0:T(8,128)(2,1)S(1)} %get-tuple-element.11), channel_id=1, source_target_pairs={{0,4},{4,8},{8,12},{12,0},{1,5},{5,9},{9,13},{13,1},{2,6},{6,10},{... | collective-permute-start | bytes 116744 | tf_op jit(solution)/shard_map/clus_exchange/ppermute | solution.py:8
  29.1 5.8 %collective-permute-start.6 = (bf16[8,384]{1,0:T(8,128)(2,1)S(1)}, bf16[8,384]{1,0:T(8,128)(2,1)S(1)}, u32[]{:S(2)}, u32[]{:S(2)}) collective-permute-start(bf16[8,384]{1,0:T(8,128)(2,1)S(1)} %pad_maximum_fusion.13), channel_id=1, source_target_pairs={{0,8},{4,12},{8,0},{12,4},{1,9},{5,13},{9,1},{13,5},{2,10},{6,14},... | collective-permute-start | bytes 18440 | tf_op jit(solution)/shard_map/clus_exchange/ppermute | solution.py:8
  34.9 4.4 %collective-permute-start.7 = (f32[8,2176]{1,0:T(8,128)S(1)}, f32[8,2176]{1,0:T(8,128)S(1)}, u32[]{:S(2)}, u32[]{:S(2)}) collective-permute-start(f32[8,2176]{1,0:T(8,128)S(1)} %pad_maximum_fusion.4), channel_id=1, source_target_pairs={{0,2},{2,0},{1,3},{3,1},{4,6},{6,4},{5,7},{7,5},{8,10},{10,8},{9,1... | collective-permute-start | bytes 208904 | tf_op jit(solution)/shard_map/pair_sums/ppermute | solution.py:8
  41.2 6.9 %collective-permute-start.8 = (bf16[8,2432]{1,0:T(8,128)(2,1)S(1)}, bf16[8,2432]{1,0:T(8,128)(2,1)S(1)}, u32[]{:S(2)}, u32[]{:S(2)}) collective-permute-start(bf16[8,2432]{1,0:T(8,128)(2,1)S(1)} %get-tuple-element.10), channel_id=1, source_target_pairs={{0,12},{4,0},{8,4},{12,8},{1,13},{5,1},{9,5},{13,9},{2,14},{6,2},{... | collective-permute-start | bytes 116744 | tf_op jit(solution)/shard_map/clus_exchange/ppermute | solution.py:8
  42.3 5.8 %collective-permute-start.9 = (bf16[8,2432]{1,0:T(8,128)(2,1)S(1)}, bf16[8,2432]{1,0:T(8,128)(2,1)S(1)}, u32[]{:S(2)}, u32[]{:S(2)}) collective-permute-start(bf16[8,2432]{1,0:T(8,128)(2,1)S(1)} %get-tuple-element.9), channel_id=1, source_target_pairs={{0,4},{4,8},{8,12},{12,0},{1,5},{5,9},{9,13},{13,1},{2,6},{6,10},{... | collective-permute-start | bytes 116744 | tf_op jit(solution)/shard_map/clus_exchange/ppermute | solution.py:8
  43.3 6.3 %collective-permute-start.10 = (bf16[8,384]{1,0:T(8,128)(2,1)S(1)}, bf16[8,384]{1,0:T(8,128)(2,1)S(1)}, u32[]{:S(2)}, u32[]{:S(2)}) collective-permute-start(bf16[8,384]{1,0:T(8,128)(2,1)S(1)} %pad_maximum_fusion.14), channel_id=1, source_target_pairs={{0,8},{4,12},{8,0},{12,4},{1,9},{5,13},{9,1},{13,5},{2,10},{6,14},... | collective-permute-start | bytes 18440 | tf_op jit(solution)/shard_map/clus_exchange/ppermute | solution.py:8
  49.6 4.4 %collective-permute-start.11 = (f32[8,2176]{1,0:T(8,128)S(1)}, f32[8,2176]{1,0:T(8,128)S(1)}, u32[]{:S(2)}, u32[]{:S(2)}) collective-permute-start(f32[8,2176]{1,0:T(8,128)S(1)} %pad_maximum_fusion.5), channel_id=1, source_target_pairs={{0,2},{2,0},{1,3},{3,1},{4,6},{6,4},{5,7},{7,5},{8,10},{10,8},{9,1... | collective-permute-start | bytes 208904 | tf_op jit(solution)/shard_map/pair_sums/ppermute | solution.py:8

commit v9 on v8

--- a/solution.py
+++ b/solution.py
@@ -54,7 +54,7 @@
     my_index = lax.axis_index("clus")
     pair_index = lax.axis_index("pair")
     my_base = my_index * clusters_here
-    source = rhs_field.reshape(rhs_here, clusters_here, leaf_size)
+    source = rhs_field.reshape(rhs_here, clusters_here, leaf_size).transpose(1, 0, 2)
 
     target_local = near_tgt - my_base
     target_hot = (target_local[:, None] == jnp.arange(clusters_here)[None, :]).astype(jnp.float32)
@@ -65,26 +65,24 @@
     far_local = far_src - my_base
     far_hot = (far_tgt[:, None] == jnp.arange(cluster_count)[None, :]).astype(jnp.float32)
     row_f32 = row_basis.astype(jnp.float32)
+    iterate_size = rhs_here * leaf_size
+    coef_size = rhs_here * rank_size
 
     iterate = (coefficients[degree_top] * source).astype(jnp.bfloat16)
     result = source
     for step in range(degree_top):
         degree = degree_top - 1 - step
         with jax.named_scope("far_partial"):
-            far_input = iterate[:, far_local, :]
+            far_input = iterate[far_local]
             coef = jnp.einsum(
-                "rjl,jkl->jrk", far_input, col_basis, preferred_element_type=jnp.float32
+                "jrl,jkl->jrk", far_input, col_basis, preferred_element_type=jnp.float32
             )
-            coef = coef.reshape(coef.shape[0], rhs_here * rank_size)
+            coef = coef.reshape(coef.shape[0], coef_size)
             partial_value = jnp.einsum("jc,jm->cm", far_hot, coef, precision=lax.Precision.HIGHEST)
-            partial_value = partial_value.reshape(peer_count, clusters_here, rhs_here, rank_size)
-            partial_value = partial_value.transpose(0, 2, 1, 3).reshape(
-                peer_count, rhs_here, clusters_here * rank_size
-            )
+            partial_value = partial_value.reshape(peer_count, clusters_here, coef_size)
         with jax.named_scope("clus_exchange"):
             far_mine = partial_value[my_index]
-            iterate_flat = iterate.reshape(rhs_here, clusters_here * leaf_size)
-            iterate_size = clusters_here * leaf_size
+            iterate_flat = iterate.reshape(clusters_here, iterate_size)
             from_minus = iterate
             from_plus = iterate
             for s in range(1, peer_count):
@@ -95,7 +93,7 @@
                 incoming = shift(outgoing, "clus", peer_count, s)
                 if carries_iterate:
                     neighbour = incoming[:, :iterate_size]
-                    neighbour = neighbour.reshape(rhs_here, clusters_here, leaf_size)
+                    neighbour = neighbour.reshape(clusters_here, rhs_here, leaf_size)
                     if s == 1:
                         from_minus = neighbour
                     if s == peer_count - 1:
@@ -103,31 +101,27 @@
                     incoming = incoming[:, iterate_size:]
                 far_mine = far_mine + join_three(incoming)
         with jax.named_scope("near_partial"):
-            extended = jnp.concatenate([iterate, from_plus, from_minus], axis=1)
-            gathered = extended[:, near_index, :]
+            extended = jnp.concatenate([iterate, from_plus, from_minus], axis=0)
+            gathered = extended[near_index]
             contrib = jnp.einsum(
-                "rjs,jts->rjt", gathered, near_blocks, preferred_element_type=jnp.float32
+                "jrs,jts->jrt", gathered, near_blocks, preferred_element_type=jnp.float32
             )
+            contrib = contrib.reshape(contrib.shape[0], iterate_size)
             near_part = jnp.einsum(
-                "rjt,jc->rct", contrib, target_hot, precision=lax.Precision.HIGHEST
+                "jc,jm->cm", target_hot, contrib, precision=lax.Precision.HIGHEST
             )
         with jax.named_scope("pair_sums"):
-            near_flat = near_part.reshape(rhs_here, clusters_here * leaf_size)
-            packed = jnp.concatenate([near_flat, far_mine], axis=1)
+            packed = jnp.concatenate([near_part, far_mine], axis=1)
             packed = pair_total(packed, pair_count, pair_index)
-            near_sum = packed[:, : clusters_here * leaf_size].reshape(
-                rhs_here, clusters_here, leaf_size
-            )
-            coef_sum = packed[:, clusters_here * leaf_size :].reshape(
-                rhs_here, clusters_here, rank_size
-            )
+            near_sum = packed[:, :iterate_size].reshape(clusters_here, rhs_here, leaf_size)
+            coef_sum = packed[:, iterate_size:].reshape(clusters_here, rhs_here, rank_size)
         with jax.named_scope("far_field"):
             far_field = jnp.einsum(
-                "rck,ckl->rcl", coef_sum, row_f32, precision=lax.Precision.HIGHEST
+                "crk,ckl->crl", coef_sum, row_f32, precision=lax.Precision.HIGHEST
             )
         result = near_sum + far_field + coefficients[degree] * source
         iterate = result.astype(jnp.bfloat16)
-    return result.reshape(rhs_here, clusters_here * leaf_size)
+    return result.transpose(1, 0, 2).reshape(rhs_here, clusters_here * leaf_size)
 
 
 def solution(mesh):

time: 55.2 us -> 54.6 us (0.989)
    dot_general x12, matrix products: 4.76 us -> 5.62 us  [the longest x3 1.91 us: shards(): jnp.einsum('jrs,jts->jrt', gathered, near_blocks, preferred_element_type=...]
    dot_general x3, matrix products: 1.29 us -> 0.53 us  [shards(): jnp.einsum('jc,jm->cm', far_hot, coef, precision=lax.Precision.HIGHEST)]
    add x1 -> x0, other arithmetic: 0.64 us -> none  [shards(): result = near_sum + far_field + coefficients[degree] * source]
  transfers between devices with their start and end apart: 12 -> 12, of which waited for: 6 -> 6; matrix products, arithmetic and copies ran while one was open for 8% -> 9% of each run, Pallas kernels for 0% -> 0%
where the time goes in v9:
time: 54.6 us; the launch traced here: 54.3 us
  waiting for transfers between devices  21.1 us (39%)
  starting transfers between devices  16.1 us (29%)
  matrix products  6.14 us (11%)
  local copies, waits for them, and re-layouts  5.97 us (11%)
  other arithmetic  4.52 us (8%)
  between operations  0.55 us (1%)
    ppermute x12, waiting for transfers between devices, shift(): lax.ppermute(value, axis, [(i, (i + step) % count) for i in range(count)])  21.1 us
    ppermute x12, starting transfers between devices, shift(): lax.ppermute(value, axis, [(i, (i + step) % count) for i in range(count)])  16.1 us
    convert_element_type x1, other arithmetic, shards(): iterate = (coefficients[degree_top] * source).astype(jnp.bfloat16)  3.43 us
    dot_general x3, matrix products, shards(): jnp.einsum('jrs,jts->jrt', gathered, near_blocks, preferred_element_type=...  1.91 us
    gather x3, local copies, waits for them, and re-layouts, shards(): far_input = iterate[far_local]  1.79 us
    dot_general x3, matrix products, shards(): jnp.einsum('jrl,jkl->jrk', far_input, col_basis, preferred_element_type=j...  1.73 us
    gather x3, local copies, waits for them, and re-layouts, shards(): gathered = extended[near_index]  1.67 us
    slice x1, local copies, waits for them, and re-layouts, shards(): iterate = (coefficients[degree_top] * source).astype(jnp.bfloat16)  1.51 us
  transfers between devices with their start and end apart: 12, of which 6 were waited for; matrix products, arithmetic and copies ran while one was open for 9% of the time, Pallas kernels for 0%

profile of v9, /device:TPU:0, one launch (start us, length us, event | category | flops | bytes accessed | tf_op | source)
XLA Modules:
  0.0 54.3 jit_solution(14968650179956327058)
XLA Ops:
  0.1 1.5 %fusion.44 = (f32[1]{0:T(128)}, f32[1]{0:T(128)}, f32[1]{0:T(128)}, f32[1]{0:T(128)}) fusion(f32[4]{0:T(128)} %param.10), kind=kLoop, calls=%fused_computation.132 | loop fusion | bytes 32 | tf_op jit(solution)/shard_map/slice | solution.py:71
  1.6 0.7 %compare_select_fusion.1 = s32[64]{0:T(128)S(1)} fusion(s32[64]{0:T(128)} %param.16, s32[]{:T(128)S(6)} %mul.50), kind=kLoop, calls=%fused_computation.113 | loop fusion | flops 256 | bytes 516 | tf_op jit(solution)/shard_map/far_partial/select_n | solution.py:76
  2.3 3.4 %multiply_convert_fusion = (bf16[8,2048]{1,0:T(8,128)(2,1)S(1)}, f32[8,2048]{1,0:T(8,128)S(1)}, f32[8,2048]{1,0:T(8,128)S(1)}, f32[8,2048]{1,0:T(8,128)S(1)}) fusion(f32[8,2048]{1,0:T(8,128)} %param.9, f32[]{:T(128)} %bitcast, f32[]{:T(128)} %bitcast.13, f32[]{:T(128)} %bitcast.33, f32[]{:T(128)} %bitcast.23), kind=kLoop, calls=%fused_computation.20 | loop fusion | flops 81920 | bytes 294928 | tf_op jit(solution)/shard_map/convert_element_type | solution.py:71
  5.7 0.6 %gather_fusion = bf16[64,8,256]{2,1,0:T(8,128)(2,1)S(1)} fusion(bf16[8,8,256]{2,1,0:T(8,128)(2,1)S(1)} %bitcast.164, s32[1024]{0:T(1024)S(1)} %pad_clamp_fusion.1), kind=kCustom, calls=%fused_computation | custom fusion | bytes 524544 | tf_op jit(solution)/shard_map/far_partial/gather | solution.py:76
  6.3 1.3 %fusion.45 = f32[64,8,16]{2,1,0:T(8,128)S(1)} fusion(bf16[64,8,256]{2,1,0:T(8,128)(2,1)S(1)} %gather_fusion, bf16[64,16,256]{2,1,0:T(8,128)(2,1)} %param.15), kind=kOutput, calls=%fused_computation.133 | convolution fusion | flops 4194304 | bytes 819200 | tf_op jit(solution)/shard_map/far_partial/jrl,jkl->jrk/dot_general | solution.py:77
  8.0 5.1 %collective-permute-start = (bf16[8,2432]{1,0:T(8,128)(2,1)S(1)}, bf16[8,2432]{1,0:T(8,128)(2,1)S(1)}, u32[]{:S(2)}, u32[]{:S(2)}) collective-permute-start(bf16[8,2432]{1,0:T(8,128)(2,1)S(1)} %get-tuple-element.14), channel_id=1, source_target_pairs={{0,12},{4,0},{8,4},{12,8},{1,13},{5,1},{9,5},{13,9},{2,14},{6,2},{... | collective-permute-start | bytes 116744 | tf_op jit(solution)/shard_map/clus_exchange/ppermute | solution.py:8
  13.1 1.0 %collective-permute-start.1 = (bf16[8,2432]{1,0:T(8,128)(2,1)S(1)}, bf16[8,2432]{1,0:T(8,128)(2,1)S(1)}, u32[]{:S(2)}, u32[]{:S(2)}) collective-permute-start(bf16[8,2432]{1,0:T(8,128)(2,1)S(1)} %get-tuple-element.13), channel_id=1, source_target_pairs={{0,4},{4,8},{8,12},{12,0},{1,5},{5,9},{9,13},{13,1},{2,6},{6,10},{... | collective-permute-start | bytes 116744 | tf_op jit(solution)/shard_map/clus_exchange/ppermute | solution.py:8
  14.2 4.7 %collective-permute-done.1 = bf16[8,2432]{1,0:T(8,128)(2,1)S(1)} collective-permute-done((bf16[8,2432]{1,0:T(8,128)(2,1)S(1)}, bf16[8,2432]{1,0:T(8,128)(2,1)S(1)}, u32[]{:S(2)}, u32[]{:S(2)}) %collective-permute-start.1) | collective-permute-done | bytes 38944 | tf_op jit(solution)/shard_map/clus_exchange/ppermute | solution.py:8
  19.0 0.6 %gather_fusion.1 = bf16[16,8,256]{2,1,0:T(8,128)(2,1)S(1)} fusion(bf16[24,8,256]{2,1,0:T(8,128)(2,1)S(1)} %pad_maximum_fusion, s32[1024]{0:T(1024)S(1)} %pad_clamp_fusion), kind=kCustom, calls=%fused_computation.1 | custom fusion | bytes 131136 | tf_op jit(solution)/shard_map/near_partial/gather | solution.py:105
  19.6 0.6 %fusion.46 = f32[16,8,256]{2,1,0:T(8,128)S(1)} fusion(bf16[16,8,256]{2,1,0:T(8,128)(2,1)S(1)} %gather_fusion.1, bf16[16,256,256]{2,1,0:T(8,128)(2,1)S(1)} %copy-done), kind=kOutput, calls=%fused_computation.134 | convolution fusion | flops 16777216 | bytes 2293760 | tf_op jit(solution)/shard_map/near_partial/jrs,jts->jrt/dot_general | solution.py:106
  20.3 0.3 fusion.19
  20.6 1.6 %collective-permute-start.3 = (f32[8,2176]{1,0:T(8,128)S(1)}, f32[8,2176]{1,0:T(8,128)S(1)}, u32[]{:S(2)}, u32[]{:S(2)}) collective-permute-start(f32[8,2176]{1,0:T(8,128)S(1)} %pad_maximum_fusion.3), channel_id=1, source_target_pairs={{0,2},{2,0},{1,3},{3,1},{4,6},{6,4},{5,7},{7,5},{8,10},{10,8},{9,1... | collective-permute-start | bytes 208904 | tf_op jit(solution)/shard_map/pair_sums/ppermute | solution.py:8
  22.2 2.8 %collective-permute-done.3 = f32[8,2176]{1,0:T(8,128)S(1)} collective-permute-done((f32[8,2176]{1,0:T(8,128)S(1)}, f32[8,2176]{1,0:T(8,128)S(1)}, u32[]{:S(2)}, u32[]{:S(2)}) %collective-permute-start.3) | collective-permute-done | bytes 69664 | tf_op jit(solution)/shard_map/pair_sums/ppermute | solution.py:8
  25.3 0.6 %gather_fusion.2 = bf16[64,8,256]{2,1,0:T(8,128)(2,1)S(1)} fusion(bf16[8,8,256]{2,1,0:T(8,128)(2,1)S(1)} %fusion.4, s32[1024]{0:T(1024)S(1)} %pad_clamp_fusion.1), kind=kCustom, calls=%fused_computation.2 | custom fusion | bytes 524544 | tf_op jit(solution)/shard_map/far_partial/gather | solution.py:76
  26.6 0.6 %collective-permute-start.4 = (bf16[8,2432]{1,0:T(8,128)(2,1)S(1)}, bf16[8,2432]{1,0:T(8,128)(2,1)S(1)}, u32[]{:S(2)}, u32[]{:S(2)}) collective-permute-start(bf16[8,2432]{1,0:T(8,128)(2,1)S(1)} %get-tuple-element.12), channel_id=1, source_target_pairs={{0,12},{4,0},{8,4},{12,8},{1,13},{5,1},{9,5},{13,9},{2,14},{6,2},{... | collective-permute-start | bytes 116744 | tf_op jit(solution)/shard_map/clus_exchange/ppermute | solution.py:8
  27.2 1.5 %collective-permute-start.5 = (bf16[8,2432]{1,0:T(8,128)(2,1)S(1)}, bf16[8,2432]{1,0:T(8,128)(2,1)S(1)}, u32[]{:S(2)}, u32[]{:S(2)}) collective-permute-start(bf16[8,2432]{1,0:T(8,128)(2,1)S(1)} %get-tuple-element.11), channel_id=1, source_target_pairs={{0,4},{4,8},{8,12},{12,0},{1,5},{5,9},{9,13},{13,1},{2,6},{6,10},{... | collective-permute-start | bytes 116744 | tf_op jit(solution)/shard_map/clus_exchange/ppermute | solution.py:8
  28.7 1.1 %collective-permute-start.6 = (bf16[8,384]{1,0:T(8,128)(2,1)S(1)}, bf16[8,384]{1,0:T(8,128)(2,1)S(1)}, u32[]{:S(2)}, u32[]{:S(2)}) collective-permute-start(bf16[8,384]{1,0:T(8,128)(2,1)S(1)} %pad_maximum_fusion.13), channel_id=1, source_target_pairs={{0,8},{4,12},{8,0},{12,4},{1,9},{5,13},{9,1},{13,5},{2,10},{6,14},... | collective-permute-start | bytes 18440 | tf_op jit(solution)/shard_map/clus_exchange/ppermute | solution.py:8
  29.8 3.2 %collective-permute-done.5 = bf16[8,2432]{1,0:T(8,128)(2,1)S(1)} collective-permute-done((bf16[8,2432]{1,0:T(8,128)(2,1)S(1)}, bf16[8,2432]{1,0:T(8,128)(2,1)S(1)}, u32[]{:S(2)}, u32[]{:S(2)}) %collective-permute-start.5) | collective-permute-done | bytes 38944 | tf_op jit(solution)/shard_map/clus_exchange/ppermute | solution.py:8
  33.0 0.6 %gather_fusion.3 = bf16[16,8,256]{2,1,0:T(8,128)(2,1)S(1)} fusion(bf16[24,8,256]{2,1,0:T(8,128)(2,1)S(1)} %pad_maximum_fusion.1, s32[1024]{0:T(1024)S(1)} %pad_clamp_fusion), kind=kCustom, calls=%fused_computation.3 | custom fusion | bytes 131136 | tf_op jit(solution)/shard_map/near_partial/gather | solution.py:105
  33.6 0.6 %fusion.48 = f32[16,8,256]{2,1,0:T(8,128)S(1)} fusion(bf16[16,8,256]{2,1,0:T(8,128)(2,1)S(1)} %gather_fusion.3, bf16[16,256,256]{2,1,0:T(8,128)(2,1)S(1)} %copy-done), kind=kOutput, calls=%fused_computation.136 | convolution fusion | flops 16777216 | bytes 2293760 | tf_op jit(solution)/shard_map/near_partial/jrs,jts->jrt/dot_general | solution.py:106
  34.6 1.6 %collective-permute-start.7 = (f32[8,2176]{1,0:T(8,128)S(1)}, f32[8,2176]{1,0:T(8,128)S(1)}, u32[]{:S(2)}, u32[]{:S(2)}) collective-permute-start(f32[8,2176]{1,0:T(8,128)S(1)} %pad_maximum_fusion.4), channel_id=1, source_target_pairs={{0,2},{2,0},{1,3},{3,1},{4,6},{6,4},{5,7},{7,5},{8,10},{10,8},{9,1... | collective-permute-start | bytes 208904 | tf_op jit(solution)/shard_map/pair_sums/ppermute | solution.py:8
  36.2 2.8 %collective-permute-done.7 = f32[8,2176]{1,0:T(8,128)S(1)} collective-permute-done((f32[8,2176]{1,0:T(8,128)S(1)}, f32[8,2176]{1,0:T(8,128)S(1)}, u32[]{:S(2)}, u32[]{:S(2)}) %collective-permute-start.7) | collective-permute-done | bytes 69664 | tf_op jit(solution)/shard_map/pair_sums/ppermute | solution.py:8
  39.3 0.6 %gather_fusion.4 = bf16[64,8,256]{2,1,0:T(8,128)(2,1)S(1)} fusion(bf16[8,8,256]{2,1,0:T(8,128)(2,1)S(1)} %fusion.2, s32[1024]{0:T(1024)S(1)} %pad_clamp_fusion.1), kind=kCustom, calls=%fused_computation.4 | custom fusion | bytes 524544 | tf_op jit(solution)/shard_map/far_partial/gather | solution.py:76
  40.6 1.0 %collective-permute-start.8 = (bf16[8,2432]{1,0:T(8,128)(2,1)S(1)}, bf16[8,2432]{1,0:T(8,128)(2,1)S(1)}, u32[]{:S(2)}, u32[]{:S(2)}) collective-permute-start(bf16[8,2432]{1,0:T(8,128)(2,1)S(1)} %get-tuple-element.10), channel_id=1, source_target_pairs={{0,12},{4,0},{8,4},{12,8},{1,13},{5,1},{9,5},{13,9},{2,14},{6,2},{... | collective-permute-start | bytes 116744 | tf_op jit(solution)/shard_map/clus_exchange/ppermute | solution.py:8
  41.6 1.1 %collective-permute-start.9 = (bf16[8,2432]{1,0:T(8,128)(2,1)S(1)}, bf16[8,2432]{1,0:T(8,128)(2,1)S(1)}, u32[]{:S(2)}, u32[]{:S(2)}) collective-permute-start(bf16[8,2432]{1,0:T(8,128)(2,1)S(1)} %get-tuple-element.9), channel_id=1, source_target_pairs={{0,4},{4,8},{8,12},{12,0},{1,5},{5,9},{9,13},{13,1},{2,6},{6,10},{... | collective-permute-start | bytes 116744 | tf_op jit(solution)/shard_map/clus_exchange/ppermute | solution.py:8
  42.7 4.7 %collective-permute-done.9 = bf16[8,2432]{1,0:T(8,128)(2,1)S(1)} collective-permute-done((bf16[8,2432]{1,0:T(8,128)(2,1)S(1)}, bf16[8,2432]{1,0:T(8,128)(2,1)S(1)}, u32[]{:S(2)}, u32[]{:S(2)}) %collective-permute-start.9) | collective-permute-done | bytes 38944 | tf_op jit(solution)/shard_map/clus_exchange/ppermute | solution.py:8
  47.4 0.6 %gather_fusion.5 = bf16[16,8,256]{2,1,0:T(8,128)(2,1)S(1)} fusion(bf16[24,8,256]{2,1,0:T(8,128)(2,1)S(1)} %pad_maximum_fusion.2, s32[1024]{0:T(1024)S(1)} %pad_clamp_fusion), kind=kCustom, calls=%fused_computation.5 | custom fusion | bytes 131136 | tf_op jit(solution)/shard_map/near_partial/gather | solution.py:105
  48.0 0.6 %fusion.50 = f32[16,8,256]{2,1,0:T(8,128)S(1)} fusion(bf16[16,8,256]{2,1,0:T(8,128)(2,1)S(1)} %gather_fusion.5, bf16[16,256,256]{2,1,0:T(8,128)(2,1)S(1)} %copy-done), kind=kOutput, calls=%fused_computation.138 | convolution fusion | flops 16777216 | bytes 2293760 | tf_op jit(solution)/shard_map/near_partial/jrs,jts->jrt/dot_general | solution.py:106
  48.7 0.3 fusion.17
  49.0 1.6 %collective-permute-start.11 = (f32[8,2176]{1,0:T(8,128)S(1)}, f32[8,2176]{1,0:T(8,128)S(1)}, u32[]{:S(2)}, u32[]{:S(2)}) collective-permute-start(f32[8,2176]{1,0:T(8,128)S(1)} %pad_maximum_fusion.5), channel_id=1, source_target_pairs={{0,2},{2,0},{1,3},{3,1},{4,6},{6,4},{5,7},{7,5},{8,10},{10,8},{9,1... | collective-permute-start | bytes 208904 | tf_op jit(solution)/shard_map/pair_sums/ppermute | solution.py:8
  50.6 2.8 %collective-permute-done.11 = f32[8,2176]{1,0:T(8,128)S(1)} collective-permute-done((f32[8,2176]{1,0:T(8,128)S(1)}, f32[8,2176]{1,0:T(8,128)S(1)}, u32[]{:S(2)}, u32[]{:S(2)}) %collective-permute-start.11) | collective-permute-done | bytes 69664 | tf_op jit(solution)/shard_map/pair_sums/ppermute | solution.py:8
  53.5 0.8 %fusion = f32[8,8,256]{2,1,0:T(8,128)} fusion(f32[8,8,256]{2,1,0:T(8,128)S(1)} %bitcast.181, f32[8,8,256]{2,0,1:T(8,128)S(1)} %bitcast.178, f32[8,8,16]{2,1,0:T(8,128)S(1)} %reshape.122, bf16[8,16,256]{2,1,0:T(8,128)(2,1)S(1)} %copy-done.2), kind=kOutput, calls=%fused_computation.13 | convolution fusion | flops 3178496 | bytes 266240 | tf_op jit(solution)/shard_map/far_field/crk,ckl->crl/dot_general | solution.py:119
  (83 shorter events, 3.0 us)
Async XLA Ops:
  0.0 19.6 %copy-start = (bf16[16,256,256]{2,1,0:T(8,128)(2,1)S(1)}, bf16[16,256,256]{2,1,0:T(8,128)(2,1)}, u32[]{:S(2)}) copy-start(bf16[16,256,256]{2,1,0:T(8,128)(2,1)} %param.11) | copy-start | bytes 6291460
  0.0 7.8 %copy-start.3 = (s32[64]{0:T(128)S(1)}, s32[64]{0:T(128)}, u32[]{:S(2)}) copy-start(s32[64]{0:T(128)} %param.17) | copy-start | bytes 772
  0.0 14.2 %copy-start.4 = (s32[16]{0:T(128)S(1)}, s32[16]{0:T(128)}, u32[]{:S(2)}) copy-start(s32[16]{0:T(128)} %param.13) | copy-start | bytes 196
  0.0 14.2 %copy-start.5 = (s32[16]{0:T(128)S(1)}, s32[16]{0:T(128)}, u32[]{:S(2)}) copy-start(s32[16]{0:T(128)} %param.12) | copy-start | bytes 196
  7.8 17.4 %copy-start.2 = (bf16[8,16,256]{2,1,0:T(8,128)(2,1)S(1)}, bf16[8,16,256]{2,1,0:T(8,128)(2,1)}, u32[]{:S(2)}) copy-start(bf16[8,16,256]{2,1,0:T(8,128)(2,1)} %param.14) | copy-start | bytes 196612
  8.0 10.9 %collective-permute-start = (bf16[8,2432]{1,0:T(8,128)(2,1)S(1)}, bf16[8,2432]{1,0:T(8,128)(2,1)S(1)}, u32[]{:S(2)}, u32[]{:S(2)}) collective-permute-start(bf16[8,2432]{1,0:T(8,128)(2,1)S(1)} %get-tuple-element.14), channel_id=1, source_target_pairs={{0,12},{4,0},{8,4},{12,8},{1,13},{5,1},{9,5},{13,9},{2,14},{6,2},{... | collective-permute-start | bytes 116744 | tf_op jit(solution)/shard_map/clus_exchange/ppermute | solution.py:8
  13.1 7.4 %collective-permute-start.2 = (bf16[8,384]{1,0:T(8,128)(2,1)S(1)}, bf16[8,384]{1,0:T(8,128)(2,1)S(1)}, u32[]{:S(2)}, u32[]{:S(2)}) collective-permute-start(bf16[8,384]{1,0:T(8,128)(2,1)S(1)} %pad_maximum_fusion.12), channel_id=1, source_target_pairs={{0,8},{4,12},{8,0},{12,4},{1,9},{5,13},{9,1},{13,5},{2,10},{6,14},... | collective-permute-start | bytes 18440 | tf_op jit(solution)/shard_map/clus_exchange/ppermute | solution.py:8
  13.1 5.8 %collective-permute-start.1 = (bf16[8,2432]{1,0:T(8,128)(2,1)S(1)}, bf16[8,2432]{1,0:T(8,128)(2,1)S(1)}, u32[]{:S(2)}, u32[]{:S(2)}) collective-permute-start(bf16[8,2432]{1,0:T(8,128)(2,1)S(1)} %get-tuple-element.13), channel_id=1, source_target_pairs={{0,4},{4,8},{8,12},{12,0},{1,5},{5,9},{9,13},{13,1},{2,6},{6,10},{... | collective-permute-start | bytes 116744 | tf_op jit(solution)/shard_map/clus_exchange/ppermute | solution.py:8
  19.0 6.9 %copy-start.1 = (bf16[64,16,256]{2,1,0:T(8,128)(2,1)S(1)}, bf16[64,16,256]{2,1,0:T(8,128)(2,1)}, u32[]{:S(2)}) copy-start(bf16[64,16,256]{2,1,0:T(8,128)(2,1)} %param.15) | copy-start | bytes 1572868
  20.6 4.4 %collective-permute-start.3 = (f32[8,2176]{1,0:T(8,128)S(1)}, f32[8,2176]{1,0:T(8,128)S(1)}, u32[]{:S(2)}, u32[]{:S(2)}) collective-permute-start(f32[8,2176]{1,0:T(8,128)S(1)} %pad_maximum_fusion.3), channel_id=1, source_target_pairs={{0,2},{2,0},{1,3},{3,1},{4,6},{6,4},{5,7},{7,5},{8,10},{10,8},{9,1... | collective-permute-start | bytes 208904 | tf_op jit(solution)/shard_map/pair_sums/ppermute | solution.py:8
  26.6 6.4 %collective-permute-start.4 = (bf16[8,2432]{1,0:T(8,128)(2,1)S(1)}, bf16[8,2432]{1,0:T(8,128)(2,1)S(1)}, u32[]{:S(2)}, u32[]{:S(2)}) collective-permute-start(bf16[8,2432]{1,0:T(8,128)(2,1)S(1)} %get-tuple-element.12), channel_id=1, source_target_pairs={{0,12},{4,0},{8,4},{12,8},{1,13},{5,1},{9,5},{13,9},{2,14},{6,2},{... | collective-permute-start | bytes 116744 | tf_op jit(solution)/shard_map/clus_exchange/ppermute | solution.py:8
  27.2 5.8 %collective-permute-start.5 = (bf16[8,2432]{1,0:T(8,128)(2,1)S(1)}, bf16[8,2432]{1,0:T(8,128)(2,1)S(1)}, u32[]{:S(2)}, u32[]{:S(2)}) collective-permute-start(bf16[8,2432]{1,0:T(8,128)(2,1)S(1)} %get-tuple-element.11), channel_id=1, source_target_pairs={{0,4},{4,8},{8,12},{12,0},{1,5},{5,9},{9,13},{13,1},{2,6},{6,10},{... | collective-permute-start | bytes 116744 | tf_op jit(solution)/shard_map/clus_exchange/ppermute | solution.py:8
  28.7 5.9 %collective-permute-start.6 = (bf16[8,384]{1,0:T(8,128)(2,1)S(1)}, bf16[8,384]{1,0:T(8,128)(2,1)S(1)}, u32[]{:S(2)}, u32[]{:S(2)}) collective-permute-start(bf16[8,384]{1,0:T(8,128)(2,1)S(1)} %pad_maximum_fusion.13), channel_id=1, source_target_pairs={{0,8},{4,12},{8,0},{12,4},{1,9},{5,13},{9,1},{13,5},{2,10},{6,14},... | collective-permute-start | bytes 18440 | tf_op jit(solution)/shard_map/clus_exchange/ppermute | solution.py:8
  34.6 4.4 %collective-permute-start.7 = (f32[8,2176]{1,0:T(8,128)S(1)}, f32[8,2176]{1,0:T(8,128)S(1)}, u32[]{:S(2)}, u32[]{:S(2)}) collective-permute-start(f32[8,2176]{1,0:T(8,128)S(1)} %pad_maximum_fusion.4), channel_id=1, source_target_pairs={{0,2},{2,0},{1,3},{3,1},{4,6},{6,4},{5,7},{7,5},{8,10},{10,8},{9,1... | collective-permute-start | bytes 208904 | tf_op jit(solution)/shard_map/pair_sums/ppermute | solution.py:8
  40.6 6.8 %collective-permute-start.8 = (bf16[8,2432]{1,0:T(8,128)(2,1)S(1)}, bf16[8,2432]{1,0:T(8,128)(2,1)S(1)}, u32[]{:S(2)}, u32[]{:S(2)}) collective-permute-start(bf16[8,2432]{1,0:T(8,128)(2,1)S(1)} %get-tuple-element.10), channel_id=1, source_target_pairs={{0,12},{4,0},{8,4},{12,8},{1,13},{5,1},{9,5},{13,9},{2,14},{6,2},{... | collective-permute-start | bytes 116744 | tf_op jit(solution)/shard_map/clus_exchange/ppermute | solution.py:8
  41.6 5.8 %collective-permute-start.9 = (bf16[8,2432]{1,0:T(8,128)(2,1)S(1)}, bf16[8,2432]{1,0:T(8,128)(2,1)S(1)}, u32[]{:S(2)}, u32[]{:S(2)}) collective-permute-start(bf16[8,2432]{1,0:T(8,128)(2,1)S(1)} %get-tuple-element.9), channel_id=1, source_target_pairs={{0,4},{4,8},{8,12},{12,0},{1,5},{5,9},{9,13},{13,1},{2,6},{6,10},{... | collective-permute-start | bytes 116744 | tf_op jit(solution)/shard_map/clus_exchange/ppermute | solution.py:8
  42.6 6.4 %collective-permute-start.10 = (bf16[8,384]{1,0:T(8,128)(2,1)S(1)}, bf16[8,384]{1,0:T(8,128)(2,1)S(1)}, u32[]{:S(2)}, u32[]{:S(2)}) collective-permute-start(bf16[8,384]{1,0:T(8,128)(2,1)S(1)} %pad_maximum_fusion.14), channel_id=1, source_target_pairs={{0,8},{4,12},{8,0},{12,4},{1,9},{5,13},{9,1},{13,5},{2,10},{6,14},... | collective-permute-start | bytes 18440 | tf_op jit(solution)/shard_map/clus_exchange/ppermute | solution.py:8
  49.0 4.4 %collective-permute-start.11 = (f32[8,2176]{1,0:T(8,128)S(1)}, f32[8,2176]{1,0:T(8,128)S(1)}, u32[]{:S(2)}, u32[]{:S(2)}) collective-permute-start(f32[8,2176]{1,0:T(8,128)S(1)} %pad_maximum_fusion.5), channel_id=1, source_target_pairs={{0,2},{2,0},{1,3},{3,1},{4,6},{6,4},{5,7},{7,5},{8,10},{10,8},{9,1... | collective-permute-start | bytes 208904 | tf_op jit(solution)/shard_map/pair_sums/ppermute | solution.py:8

commit v10 on v9

--- a/solution.py
+++ b/solution.py
@@ -61,9 +61,11 @@
     relative = (near_src // clusters_here - my_index) % peer_count
     slot = jnp.where(relative == 0, 0, jnp.where(relative == 1, 1, 2))
     near_index = slot * clusters_here + near_src % clusters_here
+    near_pick = (near_index[:, None] == jnp.arange(3 * clusters_here)[None, :]).astype(jnp.bfloat16)
 
     far_local = far_src - my_base
     far_hot = (far_tgt[:, None] == jnp.arange(cluster_count)[None, :]).astype(jnp.float32)
+    far_pick = (far_local[:, None] == jnp.arange(clusters_here)[None, :]).astype(jnp.bfloat16)
     row_f32 = row_basis.astype(jnp.float32)
     iterate_size = rhs_here * leaf_size
     coef_size = rhs_here * rank_size
@@ -73,7 +75,12 @@
     for step in range(degree_top):
         degree = degree_top - 1 - step
         with jax.named_scope("far_partial"):
-            far_input = iterate[far_local]
+            far_input = jnp.einsum(
+                "jc,cm->jm",
+                far_pick,
+                iterate.reshape(clusters_here, iterate_size),
+                preferred_element_type=jnp.bfloat16,
+            ).reshape(far_pick.shape[0], rhs_here, leaf_size)
             coef = jnp.einsum(
                 "jrl,jkl->jrk", far_input, col_basis, preferred_element_type=jnp.float32
             )
@@ -102,7 +109,12 @@
                 far_mine = far_mine + join_three(incoming)
         with jax.named_scope("near_partial"):
             extended = jnp.concatenate([iterate, from_plus, from_minus], axis=0)
-            gathered = extended[near_index]
+            gathered = jnp.einsum(
+                "jc,cm->jm",
+                near_pick,
+                extended.reshape(3 * clusters_here, iterate_size),
+                preferred_element_type=jnp.bfloat16,
+            ).reshape(near_pick.shape[0], rhs_here, leaf_size)
             contrib = jnp.einsum(
                 "jrs,jts->jrt", gathered, near_blocks, preferred_element_type=jnp.float32
             )

time: 54.6 us -> 52.8 us (0.967)
  local copies, waits for them, and re-layouts: 5.97 us -> 2.39 us
  matrix products: 6.14 us -> 7.72 us
    gather x6 -> x0, local copies, waits for them, and re-layouts: 3.46 us -> none  [the longest x3 1.79 us: shards(): far_input = iterate[far_local]]
    dot_general x0 -> x6, matrix products: none -> 1.4 us  [the longest x3 0.79 us: shards(): jnp.einsum('jc,cm->jm', far_pick, iterate.reshape(clusters_here, iterate_...]
    select_n x2 -> x0, other arithmetic: 0.68 us -> none  [the longest x1 0.66 us: shards(): far_input = iterate[far_local]]
    sub x0 -> x1, other arithmetic: none -> 0.66 us  [shards(): far_local = far_src - my_base]
  transfers between devices with their start and end apart: 12 -> 12, of which waited for: 6 -> 6; matrix products, arithmetic and copies ran while one was open for 9% -> 7% of each run, Pallas kernels for 0% -> 0%
where the time goes in v10:
time: 52.8 us; the launch traced here: 52.6 us
  waiting for transfers between devices  21.4 us (41%)
  starting transfers between devices  16.2 us (31%)
  matrix products  7.72 us (15%)
  other arithmetic  4.5 us (9%)
  local copies, waits for them, and re-layouts  2.39 us (5%)
    ppermute x12, waiting for transfers between devices, shift(): lax.ppermute(value, axis, [(i, (i + step) % count) for i in range(count)])  21.4 us
    ppermute x12, starting transfers between devices, shift(): lax.ppermute(value, axis, [(i, (i + step) % count) for i in range(count)])  16.2 us
    convert_element_type x1, other arithmetic, shards(): iterate = (coefficients[degree_top] * source).astype(jnp.bfloat16)  3.43 us
    dot_general x3, matrix products, shards(): jnp.einsum('jrs,jts->jrt', gathered, near_blocks, preferred_element_type=...  1.93 us
    dot_general x3, matrix products, shards(): jnp.einsum('jrl,jkl->jrk', far_input, col_basis, preferred_element_type=j...  1.87 us
    slice x1, local copies, waits for them, and re-layouts, shards(): iterate = (coefficients[degree_top] * source).astype(jnp.bfloat16)  1.51 us
    dot_general x3, matrix products, shards(): jnp.einsum('crk,ckl->crl', coef_sum, row_f32, precision=lax.Precision.HIG...  1.12 us
  transfers between devices with their start and end apart: 12, of which 6 were waited for; matrix products, arithmetic and copies ran while one was open for 7% of the time, Pallas kernels for 0%

profile of v10, /device:TPU:0, one launch (start us, length us, event | category | flops | bytes accessed | tf_op | source)
XLA Modules:
  0.0 52.6 jit_solution(163090679187667287)
XLA Ops:
  0.1 1.5 %fusion.86 = (f32[1]{0:T(128)}, f32[1]{0:T(128)}, f32[1]{0:T(128)}, f32[1]{0:T(128)}) fusion(f32[4]{0:T(128)} %param.10), kind=kLoop, calls=%fused_computation.157 | loop fusion | bytes 32 | tf_op jit(solution)/shard_map/slice | solution.py:73
  1.6 3.4 %multiply_convert_fusion = (bf16[8,2048]{1,0:T(8,128)(2,1)S(1)}, f32[8,2048]{1,0:T(8,128)S(1)}, f32[8,2048]{1,0:T(8,128)S(1)}, f32[8,2048]{1,0:T(8,128)S(1)}) fusion(f32[8,2048]{1,0:T(8,128)} %param.9, f32[]{:T(128)} %bitcast.1, f32[]{:T(128)} %bitcast.17, f32[]{:T(128)} %bitcast.43, f32[]{:T(128)} %bitcast.30), kind=kLoop, calls=%fused_computation.35 | loop fusion | flops 81920 | bytes 294928 | tf_op jit(solution)/shard_map/convert_element_type | solution.py:73
  5.0 0.7 %broadcast_subtract_fusion = s32[64]{0:T(128)S(1)} fusion(s32[64]{0:T(128)} %param.16, s32[]{:T(128)S(6)} %mul.50), kind=kLoop, calls=%fused_computation.151 | loop fusion | flops 64 | bytes 516 | tf_op jit(solution)/shard_map/sub | solution.py:66
  5.7 0.3 fusion.28
  6.0 1.3 %fusion.4 = f32[64,8,16]{2,1,0:T(8,128)S(1)} fusion(bf16[64,16,256]{2,1,0:T(8,128)(2,1)} %param.15, bf16[64,8,256]{2,0,1:T(8,128)(2,1)S(1)} %fusion.28), kind=kOutput, calls=%fused_computation.4 | convolution fusion | flops 4194304 | bytes 819200 | tf_op jit(solution)/shard_map/far_partial/jrl,jkl->jrk/dot_general | solution.py:84
  7.7 5.1 %collective-permute-start = (bf16[8,2432]{1,0:T(8,128)(2,1)S(1)}, bf16[8,2432]{1,0:T(8,128)(2,1)S(1)}, u32[]{:S(2)}, u32[]{:S(2)}) collective-permute-start(bf16[8,2432]{1,0:T(8,128)(2,1)S(1)} %get-tuple-element.14), channel_id=1, source_target_pairs={{0,12},{4,0},{8,4},{12,8},{1,13},{5,1},{9,5},{13,9},{2,14},{6,2},{... | collective-permute-start | bytes 116744 | tf_op jit(solution)/shard_map/clus_exchange/ppermute | solution.py:8
  12.8 1.0 %collective-permute-start.1 = (bf16[8,2432]{1,0:T(8,128)(2,1)S(1)}, bf16[8,2432]{1,0:T(8,128)(2,1)S(1)}, u32[]{:S(2)}, u32[]{:S(2)}) collective-permute-start(bf16[8,2432]{1,0:T(8,128)(2,1)S(1)} %get-tuple-element.13), channel_id=1, source_target_pairs={{0,4},{4,8},{8,12},{12,0},{1,5},{5,9},{9,13},{13,1},{2,6},{6,10},{... | collective-permute-start | bytes 116744 | tf_op jit(solution)/shard_map/clus_exchange/ppermute | solution.py:8
  13.9 4.7 %collective-permute-done.1 = bf16[8,2432]{1,0:T(8,128)(2,1)S(1)} collective-permute-done((bf16[8,2432]{1,0:T(8,128)(2,1)S(1)}, bf16[8,2432]{1,0:T(8,128)(2,1)S(1)}, u32[]{:S(2)}, u32[]{:S(2)}) %collective-permute-start.1) | collective-permute-done | bytes 38944 | tf_op jit(solution)/shard_map/clus_exchange/ppermute | solution.py:8
  18.9 0.6 %fusion.19 = f32[16,8,256]{2,1,0:T(8,128)S(1)} fusion(bf16[16,256,256]{2,1,0:T(8,128)(2,1)S(1)} %copy-done, bf16[16,8,256]{2,0,1:T(8,128)(2,1)S(1)} %fusion.12), kind=kOutput, calls=%fused_computation.25 | convolution fusion | flops 16777216 | bytes 2293760 | tf_op jit(solution)/shard_map/near_partial/jrs,jts->jrt/dot_general | solution.py:118
  19.6 0.3 fusion.53
  19.9 1.6 %collective-permute-start.3 = (f32[8,2176]{1,0:T(8,128)S(1)}, f32[8,2176]{1,0:T(8,128)S(1)}, u32[]{:S(2)}, u32[]{:S(2)}) collective-permute-start(f32[8,2176]{1,0:T(8,128)S(1)} %pad_maximum_fusion.3), channel_id=1, source_target_pairs={{0,2},{2,0},{1,3},{3,1},{4,6},{6,4},{5,7},{7,5},{8,10},{10,8},{9,1... | collective-permute-start | bytes 208904 | tf_op jit(solution)/shard_map/pair_sums/ppermute | solution.py:8
  21.5 2.8 %collective-permute-done.3 = f32[8,2176]{1,0:T(8,128)S(1)} collective-permute-done((f32[8,2176]{1,0:T(8,128)S(1)}, f32[8,2176]{1,0:T(8,128)S(1)}, u32[]{:S(2)}, u32[]{:S(2)}) %collective-permute-start.3) | collective-permute-done | bytes 69664 | tf_op jit(solution)/shard_map/pair_sums/ppermute | solution.py:8
  24.6 0.3 fusion.33
  24.9 0.3 fusion.2
  25.5 0.6 %collective-permute-start.4 = (bf16[8,2432]{1,0:T(8,128)(2,1)S(1)}, bf16[8,2432]{1,0:T(8,128)(2,1)S(1)}, u32[]{:S(2)}, u32[]{:S(2)}) collective-permute-start(bf16[8,2432]{1,0:T(8,128)(2,1)S(1)} %get-tuple-element.12), channel_id=1, source_target_pairs={{0,12},{4,0},{8,4},{12,8},{1,13},{5,1},{9,5},{13,9},{2,14},{6,2},{... | collective-permute-start | bytes 116744 | tf_op jit(solution)/shard_map/clus_exchange/ppermute | solution.py:8
  26.2 1.5 %collective-permute-start.5 = (bf16[8,2432]{1,0:T(8,128)(2,1)S(1)}, bf16[8,2432]{1,0:T(8,128)(2,1)S(1)}, u32[]{:S(2)}, u32[]{:S(2)}) collective-permute-start(bf16[8,2432]{1,0:T(8,128)(2,1)S(1)} %get-tuple-element.11), channel_id=1, source_target_pairs={{0,4},{4,8},{8,12},{12,0},{1,5},{5,9},{9,13},{13,1},{2,6},{6,10},{... | collective-permute-start | bytes 116744 | tf_op jit(solution)/shard_map/clus_exchange/ppermute | solution.py:8
  27.6 1.1 %collective-permute-start.6 = (bf16[8,384]{1,0:T(8,128)(2,1)S(1)}, bf16[8,384]{1,0:T(8,128)(2,1)S(1)}, u32[]{:S(2)}, u32[]{:S(2)}) collective-permute-start(bf16[8,384]{1,0:T(8,128)(2,1)S(1)} %pad_maximum_fusion.13), channel_id=1, source_target_pairs={{0,8},{4,12},{8,0},{12,4},{1,9},{5,13},{9,1},{13,5},{2,10},{6,14},... | collective-permute-start | bytes 18440 | tf_op jit(solution)/shard_map/clus_exchange/ppermute | solution.py:8
  28.7 3.2 %collective-permute-done.5 = bf16[8,2432]{1,0:T(8,128)(2,1)S(1)} collective-permute-done((bf16[8,2432]{1,0:T(8,128)(2,1)S(1)}, bf16[8,2432]{1,0:T(8,128)(2,1)S(1)}, u32[]{:S(2)}, u32[]{:S(2)}) %collective-permute-start.5) | collective-permute-done | bytes 38944 | tf_op jit(solution)/shard_map/clus_exchange/ppermute | solution.py:8
  32.2 0.6 %fusion.17 = f32[16,8,256]{2,1,0:T(8,128)S(1)} fusion(bf16[16,256,256]{2,1,0:T(8,128)(2,1)S(1)} %copy-done, bf16[16,8,256]{2,0,1:T(8,128)(2,1)S(1)} %fusion.9), kind=kOutput, calls=%fused_computation.23 | convolution fusion | flops 16777216 | bytes 2293760 | tf_op jit(solution)/shard_map/near_partial/jrs,jts->jrt/dot_general | solution.py:118
  32.9 0.3 fusion.52
  33.2 1.6 %collective-permute-start.7 = (f32[8,2176]{1,0:T(8,128)S(1)}, f32[8,2176]{1,0:T(8,128)S(1)}, u32[]{:S(2)}, u32[]{:S(2)}) collective-permute-start(f32[8,2176]{1,0:T(8,128)S(1)} %pad_maximum_fusion.4), channel_id=1, source_target_pairs={{0,2},{2,0},{1,3},{3,1},{4,6},{6,4},{5,7},{7,5},{8,10},{10,8},{9,1... | collective-permute-start | bytes 208904 | tf_op jit(solution)/shard_map/pair_sums/ppermute | solution.py:8
  34.8 2.8 %collective-permute-done.7 = f32[8,2176]{1,0:T(8,128)S(1)} collective-permute-done((f32[8,2176]{1,0:T(8,128)S(1)}, f32[8,2176]{1,0:T(8,128)S(1)}, u32[]{:S(2)}, u32[]{:S(2)}) %collective-permute-start.7) | collective-permute-done | bytes 69664 | tf_op jit(solution)/shard_map/pair_sums/ppermute | solution.py:8
  37.9 0.3 fusion.31
  38.2 0.3 fusion
  38.9 1.4 %collective-permute-start.8 = (bf16[8,2432]{1,0:T(8,128)(2,1)S(1)}, bf16[8,2432]{1,0:T(8,128)(2,1)S(1)}, u32[]{:S(2)}, u32[]{:S(2)}) collective-permute-start(bf16[8,2432]{1,0:T(8,128)(2,1)S(1)} %get-tuple-element.10), channel_id=1, source_target_pairs={{0,12},{4,0},{8,4},{12,8},{1,13},{5,1},{9,5},{13,9},{2,14},{6,2},{... | collective-permute-start | bytes 116744 | tf_op jit(solution)/shard_map/clus_exchange/ppermute | solution.py:8
  40.2 0.7 %collective-permute-start.9 = (bf16[8,2432]{1,0:T(8,128)(2,1)S(1)}, bf16[8,2432]{1,0:T(8,128)(2,1)S(1)}, u32[]{:S(2)}, u32[]{:S(2)}) collective-permute-start(bf16[8,2432]{1,0:T(8,128)(2,1)S(1)} %get-tuple-element.9), channel_id=1, source_target_pairs={{0,4},{4,8},{8,12},{12,0},{1,5},{5,9},{9,13},{13,1},{2,6},{6,10},{... | collective-permute-start | bytes 116744 | tf_op jit(solution)/shard_map/clus_exchange/ppermute | solution.py:8
  41.0 5.0 %collective-permute-done.9 = bf16[8,2432]{1,0:T(8,128)(2,1)S(1)} collective-permute-done((bf16[8,2432]{1,0:T(8,128)(2,1)S(1)}, bf16[8,2432]{1,0:T(8,128)(2,1)S(1)}, u32[]{:S(2)}, u32[]{:S(2)}) %collective-permute-start.9) | collective-permute-done | bytes 38944 | tf_op jit(solution)/shard_map/clus_exchange/ppermute | solution.py:8
  46.2 0.6 %fusion.15 = f32[16,8,256]{2,1,0:T(8,128)S(1)} fusion(bf16[16,256,256]{2,1,0:T(8,128)(2,1)S(1)} %copy-done, bf16[16,8,256]{2,0,1:T(8,128)(2,1)S(1)} %fusion.6), kind=kOutput, calls=%fused_computation.21 | convolution fusion | flops 16777216 | bytes 2293760 | tf_op jit(solution)/shard_map/near_partial/jrs,jts->jrt/dot_general | solution.py:118
  46.9 0.3 fusion.51
  47.3 1.6 %collective-permute-start.11 = (f32[8,2176]{1,0:T(8,128)S(1)}, f32[8,2176]{1,0:T(8,128)S(1)}, u32[]{:S(2)}, u32[]{:S(2)}) collective-permute-start(f32[8,2176]{1,0:T(8,128)S(1)} %pad_maximum_fusion.5), channel_id=1, source_target_pairs={{0,2},{2,0},{1,3},{3,1},{4,6},{6,4},{5,7},{7,5},{8,10},{10,8},{9,1... | collective-permute-start | bytes 208904 | tf_op jit(solution)/shard_map/pair_sums/ppermute | solution.py:8
  48.8 2.8 %collective-permute-done.11 = f32[8,2176]{1,0:T(8,128)S(1)} collective-permute-done((f32[8,2176]{1,0:T(8,128)S(1)}, f32[8,2176]{1,0:T(8,128)S(1)}, u32[]{:S(2)}, u32[]{:S(2)}) %collective-permute-start.11) | collective-permute-done | bytes 69664 | tf_op jit(solution)/shard_map/pair_sums/ppermute | solution.py:8
  51.8 0.8 %fusion.21 = f32[8,8,256]{2,1,0:T(8,128)} fusion(f32[8,8,256]{2,1,0:T(8,128)S(1)} %bitcast.209, f32[8,8,256]{2,0,1:T(8,128)S(1)} %bitcast.206, f32[8,8,16]{2,1,0:T(8,128)S(1)} %reshape.130, bf16[8,16,256]{2,1,0:T(8,128)(2,1)S(1)} %copy-done.2), kind=kOutput, calls=%fused_computation.28 | convolution fusion | flops 3178496 | bytes 266240 | tf_op jit(solution)/shard_map/far_field/crk,ckl->crl/dot_general | solution.py:131
  (76 shorter events, 2.9 us)
Async XLA Ops:
  0.0 18.8 %copy-start = (bf16[16,256,256]{2,1,0:T(8,128)(2,1)S(1)}, bf16[16,256,256]{2,1,0:T(8,128)(2,1)}, u32[]{:S(2)}) copy-start(bf16[16,256,256]{2,1,0:T(8,128)(2,1)} %param.11) | copy-start | bytes 6291460
  0.0 7.4 %copy-start.3 = (s32[64]{0:T(128)S(1)}, s32[64]{0:T(128)}, u32[]{:S(2)}) copy-start(s32[64]{0:T(128)} %param.17) | copy-start | bytes 772
  0.0 13.8 %copy-start.4 = (s32[16]{0:T(128)S(1)}, s32[16]{0:T(128)}, u32[]{:S(2)}) copy-start(s32[16]{0:T(128)} %param.13) | copy-start | bytes 196
  0.0 13.8 %copy-start.5 = (s32[16]{0:T(128)S(1)}, s32[16]{0:T(128)}, u32[]{:S(2)}) copy-start(s32[16]{0:T(128)} %param.12) | copy-start | bytes 196
  7.4 17.0 %copy-start.2 = (bf16[8,16,256]{2,1,0:T(8,128)(2,1)S(1)}, bf16[8,16,256]{2,1,0:T(8,128)(2,1)}, u32[]{:S(2)}) copy-start(bf16[8,16,256]{2,1,0:T(8,128)(2,1)} %param.14) | copy-start | bytes 196612
  7.7 10.9 %collective-permute-start = (bf16[8,2432]{1,0:T(8,128)(2,1)S(1)}, bf16[8,2432]{1,0:T(8,128)(2,1)S(1)}, u32[]{:S(2)}, u32[]{:S(2)}) collective-permute-start(bf16[8,2432]{1,0:T(8,128)(2,1)S(1)} %get-tuple-element.14), channel_id=1, source_target_pairs={{0,12},{4,0},{8,4},{12,8},{1,13},{5,1},{9,5},{13,9},{2,14},{6,2},{... | collective-permute-start | bytes 116744 | tf_op jit(solution)/shard_map/clus_exchange/ppermute | solution.py:8
  12.8 7.0 %collective-permute-start.2 = (bf16[8,384]{1,0:T(8,128)(2,1)S(1)}, bf16[8,384]{1,0:T(8,128)(2,1)S(1)}, u32[]{:S(2)}, u32[]{:S(2)}) collective-permute-start(bf16[8,384]{1,0:T(8,128)(2,1)S(1)} %pad_maximum_fusion.12), channel_id=1, source_target_pairs={{0,8},{4,12},{8,0},{12,4},{1,9},{5,13},{9,1},{13,5},{2,10},{6,14},... | collective-permute-start | bytes 18440 | tf_op jit(solution)/shard_map/clus_exchange/ppermute | solution.py:8
  12.8 5.8 %collective-permute-start.1 = (bf16[8,2432]{1,0:T(8,128)(2,1)S(1)}, bf16[8,2432]{1,0:T(8,128)(2,1)S(1)}, u32[]{:S(2)}, u32[]{:S(2)}) collective-permute-start(bf16[8,2432]{1,0:T(8,128)(2,1)S(1)} %get-tuple-element.13), channel_id=1, source_target_pairs={{0,4},{4,8},{8,12},{12,0},{1,5},{5,9},{9,13},{13,1},{2,6},{6,10},{... | collective-permute-start | bytes 116744 | tf_op jit(solution)/shard_map/clus_exchange/ppermute | solution.py:8
  18.6 6.2 %copy-start.1 = (bf16[64,16,256]{2,1,0:T(8,128)(2,1)S(1)}, bf16[64,16,256]{2,1,0:T(8,128)(2,1)}, u32[]{:S(2)}) copy-start(bf16[64,16,256]{2,1,0:T(8,128)(2,1)} %param.15) | copy-start | bytes 1572868
  19.9 4.4 %collective-permute-start.3 = (f32[8,2176]{1,0:T(8,128)S(1)}, f32[8,2176]{1,0:T(8,128)S(1)}, u32[]{:S(2)}, u32[]{:S(2)}) collective-permute-start(f32[8,2176]{1,0:T(8,128)S(1)} %pad_maximum_fusion.3), channel_id=1, source_target_pairs={{0,2},{2,0},{1,3},{3,1},{4,6},{6,4},{5,7},{7,5},{8,10},{10,8},{9,1... | collective-permute-start | bytes 208904 | tf_op jit(solution)/shard_map/pair_sums/ppermute | solution.py:8
  25.5 6.4 %collective-permute-start.4 = (bf16[8,2432]{1,0:T(8,128)(2,1)S(1)}, bf16[8,2432]{1,0:T(8,128)(2,1)S(1)}, u32[]{:S(2)}, u32[]{:S(2)}) collective-permute-start(bf16[8,2432]{1,0:T(8,128)(2,1)S(1)} %get-tuple-element.12), channel_id=1, source_target_pairs={{0,12},{4,0},{8,4},{12,8},{1,13},{5,1},{9,5},{13,9},{2,14},{6,2},{... | collective-permute-start | bytes 116744 | tf_op jit(solution)/shard_map/clus_exchange/ppermute | solution.py:8
  26.2 5.8 %collective-permute-start.5 = (bf16[8,2432]{1,0:T(8,128)(2,1)S(1)}, bf16[8,2432]{1,0:T(8,128)(2,1)S(1)}, u32[]{:S(2)}, u32[]{:S(2)}) collective-permute-start(bf16[8,2432]{1,0:T(8,128)(2,1)S(1)} %get-tuple-element.11), channel_id=1, source_target_pairs={{0,4},{4,8},{8,12},{12,0},{1,5},{5,9},{9,13},{13,1},{2,6},{6,10},{... | collective-permute-start | bytes 116744 | tf_op jit(solution)/shard_map/clus_exchange/ppermute | solution.py:8
  27.6 5.5 %collective-permute-start.6 = (bf16[8,384]{1,0:T(8,128)(2,1)S(1)}, bf16[8,384]{1,0:T(8,128)(2,1)S(1)}, u32[]{:S(2)}, u32[]{:S(2)}) collective-permute-start(bf16[8,384]{1,0:T(8,128)(2,1)S(1)} %pad_maximum_fusion.13), channel_id=1, source_target_pairs={{0,8},{4,12},{8,0},{12,4},{1,9},{5,13},{9,1},{13,5},{2,10},{6,14},... | collective-permute-start | bytes 18440 | tf_op jit(solution)/shard_map/clus_exchange/ppermute | solution.py:8
  33.2 4.4 %collective-permute-start.7 = (f32[8,2176]{1,0:T(8,128)S(1)}, f32[8,2176]{1,0:T(8,128)S(1)}, u32[]{:S(2)}, u32[]{:S(2)}) collective-permute-start(f32[8,2176]{1,0:T(8,128)S(1)} %pad_maximum_fusion.4), channel_id=1, source_target_pairs={{0,2},{2,0},{1,3},{3,1},{4,6},{6,4},{5,7},{7,5},{8,10},{10,8},{9,1... | collective-permute-start | bytes 208904 | tf_op jit(solution)/shard_map/pair_sums/ppermute | solution.py:8
  38.9 7.2 %collective-permute-start.8 = (bf16[8,2432]{1,0:T(8,128)(2,1)S(1)}, bf16[8,2432]{1,0:T(8,128)(2,1)S(1)}, u32[]{:S(2)}, u32[]{:S(2)}) collective-permute-start(bf16[8,2432]{1,0:T(8,128)(2,1)S(1)} %get-tuple-element.10), channel_id=1, source_target_pairs={{0,12},{4,0},{8,4},{12,8},{1,13},{5,1},{9,5},{13,9},{2,14},{6,2},{... | collective-permute-start | bytes 116744 | tf_op jit(solution)/shard_map/clus_exchange/ppermute | solution.py:8
  40.2 5.8 %collective-permute-start.9 = (bf16[8,2432]{1,0:T(8,128)(2,1)S(1)}, bf16[8,2432]{1,0:T(8,128)(2,1)S(1)}, u32[]{:S(2)}, u32[]{:S(2)}) collective-permute-start(bf16[8,2432]{1,0:T(8,128)(2,1)S(1)} %get-tuple-element.9), channel_id=1, source_target_pairs={{0,4},{4,8},{8,12},{12,0},{1,5},{5,9},{9,13},{13,1},{2,6},{6,10},{... | collective-permute-start | bytes 116744 | tf_op jit(solution)/shard_map/clus_exchange/ppermute | solution.py:8
  40.9 6.3 %collective-permute-start.10 = (bf16[8,384]{1,0:T(8,128)(2,1)S(1)}, bf16[8,384]{1,0:T(8,128)(2,1)S(1)}, u32[]{:S(2)}, u32[]{:S(2)}) collective-permute-start(bf16[8,384]{1,0:T(8,128)(2,1)S(1)} %pad_maximum_fusion.14), channel_id=1, source_target_pairs={{0,8},{4,12},{8,0},{12,4},{1,9},{5,13},{9,1},{13,5},{2,10},{6,14},... | collective-permute-start | bytes 18440 | tf_op jit(solution)/shard_map/clus_exchange/ppermute | solution.py:8
  47.3 4.4 %collective-permute-start.11 = (f32[8,2176]{1,0:T(8,128)S(1)}, f32[8,2176]{1,0:T(8,128)S(1)}, u32[]{:S(2)}, u32[]{:S(2)}) collective-permute-start(f32[8,2176]{1,0:T(8,128)S(1)} %pad_maximum_fusion.5), channel_id=1, source_target_pairs={{0,2},{2,0},{1,3},{3,1},{4,6},{6,4},{5,7},{7,5},{8,10},{10,8},{9,1... | collective-permute-start | bytes 208904 | tf_op jit(solution)/shard_map/pair_sums/ppermute | solution.py:8

commit v11 on v10

--- a/solution.py
+++ b/solution.py
@@ -131,7 +131,8 @@
             far_field = jnp.einsum(
                 "crk,ckl->crl", coef_sum, row_f32, precision=lax.Precision.HIGHEST
             )
-        result = near_sum + far_field + coefficients[degree] * source
+        scale, near_sum = lax.optimization_barrier((coefficients[degree], near_sum))
+        result = near_sum + far_field + scale * source
         iterate = result.astype(jnp.bfloat16)
     return result.transpose(1, 0, 2).reshape(rhs_here, clusters_here * leaf_size)
 

time: 52.8 us -> 53.6 us (1.015)
  matrix products: 7.72 us -> 8.4 us
    mul x0 -> x3, other arithmetic: none -> 1.95 us  [shards(): result = near_sum + far_field + scale * source]
    convert_element_type x1, other arithmetic: 3.43 us -> 1.49 us  [shards(): iterate = (coefficients[degree_top] * source).astype(jnp.bfloat16)]
    dot_general x3, matrix products: 0.54 us -> 1.22 us  [shards(): jnp.einsum('jc,jm->cm', far_hot, coef, precision=lax.Precision.HIGHEST)]
where the time goes in v11:
time: 53.6 us; the launch traced here: 53.3 us
  waiting for transfers between devices  21.4 us (40%)
  starting transfers between devices  16.2 us (30%)
  matrix products  8.4 us (16%)
  other arithmetic  4.51 us (8%)
  local copies, waits for them, and re-layouts  2.4 us (4%)
    ppermute x12, waiting for transfers between devices, shift(): lax.ppermute(value, axis, [(i, (i + step) % count) for i in range(count)])  21.4 us
    ppermute x12, starting transfers between devices, shift(): lax.ppermute(value, axis, [(i, (i + step) % count) for i in range(count)])  16.2 us
    mul x3, other arithmetic, shards(): result = near_sum + far_field + scale * source  1.95 us
    dot_general x3, matrix products, shards(): jnp.einsum('jrs,jts->jrt', gathered, near_blocks, preferred_element_type=...  1.92 us
    dot_general x3, matrix products, shards(): jnp.einsum('jrl,jkl->jrk', far_input, col_basis, preferred_element_type=j...  1.87 us
    slice x1, local copies, waits for them, and re-layouts, shards(): iterate = (coefficients[degree_top] * source).astype(jnp.bfloat16)  1.51 us
    convert_element_type x1, other arithmetic, shards(): iterate = (coefficients[degree_top] * source).astype(jnp.bfloat16)  1.49 us
    dot_general x3, matrix products, shards(): jnp.einsum('jc,jm->cm', far_hot, coef, precision=lax.Precision.HIGHEST)  1.22 us
  transfers between devices with their start and end apart: 12, of which 6 were waited for; matrix products, arithmetic and copies ran while one was open for 7% of the time, Pallas kernels for 0%

profile of v11, /device:TPU:0, one launch (start us, length us, event | category | flops | bytes accessed | tf_op | source)
XLA Modules:
  0.0 53.3 jit_solution(17993666448185193350)
XLA Ops:
  0.1 1.5 %fusion.86 = (f32[1]{0:T(128)}, f32[1]{0:T(128)}, f32[1]{0:T(128)}, f32[1]{0:T(128)}) fusion(f32[4]{0:T(128)} %param.10), kind=kLoop, calls=%fused_computation.157 | loop fusion | bytes 32 | tf_op jit(solution)/shard_map/slice | solution.py:73
  1.6 1.5 %multiply_convert_fusion = bf16[8,2048]{1,0:T(8,128)(2,1)S(1)} fusion(f32[8,2048]{1,0:T(8,128)} %param.9, f32[]{:T(128)} %bitcast.4), kind=kLoop, calls=%fused_computation.37 | loop fusion | flops 32768 | bytes 98308 | tf_op jit(solution)/shard_map/convert_element_type | solution.py:73
  3.1 0.7 %broadcast_subtract_fusion = s32[64]{0:T(128)S(1)} fusion(s32[64]{0:T(128)} %param.16, s32[]{:T(128)S(6)} %mul.50), kind=kLoop, calls=%fused_computation.151 | loop fusion | flops 64 | bytes 516 | tf_op jit(solution)/shard_map/sub | solution.py:66
  4.0 1.3 %fusion.11 = f32[64,8,16]{2,1,0:T(8,128)S(1)} fusion(bf16[64,16,256]{2,1,0:T(8,128)(2,1)} %param.15, bf16[64,8,256]{2,0,1:T(8,128)(2,1)S(1)} %fusion.28), kind=kOutput, calls=%fused_computation.14 | convolution fusion | flops 4194304 | bytes 819200 | tf_op jit(solution)/shard_map/far_partial/jrl,jkl->jrk/dot_general | solution.py:84
  5.5 0.9 %fusion.40 = f32[4,8,128]{2,1,0:T(8,128)S(1)} fusion(f32[64,128,1]{0,1,2:T(8,128)S(1)} %bitcast.203, s32[4,8]{1,0:T(4,128)S(1)} %multiply_add_fusion, s32[64]{0:T(128)} %param.17), kind=kOutput, calls=%fused_computation.57 | convolution fusion | flops 3147776 | bytes 49536 | tf_op jit(solution)/shard_map/far_partial/jc,jm->cm/dot_general | solution.py:88
  6.4 5.1 %collective-permute-start = (bf16[8,2432]{1,0:T(8,128)(2,1)S(1)}, bf16[8,2432]{1,0:T(8,128)(2,1)S(1)}, u32[]{:S(2)}, u32[]{:S(2)}) collective-permute-start(bf16[8,2432]{1,0:T(8,128)(2,1)S(1)} %get-tuple-element.22), channel_id=1, source_target_pairs={{0,12},{4,0},{8,4},{12,8},{1,13},{5,1},{9,5},{13,9},{2,14},{6,2},{... | collective-permute-start | bytes 116744 | tf_op jit(solution)/shard_map/clus_exchange/ppermute | solution.py:8
  11.5 1.0 %collective-permute-start.1 = (bf16[8,2432]{1,0:T(8,128)(2,1)S(1)}, bf16[8,2432]{1,0:T(8,128)(2,1)S(1)}, u32[]{:S(2)}, u32[]{:S(2)}) collective-permute-start(bf16[8,2432]{1,0:T(8,128)(2,1)S(1)} %get-tuple-element.21), channel_id=1, source_target_pairs={{0,4},{4,8},{8,12},{12,0},{1,5},{5,9},{9,13},{13,1},{2,6},{6,10},{... | collective-permute-start | bytes 116744 | tf_op jit(solution)/shard_map/clus_exchange/ppermute | solution.py:8
  12.6 4.7 %collective-permute-done.1 = bf16[8,2432]{1,0:T(8,128)(2,1)S(1)} collective-permute-done((bf16[8,2432]{1,0:T(8,128)(2,1)S(1)}, bf16[8,2432]{1,0:T(8,128)(2,1)S(1)}, u32[]{:S(2)}, u32[]{:S(2)}) %collective-permute-start.1) | collective-permute-done | bytes 38944 | tf_op jit(solution)/shard_map/clus_exchange/ppermute | solution.py:8
  17.6 0.6 %fusion.26 = f32[16,8,256]{2,1,0:T(8,128)S(1)} fusion(bf16[16,256,256]{2,1,0:T(8,128)(2,1)S(1)} %copy-done, bf16[16,8,256]{2,0,1:T(8,128)(2,1)S(1)} %fusion.19), kind=kOutput, calls=%fused_computation.35 | convolution fusion | flops 16777216 | bytes 2293760 | tf_op jit(solution)/shard_map/near_partial/jrs,jts->jrt/dot_general | solution.py:118
  18.3 0.3 fusion.53
  18.6 1.6 %collective-permute-start.3 = (f32[8,2176]{1,0:T(8,128)S(1)}, f32[8,2176]{1,0:T(8,128)S(1)}, u32[]{:S(2)}, u32[]{:S(2)}) collective-permute-start(f32[8,2176]{1,0:T(8,128)S(1)} %pad_maximum_fusion.3), channel_id=1, source_target_pairs={{0,2},{2,0},{1,3},{3,1},{4,6},{6,4},{5,7},{7,5},{8,10},{10,8},{9,1... | collective-permute-start | bytes 208904 | tf_op jit(solution)/shard_map/pair_sums/ppermute | solution.py:8
  20.2 2.8 %collective-permute-done.3 = f32[8,2176]{1,0:T(8,128)S(1)} collective-permute-done((f32[8,2176]{1,0:T(8,128)S(1)}, f32[8,2176]{1,0:T(8,128)S(1)}, u32[]{:S(2)}, u32[]{:S(2)}) %collective-permute-start.3) | collective-permute-done | bytes 69664 | tf_op jit(solution)/shard_map/pair_sums/ppermute | solution.py:8
  23.0 0.7 %broadcast_multiply_fusion.2 = f32[8,2048]{1,0:T(8,128)S(1)} fusion(f32[8,2048]{1,0:T(8,128)S(1)} %copy-done.2, f32[]{:T(128)} %bitcast.3), kind=kLoop, calls=%fused_computation.48 | loop fusion | flops 16384 | bytes 131076 | tf_op jit(solution)/shard_map/mul | solution.py:135
  24.3 0.3 fusion.9
  25.0 0.6 %collective-permute-start.4 = (bf16[8,2432]{1,0:T(8,128)(2,1)S(1)}, bf16[8,2432]{1,0:T(8,128)(2,1)S(1)}, u32[]{:S(2)}, u32[]{:S(2)}) collective-permute-start(bf16[8,2432]{1,0:T(8,128)(2,1)S(1)} %get-tuple-element.20), channel_id=1, source_target_pairs={{0,12},{4,0},{8,4},{12,8},{1,13},{5,1},{9,5},{13,9},{2,14},{6,2},{... | collective-permute-start | bytes 116744 | tf_op jit(solution)/shard_map/clus_exchange/ppermute | solution.py:8
  25.6 1.5 %collective-permute-start.5 = (bf16[8,2432]{1,0:T(8,128)(2,1)S(1)}, bf16[8,2432]{1,0:T(8,128)(2,1)S(1)}, u32[]{:S(2)}, u32[]{:S(2)}) collective-permute-start(bf16[8,2432]{1,0:T(8,128)(2,1)S(1)} %get-tuple-element.19), channel_id=1, source_target_pairs={{0,4},{4,8},{8,12},{12,0},{1,5},{5,9},{9,13},{13,1},{2,6},{6,10},{... | collective-permute-start | bytes 116744 | tf_op jit(solution)/shard_map/clus_exchange/ppermute | solution.py:8
  27.1 1.1 %collective-permute-start.6 = (bf16[8,384]{1,0:T(8,128)(2,1)S(1)}, bf16[8,384]{1,0:T(8,128)(2,1)S(1)}, u32[]{:S(2)}, u32[]{:S(2)}) collective-permute-start(bf16[8,384]{1,0:T(8,128)(2,1)S(1)} %pad_maximum_fusion.13), channel_id=1, source_target_pairs={{0,8},{4,12},{8,0},{12,4},{1,9},{5,13},{9,1},{13,5},{2,10},{6,14},... | collective-permute-start | bytes 18440 | tf_op jit(solution)/shard_map/clus_exchange/ppermute | solution.py:8
  28.2 3.2 %collective-permute-done.5 = bf16[8,2432]{1,0:T(8,128)(2,1)S(1)} collective-permute-done((bf16[8,2432]{1,0:T(8,128)(2,1)S(1)}, bf16[8,2432]{1,0:T(8,128)(2,1)S(1)}, u32[]{:S(2)}, u32[]{:S(2)}) %collective-permute-start.5) | collective-permute-done | bytes 38944 | tf_op jit(solution)/shard_map/clus_exchange/ppermute | solution.py:8
  31.6 0.6 %fusion.24 = f32[16,8,256]{2,1,0:T(8,128)S(1)} fusion(bf16[16,256,256]{2,1,0:T(8,128)(2,1)S(1)} %copy-done, bf16[16,8,256]{2,0,1:T(8,128)(2,1)S(1)} %fusion.16), kind=kOutput, calls=%fused_computation.33 | convolution fusion | flops 16777216 | bytes 2293760 | tf_op jit(solution)/shard_map/near_partial/jrs,jts->jrt/dot_general | solution.py:118
  32.3 0.3 fusion.52
  32.6 1.6 %collective-permute-start.7 = (f32[8,2176]{1,0:T(8,128)S(1)}, f32[8,2176]{1,0:T(8,128)S(1)}, u32[]{:S(2)}, u32[]{:S(2)}) collective-permute-start(f32[8,2176]{1,0:T(8,128)S(1)} %pad_maximum_fusion.4), channel_id=1, source_target_pairs={{0,2},{2,0},{1,3},{3,1},{4,6},{6,4},{5,7},{7,5},{8,10},{10,8},{9,1... | collective-permute-start | bytes 208904 | tf_op jit(solution)/shard_map/pair_sums/ppermute | solution.py:8
  34.2 2.8 %collective-permute-done.7 = f32[8,2176]{1,0:T(8,128)S(1)} collective-permute-done((f32[8,2176]{1,0:T(8,128)S(1)}, f32[8,2176]{1,0:T(8,128)S(1)}, u32[]{:S(2)}, u32[]{:S(2)}) %collective-permute-start.7) | collective-permute-done | bytes 69664 | tf_op jit(solution)/shard_map/pair_sums/ppermute | solution.py:8
  37.1 0.7 %broadcast_multiply_fusion.1 = f32[8,2048]{1,0:T(8,128)S(1)} fusion(f32[8,2048]{1,0:T(8,128)S(1)} %copy-done.2, f32[]{:T(128)} %bitcast.2), kind=kLoop, calls=%fused_computation.47 | loop fusion | flops 16384 | bytes 131076 | tf_op jit(solution)/shard_map/mul | solution.py:135
  39.0 1.4 %collective-permute-start.8 = (bf16[8,2432]{1,0:T(8,128)(2,1)S(1)}, bf16[8,2432]{1,0:T(8,128)(2,1)S(1)}, u32[]{:S(2)}, u32[]{:S(2)}) collective-permute-start(bf16[8,2432]{1,0:T(8,128)(2,1)S(1)} %get-tuple-element.18), channel_id=1, source_target_pairs={{0,12},{4,0},{8,4},{12,8},{1,13},{5,1},{9,5},{13,9},{2,14},{6,2},{... | collective-permute-start | bytes 116744 | tf_op jit(solution)/shard_map/clus_exchange/ppermute | solution.py:8
  40.4 0.7 %collective-permute-start.9 = (bf16[8,2432]{1,0:T(8,128)(2,1)S(1)}, bf16[8,2432]{1,0:T(8,128)(2,1)S(1)}, u32[]{:S(2)}, u32[]{:S(2)}) collective-permute-start(bf16[8,2432]{1,0:T(8,128)(2,1)S(1)} %get-tuple-element.17), channel_id=1, source_target_pairs={{0,4},{4,8},{8,12},{12,0},{1,5},{5,9},{9,13},{13,1},{2,6},{6,10},{... | collective-permute-start | bytes 116744 | tf_op jit(solution)/shard_map/clus_exchange/ppermute | solution.py:8
  41.2 5.0 %collective-permute-done.9 = bf16[8,2432]{1,0:T(8,128)(2,1)S(1)} collective-permute-done((bf16[8,2432]{1,0:T(8,128)(2,1)S(1)}, bf16[8,2432]{1,0:T(8,128)(2,1)S(1)}, u32[]{:S(2)}, u32[]{:S(2)}) %collective-permute-start.9) | collective-permute-done | bytes 38944 | tf_op jit(solution)/shard_map/clus_exchange/ppermute | solution.py:8
  46.4 0.6 %fusion.22 = f32[16,8,256]{2,1,0:T(8,128)S(1)} fusion(bf16[16,256,256]{2,1,0:T(8,128)(2,1)S(1)} %copy-done, bf16[16,8,256]{2,0,1:T(8,128)(2,1)S(1)} %fusion.13), kind=kOutput, calls=%fused_computation.31 | convolution fusion | flops 16777216 | bytes 2293760 | tf_op jit(solution)/shard_map/near_partial/jrs,jts->jrt/dot_general | solution.py:118
  47.1 0.3 fusion.51
  47.4 1.6 %collective-permute-start.11 = (f32[8,2176]{1,0:T(8,128)S(1)}, f32[8,2176]{1,0:T(8,128)S(1)}, u32[]{:S(2)}, u32[]{:S(2)}) collective-permute-start(f32[8,2176]{1,0:T(8,128)S(1)} %pad_maximum_fusion.5), channel_id=1, source_target_pairs={{0,2},{2,0},{1,3},{3,1},{4,6},{6,4},{5,7},{7,5},{8,10},{10,8},{9,1... | collective-permute-start | bytes 208904 | tf_op jit(solution)/shard_map/pair_sums/ppermute | solution.py:8
  49.0 2.8 %collective-permute-done.11 = f32[8,2176]{1,0:T(8,128)S(1)} collective-permute-done((f32[8,2176]{1,0:T(8,128)S(1)}, f32[8,2176]{1,0:T(8,128)S(1)}, u32[]{:S(2)}, u32[]{:S(2)}) %collective-permute-start.11) | collective-permute-done | bytes 69664 | tf_op jit(solution)/shard_map/pair_sums/ppermute | solution.py:8
  51.8 0.6 %broadcast_multiply_fusion = f32[8,2048]{1,0:T(8,128)S(1)} fusion(f32[8,2048]{1,0:T(8,128)S(1)} %copy-done.2, f32[]{:T(128)} %bitcast), kind=kLoop, calls=%fused_computation.46 | loop fusion | flops 16384 | bytes 131076 | tf_op jit(solution)/shard_map/mul | solution.py:135
  52.5 0.8 %fusion = f32[8,8,256]{2,1,0:T(8,128)} fusion(f32[8,8,256]{2,1,0:T(8,128)S(1)} %bitcast.211, f32[8,8,16]{2,1,0:T(8,128)S(1)} %reshape.130, bf16[8,16,256]{2,1,0:T(8,128)(2,1)S(1)} %copy-done.3, f32[8,8,256]{2,0,1:T(8,128)S(1)} %bitcast.206), kind=kOutput, calls=%fused_computation.1 | convolution fusion | flops 3178496 | bytes 266240 | tf_op jit(solution)/shard_map/far_field/crk,ckl->crl/dot_general | solution.py:131
  (81 shorter events, 3.8 us)
Async XLA Ops:
  0.0 17.6 %copy-start = (bf16[16,256,256]{2,1,0:T(8,128)(2,1)S(1)}, bf16[16,256,256]{2,1,0:T(8,128)(2,1)}, u32[]{:S(2)}) copy-start(bf16[16,256,256]{2,1,0:T(8,128)(2,1)} %param.11) | copy-start | bytes 6291460
  0.0 12.6 %copy-start.5 = (s32[16]{0:T(128)S(1)}, s32[16]{0:T(128)}, u32[]{:S(2)}) copy-start(s32[16]{0:T(128)} %param.13) | copy-start | bytes 196
  0.0 12.6 %copy-start.6 = (s32[16]{0:T(128)S(1)}, s32[16]{0:T(128)}, u32[]{:S(2)}) copy-start(s32[16]{0:T(128)} %param.12) | copy-start | bytes 196
  5.5 17.6 %copy-start.2 = (f32[8,2048]{1,0:T(8,128)S(1)}, f32[8,2048]{1,0:T(8,128)}, u32[]{:S(2)}) copy-start(f32[8,2048]{1,0:T(8,128)} %param.9) | copy-start | bytes 196612
  5.5 18.3 %copy-start.3 = (bf16[8,16,256]{2,1,0:T(8,128)(2,1)S(1)}, bf16[8,16,256]{2,1,0:T(8,128)(2,1)}, u32[]{:S(2)}) copy-start(bf16[8,16,256]{2,1,0:T(8,128)(2,1)} %param.14) | copy-start | bytes 196612
  6.4 10.9 %collective-permute-start = (bf16[8,2432]{1,0:T(8,128)(2,1)S(1)}, bf16[8,2432]{1,0:T(8,128)(2,1)S(1)}, u32[]{:S(2)}, u32[]{:S(2)}) collective-permute-start(bf16[8,2432]{1,0:T(8,128)(2,1)S(1)} %get-tuple-element.22), channel_id=1, source_target_pairs={{0,12},{4,0},{8,4},{12,8},{1,13},{5,1},{9,5},{13,9},{2,14},{6,2},{... | collective-permute-start | bytes 116744 | tf_op jit(solution)/shard_map/clus_exchange/ppermute | solution.py:8
  11.5 7.0 %collective-permute-start.2 = (bf16[8,384]{1,0:T(8,128)(2,1)S(1)}, bf16[8,384]{1,0:T(8,128)(2,1)S(1)}, u32[]{:S(2)}, u32[]{:S(2)}) collective-permute-start(bf16[8,384]{1,0:T(8,128)(2,1)S(1)} %pad_maximum_fusion.12), channel_id=1, source_target_pairs={{0,8},{4,12},{8,0},{12,4},{1,9},{5,13},{9,1},{13,5},{2,10},{6,14},... | collective-permute-start | bytes 18440 | tf_op jit(solution)/shard_map/clus_exchange/ppermute | solution.py:8
  11.5 5.8 %collective-permute-start.1 = (bf16[8,2432]{1,0:T(8,128)(2,1)S(1)}, bf16[8,2432]{1,0:T(8,128)(2,1)S(1)}, u32[]{:S(2)}, u32[]{:S(2)}) collective-permute-start(bf16[8,2432]{1,0:T(8,128)(2,1)S(1)} %get-tuple-element.21), channel_id=1, source_target_pairs={{0,4},{4,8},{8,12},{12,0},{1,5},{5,9},{9,13},{13,1},{2,6},{6,10},{... | collective-permute-start | bytes 116744 | tf_op jit(solution)/shard_map/clus_exchange/ppermute | solution.py:8
  17.4 6.9 %copy-start.1 = (bf16[64,16,256]{2,1,0:T(8,128)(2,1)S(1)}, bf16[64,16,256]{2,1,0:T(8,128)(2,1)}, u32[]{:S(2)}) copy-start(bf16[64,16,256]{2,1,0:T(8,128)(2,1)} %param.15) | copy-start | bytes 1572868
  18.2 6.5 %copy-start.4 = (s32[64]{0:T(128)S(1)}, s32[64]{0:T(128)}, u32[]{:S(2)}) copy-start(s32[64]{0:T(128)} %param.17) | copy-start | bytes 772
  18.6 4.4 %collective-permute-start.3 = (f32[8,2176]{1,0:T(8,128)S(1)}, f32[8,2176]{1,0:T(8,128)S(1)}, u32[]{:S(2)}, u32[]{:S(2)}) collective-permute-start(f32[8,2176]{1,0:T(8,128)S(1)} %pad_maximum_fusion.3), channel_id=1, source_target_pairs={{0,2},{2,0},{1,3},{3,1},{4,6},{6,4},{5,7},{7,5},{8,10},{10,8},{9,1... | collective-permute-start | bytes 208904 | tf_op jit(solution)/shard_map/pair_sums/ppermute | solution.py:8
  25.0 6.4 %collective-permute-start.4 = (bf16[8,2432]{1,0:T(8,128)(2,1)S(1)}, bf16[8,2432]{1,0:T(8,128)(2,1)S(1)}, u32[]{:S(2)}, u32[]{:S(2)}) collective-permute-start(bf16[8,2432]{1,0:T(8,128)(2,1)S(1)} %get-tuple-element.20), channel_id=1, source_target_pairs={{0,12},{4,0},{8,4},{12,8},{1,13},{5,1},{9,5},{13,9},{2,14},{6,2},{... | collective-permute-start | bytes 116744 | tf_op jit(solution)/shard_map/clus_exchange/ppermute | solution.py:8
  25.6 5.8 %collective-permute-start.5 = (bf16[8,2432]{1,0:T(8,128)(2,1)S(1)}, bf16[8,2432]{1,0:T(8,128)(2,1)S(1)}, u32[]{:S(2)}, u32[]{:S(2)}) collective-permute-start(bf16[8,2432]{1,0:T(8,128)(2,1)S(1)} %get-tuple-element.19), channel_id=1, source_target_pairs={{0,4},{4,8},{8,12},{12,0},{1,5},{5,9},{9,13},{13,1},{2,6},{6,10},{... | collective-permute-start | bytes 116744 | tf_op jit(solution)/shard_map/clus_exchange/ppermute | solution.py:8
  27.1 5.6 %collective-permute-start.6 = (bf16[8,384]{1,0:T(8,128)(2,1)S(1)}, bf16[8,384]{1,0:T(8,128)(2,1)S(1)}, u32[]{:S(2)}, u32[]{:S(2)}) collective-permute-start(bf16[8,384]{1,0:T(8,128)(2,1)S(1)} %pad_maximum_fusion.13), channel_id=1, source_target_pairs={{0,8},{4,12},{8,0},{12,4},{1,9},{5,13},{9,1},{13,5},{2,10},{6,14},... | collective-permute-start | bytes 18440 | tf_op jit(solution)/shard_map/clus_exchange/ppermute | solution.py:8
  32.6 4.4 %collective-permute-start.7 = (f32[8,2176]{1,0:T(8,128)S(1)}, f32[8,2176]{1,0:T(8,128)S(1)}, u32[]{:S(2)}, u32[]{:S(2)}) collective-permute-start(f32[8,2176]{1,0:T(8,128)S(1)} %pad_maximum_fusion.4), channel_id=1, source_target_pairs={{0,2},{2,0},{1,3},{3,1},{4,6},{6,4},{5,7},{7,5},{8,10},{10,8},{9,1... | collective-permute-start | bytes 208904 | tf_op jit(solution)/shard_map/pair_sums/ppermute | solution.py:8
  39.0 7.2 %collective-permute-start.8 = (bf16[8,2432]{1,0:T(8,128)(2,1)S(1)}, bf16[8,2432]{1,0:T(8,128)(2,1)S(1)}, u32[]{:S(2)}, u32[]{:S(2)}) collective-permute-start(bf16[8,2432]{1,0:T(8,128)(2,1)S(1)} %get-tuple-element.18), channel_id=1, source_target_pairs={{0,12},{4,0},{8,4},{12,8},{1,13},{5,1},{9,5},{13,9},{2,14},{6,2},{... | collective-permute-start | bytes 116744 | tf_op jit(solution)/shard_map/clus_exchange/ppermute | solution.py:8
  40.4 5.8 %collective-permute-start.9 = (bf16[8,2432]{1,0:T(8,128)(2,1)S(1)}, bf16[8,2432]{1,0:T(8,128)(2,1)S(1)}, u32[]{:S(2)}, u32[]{:S(2)}) collective-permute-start(bf16[8,2432]{1,0:T(8,128)(2,1)S(1)} %get-tuple-element.17), channel_id=1, source_target_pairs={{0,4},{4,8},{8,12},{12,0},{1,5},{5,9},{9,13},{13,1},{2,6},{6,10},{... | collective-permute-start | bytes 116744 | tf_op jit(solution)/shard_map/clus_exchange/ppermute | solution.py:8
  41.1 6.3 %collective-permute-start.10 = (bf16[8,384]{1,0:T(8,128)(2,1)S(1)}, bf16[8,384]{1,0:T(8,128)(2,1)S(1)}, u32[]{:S(2)}, u32[]{:S(2)}) collective-permute-start(bf16[8,384]{1,0:T(8,128)(2,1)S(1)} %pad_maximum_fusion.14), channel_id=1, source_target_pairs={{0,8},{4,12},{8,0},{12,4},{1,9},{5,13},{9,1},{13,5},{2,10},{6,14},... | collective-permute-start | bytes 18440 | tf_op jit(solution)/shard_map/clus_exchange/ppermute | solution.py:8
  47.4 4.4 %collective-permute-start.11 = (f32[8,2176]{1,0:T(8,128)S(1)}, f32[8,2176]{1,0:T(8,128)S(1)}, u32[]{:S(2)}, u32[]{:S(2)}) collective-permute-start(f32[8,2176]{1,0:T(8,128)S(1)} %pad_maximum_fusion.5), channel_id=1, source_target_pairs={{0,2},{2,0},{1,3},{3,1},{4,6},{6,4},{5,7},{7,5},{8,10},{10,8},{9,1... | collective-permute-start | bytes 208904 | tf_op jit(solution)/shard_map/pair_sums/ppermute | solution.py:8

commit v12 on v10

--- a/solution.py
+++ b/solution.py
@@ -72,6 +72,7 @@
 
     iterate = (coefficients[degree_top] * source).astype(jnp.bfloat16)
     result = source
+    scaled = None
     for step in range(degree_top):
         degree = degree_top - 1 - step
         with jax.named_scope("far_partial"):
@@ -97,6 +98,9 @@
                 carries_iterate = s == 1 or s == peer_count - 1
                 if carries_iterate:
                     outgoing = jnp.concatenate([iterate_flat, outgoing], axis=1)
+                if s == 1 and scaled is None:
+                    scales, outgoing = lax.optimization_barrier((coefficients, outgoing))
+                    scaled = [scales[d] * source for d in range(degree_top)]
                 incoming = shift(outgoing, "clus", peer_count, s)
                 if carries_iterate:
                     neighbour = incoming[:, :iterate_size]
@@ -123,6 +127,10 @@
                 "jc,jm->cm", target_hot, contrib, precision=lax.Precision.HIGHEST
             )
         with jax.named_scope("pair_sums"):
+            if scaled is None:
+                scaled = [coefficients[d] * source for d in range(degree_top)]
+            if step == 0:
+                scaled, near_part = lax.optimization_barrier((scaled, near_part))
             packed = jnp.concatenate([near_part, far_mine], axis=1)
             packed = pair_total(packed, pair_count, pair_index)
             near_sum = packed[:, :iterate_size].reshape(clusters_here, rhs_here, leaf_size)
@@ -131,7 +139,7 @@
             far_field = jnp.einsum(
                 "crk,ckl->crl", coef_sum, row_f32, precision=lax.Precision.HIGHEST
             )
-        result = near_sum + far_field + coefficients[degree] * source
+        result = near_sum + far_field + scaled[degree]
         iterate = result.astype(jnp.bfloat16)
     return result.transpose(1, 0, 2).reshape(rhs_here, clusters_here * leaf_size)
 

time: 52.8 us -> 52.1 us (0.987)
  waiting for transfers between devices: 21.4 us -> 15 us
  starting transfers between devices: 16.2 us -> 20.4 us
  matrix products: 7.72 us -> 8.39 us
  local copies, waits for them, and re-layouts: 2.39 us -> 2.94 us
    ppermute x12, waiting for transfers between devices: 21.4 us -> 15 us  [shift(): lax.ppermute(value, axis, [(i, (i + step) % count) for i in range(count)])]
    ppermute x12, starting transfers between devices: 16.2 us -> 20.4 us  [shift(): lax.ppermute(value, axis, [(i, (i + step) % count) for i in range(count)])]
    mul x0 -> x1, other arithmetic: none -> 2.02 us  [shards(): scaled = [scales[d] * source for d in range(degree_top)]]
    convert_element_type x1, other arithmetic: 3.43 us -> 1.49 us  [shards(): iterate = (coefficients[degree_top] * source).astype(jnp.bfloat16)]
    slice x0 -> x1, local copies, waits for them, and re-layouts: none -> 0.67 us  [shards(): scaled = [scales[d] * source for d in range(degree_top)]]
    dot_general x3, matrix products: 0.54 us -> 1.2 us  [shards(): jnp.einsum('jc,jm->cm', far_hot, coef, precision=lax.Precision.HIGHEST)]
  transfers between devices with their start and end apart: 12 -> 12, of which waited for: 6 -> 7; matrix products, arithmetic and copies ran while one was open for 7% -> 12% of each run, Pallas kernels for 0% -> 0%
where the time goes in v12:
time: 52.1 us; the launch traced here: 51.8 us
  starting transfers between devices  20.4 us (39%)
  waiting for transfers between devices  15 us (29%)
  matrix products  8.39 us (16%)
  other arithmetic  4.56 us (9%)
  local copies, waits for them, and re-layouts  2.94 us (6%)
    ppermute x12, starting transfers between devices, shift(): lax.ppermute(value, axis, [(i, (i + step) % count) for i in range(count)])  20.4 us
    ppermute x12, waiting for transfers between devices, shift(): lax.ppermute(value, axis, [(i, (i + step) % count) for i in range(count)])  15 us
    mul x1, other arithmetic, shards(): scaled = [scales[d] * source for d in range(degree_top)]  2.02 us
    dot_general x3, matrix products, shards(): jnp.einsum('jrs,jts->jrt', gathered, near_blocks, preferred_element_type=...  1.93 us
    dot_general x3, matrix products, shards(): jnp.einsum('jrl,jkl->jrk', far_input, col_basis, preferred_element_type=j...  1.87 us
    convert_element_type x1, other arithmetic, shards(): iterate = (coefficients[degree_top] * source).astype(jnp.bfloat16)  1.49 us
    slice x1, local copies, waits for them, and re-layouts, shards(): iterate = (coefficients[degree_top] * source).astype(jnp.bfloat16)  1.38 us
    dot_general x3, matrix products, shards(): jnp.einsum('jc,jm->cm', far_hot, coef, precision=lax.Precision.HIGHEST)  1.2 us
  transfers between devices with their start and end apart: 12, of which 7 were waited for; matrix products, arithmetic and copies ran while one was open for 12% of the time, Pallas kernels for 0%

profile of v12, /device:TPU:0, one launch (start us, length us, event | category | flops | bytes accessed | tf_op | source)
XLA Modules:
  0.0 51.8 jit_solution(8326426057777424021)
XLA Ops:
  0.1 1.4 %slice.153 = f32[1]{0:T(128)} slice(f32[4]{0:T(128)} %param.10), slice={[3:4]} | slice | bytes 8 | tf_op jit(solution)/shard_map/slice | solution.py:73
  1.5 0.7 %broadcast_subtract_fusion = s32[64]{0:T(128)S(1)} fusion(s32[64]{0:T(128)} %param.16, s32[]{:T(128)S(6)} %mul.50), kind=kLoop, calls=%fused_computation.151 | loop fusion | flops 64 | bytes 516 | tf_op jit(solution)/shard_map/sub | solution.py:66
  2.1 1.5 %multiply_convert_fusion = bf16[8,2048]{1,0:T(8,128)(2,1)S(1)} fusion(f32[8,2048]{1,0:T(8,128)} %param.9, f32[]{:T(128)} %bitcast.1), kind=kLoop, calls=%fused_computation.35 | loop fusion | flops 32768 | bytes 98308 | tf_op jit(solution)/shard_map/convert_element_type | solution.py:73
  3.9 1.3 %fusion.4 = f32[64,8,16]{2,1,0:T(8,128)S(1)} fusion(bf16[64,16,256]{2,1,0:T(8,128)(2,1)} %param.15, bf16[64,8,256]{2,0,1:T(8,128)(2,1)S(1)} %fusion.28), kind=kOutput, calls=%fused_computation.4 | convolution fusion | flops 4194304 | bytes 819200 | tf_op jit(solution)/shard_map/far_partial/jrl,jkl->jrk/dot_general | solution.py:85
  5.3 0.8 %fusion.40 = f32[4,8,128]{2,1,0:T(8,128)S(1)} fusion(f32[64,128,1]{0,1,2:T(8,128)S(1)} %bitcast.203, s32[4,8]{1,0:T(4,128)S(1)} %multiply_add_fusion, s32[64]{0:T(128)} %param.17), kind=kOutput, calls=%fused_computation.57 | convolution fusion | flops 3147776 | bytes 49536 | tf_op jit(solution)/shard_map/far_partial/jc,jm->cm/dot_general | solution.py:89
  6.3 4.1 %collective-permute-start.2 = (bf16[8,384]{1,0:T(8,128)(2,1)S(1)}, bf16[8,384]{1,0:T(8,128)(2,1)S(1)}, u32[]{:S(2)}, u32[]{:S(2)}) collective-permute-start(bf16[8,384]{1,0:T(8,128)(2,1)S(1)} %pad_maximum_fusion.12), channel_id=1, source_target_pairs={{0,8},{4,12},{8,0},{12,4},{1,9},{5,13},{9,1},{13,5},{2,10},{6,14},... | collective-permute-start | bytes 18440 | tf_op jit(solution)/shard_map/clus_exchange/ppermute | solution.py:8
  10.4 1.6 %collective-permute-start.1 = (bf16[8,2432]{1,0:T(8,128)(2,1)S(1)}, bf16[8,2432]{1,0:T(8,128)(2,1)S(1)}, u32[]{:S(2)}, u32[]{:S(2)}) collective-permute-start(bf16[8,2432]{1,0:T(8,128)(2,1)S(1)} %get-tuple-element.12), channel_id=1, source_target_pairs={{0,4},{4,8},{8,12},{12,0},{1,5},{5,9},{9,13},{13,1},{2,6},{6,10},{... | collective-permute-start | bytes 116744 | tf_op jit(solution)/shard_map/clus_exchange/ppermute | solution.py:8
  12.0 2.2 %collective-permute-start = (bf16[8,2432]{1,0:T(8,128)(2,1)S(1)}, bf16[8,2432]{1,0:T(8,128)(2,1)S(1)}, u32[]{:S(2)}, u32[]{:S(2)}) collective-permute-start(bf16[8,2432]{1,0:T(8,128)(2,1)S(1)} %get-tuple-element.24), channel_id=1, source_target_pairs={{0,12},{4,0},{8,4},{12,8},{1,13},{5,1},{9,5},{13,9},{2,14},{6,2},{... | collective-permute-start | bytes 116744 | tf_op jit(solution)/shard_map/clus_exchange/ppermute | solution.py:8
  14.3 0.7 %fusion.86 = (f32[1]{0:T(128)}, f32[1]{0:T(128)}, f32[1]{0:T(128)}) fusion(f32[4]{0:T(128)S(1)} %copy-done.5), kind=kLoop, calls=%fused_computation.157 | loop fusion | bytes 24 | tf_op jit(solution)/shard_map/clus_exchange/slice | solution.py:103
  15.0 2.0 %broadcast_multiply_fusion = (f32[8,2048]{1,0:T(8,128)S(1)}, f32[8,2048]{1,0:T(8,128)S(1)}, f32[8,2048]{1,0:T(8,128)S(1)}) fusion(f32[8,2048]{1,0:T(8,128)S(1)} %copy-done.3, f32[]{:T(128)} %bitcast.18, f32[]{:T(128)} %bitcast.12, f32[]{:T(128)} %bitcast.15), kind=kLoop, calls=%fused_computation.46 | loop fusion | flops 49152 | bytes 262156 | tf_op jit(solution)/shard_map/clus_exchange/mul | solution.py:103
  17.3 0.6 %fusion.19 = f32[16,8,256]{2,1,0:T(8,128)S(1)} fusion(bf16[16,256,256]{2,1,0:T(8,128)(2,1)S(1)} %copy-done, bf16[16,8,256]{2,0,1:T(8,128)(2,1)S(1)} %fusion.12), kind=kOutput, calls=%fused_computation.25 | convolution fusion | flops 16777216 | bytes 2293760 | tf_op jit(solution)/shard_map/near_partial/jrs,jts->jrt/dot_general | solution.py:122
  18.0 0.3 fusion.53
  18.4 1.6 %collective-permute-start.3 = (f32[8,2176]{1,0:T(8,128)S(1)}, f32[8,2176]{1,0:T(8,128)S(1)}, u32[]{:S(2)}, u32[]{:S(2)}) collective-permute-start(f32[8,2176]{1,0:T(8,128)S(1)} %pad_maximum_fusion.3), channel_id=1, source_target_pairs={{0,2},{2,0},{1,3},{3,1},{4,6},{6,4},{5,7},{7,5},{8,10},{10,8},{9,1... | collective-permute-start | bytes 208904 | tf_op jit(solution)/shard_map/pair_sums/ppermute | solution.py:8
  19.9 2.8 %collective-permute-done.3 = f32[8,2176]{1,0:T(8,128)S(1)} collective-permute-done((f32[8,2176]{1,0:T(8,128)S(1)}, f32[8,2176]{1,0:T(8,128)S(1)}, u32[]{:S(2)}, u32[]{:S(2)}) %collective-permute-start.3) | collective-permute-done | bytes 69664 | tf_op jit(solution)/shard_map/pair_sums/ppermute | solution.py:8
  23.3 0.3 fusion.2
  24.1 3.8 %collective-permute-start.4 = (bf16[8,2432]{1,0:T(8,128)(2,1)S(1)}, bf16[8,2432]{1,0:T(8,128)(2,1)S(1)}, u32[]{:S(2)}, u32[]{:S(2)}) collective-permute-start(bf16[8,2432]{1,0:T(8,128)(2,1)S(1)} %get-tuple-element.23), channel_id=1, source_target_pairs={{0,12},{4,0},{8,4},{12,8},{1,13},{5,1},{9,5},{13,9},{2,14},{6,2},{... | collective-permute-start | bytes 116744 | tf_op jit(solution)/shard_map/clus_exchange/ppermute | solution.py:8
  27.9 2.1 %collective-permute-done.5 = bf16[8,2432]{1,0:T(8,128)(2,1)S(1)} collective-permute-done((bf16[8,2432]{1,0:T(8,128)(2,1)S(1)}, bf16[8,2432]{1,0:T(8,128)(2,1)S(1)}, u32[]{:S(2)}, u32[]{:S(2)}) %collective-permute-start.5) | collective-permute-done | bytes 38944 | tf_op jit(solution)/shard_map/clus_exchange/ppermute | solution.py:8
  30.2 0.6 %fusion.17 = f32[16,8,256]{2,1,0:T(8,128)S(1)} fusion(bf16[16,256,256]{2,1,0:T(8,128)(2,1)S(1)} %copy-done, bf16[16,8,256]{2,0,1:T(8,128)(2,1)S(1)} %fusion.9), kind=kOutput, calls=%fused_computation.23 | convolution fusion | flops 16777216 | bytes 2293760 | tf_op jit(solution)/shard_map/near_partial/jrs,jts->jrt/dot_general | solution.py:122
  30.9 0.3 fusion.52
  31.2 1.2 %collective-permute-done.6 = bf16[8,384]{1,0:T(8,128)(2,1)S(1)} collective-permute-done((bf16[8,384]{1,0:T(8,128)(2,1)S(1)}, bf16[8,384]{1,0:T(8,128)(2,1)S(1)}, u32[]{:S(2)}, u32[]{:S(2)}) %collective-permute-start.6) | collective-permute-done | bytes 6176 | tf_op jit(solution)/shard_map/clus_exchange/ppermute | solution.py:8
  32.5 1.6 %collective-permute-start.7 = (f32[8,2176]{1,0:T(8,128)S(1)}, f32[8,2176]{1,0:T(8,128)S(1)}, u32[]{:S(2)}, u32[]{:S(2)}) collective-permute-start(f32[8,2176]{1,0:T(8,128)S(1)} %pad_maximum_fusion.4), channel_id=1, source_target_pairs={{0,2},{2,0},{1,3},{3,1},{4,6},{6,4},{5,7},{7,5},{8,10},{10,8},{9,1... | collective-permute-start | bytes 208904 | tf_op jit(solution)/shard_map/pair_sums/ppermute | solution.py:8
  34.0 2.8 %collective-permute-done.7 = f32[8,2176]{1,0:T(8,128)S(1)} collective-permute-done((f32[8,2176]{1,0:T(8,128)S(1)}, f32[8,2176]{1,0:T(8,128)S(1)}, u32[]{:S(2)}, u32[]{:S(2)}) %collective-permute-start.7) | collective-permute-done | bytes 69664 | tf_op jit(solution)/shard_map/pair_sums/ppermute | solution.py:8
  37.1 0.3 fusion.31
  37.4 0.3 fusion
  38.2 3.8 %collective-permute-start.8 = (bf16[8,2432]{1,0:T(8,128)(2,1)S(1)}, bf16[8,2432]{1,0:T(8,128)(2,1)S(1)}, u32[]{:S(2)}, u32[]{:S(2)}) collective-permute-start(bf16[8,2432]{1,0:T(8,128)(2,1)S(1)} %get-tuple-element.21), channel_id=1, source_target_pairs={{0,12},{4,0},{8,4},{12,8},{1,13},{5,1},{9,5},{13,9},{2,14},{6,2},{... | collective-permute-start | bytes 116744 | tf_op jit(solution)/shard_map/clus_exchange/ppermute | solution.py:8
  42.0 1.9 %collective-permute-done.9 = bf16[8,2432]{1,0:T(8,128)(2,1)S(1)} collective-permute-done((bf16[8,2432]{1,0:T(8,128)(2,1)S(1)}, bf16[8,2432]{1,0:T(8,128)(2,1)S(1)}, u32[]{:S(2)}, u32[]{:S(2)}) %collective-permute-start.9) | collective-permute-done | bytes 38944 | tf_op jit(solution)/shard_map/clus_exchange/ppermute | solution.py:8
  44.2 0.6 %fusion.15 = f32[16,8,256]{2,1,0:T(8,128)S(1)} fusion(bf16[16,256,256]{2,1,0:T(8,128)(2,1)S(1)} %copy-done, bf16[16,8,256]{2,0,1:T(8,128)(2,1)S(1)} %fusion.6), kind=kOutput, calls=%fused_computation.21 | convolution fusion | flops 16777216 | bytes 2293760 | tf_op jit(solution)/shard_map/near_partial/jrs,jts->jrt/dot_general | solution.py:122
  44.9 0.3 fusion.51
  45.2 1.3 %collective-permute-done.10 = bf16[8,384]{1,0:T(8,128)(2,1)S(1)} collective-permute-done((bf16[8,384]{1,0:T(8,128)(2,1)S(1)}, bf16[8,384]{1,0:T(8,128)(2,1)S(1)}, u32[]{:S(2)}, u32[]{:S(2)}) %collective-permute-start.10) | collective-permute-done | bytes 6176 | tf_op jit(solution)/shard_map/clus_exchange/ppermute | solution.py:8
  46.5 1.6 %collective-permute-start.11 = (f32[8,2176]{1,0:T(8,128)S(1)}, f32[8,2176]{1,0:T(8,128)S(1)}, u32[]{:S(2)}, u32[]{:S(2)}) collective-permute-start(f32[8,2176]{1,0:T(8,128)S(1)} %pad_maximum_fusion.5), channel_id=1, source_target_pairs={{0,2},{2,0},{1,3},{3,1},{4,6},{6,4},{5,7},{7,5},{8,10},{10,8},{9,1... | collective-permute-start | bytes 208904 | tf_op jit(solution)/shard_map/pair_sums/ppermute | solution.py:8
  48.1 2.8 %collective-permute-done.11 = f32[8,2176]{1,0:T(8,128)S(1)} collective-permute-done((f32[8,2176]{1,0:T(8,128)S(1)}, f32[8,2176]{1,0:T(8,128)S(1)}, u32[]{:S(2)}, u32[]{:S(2)}) %collective-permute-start.11) | collective-permute-done | bytes 69664 | tf_op jit(solution)/shard_map/pair_sums/ppermute | solution.py:8
  51.0 0.8 %fusion.21 = f32[8,8,256]{2,1,0:T(8,128)} fusion(f32[8,8,256]{2,1,0:T(8,128)S(1)} %bitcast.209, f32[8,8,256]{2,0,1:T(8,128)S(1)} %bitcast.208, f32[8,8,16]{2,1,0:T(8,128)S(1)} %reshape.133, bf16[8,16,256]{2,1,0:T(8,128)(2,1)S(1)} %copy-done.2), kind=kOutput, calls=%fused_computation.28 | convolution fusion | flops 3178496 | bytes 266240 | tf_op jit(solution)/shard_map/far_field/crk,ckl->crl/dot_general | solution.py:139
  (82 shorter events, 3.3 us)
Async XLA Ops:
  0.0 17.3 %copy-start = (bf16[16,256,256]{2,1,0:T(8,128)(2,1)S(1)}, bf16[16,256,256]{2,1,0:T(8,128)(2,1)}, u32[]{:S(2)}) copy-start(bf16[16,256,256]{2,1,0:T(8,128)(2,1)} %param.11) | copy-start | bytes 6291460
  0.0 14.3 %copy-start.5 = (f32[4]{0:T(128)S(1)}, f32[4]{0:T(128)}, u32[]{:S(2)}) copy-start(f32[4]{0:T(128)} %param.10) | copy-start | bytes 52
  0.0 15.0 %copy-start.3 = (f32[8,2048]{1,0:T(8,128)S(1)}, f32[8,2048]{1,0:T(8,128)}, u32[]{:S(2)}) copy-start(f32[8,2048]{1,0:T(8,128)} %param.9) | copy-start | bytes 196612
  0.0 14.3 %copy-start.6 = (s32[16]{0:T(128)S(1)}, s32[16]{0:T(128)}, u32[]{:S(2)}) copy-start(s32[16]{0:T(128)} %param.13) | copy-start | bytes 196
  0.0 17.0 %copy-start.7 = (s32[16]{0:T(128)S(1)}, s32[16]{0:T(128)}, u32[]{:S(2)}) copy-start(s32[16]{0:T(128)} %param.12) | copy-start | bytes 196
  6.3 12.1 %collective-permute-start.2 = (bf16[8,384]{1,0:T(8,128)(2,1)S(1)}, bf16[8,384]{1,0:T(8,128)(2,1)S(1)}, u32[]{:S(2)}, u32[]{:S(2)}) collective-permute-start(bf16[8,384]{1,0:T(8,128)(2,1)S(1)} %pad_maximum_fusion.12), channel_id=1, source_target_pairs={{0,8},{4,12},{8,0},{12,4},{1,9},{5,13},{9,1},{13,5},{2,10},{6,14},... | collective-permute-start | bytes 18440 | tf_op jit(solution)/shard_map/clus_exchange/ppermute | solution.py:8
  10.4 12.5 %copy-start.2 = (bf16[8,16,256]{2,1,0:T(8,128)(2,1)S(1)}, bf16[8,16,256]{2,1,0:T(8,128)(2,1)}, u32[]{:S(2)}) copy-start(bf16[8,16,256]{2,1,0:T(8,128)(2,1)} %param.14) | copy-start | bytes 196612
  10.4 6.6 %collective-permute-start.1 = (bf16[8,2432]{1,0:T(8,128)(2,1)S(1)}, bf16[8,2432]{1,0:T(8,128)(2,1)S(1)}, u32[]{:S(2)}, u32[]{:S(2)}) collective-permute-start(bf16[8,2432]{1,0:T(8,128)(2,1)S(1)} %get-tuple-element.12), channel_id=1, source_target_pairs={{0,4},{4,8},{8,12},{12,0},{1,5},{5,9},{9,13},{13,1},{2,6},{6,10},{... | collective-permute-start | bytes 116744 | tf_op jit(solution)/shard_map/clus_exchange/ppermute | solution.py:8
  12.0 5.0 %collective-permute-start = (bf16[8,2432]{1,0:T(8,128)(2,1)S(1)}, bf16[8,2432]{1,0:T(8,128)(2,1)S(1)}, u32[]{:S(2)}, u32[]{:S(2)}) collective-permute-start(bf16[8,2432]{1,0:T(8,128)(2,1)S(1)} %get-tuple-element.24), channel_id=1, source_target_pairs={{0,12},{4,0},{8,4},{12,8},{1,13},{5,1},{9,5},{13,9},{2,14},{6,2},{... | collective-permute-start | bytes 116744 | tf_op jit(solution)/shard_map/clus_exchange/ppermute | solution.py:8
  17.1 6.2 %copy-start.1 = (bf16[64,16,256]{2,1,0:T(8,128)(2,1)S(1)}, bf16[64,16,256]{2,1,0:T(8,128)(2,1)}, u32[]{:S(2)}) copy-start(bf16[64,16,256]{2,1,0:T(8,128)(2,1)} %param.15) | copy-start | bytes 1572868
  17.3 6.4 %copy-start.4 = (s32[64]{0:T(128)S(1)}, s32[64]{0:T(128)}, u32[]{:S(2)}) copy-start(s32[64]{0:T(128)} %param.17) | copy-start | bytes 772
  18.4 4.4 %collective-permute-start.3 = (f32[8,2176]{1,0:T(8,128)S(1)}, f32[8,2176]{1,0:T(8,128)S(1)}, u32[]{:S(2)}, u32[]{:S(2)}) collective-permute-start(f32[8,2176]{1,0:T(8,128)S(1)} %pad_maximum_fusion.3), channel_id=1, source_target_pairs={{0,2},{2,0},{1,3},{3,1},{4,6},{6,4},{5,7},{7,5},{8,10},{10,8},{9,1... | collective-permute-start | bytes 208904 | tf_op jit(solution)/shard_map/pair_sums/ppermute | solution.py:8
  24.0 5.9 %collective-permute-start.5 = (bf16[8,2432]{1,0:T(8,128)(2,1)S(1)}, bf16[8,2432]{1,0:T(8,128)(2,1)S(1)}, u32[]{:S(2)}, u32[]{:S(2)}) collective-permute-start(bf16[8,2432]{1,0:T(8,128)(2,1)S(1)} %get-tuple-element.22), channel_id=1, source_target_pairs={{0,4},{4,8},{8,12},{12,0},{1,5},{5,9},{9,13},{13,1},{2,6},{6,10},{... | collective-permute-start | bytes 116744 | tf_op jit(solution)/shard_map/clus_exchange/ppermute | solution.py:8
  24.1 5.9 %collective-permute-start.4 = (bf16[8,2432]{1,0:T(8,128)(2,1)S(1)}, bf16[8,2432]{1,0:T(8,128)(2,1)S(1)}, u32[]{:S(2)}, u32[]{:S(2)}) collective-permute-start(bf16[8,2432]{1,0:T(8,128)(2,1)S(1)} %get-tuple-element.23), channel_id=1, source_target_pairs={{0,12},{4,0},{8,4},{12,8},{1,13},{5,1},{9,5},{13,9},{2,14},{6,2},{... | collective-permute-start | bytes 116744 | tf_op jit(solution)/shard_map/clus_exchange/ppermute | solution.py:8
  27.9 4.5 %collective-permute-start.6 = (bf16[8,384]{1,0:T(8,128)(2,1)S(1)}, bf16[8,384]{1,0:T(8,128)(2,1)S(1)}, u32[]{:S(2)}, u32[]{:S(2)}) collective-permute-start(bf16[8,384]{1,0:T(8,128)(2,1)S(1)} %pad_maximum_fusion.13), channel_id=1, source_target_pairs={{0,8},{4,12},{8,0},{12,4},{1,9},{5,13},{9,1},{13,5},{2,10},{6,14},... | collective-permute-start | bytes 18440 | tf_op jit(solution)/shard_map/clus_exchange/ppermute | solution.py:8
  32.5 4.4 %collective-permute-start.7 = (f32[8,2176]{1,0:T(8,128)S(1)}, f32[8,2176]{1,0:T(8,128)S(1)}, u32[]{:S(2)}, u32[]{:S(2)}) collective-permute-start(f32[8,2176]{1,0:T(8,128)S(1)} %pad_maximum_fusion.4), channel_id=1, source_target_pairs={{0,2},{2,0},{1,3},{3,1},{4,6},{6,4},{5,7},{7,5},{8,10},{10,8},{9,1... | collective-permute-start | bytes 208904 | tf_op jit(solution)/shard_map/pair_sums/ppermute | solution.py:8
  38.1 5.8 %collective-permute-start.9 = (bf16[8,2432]{1,0:T(8,128)(2,1)S(1)}, bf16[8,2432]{1,0:T(8,128)(2,1)S(1)}, u32[]{:S(2)}, u32[]{:S(2)}) collective-permute-start(bf16[8,2432]{1,0:T(8,128)(2,1)S(1)} %get-tuple-element.20), channel_id=1, source_target_pairs={{0,4},{4,8},{8,12},{12,0},{1,5},{5,9},{9,13},{13,1},{2,6},{6,10},{... | collective-permute-start | bytes 116744 | tf_op jit(solution)/shard_map/clus_exchange/ppermute | solution.py:8
  38.2 5.8 %collective-permute-start.8 = (bf16[8,2432]{1,0:T(8,128)(2,1)S(1)}, bf16[8,2432]{1,0:T(8,128)(2,1)S(1)}, u32[]{:S(2)}, u32[]{:S(2)}) collective-permute-start(bf16[8,2432]{1,0:T(8,128)(2,1)S(1)} %get-tuple-element.21), channel_id=1, source_target_pairs={{0,12},{4,0},{8,4},{12,8},{1,13},{5,1},{9,5},{13,9},{2,14},{6,2},{... | collective-permute-start | bytes 116744 | tf_op jit(solution)/shard_map/clus_exchange/ppermute | solution.py:8
  42.0 4.5 %collective-permute-start.10 = (bf16[8,384]{1,0:T(8,128)(2,1)S(1)}, bf16[8,384]{1,0:T(8,128)(2,1)S(1)}, u32[]{:S(2)}, u32[]{:S(2)}) collective-permute-start(bf16[8,384]{1,0:T(8,128)(2,1)S(1)} %pad_maximum_fusion.14), channel_id=1, source_target_pairs={{0,8},{4,12},{8,0},{12,4},{1,9},{5,13},{9,1},{13,5},{2,10},{6,14},... | collective-permute-start | bytes 18440 | tf_op jit(solution)/shard_map/clus_exchange/ppermute | solution.py:8
  46.5 4.4 %collective-permute-start.11 = (f32[8,2176]{1,0:T(8,128)S(1)}, f32[8,2176]{1,0:T(8,128)S(1)}, u32[]{:S(2)}, u32[]{:S(2)}) collective-permute-start(f32[8,2176]{1,0:T(8,128)S(1)} %pad_maximum_fusion.5), channel_id=1, source_target_pairs={{0,2},{2,0},{1,3},{3,1},{4,6},{6,4},{5,7},{7,5},{8,10},{10,8},{9,1... | collective-permute-start | bytes 208904 | tf_op jit(solution)/shard_map/pair_sums/ppermute | solution.py:8

commit v13 on v12

--- a/solution.py
+++ b/solution.py
@@ -101,6 +101,7 @@
                 if s == 1 and scaled is None:
                     scales, outgoing = lax.optimization_barrier((coefficients, outgoing))
                     scaled = [scales[d] * source for d in range(degree_top)]
+                    scaled[0] = scales[0] * rhs_field
                 incoming = shift(outgoing, "clus", peer_count, s)
                 if carries_iterate:
                     neighbour = incoming[:, :iterate_size]
@@ -122,26 +123,47 @@
             contrib = jnp.einsum(
                 "jrs,jts->jrt", gathered, near_blocks, preferred_element_type=jnp.float32
             )
-            contrib = contrib.reshape(contrib.shape[0], iterate_size)
-            near_part = jnp.einsum(
-                "jc,jm->cm", target_hot, contrib, precision=lax.Precision.HIGHEST
-            )
+            last = degree == 0
+            if last:
+                near_part = jnp.einsum(
+                    "jc,jrt->rct", target_hot, contrib, precision=lax.Precision.HIGHEST
+                ).reshape(rhs_here, clusters_here * leaf_size)
+                far_mine = far_mine.reshape(clusters_here, rhs_here, rank_size)
+                far_mine = far_mine.transpose(1, 0, 2).reshape(rhs_here, clusters_here * rank_size)
+            else:
+                contrib = contrib.reshape(contrib.shape[0], iterate_size)
+                near_part = jnp.einsum(
+                    "jc,jm->cm", target_hot, contrib, precision=lax.Precision.HIGHEST
+                )
         with jax.named_scope("pair_sums"):
             if scaled is None:
                 scaled = [coefficients[d] * source for d in range(degree_top)]
+                scaled[0] = coefficients[0] * rhs_field
             if step == 0:
                 scaled, near_part = lax.optimization_barrier((scaled, near_part))
             packed = jnp.concatenate([near_part, far_mine], axis=1)
             packed = pair_total(packed, pair_count, pair_index)
-            near_sum = packed[:, :iterate_size].reshape(clusters_here, rhs_here, leaf_size)
-            coef_sum = packed[:, iterate_size:].reshape(clusters_here, rhs_here, rank_size)
+            if last:
+                near_width = clusters_here * leaf_size
+                near_sum = packed[:, :near_width]
+                coef_sum = packed[:, near_width:].reshape(rhs_here, clusters_here, rank_size)
+            else:
+                near_sum = packed[:, :iterate_size].reshape(clusters_here, rhs_here, leaf_size)
+                coef_sum = packed[:, iterate_size:].reshape(clusters_here, rhs_here, rank_size)
         with jax.named_scope("far_field"):
-            far_field = jnp.einsum(
-                "crk,ckl->crl", coef_sum, row_f32, precision=lax.Precision.HIGHEST
-            )
+            if last:
+                far_field = jnp.einsum(
+                    "rck,ckl->rcl", coef_sum, row_f32, precision=lax.Precision.HIGHEST
+                ).reshape(rhs_here, clusters_here * leaf_size)
+            else:
+                far_field = jnp.einsum(
+                    "crk,ckl->crl", coef_sum, row_f32, precision=lax.Precision.HIGHEST
+                )
         result = near_sum + far_field + scaled[degree]
         iterate = result.astype(jnp.bfloat16)
-    return result.transpose(1, 0, 2).reshape(rhs_here, clusters_here * leaf_size)
+    if degree_top == 0:
+        return rhs_field
+    return result
 
 
 def solution(mesh):

time: 52.1 us -> 53.1 us (1.019)
  waiting for transfers between devices: 15 us -> 17 us
  matrix products: 8.39 us -> 7.43 us
  starting transfers between devices: 20.4 us -> 19.6 us
  other arithmetic: 4.56 us -> 5.2 us
    ppermute x12, waiting for transfers between devices: 15 us -> 17 us  [shift(): lax.ppermute(value, axis, [(i, (i + step) % count) for i in range(count)])]
    ppermute x12, starting transfers between devices: 20.4 us -> 19.6 us  [shift(): lax.ppermute(value, axis, [(i, (i + step) % count) for i in range(count)])]
    dot_general x3 -> x2, matrix products: 1.12 us -> 0.33 us  [shards(): jnp.einsum('crk,ckl->crl', coef_sum, row_f32, precision=lax.Precision.HIG...]
    add x0 -> x1, other arithmetic: none -> 0.64 us  [shards(): result = near_sum + far_field + scaled[degree]]
  transfers between devices with their start and end apart: 12 -> 12, of which waited for: 7 -> 7; matrix products, arithmetic and copies ran while one was open for 12% -> 10% of each run, Pallas kernels for 0% -> 0%
where the time goes in v13:
time: 53.1 us; the launch traced here: 52.8 us
  starting transfers between devices  19.6 us (37%)
  waiting for transfers between devices  17 us (32%)
  matrix products  7.43 us (14%)
  other arithmetic  5.2 us (10%)
  local copies, waits for them, and re-layouts  3.07 us (6%)
    ppermute x12, starting transfers between devices, shift(): lax.ppermute(value, axis, [(i, (i + step) % count) for i in range(count)])  19.6 us
    ppermute x12, waiting for transfers between devices, shift(): lax.ppermute(value, axis, [(i, (i + step) % count) for i in range(count)])  17 us
    mul x1, other arithmetic, shards(): scaled = [scales[d] * source for d in range(degree_top)]  2.02 us
    dot_general x3, matrix products, shards(): jnp.einsum('jrs,jts->jrt', gathered, near_blocks, preferred_element_type=...  1.92 us
    dot_general x3, matrix products, shards(): jnp.einsum('jrl,jkl->jrk', far_input, col_basis, preferred_element_type=j...  1.87 us
    convert_element_type x1, other arithmetic, shards(): iterate = (coefficients[degree_top] * source).astype(jnp.bfloat16)  1.49 us
    slice x1, local copies, waits for them, and re-layouts, shards(): iterate = (coefficients[degree_top] * source).astype(jnp.bfloat16)  1.38 us
    dot_general x3, matrix products, shards(): jnp.einsum('jc,jm->cm', far_hot, coef, precision=lax.Precision.HIGHEST)  1.2 us
  transfers between devices with their start and end apart: 12, of which 7 were waited for; matrix products, arithmetic and copies ran while one was open for 10% of the time, Pallas kernels for 0%

profile of v13, /device:TPU:0, one launch (start us, length us, event | category | flops | bytes accessed | tf_op | source)
XLA Modules:
  0.0 52.8 jit_solution(979034133910501708)
XLA Ops:
  0.1 1.4 %slice.153 = f32[1]{0:T(128)} slice(f32[4]{0:T(128)} %param.10), slice={[3:4]} | slice | bytes 8 | tf_op jit(solution)/shard_map/slice | solution.py:73
  1.5 0.7 %broadcast_subtract_fusion = s32[64]{0:T(128)S(1)} fusion(s32[64]{0:T(128)} %param.16, s32[]{:T(128)S(6)} %mul.45), kind=kLoop, calls=%fused_computation.157 | loop fusion | flops 64 | bytes 516 | tf_op jit(solution)/shard_map/sub | solution.py:66
  2.1 1.5 %multiply_convert_fusion = bf16[8,2048]{1,0:T(8,128)(2,1)S(1)} fusion(f32[8,2048]{1,0:T(8,128)} %param.9, f32[]{:T(128)} %bitcast.1), kind=kLoop, calls=%fused_computation.36 | loop fusion | flops 32768 | bytes 98308 | tf_op jit(solution)/shard_map/convert_element_type | solution.py:73
  3.6 0.3 fusion.29
  3.9 1.3 %fusion.4 = f32[64,8,16]{2,1,0:T(8,128)S(1)} fusion(bf16[64,16,256]{2,1,0:T(8,128)(2,1)} %param.15, bf16[64,8,256]{2,0,1:T(8,128)(2,1)S(1)} %fusion.29), kind=kOutput, calls=%fused_computation.5 | convolution fusion | flops 4194304 | bytes 819200 | tf_op jit(solution)/shard_map/far_partial/jrl,jkl->jrk/dot_general | solution.py:85
  5.3 0.8 %fusion.43 = f32[4,8,128]{2,1,0:T(8,128)S(1)} fusion(f32[64,128,1]{0,1,2:T(8,128)S(1)} %bitcast.203, s32[4,8]{1,0:T(4,128)S(1)} %multiply_add_fusion, s32[64]{0:T(128)} %param.17), kind=kOutput, calls=%fused_computation.61 | convolution fusion | flops 3147776 | bytes 49536 | tf_op jit(solution)/shard_map/far_partial/jc,jm->cm/dot_general | solution.py:89
  6.3 4.1 %collective-permute-start.2 = (bf16[8,384]{1,0:T(8,128)(2,1)S(1)}, bf16[8,384]{1,0:T(8,128)(2,1)S(1)}, u32[]{:S(2)}, u32[]{:S(2)}) collective-permute-start(bf16[8,384]{1,0:T(8,128)(2,1)S(1)} %pad_maximum_fusion.11), channel_id=1, source_target_pairs={{0,8},{4,12},{8,0},{12,4},{1,9},{5,13},{9,1},{13,5},{2,10},{6,14},... | collective-permute-start | bytes 18440 | tf_op jit(solution)/shard_map/clus_exchange/ppermute | solution.py:8
  10.4 1.6 %collective-permute-start.1 = (bf16[8,2432]{1,0:T(8,128)(2,1)S(1)}, bf16[8,2432]{1,0:T(8,128)(2,1)S(1)}, u32[]{:S(2)}, u32[]{:S(2)}) collective-permute-start(bf16[8,2432]{1,0:T(8,128)(2,1)S(1)} %get-tuple-element.12), channel_id=1, source_target_pairs={{0,4},{4,8},{8,12},{12,0},{1,5},{5,9},{9,13},{13,1},{2,6},{6,10},{... | collective-permute-start | bytes 116744 | tf_op jit(solution)/shard_map/clus_exchange/ppermute | solution.py:8
  12.0 2.2 %collective-permute-start = (bf16[8,2432]{1,0:T(8,128)(2,1)S(1)}, bf16[8,2432]{1,0:T(8,128)(2,1)S(1)}, u32[]{:S(2)}, u32[]{:S(2)}) collective-permute-start(bf16[8,2432]{1,0:T(8,128)(2,1)S(1)} %get-tuple-element.24), channel_id=1, source_target_pairs={{0,12},{4,0},{8,4},{12,8},{1,13},{5,1},{9,5},{13,9},{2,14},{6,2},{... | collective-permute-start | bytes 116744 | tf_op jit(solution)/shard_map/clus_exchange/ppermute | solution.py:8
  14.3 0.7 %fusion.89 = (f32[1]{0:T(128)}, f32[1]{0:T(128)}, f32[1]{0:T(128)}) fusion(f32[4]{0:T(128)S(1)} %copy-done.5), kind=kLoop, calls=%fused_computation.162 | loop fusion | bytes 24 | tf_op jit(solution)/shard_map/clus_exchange/slice | solution.py:103
  15.0 2.0 %broadcast_multiply_fusion = (f32[8,2048]{1,0:T(8,128)S(1)}, f32[8,2048]{1,0:T(8,128)S(1)}, f32[8,2048]{1,0:T(8,128)S(1)}) fusion(f32[8,2048]{1,0:T(8,128)S(1)} %copy-done.3, f32[]{:T(128)} %bitcast.16, f32[]{:T(128)} %bitcast.12, f32[]{:T(128)} %bitcast.13), kind=kLoop, calls=%fused_computation.50 | loop fusion | flops 49152 | bytes 262156 | tf_op jit(solution)/shard_map/clus_exchange/mul | solution.py:103
  17.3 0.6 %fusion.21 = f32[16,8,256]{2,1,0:T(8,128)S(1)} fusion(bf16[16,256,256]{2,1,0:T(8,128)(2,1)S(1)} %copy-done, bf16[16,8,256]{2,0,1:T(8,128)(2,1)S(1)} %fusion.13), kind=kOutput, calls=%fused_computation.28 | convolution fusion | flops 16777216 | bytes 2293760 | tf_op jit(solution)/shard_map/near_partial/jrs,jts->jrt/dot_general | solution.py:123
  18.2 1.6 %collective-permute-start.3 = (f32[8,2176]{1,0:T(8,128)S(1)}, f32[8,2176]{1,0:T(8,128)S(1)}, u32[]{:S(2)}, u32[]{:S(2)}) collective-permute-start(f32[8,2176]{1,0:T(8,128)S(1)} %pad_maximum_fusion.3), channel_id=1, source_target_pairs={{0,2},{2,0},{1,3},{3,1},{4,6},{6,4},{5,7},{7,5},{8,10},{10,8},{9,1... | collective-permute-start | bytes 208904 | tf_op jit(solution)/shard_map/pair_sums/ppermute | solution.py:8
  19.8 2.8 %collective-permute-done.3 = f32[8,2176]{1,0:T(8,128)S(1)} collective-permute-done((f32[8,2176]{1,0:T(8,128)S(1)}, f32[8,2176]{1,0:T(8,128)S(1)}, u32[]{:S(2)}, u32[]{:S(2)}) %collective-permute-start.3) | collective-permute-done | bytes 69664 | tf_op jit(solution)/shard_map/pair_sums/ppermute | solution.py:8
  22.9 0.3 fusion.36
  23.2 0.3 fusion.2
  24.0 3.8 %collective-permute-start.4 = (bf16[8,2432]{1,0:T(8,128)(2,1)S(1)}, bf16[8,2432]{1,0:T(8,128)(2,1)S(1)}, u32[]{:S(2)}, u32[]{:S(2)}) collective-permute-start(bf16[8,2432]{1,0:T(8,128)(2,1)S(1)} %get-tuple-element.23), channel_id=1, source_target_pairs={{0,12},{4,0},{8,4},{12,8},{1,13},{5,1},{9,5},{13,9},{2,14},{6,2},{... | collective-permute-start | bytes 116744 | tf_op jit(solution)/shard_map/clus_exchange/ppermute | solution.py:8
  27.8 2.1 %collective-permute-done.5 = bf16[8,2432]{1,0:T(8,128)(2,1)S(1)} collective-permute-done((bf16[8,2432]{1,0:T(8,128)(2,1)S(1)}, bf16[8,2432]{1,0:T(8,128)(2,1)S(1)}, u32[]{:S(2)}, u32[]{:S(2)}) %collective-permute-start.5) | collective-permute-done | bytes 38944 | tf_op jit(solution)/shard_map/clus_exchange/ppermute | solution.py:8
  30.1 0.6 %fusion.19 = f32[16,8,256]{2,1,0:T(8,128)S(1)} fusion(bf16[16,256,256]{2,1,0:T(8,128)(2,1)S(1)} %copy-done, bf16[16,8,256]{2,0,1:T(8,128)(2,1)S(1)} %fusion.10), kind=kOutput, calls=%fused_computation.26 | convolution fusion | flops 16777216 | bytes 2293760 | tf_op jit(solution)/shard_map/near_partial/jrs,jts->jrt/dot_general | solution.py:123
  30.9 1.4 %collective-permute-done.6 = bf16[8,384]{1,0:T(8,128)(2,1)S(1)} collective-permute-done((bf16[8,384]{1,0:T(8,128)(2,1)S(1)}, bf16[8,384]{1,0:T(8,128)(2,1)S(1)}, u32[]{:S(2)}, u32[]{:S(2)}) %collective-permute-start.6) | collective-permute-done | bytes 6176 | tf_op jit(solution)/shard_map/clus_exchange/ppermute | solution.py:8
  32.3 1.6 %collective-permute-start.7 = (f32[8,2176]{1,0:T(8,128)S(1)}, f32[8,2176]{1,0:T(8,128)S(1)}, u32[]{:S(2)}, u32[]{:S(2)}) collective-permute-start(f32[8,2176]{1,0:T(8,128)S(1)} %pad_maximum_fusion.4), channel_id=1, source_target_pairs={{0,2},{2,0},{1,3},{3,1},{4,6},{6,4},{5,7},{7,5},{8,10},{10,8},{9,1... | collective-permute-start | bytes 208904 | tf_op jit(solution)/shard_map/pair_sums/ppermute | solution.py:8
  33.9 2.8 %collective-permute-done.7 = f32[8,2176]{1,0:T(8,128)S(1)} collective-permute-done((f32[8,2176]{1,0:T(8,128)S(1)}, f32[8,2176]{1,0:T(8,128)S(1)}, u32[]{:S(2)}, u32[]{:S(2)}) %collective-permute-start.7) | collective-permute-done | bytes 69664 | tf_op jit(solution)/shard_map/pair_sums/ppermute | solution.py:8
  37.0 0.3 fusion.34
  37.3 0.3 fusion
  38.0 2.4 %collective-permute-start.8 = (bf16[8,2432]{1,0:T(8,128)(2,1)S(1)}, bf16[8,2432]{1,0:T(8,128)(2,1)S(1)}, u32[]{:S(2)}, u32[]{:S(2)}) collective-permute-start(bf16[8,2432]{1,0:T(8,128)(2,1)S(1)} %get-tuple-element.20), channel_id=1, source_target_pairs={{0,12},{4,0},{8,4},{12,8},{1,13},{5,1},{9,5},{13,9},{2,14},{6,2},{... | collective-permute-start | bytes 116744 | tf_op jit(solution)/shard_map/clus_exchange/ppermute | solution.py:8
  40.4 0.6 %collective-permute-start.10 = (bf16[8,384]{1,0:T(8,128)(2,1)S(1)}, bf16[8,384]{1,0:T(8,128)(2,1)S(1)}, u32[]{:S(2)}, u32[]{:S(2)}) collective-permute-start(bf16[8,384]{1,0:T(8,128)(2,1)S(1)} %pad_maximum_fusion.13), channel_id=1, source_target_pairs={{0,8},{4,12},{8,0},{12,4},{1,9},{5,13},{9,1},{13,5},{2,10},{6,14},... | collective-permute-start | bytes 18440 | tf_op jit(solution)/shard_map/clus_exchange/ppermute | solution.py:8
  41.0 1.0 %collective-permute-done.8 = bf16[8,2432]{1,0:T(8,128)(2,1)S(1)} collective-permute-done((bf16[8,2432]{1,0:T(8,128)(2,1)S(1)}, bf16[8,2432]{1,0:T(8,128)(2,1)S(1)}, u32[]{:S(2)}, u32[]{:S(2)}) %collective-permute-start.8) | collective-permute-done | bytes 38944 | tf_op jit(solution)/shard_map/clus_exchange/ppermute | solution.py:8
  42.1 4.1 %collective-permute-done.9 = bf16[8,2432]{1,0:T(8,128)(2,1)S(1)} collective-permute-done((bf16[8,2432]{1,0:T(8,128)(2,1)S(1)}, bf16[8,2432]{1,0:T(8,128)(2,1)S(1)}, u32[]{:S(2)}, u32[]{:S(2)}) %collective-permute-start.9) | collective-permute-done | bytes 38944 | tf_op jit(solution)/shard_map/clus_exchange/ppermute | solution.py:8
  46.6 0.6 %fusion.17 = f32[16,8,256]{2,1,0:T(8,128)S(1)} fusion(bf16[16,256,256]{2,1,0:T(8,128)(2,1)S(1)} %copy-done, bf16[16,8,256]{2,0,1:T(8,128)(2,1)S(1)} %fusion.7), kind=kOutput, calls=%fused_computation.24 | convolution fusion | flops 16777216 | bytes 2293760 | tf_op jit(solution)/shard_map/near_partial/jrs,jts->jrt/dot_general | solution.py:123
  47.5 1.6 %collective-permute-start.11 = (f32[8,2176]{1,0:T(8,128)S(1)}, f32[8,2176]{1,0:T(8,128)S(1)}, u32[]{:S(2)}, u32[]{:S(2)}) collective-permute-start(f32[8,2176]{1,0:T(8,128)S(1)} %constant_dynamic-update-slice_fusion), channel_id=1, source_target_pairs={{0,2},{2,0},{1,3},{3,1},{4,6},{6,4},{5,7},{7,5},{8,10},{10,8},{9,1... | collective-permute-start | bytes 208904 | tf_op jit(solution)/shard_map/pair_sums/ppermute | solution.py:8
  49.1 2.8 %collective-permute-done.11 = f32[8,2176]{1,0:T(8,128)S(1)} collective-permute-done((f32[8,2176]{1,0:T(8,128)S(1)}, f32[8,2176]{1,0:T(8,128)S(1)}, u32[]{:S(2)}, u32[]{:S(2)}) %collective-permute-start.11) | collective-permute-done | bytes 69664 | tf_op jit(solution)/shard_map/pair_sums/ppermute | solution.py:8
  52.1 0.6 %fusion.16 = f32[8,2048]{1,0:T(8,128)} fusion(f32[8,2048]{1,0:T(8,128)S(1)} %get-tuple-element.16, f32[8,2048]{1,0:T(8,128)S(1)} %bitcast.209, f32[8,2176]{1,0:T(8,128)S(1)} %add.223), kind=kLoop, calls=%fused_computation.23 | loop fusion | flops 32768 | bytes 262144 | tf_op jit(solution)/shard_map/add | solution.py:162
  (86 shorter events, 3.5 us)
Async XLA Ops:
  0.0 17.3 %copy-start = (bf16[16,256,256]{2,1,0:T(8,128)(2,1)S(1)}, bf16[16,256,256]{2,1,0:T(8,128)(2,1)}, u32[]{:S(2)}) copy-start(bf16[16,256,256]{2,1,0:T(8,128)(2,1)} %param.11) | copy-start | bytes 6291460
  0.0 14.3 %copy-start.5 = (f32[4]{0:T(128)S(1)}, f32[4]{0:T(128)}, u32[]{:S(2)}) copy-start(f32[4]{0:T(128)} %param.10) | copy-start | bytes 52
  0.0 15.0 %copy-start.3 = (f32[8,2048]{1,0:T(8,128)S(1)}, f32[8,2048]{1,0:T(8,128)}, u32[]{:S(2)}) copy-start(f32[8,2048]{1,0:T(8,128)} %param.9) | copy-start | bytes 196612
  0.0 14.3 %copy-start.6 = (s32[16]{0:T(128)S(1)}, s32[16]{0:T(128)}, u32[]{:S(2)}) copy-start(s32[16]{0:T(128)} %param.13) | copy-start | bytes 196
  0.0 17.0 %copy-start.7 = (s32[16]{0:T(128)S(1)}, s32[16]{0:T(128)}, u32[]{:S(2)}) copy-start(s32[16]{0:T(128)} %param.12) | copy-start | bytes 196
  6.3 11.9 %collective-permute-start.2 = (bf16[8,384]{1,0:T(8,128)(2,1)S(1)}, bf16[8,384]{1,0:T(8,128)(2,1)S(1)}, u32[]{:S(2)}, u32[]{:S(2)}) collective-permute-start(bf16[8,384]{1,0:T(8,128)(2,1)S(1)} %pad_maximum_fusion.11), channel_id=1, source_target_pairs={{0,8},{4,12},{8,0},{12,4},{1,9},{5,13},{9,1},{13,5},{2,10},{6,14},... | collective-permute-start | bytes 18440 | tf_op jit(solution)/shard_map/clus_exchange/ppermute | solution.py:8
  10.4 12.4 %copy-start.2 = (bf16[8,16,256]{2,1,0:T(8,128)(2,1)S(1)}, bf16[8,16,256]{2,1,0:T(8,128)(2,1)}, u32[]{:S(2)}) copy-start(bf16[8,16,256]{2,1,0:T(8,128)(2,1)} %param.14) | copy-start | bytes 196612
  10.4 6.6 %collective-permute-start.1 = (bf16[8,2432]{1,0:T(8,128)(2,1)S(1)}, bf16[8,2432]{1,0:T(8,128)(2,1)S(1)}, u32[]{:S(2)}, u32[]{:S(2)}) collective-permute-start(bf16[8,2432]{1,0:T(8,128)(2,1)S(1)} %get-tuple-element.12), channel_id=1, source_target_pairs={{0,4},{4,8},{8,12},{12,0},{1,5},{5,9},{9,13},{13,1},{2,6},{6,10},{... | collective-permute-start | bytes 116744 | tf_op jit(solution)/shard_map/clus_exchange/ppermute | solution.py:8
  12.0 5.0 %collective-permute-start = (bf16[8,2432]{1,0:T(8,128)(2,1)S(1)}, bf16[8,2432]{1,0:T(8,128)(2,1)S(1)}, u32[]{:S(2)}, u32[]{:S(2)}) collective-permute-start(bf16[8,2432]{1,0:T(8,128)(2,1)S(1)} %get-tuple-element.24), channel_id=1, source_target_pairs={{0,12},{4,0},{8,4},{12,8},{1,13},{5,1},{9,5},{13,9},{2,14},{6,2},{... | collective-permute-start | bytes 116744 | tf_op jit(solution)/shard_map/clus_exchange/ppermute | solution.py:8
  17.1 6.1 %copy-start.1 = (bf16[64,16,256]{2,1,0:T(8,128)(2,1)S(1)}, bf16[64,16,256]{2,1,0:T(8,128)(2,1)}, u32[]{:S(2)}) copy-start(bf16[64,16,256]{2,1,0:T(8,128)(2,1)} %param.15) | copy-start | bytes 1572868
  17.3 6.3 %copy-start.4 = (s32[64]{0:T(128)S(1)}, s32[64]{0:T(128)}, u32[]{:S(2)}) copy-start(s32[64]{0:T(128)} %param.17) | copy-start | bytes 772
  18.2 4.4 %collective-permute-start.3 = (f32[8,2176]{1,0:T(8,128)S(1)}, f32[8,2176]{1,0:T(8,128)S(1)}, u32[]{:S(2)}, u32[]{:S(2)}) collective-permute-start(f32[8,2176]{1,0:T(8,128)S(1)} %pad_maximum_fusion.3), channel_id=1, source_target_pairs={{0,2},{2,0},{1,3},{3,1},{4,6},{6,4},{5,7},{7,5},{8,10},{10,8},{9,1... | collective-permute-start | bytes 208904 | tf_op jit(solution)/shard_map/pair_sums/ppermute | solution.py:8
  23.9 5.9 %collective-permute-start.5 = (bf16[8,2432]{1,0:T(8,128)(2,1)S(1)}, bf16[8,2432]{1,0:T(8,128)(2,1)S(1)}, u32[]{:S(2)}, u32[]{:S(2)}) collective-permute-start(bf16[8,2432]{1,0:T(8,128)(2,1)S(1)} %get-tuple-element.22), channel_id=1, source_target_pairs={{0,4},{4,8},{8,12},{12,0},{1,5},{5,9},{9,13},{13,1},{2,6},{6,10},{... | collective-permute-start | bytes 116744 | tf_op jit(solution)/shard_map/clus_exchange/ppermute | solution.py:8
  24.0 5.9 %collective-permute-start.4 = (bf16[8,2432]{1,0:T(8,128)(2,1)S(1)}, bf16[8,2432]{1,0:T(8,128)(2,1)S(1)}, u32[]{:S(2)}, u32[]{:S(2)}) collective-permute-start(bf16[8,2432]{1,0:T(8,128)(2,1)S(1)} %get-tuple-element.23), channel_id=1, source_target_pairs={{0,12},{4,0},{8,4},{12,8},{1,13},{5,1},{9,5},{13,9},{2,14},{6,2},{... | collective-permute-start | bytes 116744 | tf_op jit(solution)/shard_map/clus_exchange/ppermute | solution.py:8
  27.8 4.5 %collective-permute-start.6 = (bf16[8,384]{1,0:T(8,128)(2,1)S(1)}, bf16[8,384]{1,0:T(8,128)(2,1)S(1)}, u32[]{:S(2)}, u32[]{:S(2)}) collective-permute-start(bf16[8,384]{1,0:T(8,128)(2,1)S(1)} %pad_maximum_fusion.12), channel_id=1, source_target_pairs={{0,8},{4,12},{8,0},{12,4},{1,9},{5,13},{9,1},{13,5},{2,10},{6,14},... | collective-permute-start | bytes 18440 | tf_op jit(solution)/shard_map/clus_exchange/ppermute | solution.py:8
  32.3 4.4 %collective-permute-start.7 = (f32[8,2176]{1,0:T(8,128)S(1)}, f32[8,2176]{1,0:T(8,128)S(1)}, u32[]{:S(2)}, u32[]{:S(2)}) collective-permute-start(f32[8,2176]{1,0:T(8,128)S(1)} %pad_maximum_fusion.4), channel_id=1, source_target_pairs={{0,2},{2,0},{1,3},{3,1},{4,6},{6,4},{5,7},{7,5},{8,10},{10,8},{9,1... | collective-permute-start | bytes 208904 | tf_op jit(solution)/shard_map/pair_sums/ppermute | solution.py:8
  38.0 4.1 %collective-permute-start.8 = (bf16[8,2432]{1,0:T(8,128)(2,1)S(1)}, bf16[8,2432]{1,0:T(8,128)(2,1)S(1)}, u32[]{:S(2)}, u32[]{:S(2)}) collective-permute-start(bf16[8,2432]{1,0:T(8,128)(2,1)S(1)} %get-tuple-element.20), channel_id=1, source_target_pairs={{0,12},{4,0},{8,4},{12,8},{1,13},{5,1},{9,5},{13,9},{2,14},{6,2},{... | collective-permute-start | bytes 116744 | tf_op jit(solution)/shard_map/clus_exchange/ppermute | solution.py:8
  40.4 5.8 %collective-permute-start.9 = (bf16[8,2432]{1,0:T(8,128)(2,1)S(1)}, bf16[8,2432]{1,0:T(8,128)(2,1)S(1)}, u32[]{:S(2)}, u32[]{:S(2)}) collective-permute-start(bf16[8,2432]{1,0:T(8,128)(2,1)S(1)} %get-tuple-element.21), channel_id=1, source_target_pairs={{0,4},{4,8},{8,12},{12,0},{1,5},{5,9},{9,13},{13,1},{2,6},{6,10},{... | collective-permute-start | bytes 116744 | tf_op jit(solution)/shard_map/clus_exchange/ppermute | solution.py:8
  40.4 6.0 %collective-permute-start.10 = (bf16[8,384]{1,0:T(8,128)(2,1)S(1)}, bf16[8,384]{1,0:T(8,128)(2,1)S(1)}, u32[]{:S(2)}, u32[]{:S(2)}) collective-permute-start(bf16[8,384]{1,0:T(8,128)(2,1)S(1)} %pad_maximum_fusion.13), channel_id=1, source_target_pairs={{0,8},{4,12},{8,0},{12,4},{1,9},{5,13},{9,1},{13,5},{2,10},{6,14},... | collective-permute-start | bytes 18440 | tf_op jit(solution)/shard_map/clus_exchange/ppermute | solution.py:8
  47.5 4.4 %collective-permute-start.11 = (f32[8,2176]{1,0:T(8,128)S(1)}, f32[8,2176]{1,0:T(8,128)S(1)}, u32[]{:S(2)}, u32[]{:S(2)}) collective-permute-start(f32[8,2176]{1,0:T(8,128)S(1)} %constant_dynamic-update-slice_fusion), channel_id=1, source_target_pairs={{0,2},{2,0},{1,3},{3,1},{4,6},{6,4},{5,7},{7,5},{8,10},{10,8},{9,1... | collective-permute-start | bytes 208904 | tf_op jit(solution)/shard_map/pair_sums/ppermute | solution.py:8

commit v14 on v12

--- a/solution.py
+++ b/solution.py
@@ -93,24 +93,24 @@
             iterate_flat = iterate.reshape(clusters_here, iterate_size)
             from_minus = iterate
             from_plus = iterate
-            for s in range(1, peer_count):
+            long_shifts = sorted({1, peer_count - 1}) if peer_count > 1 else []
+            short_shifts = list(range(2, peer_count - 1))
+            for s in long_shifts:
                 outgoing = split_three(partial_value[(my_index + s) % peer_count])
-                carries_iterate = s == 1 or s == peer_count - 1
-                if carries_iterate:
-                    outgoing = jnp.concatenate([iterate_flat, outgoing], axis=1)
+                outgoing = jnp.concatenate([iterate_flat, outgoing], axis=1)
                 if s == 1 and scaled is None:
                     scales, outgoing = lax.optimization_barrier((coefficients, outgoing))
                     scaled = [scales[d] * source for d in range(degree_top)]
                 incoming = shift(outgoing, "clus", peer_count, s)
-                if carries_iterate:
-                    neighbour = incoming[:, :iterate_size]
-                    neighbour = neighbour.reshape(clusters_here, rhs_here, leaf_size)
-                    if s == 1:
-                        from_minus = neighbour
-                    if s == peer_count - 1:
-                        from_plus = neighbour
-                    incoming = incoming[:, iterate_size:]
-                far_mine = far_mine + join_three(incoming)
+                neighbour = incoming[:, :iterate_size]
+                neighbour = neighbour.reshape(clusters_here, rhs_here, leaf_size)
+                if s == 1:
+                    from_minus = neighbour
+                if s == peer_count - 1:
+                    from_plus = neighbour
+                far_mine = far_mine + join_three(incoming[:, iterate_size:])
+            if short_shifts:
+                far_pair = pair_total(partial_value, pair_count, pair_index)
         with jax.named_scope("near_partial"):
             extended = jnp.concatenate([iterate, from_plus, from_minus], axis=0)
             gathered = jnp.einsum(
@@ -134,7 +134,12 @@
             packed = jnp.concatenate([near_part, far_mine], axis=1)
             packed = pair_total(packed, pair_count, pair_index)
             near_sum = packed[:, :iterate_size].reshape(clusters_here, rhs_here, leaf_size)
-            coef_sum = packed[:, iterate_size:].reshape(clusters_here, rhs_here, rank_size)
+            coef_flat = packed[:, iterate_size:]
+            for s in short_shifts:
+                coef_flat = coef_flat + shift(
+                    far_pair[(my_index + s) % peer_count], "clus", peer_count, s
+                )
+            coef_sum = coef_flat.reshape(clusters_here, rhs_here, rank_size)
         with jax.named_scope("far_field"):
             far_field = jnp.einsum(
                 "crk,ckl->crl", coef_sum, row_f32, precision=lax.Precision.HIGHEST

time: 52.1 us -> 51.3 us (0.985)
  waiting for transfers between devices: 15 us -> 9.79 us
  starting transfers between devices: 20.4 us -> 25 us
    ppermute x12 -> x15, waiting for transfers between devices: 15 us -> 9.79 us  [shift(): lax.ppermute(value, axis, [(i, (i + step) % count) for i in range(count)])]
    ppermute x12 -> x15, starting transfers between devices: 20.4 us -> 25 us  [shift(): lax.ppermute(value, axis, [(i, (i + step) % count) for i in range(count)])]
  transfers between devices with their start and end apart: 12 -> 15, of which waited for: 7 -> 9; matrix products, arithmetic and copies ran while one was open for 12% -> 13% of each run, Pallas kernels for 0% -> 0%
where the time goes in v14:
time: 51.3 us; the launch traced here: 51 us
  starting transfers between devices  25 us (49%)
  waiting for transfers between devices  9.79 us (19%)
  matrix products  8.38 us (16%)
  other arithmetic  4.46 us (9%)
  local copies, waits for them, and re-layouts  2.95 us (6%)
    ppermute x15, starting transfers between devices, shift(): lax.ppermute(value, axis, [(i, (i + step) % count) for i in range(count)])  25 us
    ppermute x15, waiting for transfers between devices, shift(): lax.ppermute(value, axis, [(i, (i + step) % count) for i in range(count)])  9.79 us
    mul x1, other arithmetic, shards(): scaled = [scales[d] * source for d in range(degree_top)]  1.96 us
    dot_general x3, matrix products, shards(): jnp.einsum('jrs,jts->jrt', gathered, near_blocks, preferred_element_type=...  1.93 us
    dot_general x3, matrix products, shards(): jnp.einsum('jrl,jkl->jrk', far_input, col_basis, preferred_element_type=j...  1.87 us
    convert_element_type x1, other arithmetic, shards(): iterate = (coefficients[degree_top] * source).astype(jnp.bfloat16)  1.49 us
    slice x1, local copies, waits for them, and re-layouts, shards(): iterate = (coefficients[degree_top] * source).astype(jnp.bfloat16)  1.38 us
    dot_general x3, matrix products, shards(): jnp.einsum('jc,jm->cm', far_hot, coef, precision=lax.Precision.HIGHEST)  1.2 us
  transfers between devices with their start and end apart: 15, of which 9 were waited for; matrix products, arithmetic and copies ran while one was open for 13% of the time, Pallas kernels for 0%

profile of v14, /device:TPU:0, one launch (start us, length us, event | category | flops | bytes accessed | tf_op | source)
XLA Modules:
  0.0 51.0 jit_solution(6455804027492519917)
XLA Ops:
  0.0 1.4 %slice.126 = f32[1]{0:T(128)} slice(f32[4]{0:T(128)} %param.10), slice={[3:4]} | slice | bytes 8 | tf_op jit(solution)/shard_map/slice | solution.py:73
  1.4 0.7 %broadcast_subtract_fusion = s32[64]{0:T(128)S(1)} fusion(s32[64]{0:T(128)} %param.16, s32[]{:T(128)S(6)} %mul.50), kind=kLoop, calls=%fused_computation.145 | loop fusion | flops 64 | bytes 516 | tf_op jit(solution)/shard_map/sub | solution.py:66
  2.1 1.5 %multiply_convert_fusion = bf16[8,2048]{1,0:T(8,128)(2,1)S(1)} fusion(f32[8,2048]{1,0:T(8,128)} %param.9, f32[]{:T(128)} %bitcast.1), kind=kLoop, calls=%fused_computation.35 | loop fusion | flops 32768 | bytes 98308 | tf_op jit(solution)/shard_map/convert_element_type | solution.py:73
  3.8 1.3 %fusion.4 = f32[64,8,16]{2,1,0:T(8,128)S(1)} fusion(bf16[64,16,256]{2,1,0:T(8,128)(2,1)} %param.15, bf16[64,8,256]{2,0,1:T(8,128)(2,1)S(1)} %fusion.28), kind=kOutput, calls=%fused_computation.4 | convolution fusion | flops 4194304 | bytes 819200 | tf_op jit(solution)/shard_map/far_partial/jrl,jkl->jrk/dot_general | solution.py:85
  5.3 0.8 %fusion.40 = f32[4,8,128]{2,1,0:T(8,128)S(1)} fusion(f32[64,128,1]{0,1,2:T(8,128)S(1)} %bitcast.183, s32[4,8]{1,0:T(4,128)S(1)} %multiply_add_fusion, s32[64]{0:T(128)} %param.17), kind=kOutput, calls=%fused_computation.57 | convolution fusion | flops 3147776 | bytes 49536 | tf_op jit(solution)/shard_map/far_partial/jc,jm->cm/dot_general | solution.py:89
  6.1 3.0 %collective-permute-start.3 = (f32[4,8,128]{2,1,0:T(8,128)S(1)}, f32[4,8,128]{2,1,0:T(8,128)S(1)}, u32[]{:S(2)}, u32[]{:S(2)}) collective-permute-start(f32[4,8,128]{2,1,0:T(8,128)S(1)} %fusion.40), channel_id=1, source_target_pairs={{0,2},{2,0},{1,3},{3,1},{4,6},{6,4},{5,7},{7,5},{8,10},{10,8},{9,1... | collective-permute-start | bytes 49160 | tf_op jit(solution)/shard_map/clus_exchange/ppermute | solution.py:8
  9.2 1.6 %collective-permute-start.1 = (bf16[8,2432]{1,0:T(8,128)(2,1)S(1)}, bf16[8,2432]{1,0:T(8,128)(2,1)S(1)}, u32[]{:S(2)}, u32[]{:S(2)}) collective-permute-start(bf16[8,2432]{1,0:T(8,128)(2,1)S(1)} %get-tuple-element.12), channel_id=1, source_target_pairs={{0,4},{4,8},{8,12},{12,0},{1,5},{5,9},{9,13},{13,1},{2,6},{6,10},{... | collective-permute-start | bytes 116744 | tf_op jit(solution)/shard_map/clus_exchange/ppermute | solution.py:8
  10.9 2.2 %collective-permute-start = (bf16[8,2432]{1,0:T(8,128)(2,1)S(1)}, bf16[8,2432]{1,0:T(8,128)(2,1)S(1)}, u32[]{:S(2)}, u32[]{:S(2)}) collective-permute-start(bf16[8,2432]{1,0:T(8,128)(2,1)S(1)} %get-tuple-element.24), channel_id=1, source_target_pairs={{0,12},{4,0},{8,4},{12,8},{1,13},{5,1},{9,5},{13,9},{2,14},{6,2},{... | collective-permute-start | bytes 116744 | tf_op jit(solution)/shard_map/clus_exchange/ppermute | solution.py:8
  13.1 0.7 %fusion.83 = (f32[1]{0:T(128)}, f32[1]{0:T(128)}, f32[1]{0:T(128)}) fusion(f32[4]{0:T(128)S(1)} %copy-done.5), kind=kLoop, calls=%fused_computation.151 | loop fusion | bytes 24 | tf_op jit(solution)/shard_map/clus_exchange/slice | solution.py:103
  13.8 2.0 %broadcast_multiply_fusion = (f32[8,2048]{1,0:T(8,128)S(1)}, f32[8,2048]{1,0:T(8,128)S(1)}, f32[8,2048]{1,0:T(8,128)S(1)}) fusion(f32[8,2048]{1,0:T(8,128)S(1)} %copy-done.3, f32[]{:T(128)} %bitcast.18, f32[]{:T(128)} %bitcast.12, f32[]{:T(128)} %bitcast.15), kind=kLoop, calls=%fused_computation.46 | loop fusion | flops 49152 | bytes 262156 | tf_op jit(solution)/shard_map/clus_exchange/mul | solution.py:103
  16.1 0.6 %fusion.19 = f32[16,8,256]{2,1,0:T(8,128)S(1)} fusion(bf16[16,256,256]{2,1,0:T(8,128)(2,1)S(1)} %copy-done, bf16[16,8,256]{2,0,1:T(8,128)(2,1)S(1)} %fusion.12), kind=kOutput, calls=%fused_computation.25 | convolution fusion | flops 16777216 | bytes 2293760 | tf_op jit(solution)/shard_map/near_partial/jrs,jts->jrt/dot_general | solution.py:122
  17.1 0.4 collective-permute-start.2
  17.6 1.7 %collective-permute-start.4 = (f32[8,128]{1,0:T(8,128)S(1)}, f32[8,128]{1,0:T(8,128)S(1)}, u32[]{:S(2)}, u32[]{:S(2)}) collective-permute-start(f32[8,128]{1,0:T(8,128)S(1)} %fusion.66), channel_id=1, source_target_pairs={{0,8},{4,12},{8,0},{12,4},{1,9},{5,13},{9,1},{13,5},{2,10},{6,14},... | collective-permute-start | bytes 12296 | tf_op jit(solution)/shard_map/pair_sums/ppermute | solution.py:8
  19.3 2.2 %collective-permute-done.2 = f32[8,2176]{1,0:T(8,128)S(1)} collective-permute-done((f32[8,2176]{1,0:T(8,128)S(1)}, f32[8,2176]{1,0:T(8,128)S(1)}, u32[]{:S(2)}, u32[]{:S(2)}) %collective-permute-start.2) | collective-permute-done | bytes 69664 | tf_op jit(solution)/shard_map/pair_sums/ppermute | solution.py:8
  21.5 0.6 %collective-permute-done.4 = f32[8,128]{1,0:T(8,128)S(1)} collective-permute-done((f32[8,128]{1,0:T(8,128)S(1)}, f32[8,128]{1,0:T(8,128)S(1)}, u32[]{:S(2)}, u32[]{:S(2)}) %collective-permute-start.4) | collective-permute-done | bytes 4128 | tf_op jit(solution)/shard_map/pair_sums/ppermute | solution.py:8
  23.3 0.8 %collective-permute-start.6 = (bf16[8,2432]{1,0:T(8,128)(2,1)S(1)}, bf16[8,2432]{1,0:T(8,128)(2,1)S(1)}, u32[]{:S(2)}, u32[]{:S(2)}) collective-permute-start(bf16[8,2432]{1,0:T(8,128)(2,1)S(1)} %get-tuple-element.22), channel_id=1, source_target_pairs={{0,4},{4,8},{8,12},{12,0},{1,5},{5,9},{9,13},{13,1},{2,6},{6,10},{... | collective-permute-start | bytes 116744 | tf_op jit(solution)/shard_map/clus_exchange/ppermute | solution.py:8
  24.1 3.1 %collective-permute-start.5 = (bf16[8,2432]{1,0:T(8,128)(2,1)S(1)}, bf16[8,2432]{1,0:T(8,128)(2,1)S(1)}, u32[]{:S(2)}, u32[]{:S(2)}) collective-permute-start(bf16[8,2432]{1,0:T(8,128)(2,1)S(1)} %get-tuple-element.23), channel_id=1, source_target_pairs={{0,12},{4,0},{8,4},{12,8},{1,13},{5,1},{9,5},{13,9},{2,14},{6,2},{... | collective-permute-start | bytes 116744 | tf_op jit(solution)/shard_map/clus_exchange/ppermute | solution.py:8
  27.2 1.6 %collective-permute-start.8 = (f32[4,8,128]{2,1,0:T(8,128)S(1)}, f32[4,8,128]{2,1,0:T(8,128)S(1)}, u32[]{:S(2)}, u32[]{:S(2)}) collective-permute-start(f32[4,8,128]{2,1,0:T(8,128)S(1)} %fusion.38), channel_id=1, source_target_pairs={{0,2},{2,0},{1,3},{3,1},{4,6},{6,4},{5,7},{7,5},{8,10},{10,8},{9,1... | collective-permute-start | bytes 49160 | tf_op jit(solution)/shard_map/clus_exchange/ppermute | solution.py:8
  28.9 0.4 collective-permute-done.6
  29.5 0.6 %fusion.17 = f32[16,8,256]{2,1,0:T(8,128)S(1)} fusion(bf16[16,256,256]{2,1,0:T(8,128)(2,1)S(1)} %copy-done, bf16[16,8,256]{2,0,1:T(8,128)(2,1)S(1)} %fusion.9), kind=kOutput, calls=%fused_computation.23 | convolution fusion | flops 16777216 | bytes 2293760 | tf_op jit(solution)/shard_map/near_partial/jrs,jts->jrt/dot_general | solution.py:122
  30.6 1.7 %collective-permute-start.7 = (f32[8,2176]{1,0:T(8,128)S(1)}, f32[8,2176]{1,0:T(8,128)S(1)}, u32[]{:S(2)}, u32[]{:S(2)}) collective-permute-start(f32[8,2176]{1,0:T(8,128)S(1)} %pad_maximum_fusion.4), channel_id=1, source_target_pairs={{0,2},{2,0},{1,3},{3,1},{4,6},{6,4},{5,7},{7,5},{8,10},{10,8},{9,1... | collective-permute-start | bytes 208904 | tf_op jit(solution)/shard_map/pair_sums/ppermute | solution.py:8
  32.3 1.7 %collective-permute-start.9 = (f32[8,128]{1,0:T(8,128)S(1)}, f32[8,128]{1,0:T(8,128)S(1)}, u32[]{:S(2)}, u32[]{:S(2)}) collective-permute-start(f32[8,128]{1,0:T(8,128)S(1)} %fusion.65), channel_id=1, source_target_pairs={{0,8},{4,12},{8,0},{12,4},{1,9},{5,13},{9,1},{13,5},{2,10},{6,14},... | collective-permute-start | bytes 12296 | tf_op jit(solution)/shard_map/pair_sums/ppermute | solution.py:8
  33.9 1.0 %collective-permute-done.7 = f32[8,2176]{1,0:T(8,128)S(1)} collective-permute-done((f32[8,2176]{1,0:T(8,128)S(1)}, f32[8,2176]{1,0:T(8,128)S(1)}, u32[]{:S(2)}, u32[]{:S(2)}) %collective-permute-start.7) | collective-permute-done | bytes 69664 | tf_op jit(solution)/shard_map/pair_sums/ppermute | solution.py:8
  35.0 1.8 %collective-permute-done.9 = f32[8,128]{1,0:T(8,128)S(1)} collective-permute-done((f32[8,128]{1,0:T(8,128)S(1)}, f32[8,128]{1,0:T(8,128)S(1)}, u32[]{:S(2)}, u32[]{:S(2)}) %collective-permute-start.9) | collective-permute-done | bytes 4128 | tf_op jit(solution)/shard_map/pair_sums/ppermute | solution.py:8
  38.0 1.5 %collective-permute-start.11 = (bf16[8,2432]{1,0:T(8,128)(2,1)S(1)}, bf16[8,2432]{1,0:T(8,128)(2,1)S(1)}, u32[]{:S(2)}, u32[]{:S(2)}) collective-permute-start(bf16[8,2432]{1,0:T(8,128)(2,1)S(1)} %get-tuple-element.20), channel_id=1, source_target_pairs={{0,4},{4,8},{8,12},{12,0},{1,5},{5,9},{9,13},{13,1},{2,6},{6,10},{... | collective-permute-start | bytes 116744 | tf_op jit(solution)/shard_map/clus_exchange/ppermute | solution.py:8
  39.5 2.4 %collective-permute-start.10 = (bf16[8,2432]{1,0:T(8,128)(2,1)S(1)}, bf16[8,2432]{1,0:T(8,128)(2,1)S(1)}, u32[]{:S(2)}, u32[]{:S(2)}) collective-permute-start(bf16[8,2432]{1,0:T(8,128)(2,1)S(1)} %get-tuple-element.21), channel_id=1, source_target_pairs={{0,12},{4,0},{8,4},{12,8},{1,13},{5,1},{9,5},{13,9},{2,14},{6,2},{... | collective-permute-start | bytes 116744 | tf_op jit(solution)/shard_map/clus_exchange/ppermute | solution.py:8
  42.3 1.6 %collective-permute-done.11 = bf16[8,2432]{1,0:T(8,128)(2,1)S(1)} collective-permute-done((bf16[8,2432]{1,0:T(8,128)(2,1)S(1)}, bf16[8,2432]{1,0:T(8,128)(2,1)S(1)}, u32[]{:S(2)}, u32[]{:S(2)}) %collective-permute-start.11) | collective-permute-done | bytes 38944 | tf_op jit(solution)/shard_map/clus_exchange/ppermute | solution.py:8
  44.1 0.6 %fusion.15 = f32[16,8,256]{2,1,0:T(8,128)S(1)} fusion(bf16[16,256,256]{2,1,0:T(8,128)(2,1)S(1)} %copy-done, bf16[16,8,256]{2,0,1:T(8,128)(2,1)S(1)} %fusion.6), kind=kOutput, calls=%fused_computation.21 | convolution fusion | flops 16777216 | bytes 2293760 | tf_op jit(solution)/shard_map/near_partial/jrs,jts->jrt/dot_general | solution.py:122
  45.6 2.4 %collective-permute-start.14 = (f32[8,128]{1,0:T(8,128)S(1)}, f32[8,128]{1,0:T(8,128)S(1)}, u32[]{:S(2)}, u32[]{:S(2)}) collective-permute-start(f32[8,128]{1,0:T(8,128)S(1)} %fusion.64), channel_id=1, source_target_pairs={{0,8},{4,12},{8,0},{12,4},{1,9},{5,13},{9,1},{13,5},{2,10},{6,14},... | collective-permute-start | bytes 12296 | tf_op jit(solution)/shard_map/pair_sums/ppermute | solution.py:8
  48.0 1.5 %collective-permute-done.12 = f32[8,2176]{1,0:T(8,128)S(1)} collective-permute-done((f32[8,2176]{1,0:T(8,128)S(1)}, f32[8,2176]{1,0:T(8,128)S(1)}, u32[]{:S(2)}, u32[]{:S(2)}) %collective-permute-start.12) | collective-permute-done | bytes 69664 | tf_op jit(solution)/shard_map/pair_sums/ppermute | solution.py:8
  49.6 0.6 %collective-permute-done.14 = f32[8,128]{1,0:T(8,128)S(1)} collective-permute-done((f32[8,128]{1,0:T(8,128)S(1)}, f32[8,128]{1,0:T(8,128)S(1)}, u32[]{:S(2)}, u32[]{:S(2)}) %collective-permute-start.14) | collective-permute-done | bytes 4128 | tf_op jit(solution)/shard_map/pair_sums/ppermute | solution.py:8
  50.2 0.8 %fusion.21 = f32[8,8,256]{2,1,0:T(8,128)} fusion(f32[8,8,256]{2,1,0:T(8,128)S(1)} %bitcast.188, f32[8,8,256]{2,0,1:T(8,128)S(1)} %bitcast.187, f32[8,8,16]{2,1,0:T(8,128)S(1)} %reshape.133, bf16[8,16,256]{2,1,0:T(8,128)(2,1)S(1)} %copy-done.2), kind=kOutput, calls=%fused_computation.28 | convolution fusion | flops 3178496 | bytes 266240 | tf_op jit(solution)/shard_map/far_field/crk,ckl->crl/dot_general | solution.py:144
  (88 shorter events, 5.6 us)
Async XLA Ops:
  0.0 16.1 %copy-start = (bf16[16,256,256]{2,1,0:T(8,128)(2,1)S(1)}, bf16[16,256,256]{2,1,0:T(8,128)(2,1)}, u32[]{:S(2)}) copy-start(bf16[16,256,256]{2,1,0:T(8,128)(2,1)} %param.11) | copy-start | bytes 6291460
  0.0 13.1 %copy-start.5 = (f32[4]{0:T(128)S(1)}, f32[4]{0:T(128)}, u32[]{:S(2)}) copy-start(f32[4]{0:T(128)} %param.10) | copy-start | bytes 52
  0.0 13.8 %copy-start.3 = (f32[8,2048]{1,0:T(8,128)S(1)}, f32[8,2048]{1,0:T(8,128)}, u32[]{:S(2)}) copy-start(f32[8,2048]{1,0:T(8,128)} %param.9) | copy-start | bytes 196612
  0.0 13.1 %copy-start.6 = (s32[16]{0:T(128)S(1)}, s32[16]{0:T(128)}, u32[]{:S(2)}) copy-start(s32[16]{0:T(128)} %param.13) | copy-start | bytes 196
  0.0 15.8 %copy-start.7 = (s32[16]{0:T(128)S(1)}, s32[16]{0:T(128)}, u32[]{:S(2)}) copy-start(s32[16]{0:T(128)} %param.12) | copy-start | bytes 196
  6.1 11.5 %collective-permute-start.3 = (f32[4,8,128]{2,1,0:T(8,128)S(1)}, f32[4,8,128]{2,1,0:T(8,128)S(1)}, u32[]{:S(2)}, u32[]{:S(2)}) collective-permute-start(f32[4,8,128]{2,1,0:T(8,128)S(1)} %fusion.40), channel_id=1, source_target_pairs={{0,2},{2,0},{1,3},{3,1},{4,6},{6,4},{5,7},{7,5},{8,10},{10,8},{9,1... | collective-permute-start | bytes 49160 | tf_op jit(solution)/shard_map/clus_exchange/ppermute | solution.py:8
  9.2 13.0 %copy-start.2 = (bf16[8,16,256]{2,1,0:T(8,128)(2,1)S(1)}, bf16[8,16,256]{2,1,0:T(8,128)(2,1)}, u32[]{:S(2)}) copy-start(bf16[8,16,256]{2,1,0:T(8,128)(2,1)} %param.14) | copy-start | bytes 196612
  9.2 6.6 %collective-permute-start.1 = (bf16[8,2432]{1,0:T(8,128)(2,1)S(1)}, bf16[8,2432]{1,0:T(8,128)(2,1)S(1)}, u32[]{:S(2)}, u32[]{:S(2)}) collective-permute-start(bf16[8,2432]{1,0:T(8,128)(2,1)S(1)} %get-tuple-element.12), channel_id=1, source_target_pairs={{0,4},{4,8},{8,12},{12,0},{1,5},{5,9},{9,13},{13,1},{2,6},{6,10},{... | collective-permute-start | bytes 116744 | tf_op jit(solution)/shard_map/clus_exchange/ppermute | solution.py:8
  10.9 5.0 %collective-permute-start = (bf16[8,2432]{1,0:T(8,128)(2,1)S(1)}, bf16[8,2432]{1,0:T(8,128)(2,1)S(1)}, u32[]{:S(2)}, u32[]{:S(2)}) collective-permute-start(bf16[8,2432]{1,0:T(8,128)(2,1)S(1)} %get-tuple-element.24), channel_id=1, source_target_pairs={{0,12},{4,0},{8,4},{12,8},{1,13},{5,1},{9,5},{13,9},{2,14},{6,2},{... | collective-permute-start | bytes 116744 | tf_op jit(solution)/shard_map/clus_exchange/ppermute | solution.py:8
  15.9 6.8 %copy-start.1 = (bf16[64,16,256]{2,1,0:T(8,128)(2,1)S(1)}, bf16[64,16,256]{2,1,0:T(8,128)(2,1)}, u32[]{:S(2)}) copy-start(bf16[64,16,256]{2,1,0:T(8,128)(2,1)} %param.15) | copy-start | bytes 1572868
  16.1 7.0 %copy-start.4 = (s32[64]{0:T(128)S(1)}, s32[64]{0:T(128)}, u32[]{:S(2)}) copy-start(s32[64]{0:T(128)} %param.17) | copy-start | bytes 772
  17.1 4.4 %collective-permute-start.2 = (f32[8,2176]{1,0:T(8,128)S(1)}, f32[8,2176]{1,0:T(8,128)S(1)}, u32[]{:S(2)}, u32[]{:S(2)}) collective-permute-start(f32[8,2176]{1,0:T(8,128)S(1)} %pad_maximum_fusion.3), channel_id=1, source_target_pairs={{0,2},{2,0},{1,3},{3,1},{4,6},{6,4},{5,7},{7,5},{8,10},{10,8},{9,1... | collective-permute-start | bytes 208904 | tf_op jit(solution)/shard_map/pair_sums/ppermute | solution.py:8
  17.6 4.5 %collective-permute-start.4 = (f32[8,128]{1,0:T(8,128)S(1)}, f32[8,128]{1,0:T(8,128)S(1)}, u32[]{:S(2)}, u32[]{:S(2)}) collective-permute-start(f32[8,128]{1,0:T(8,128)S(1)} %fusion.66), channel_id=1, source_target_pairs={{0,8},{4,12},{8,0},{12,4},{1,9},{5,13},{9,1},{13,5},{2,10},{6,14},... | collective-permute-start | bytes 12296 | tf_op jit(solution)/shard_map/pair_sums/ppermute | solution.py:8
  23.3 5.9 %collective-permute-start.6 = (bf16[8,2432]{1,0:T(8,128)(2,1)S(1)}, bf16[8,2432]{1,0:T(8,128)(2,1)S(1)}, u32[]{:S(2)}, u32[]{:S(2)}) collective-permute-start(bf16[8,2432]{1,0:T(8,128)(2,1)S(1)} %get-tuple-element.22), channel_id=1, source_target_pairs={{0,4},{4,8},{8,12},{12,0},{1,5},{5,9},{9,13},{13,1},{2,6},{6,10},{... | collective-permute-start | bytes 116744 | tf_op jit(solution)/shard_map/clus_exchange/ppermute | solution.py:8
  24.1 5.2 %collective-permute-start.5 = (bf16[8,2432]{1,0:T(8,128)(2,1)S(1)}, bf16[8,2432]{1,0:T(8,128)(2,1)S(1)}, u32[]{:S(2)}, u32[]{:S(2)}) collective-permute-start(bf16[8,2432]{1,0:T(8,128)(2,1)S(1)} %get-tuple-element.23), channel_id=1, source_target_pairs={{0,12},{4,0},{8,4},{12,8},{1,13},{5,1},{9,5},{13,9},{2,14},{6,2},{... | collective-permute-start | bytes 116744 | tf_op jit(solution)/shard_map/clus_exchange/ppermute | solution.py:8
  27.2 5.0 %collective-permute-start.8 = (f32[4,8,128]{2,1,0:T(8,128)S(1)}, f32[4,8,128]{2,1,0:T(8,128)S(1)}, u32[]{:S(2)}, u32[]{:S(2)}) collective-permute-start(f32[4,8,128]{2,1,0:T(8,128)S(1)} %fusion.38), channel_id=1, source_target_pairs={{0,2},{2,0},{1,3},{3,1},{4,6},{6,4},{5,7},{7,5},{8,10},{10,8},{9,1... | collective-permute-start | bytes 49160 | tf_op jit(solution)/shard_map/clus_exchange/ppermute | solution.py:8
  30.6 4.4 %collective-permute-start.7 = (f32[8,2176]{1,0:T(8,128)S(1)}, f32[8,2176]{1,0:T(8,128)S(1)}, u32[]{:S(2)}, u32[]{:S(2)}) collective-permute-start(f32[8,2176]{1,0:T(8,128)S(1)} %pad_maximum_fusion.4), channel_id=1, source_target_pairs={{0,2},{2,0},{1,3},{3,1},{4,6},{6,4},{5,7},{7,5},{8,10},{10,8},{9,1... | collective-permute-start | bytes 208904 | tf_op jit(solution)/shard_map/pair_sums/ppermute | solution.py:8
  32.3 4.5 %collective-permute-start.9 = (f32[8,128]{1,0:T(8,128)S(1)}, f32[8,128]{1,0:T(8,128)S(1)}, u32[]{:S(2)}, u32[]{:S(2)}) collective-permute-start(f32[8,128]{1,0:T(8,128)S(1)} %fusion.65), channel_id=1, source_target_pairs={{0,8},{4,12},{8,0},{12,4},{1,9},{5,13},{9,1},{13,5},{2,10},{6,14},... | collective-permute-start | bytes 12296 | tf_op jit(solution)/shard_map/pair_sums/ppermute | solution.py:8
  38.0 5.9 %collective-permute-start.11 = (bf16[8,2432]{1,0:T(8,128)(2,1)S(1)}, bf16[8,2432]{1,0:T(8,128)(2,1)S(1)}, u32[]{:S(2)}, u32[]{:S(2)}) collective-permute-start(bf16[8,2432]{1,0:T(8,128)(2,1)S(1)} %get-tuple-element.20), channel_id=1, source_target_pairs={{0,4},{4,8},{8,12},{12,0},{1,5},{5,9},{9,13},{13,1},{2,6},{6,10},{... | collective-permute-start | bytes 116744 | tf_op jit(solution)/shard_map/clus_exchange/ppermute | solution.py:8
  39.5 4.4 %collective-permute-start.10 = (bf16[8,2432]{1,0:T(8,128)(2,1)S(1)}, bf16[8,2432]{1,0:T(8,128)(2,1)S(1)}, u32[]{:S(2)}, u32[]{:S(2)}) collective-permute-start(bf16[8,2432]{1,0:T(8,128)(2,1)S(1)} %get-tuple-element.21), channel_id=1, source_target_pairs={{0,12},{4,0},{8,4},{12,8},{1,13},{5,1},{9,5},{13,9},{2,14},{6,2},{... | collective-permute-start | bytes 116744 | tf_op jit(solution)/shard_map/clus_exchange/ppermute | solution.py:8
  41.9 3.7 %collective-permute-start.13 = (f32[4,8,128]{2,1,0:T(8,128)S(1)}, f32[4,8,128]{2,1,0:T(8,128)S(1)}, u32[]{:S(2)}, u32[]{:S(2)}) collective-permute-start(f32[4,8,128]{2,1,0:T(8,128)S(1)} %fusion.36), channel_id=1, source_target_pairs={{0,2},{2,0},{1,3},{3,1},{4,6},{6,4},{5,7},{7,5},{8,10},{10,8},{9,1... | collective-permute-start | bytes 49160 | tf_op jit(solution)/shard_map/clus_exchange/ppermute | solution.py:8
  45.2 4.4 %collective-permute-start.12 = (f32[8,2176]{1,0:T(8,128)S(1)}, f32[8,2176]{1,0:T(8,128)S(1)}, u32[]{:S(2)}, u32[]{:S(2)}) collective-permute-start(f32[8,2176]{1,0:T(8,128)S(1)} %pad_maximum_fusion.5), channel_id=1, source_target_pairs={{0,2},{2,0},{1,3},{3,1},{4,6},{6,4},{5,7},{7,5},{8,10},{10,8},{9,1... | collective-permute-start | bytes 208904 | tf_op jit(solution)/shard_map/pair_sums/ppermute | solution.py:8
  45.6 4.5 %collective-permute-start.14 = (f32[8,128]{1,0:T(8,128)S(1)}, f32[8,128]{1,0:T(8,128)S(1)}, u32[]{:S(2)}, u32[]{:S(2)}) collective-permute-start(f32[8,128]{1,0:T(8,128)S(1)} %fusion.64), channel_id=1, source_target_pairs={{0,8},{4,12},{8,0},{12,4},{1,9},{5,13},{9,1},{13,5},{2,10},{6,14},... | collective-permute-start | bytes 12296 | tf_op jit(solution)/shard_map/pair_sums/ppermute | solution.py:8

commit v15 on v14

--- a/solution.py
+++ b/solution.py
@@ -110,7 +110,10 @@
                     from_plus = neighbour
                 far_mine = far_mine + join_three(incoming[:, iterate_size:])
             if short_shifts:
-                far_pair = pair_total(partial_value, pair_count, pair_index)
+                far_far = jnp.stack(
+                    [partial_value[(my_index + s) % peer_count] for s in short_shifts]
+                )
+                far_pair = pair_total(far_far, pair_count, pair_index)
         with jax.named_scope("near_partial"):
             extended = jnp.concatenate([iterate, from_plus, from_minus], axis=0)
             gathered = jnp.einsum(
@@ -135,10 +138,8 @@
             packed = pair_total(packed, pair_count, pair_index)
             near_sum = packed[:, :iterate_size].reshape(clusters_here, rhs_here, leaf_size)
             coef_flat = packed[:, iterate_size:]
-            for s in short_shifts:
-                coef_flat = coef_flat + shift(
-                    far_pair[(my_index + s) % peer_count], "clus", peer_count, s
-                )
+            for k, s in enumerate(short_shifts):
+                coef_flat = coef_flat + shift(far_pair[k], "clus", peer_count, s)
             coef_sum = coef_flat.reshape(clusters_here, rhs_here, rank_size)
         with jax.named_scope("far_field"):
             far_field = jnp.einsum(

time: 51.3 us -> 51.3 us (level)
  transfers between devices with their start and end apart: 15 -> 15, of which waited for: 9 -> 8; matrix products, arithmetic and copies ran while one was open for 13% -> 13% of each run, Pallas kernels for 0% -> 0%
where the time goes in v15:
time: 51.3 us; the launch traced here: 51 us
  starting transfers between devices  25.1 us (49%)
  waiting for transfers between devices  9.62 us (19%)
  matrix products  8.39 us (16%)
  other arithmetic  4.46 us (9%)
  local copies, waits for them, and re-layouts  2.98 us (6%)
    ppermute x15, starting transfers between devices, shift(): lax.ppermute(value, axis, [(i, (i + step) % count) for i in range(count)])  25.1 us
    ppermute x15, waiting for transfers between devices, shift(): lax.ppermute(value, axis, [(i, (i + step) % count) for i in range(count)])  9.62 us
    mul x1, other arithmetic, shards(): scaled = [scales[d] * source for d in range(degree_top)]  1.96 us
    dot_general x3, matrix products, shards(): jnp.einsum('jrs,jts->jrt', gathered, near_blocks, preferred_element_type=...  1.93 us
    dot_general x3, matrix products, shards(): jnp.einsum('jrl,jkl->jrk', far_input, col_basis, preferred_element_type=j...  1.87 us
    convert_element_type x1, other arithmetic, shards(): iterate = (coefficients[degree_top] * source).astype(jnp.bfloat16)  1.49 us
    slice x1, local copies, waits for them, and re-layouts, shards(): iterate = (coefficients[degree_top] * source).astype(jnp.bfloat16)  1.38 us
    dot_general x3, matrix products, shards(): jnp.einsum('jc,jm->cm', far_hot, coef, precision=lax.Precision.HIGHEST)  1.2 us
  transfers between devices with their start and end apart: 15, of which 8 were waited for; matrix products, arithmetic and copies ran while one was open for 13% of the time, Pallas kernels for 0%

profile of v15, /device:TPU:0, one launch (start us, length us, event | category | flops | bytes accessed | tf_op | source)
XLA Modules:
  0.0 51.0 jit_solution(7160441860270154614)
XLA Ops:
  0.1 1.4 %slice.126 = f32[1]{0:T(128)} slice(f32[4]{0:T(128)} %param.10), slice={[3:4]} | slice | bytes 8 | tf_op jit(solution)/shard_map/slice | solution.py:73
  1.4 0.7 %broadcast_subtract_fusion = s32[64]{0:T(128)S(1)} fusion(s32[64]{0:T(128)} %param.16, s32[]{:T(128)S(6)} %mul.50), kind=kLoop, calls=%fused_computation.139 | loop fusion | flops 64 | bytes 516 | tf_op jit(solution)/shard_map/sub | solution.py:66
  2.1 1.5 %multiply_convert_fusion = bf16[8,2048]{1,0:T(8,128)(2,1)S(1)} fusion(f32[8,2048]{1,0:T(8,128)} %param.9, f32[]{:T(128)} %bitcast.1), kind=kLoop, calls=%fused_computation.35 | loop fusion | flops 32768 | bytes 98308 | tf_op jit(solution)/shard_map/convert_element_type | solution.py:73
  3.9 1.3 %fusion.4 = f32[64,8,16]{2,1,0:T(8,128)S(1)} fusion(bf16[64,16,256]{2,1,0:T(8,128)(2,1)} %param.15, bf16[64,8,256]{2,0,1:T(8,128)(2,1)S(1)} %fusion.28), kind=kOutput, calls=%fused_computation.4 | convolution fusion | flops 4194304 | bytes 819200 | tf_op jit(solution)/shard_map/far_partial/jrl,jkl->jrk/dot_general | solution.py:85
  5.3 0.8 %fusion.40 = f32[4,8,128]{2,1,0:T(8,128)S(1)} fusion(f32[64,128,1]{0,1,2:T(8,128)S(1)} %bitcast.182, s32[4,8]{1,0:T(4,128)S(1)} %multiply_add_fusion, s32[64]{0:T(128)} %param.17), kind=kOutput, calls=%fused_computation.57 | convolution fusion | flops 3147776 | bytes 49536 | tf_op jit(solution)/shard_map/far_partial/jc,jm->cm/dot_general | solution.py:89
  6.2 3.0 %collective-permute-start.3 = (f32[1,8,128]{2,1,0:T(8,128)S(1)}, f32[1,8,128]{2,1,0:T(8,128)S(1)}, u32[]{:S(2)}, u32[]{:S(2)}) collective-permute-start(f32[1,8,128]{2,1,0:T(8,128)S(1)} %constant_dynamic-slice_fusion.2), channel_id=1, source_target_pairs={{0,2},{2,0},{1,3},{3,1},{4,6},{6,4},{5,7},{7,5},{8,10},{10,8},{9,1... | collective-permute-start | bytes 12296 | tf_op jit(solution)/shard_map/clus_exchange/ppermute | solution.py:8
  9.3 1.6 %collective-permute-start.1 = (bf16[8,2432]{1,0:T(8,128)(2,1)S(1)}, bf16[8,2432]{1,0:T(8,128)(2,1)S(1)}, u32[]{:S(2)}, u32[]{:S(2)}) collective-permute-start(bf16[8,2432]{1,0:T(8,128)(2,1)S(1)} %get-tuple-element.12), channel_id=1, source_target_pairs={{0,4},{4,8},{8,12},{12,0},{1,5},{5,9},{9,13},{13,1},{2,6},{6,10},{... | collective-permute-start | bytes 116744 | tf_op jit(solution)/shard_map/clus_exchange/ppermute | solution.py:8
  10.9 2.2 %collective-permute-start = (bf16[8,2432]{1,0:T(8,128)(2,1)S(1)}, bf16[8,2432]{1,0:T(8,128)(2,1)S(1)}, u32[]{:S(2)}, u32[]{:S(2)}) collective-permute-start(bf16[8,2432]{1,0:T(8,128)(2,1)S(1)} %get-tuple-element.24), channel_id=1, source_target_pairs={{0,12},{4,0},{8,4},{12,8},{1,13},{5,1},{9,5},{13,9},{2,14},{6,2},{... | collective-permute-start | bytes 116744 | tf_op jit(solution)/shard_map/clus_exchange/ppermute | solution.py:8
  13.2 0.7 %fusion.80 = (f32[1]{0:T(128)}, f32[1]{0:T(128)}, f32[1]{0:T(128)}) fusion(f32[4]{0:T(128)S(1)} %copy-done.5), kind=kLoop, calls=%fused_computation.145 | loop fusion | bytes 24 | tf_op jit(solution)/shard_map/clus_exchange/slice | solution.py:103
  13.9 2.0 %broadcast_multiply_fusion = (f32[8,2048]{1,0:T(8,128)S(1)}, f32[8,2048]{1,0:T(8,128)S(1)}, f32[8,2048]{1,0:T(8,128)S(1)}) fusion(f32[8,2048]{1,0:T(8,128)S(1)} %copy-done.3, f32[]{:T(128)} %bitcast.18, f32[]{:T(128)} %bitcast.12, f32[]{:T(128)} %bitcast.15), kind=kLoop, calls=%fused_computation.46 | loop fusion | flops 49152 | bytes 262156 | tf_op jit(solution)/shard_map/clus_exchange/mul | solution.py:103
  16.2 0.6 %fusion.19 = f32[16,8,256]{2,1,0:T(8,128)S(1)} fusion(bf16[16,256,256]{2,1,0:T(8,128)(2,1)S(1)} %copy-done, bf16[16,8,256]{2,0,1:T(8,128)(2,1)S(1)} %fusion.12), kind=kOutput, calls=%fused_computation.25 | convolution fusion | flops 16777216 | bytes 2293760 | tf_op jit(solution)/shard_map/near_partial/jrs,jts->jrt/dot_general | solution.py:125
  17.2 0.4 collective-permute-start.2
  17.6 1.7 %collective-permute-start.4 = (f32[8,128]{1,0:T(8,128)S(1)}, f32[8,128]{1,0:T(8,128)S(1)}, u32[]{:S(2)}, u32[]{:S(2)}) collective-permute-start(f32[8,128]{1,0:T(8,128)S(1)} %add_bitcast_fusion.2), channel_id=1, source_target_pairs={{0,8},{4,12},{8,0},{12,4},{1,9},{5,13},{9,1},{13,5},{2,10},{6,14},... | collective-permute-start | bytes 12296 | tf_op jit(solution)/shard_map/pair_sums/ppermute | solution.py:8
  19.4 2.2 %collective-permute-done.2 = f32[8,2176]{1,0:T(8,128)S(1)} collective-permute-done((f32[8,2176]{1,0:T(8,128)S(1)}, f32[8,2176]{1,0:T(8,128)S(1)}, u32[]{:S(2)}, u32[]{:S(2)}) %collective-permute-start.2) | collective-permute-done | bytes 69664 | tf_op jit(solution)/shard_map/pair_sums/ppermute | solution.py:8
  21.6 0.6 %collective-permute-done.4 = f32[8,128]{1,0:T(8,128)S(1)} collective-permute-done((f32[8,128]{1,0:T(8,128)S(1)}, f32[8,128]{1,0:T(8,128)S(1)}, u32[]{:S(2)}, u32[]{:S(2)}) %collective-permute-start.4) | collective-permute-done | bytes 4128 | tf_op jit(solution)/shard_map/pair_sums/ppermute | solution.py:8
  23.4 0.8 %collective-permute-start.6 = (bf16[8,2432]{1,0:T(8,128)(2,1)S(1)}, bf16[8,2432]{1,0:T(8,128)(2,1)S(1)}, u32[]{:S(2)}, u32[]{:S(2)}) collective-permute-start(bf16[8,2432]{1,0:T(8,128)(2,1)S(1)} %get-tuple-element.22), channel_id=1, source_target_pairs={{0,4},{4,8},{8,12},{12,0},{1,5},{5,9},{9,13},{13,1},{2,6},{6,10},{... | collective-permute-start | bytes 116744 | tf_op jit(solution)/shard_map/clus_exchange/ppermute | solution.py:8
  24.2 3.1 %collective-permute-start.5 = (bf16[8,2432]{1,0:T(8,128)(2,1)S(1)}, bf16[8,2432]{1,0:T(8,128)(2,1)S(1)}, u32[]{:S(2)}, u32[]{:S(2)}) collective-permute-start(bf16[8,2432]{1,0:T(8,128)(2,1)S(1)} %get-tuple-element.23), channel_id=1, source_target_pairs={{0,12},{4,0},{8,4},{12,8},{1,13},{5,1},{9,5},{13,9},{2,14},{6,2},{... | collective-permute-start | bytes 116744 | tf_op jit(solution)/shard_map/clus_exchange/ppermute | solution.py:8
  27.3 1.6 %collective-permute-start.8 = (f32[1,8,128]{2,1,0:T(8,128)S(1)}, f32[1,8,128]{2,1,0:T(8,128)S(1)}, u32[]{:S(2)}, u32[]{:S(2)}) collective-permute-start(f32[1,8,128]{2,1,0:T(8,128)S(1)} %constant_dynamic-slice_fusion.1), channel_id=1, source_target_pairs={{0,2},{2,0},{1,3},{3,1},{4,6},{6,4},{5,7},{7,5},{8,10},{10,8},{9,1... | collective-permute-start | bytes 12296 | tf_op jit(solution)/shard_map/clus_exchange/ppermute | solution.py:8
  28.9 0.4 collective-permute-done.6
  29.6 0.6 %fusion.17 = f32[16,8,256]{2,1,0:T(8,128)S(1)} fusion(bf16[16,256,256]{2,1,0:T(8,128)(2,1)S(1)} %copy-done, bf16[16,8,256]{2,0,1:T(8,128)(2,1)S(1)} %fusion.9), kind=kOutput, calls=%fused_computation.23 | convolution fusion | flops 16777216 | bytes 2293760 | tf_op jit(solution)/shard_map/near_partial/jrs,jts->jrt/dot_general | solution.py:125
  30.6 1.7 %collective-permute-start.7 = (f32[8,2176]{1,0:T(8,128)S(1)}, f32[8,2176]{1,0:T(8,128)S(1)}, u32[]{:S(2)}, u32[]{:S(2)}) collective-permute-start(f32[8,2176]{1,0:T(8,128)S(1)} %pad_maximum_fusion.4), channel_id=1, source_target_pairs={{0,2},{2,0},{1,3},{3,1},{4,6},{6,4},{5,7},{7,5},{8,10},{10,8},{9,1... | collective-permute-start | bytes 208904 | tf_op jit(solution)/shard_map/pair_sums/ppermute | solution.py:8
  32.3 1.7 %collective-permute-start.9 = (f32[8,128]{1,0:T(8,128)S(1)}, f32[8,128]{1,0:T(8,128)S(1)}, u32[]{:S(2)}, u32[]{:S(2)}) collective-permute-start(f32[8,128]{1,0:T(8,128)S(1)} %add_bitcast_fusion.1), channel_id=1, source_target_pairs={{0,8},{4,12},{8,0},{12,4},{1,9},{5,13},{9,1},{13,5},{2,10},{6,14},... | collective-permute-start | bytes 12296 | tf_op jit(solution)/shard_map/pair_sums/ppermute | solution.py:8
  34.0 1.0 %collective-permute-done.7 = f32[8,2176]{1,0:T(8,128)S(1)} collective-permute-done((f32[8,2176]{1,0:T(8,128)S(1)}, f32[8,2176]{1,0:T(8,128)S(1)}, u32[]{:S(2)}, u32[]{:S(2)}) %collective-permute-start.7) | collective-permute-done | bytes 69664 | tf_op jit(solution)/shard_map/pair_sums/ppermute | solution.py:8
  35.0 1.8 %collective-permute-done.9 = f32[8,128]{1,0:T(8,128)S(1)} collective-permute-done((f32[8,128]{1,0:T(8,128)S(1)}, f32[8,128]{1,0:T(8,128)S(1)}, u32[]{:S(2)}, u32[]{:S(2)}) %collective-permute-start.9) | collective-permute-done | bytes 4128 | tf_op jit(solution)/shard_map/pair_sums/ppermute | solution.py:8
  38.0 1.5 %collective-permute-start.11 = (bf16[8,2432]{1,0:T(8,128)(2,1)S(1)}, bf16[8,2432]{1,0:T(8,128)(2,1)S(1)}, u32[]{:S(2)}, u32[]{:S(2)}) collective-permute-start(bf16[8,2432]{1,0:T(8,128)(2,1)S(1)} %get-tuple-element.20), channel_id=1, source_target_pairs={{0,4},{4,8},{8,12},{12,0},{1,5},{5,9},{9,13},{13,1},{2,6},{6,10},{... | collective-permute-start | bytes 116744 | tf_op jit(solution)/shard_map/clus_exchange/ppermute | solution.py:8
  39.5 2.4 %collective-permute-start.10 = (bf16[8,2432]{1,0:T(8,128)(2,1)S(1)}, bf16[8,2432]{1,0:T(8,128)(2,1)S(1)}, u32[]{:S(2)}, u32[]{:S(2)}) collective-permute-start(bf16[8,2432]{1,0:T(8,128)(2,1)S(1)} %get-tuple-element.21), channel_id=1, source_target_pairs={{0,12},{4,0},{8,4},{12,8},{1,13},{5,1},{9,5},{13,9},{2,14},{6,2},{... | collective-permute-start | bytes 116744 | tf_op jit(solution)/shard_map/clus_exchange/ppermute | solution.py:8
  42.3 1.6 %collective-permute-done.11 = bf16[8,2432]{1,0:T(8,128)(2,1)S(1)} collective-permute-done((bf16[8,2432]{1,0:T(8,128)(2,1)S(1)}, bf16[8,2432]{1,0:T(8,128)(2,1)S(1)}, u32[]{:S(2)}, u32[]{:S(2)}) %collective-permute-start.11) | collective-permute-done | bytes 38944 | tf_op jit(solution)/shard_map/clus_exchange/ppermute | solution.py:8
  44.2 0.6 %fusion.15 = f32[16,8,256]{2,1,0:T(8,128)S(1)} fusion(bf16[16,256,256]{2,1,0:T(8,128)(2,1)S(1)} %copy-done, bf16[16,8,256]{2,0,1:T(8,128)(2,1)S(1)} %fusion.6), kind=kOutput, calls=%fused_computation.21 | convolution fusion | flops 16777216 | bytes 2293760 | tf_op jit(solution)/shard_map/near_partial/jrs,jts->jrt/dot_general | solution.py:125
  45.6 2.5 %collective-permute-start.14 = (f32[8,128]{1,0:T(8,128)S(1)}, f32[8,128]{1,0:T(8,128)S(1)}, u32[]{:S(2)}, u32[]{:S(2)}) collective-permute-start(f32[8,128]{1,0:T(8,128)S(1)} %add_bitcast_fusion), channel_id=1, source_target_pairs={{0,8},{4,12},{8,0},{12,4},{1,9},{5,13},{9,1},{13,5},{2,10},{6,14},... | collective-permute-start | bytes 12296 | tf_op jit(solution)/shard_map/pair_sums/ppermute | solution.py:8
  48.1 1.5 %collective-permute-done.12 = f32[8,2176]{1,0:T(8,128)S(1)} collective-permute-done((f32[8,2176]{1,0:T(8,128)S(1)}, f32[8,2176]{1,0:T(8,128)S(1)}, u32[]{:S(2)}, u32[]{:S(2)}) %collective-permute-start.12) | collective-permute-done | bytes 69664 | tf_op jit(solution)/shard_map/pair_sums/ppermute | solution.py:8
  49.6 0.5 collective-permute-done.14
  50.2 0.8 %fusion.21 = f32[8,8,256]{2,1,0:T(8,128)} fusion(f32[8,8,256]{2,1,0:T(8,128)S(1)} %bitcast.188, f32[8,8,256]{2,0,1:T(8,128)S(1)} %bitcast.187, f32[8,8,16]{2,1,0:T(8,128)S(1)} %reshape.133, bf16[8,16,256]{2,1,0:T(8,128)(2,1)S(1)} %copy-done.2), kind=kOutput, calls=%fused_computation.28 | convolution fusion | flops 3178496 | bytes 266240 | tf_op jit(solution)/shard_map/far_field/crk,ckl->crl/dot_general | solution.py:145
  (91 shorter events, 5.6 us)
Async XLA Ops:
  0.0 16.1 %copy-start = (bf16[16,256,256]{2,1,0:T(8,128)(2,1)S(1)}, bf16[16,256,256]{2,1,0:T(8,128)(2,1)}, u32[]{:S(2)}) copy-start(bf16[16,256,256]{2,1,0:T(8,128)(2,1)} %param.11) | copy-start | bytes 6291460
  0.0 13.2 %copy-start.5 = (f32[4]{0:T(128)S(1)}, f32[4]{0:T(128)}, u32[]{:S(2)}) copy-start(f32[4]{0:T(128)} %param.10) | copy-start | bytes 52
  0.0 13.9 %copy-start.3 = (f32[8,2048]{1,0:T(8,128)S(1)}, f32[8,2048]{1,0:T(8,128)}, u32[]{:S(2)}) copy-start(f32[8,2048]{1,0:T(8,128)} %param.9) | copy-start | bytes 196612
  0.0 13.2 %copy-start.6 = (s32[16]{0:T(128)S(1)}, s32[16]{0:T(128)}, u32[]{:S(2)}) copy-start(s32[16]{0:T(128)} %param.13) | copy-start | bytes 196
  0.0 15.8 %copy-start.7 = (s32[16]{0:T(128)S(1)}, s32[16]{0:T(128)}, u32[]{:S(2)}) copy-start(s32[16]{0:T(128)} %param.12) | copy-start | bytes 196
  6.2 11.4 %collective-permute-start.3 = (f32[1,8,128]{2,1,0:T(8,128)S(1)}, f32[1,8,128]{2,1,0:T(8,128)S(1)}, u32[]{:S(2)}, u32[]{:S(2)}) collective-permute-start(f32[1,8,128]{2,1,0:T(8,128)S(1)} %constant_dynamic-slice_fusion.2), channel_id=1, source_target_pairs={{0,2},{2,0},{1,3},{3,1},{4,6},{6,4},{5,7},{7,5},{8,10},{10,8},{9,1... | collective-permute-start | bytes 12296 | tf_op jit(solution)/shard_map/clus_exchange/ppermute | solution.py:8
  9.3 13.0 %copy-start.2 = (bf16[8,16,256]{2,1,0:T(8,128)(2,1)S(1)}, bf16[8,16,256]{2,1,0:T(8,128)(2,1)}, u32[]{:S(2)}) copy-start(bf16[8,16,256]{2,1,0:T(8,128)(2,1)} %param.14) | copy-start | bytes 196612
  9.3 6.6 %collective-permute-start.1 = (bf16[8,2432]{1,0:T(8,128)(2,1)S(1)}, bf16[8,2432]{1,0:T(8,128)(2,1)S(1)}, u32[]{:S(2)}, u32[]{:S(2)}) collective-permute-start(bf16[8,2432]{1,0:T(8,128)(2,1)S(1)} %get-tuple-element.12), channel_id=1, source_target_pairs={{0,4},{4,8},{8,12},{12,0},{1,5},{5,9},{9,13},{13,1},{2,6},{6,10},{... | collective-permute-start | bytes 116744 | tf_op jit(solution)/shard_map/clus_exchange/ppermute | solution.py:8
  10.9 5.0 %collective-permute-start = (bf16[8,2432]{1,0:T(8,128)(2,1)S(1)}, bf16[8,2432]{1,0:T(8,128)(2,1)S(1)}, u32[]{:S(2)}, u32[]{:S(2)}) collective-permute-start(bf16[8,2432]{1,0:T(8,128)(2,1)S(1)} %get-tuple-element.24), channel_id=1, source_target_pairs={{0,12},{4,0},{8,4},{12,8},{1,13},{5,1},{9,5},{13,9},{2,14},{6,2},{... | collective-permute-start | bytes 116744 | tf_op jit(solution)/shard_map/clus_exchange/ppermute | solution.py:8
  15.9 6.8 %copy-start.1 = (bf16[64,16,256]{2,1,0:T(8,128)(2,1)S(1)}, bf16[64,16,256]{2,1,0:T(8,128)(2,1)}, u32[]{:S(2)}) copy-start(bf16[64,16,256]{2,1,0:T(8,128)(2,1)} %param.15) | copy-start | bytes 1572868
  16.1 7.0 %copy-start.4 = (s32[64]{0:T(128)S(1)}, s32[64]{0:T(128)}, u32[]{:S(2)}) copy-start(s32[64]{0:T(128)} %param.17) | copy-start | bytes 772
  17.2 4.4 %collective-permute-start.2 = (f32[8,2176]{1,0:T(8,128)S(1)}, f32[8,2176]{1,0:T(8,128)S(1)}, u32[]{:S(2)}, u32[]{:S(2)}) collective-permute-start(f32[8,2176]{1,0:T(8,128)S(1)} %pad_maximum_fusion.3), channel_id=1, source_target_pairs={{0,2},{2,0},{1,3},{3,1},{4,6},{6,4},{5,7},{7,5},{8,10},{10,8},{9,1... | collective-permute-start | bytes 208904 | tf_op jit(solution)/shard_map/pair_sums/ppermute | solution.py:8
  17.6 4.5 %collective-permute-start.4 = (f32[8,128]{1,0:T(8,128)S(1)}, f32[8,128]{1,0:T(8,128)S(1)}, u32[]{:S(2)}, u32[]{:S(2)}) collective-permute-start(f32[8,128]{1,0:T(8,128)S(1)} %add_bitcast_fusion.2), channel_id=1, source_target_pairs={{0,8},{4,12},{8,0},{12,4},{1,9},{5,13},{9,1},{13,5},{2,10},{6,14},... | collective-permute-start | bytes 12296 | tf_op jit(solution)/shard_map/pair_sums/ppermute | solution.py:8
  23.4 5.9 %collective-permute-start.6 = (bf16[8,2432]{1,0:T(8,128)(2,1)S(1)}, bf16[8,2432]{1,0:T(8,128)(2,1)S(1)}, u32[]{:S(2)}, u32[]{:S(2)}) collective-permute-start(bf16[8,2432]{1,0:T(8,128)(2,1)S(1)} %get-tuple-element.22), channel_id=1, source_target_pairs={{0,4},{4,8},{8,12},{12,0},{1,5},{5,9},{9,13},{13,1},{2,6},{6,10},{... | collective-permute-start | bytes 116744 | tf_op jit(solution)/shard_map/clus_exchange/ppermute | solution.py:8
  24.2 5.2 %collective-permute-start.5 = (bf16[8,2432]{1,0:T(8,128)(2,1)S(1)}, bf16[8,2432]{1,0:T(8,128)(2,1)S(1)}, u32[]{:S(2)}, u32[]{:S(2)}) collective-permute-start(bf16[8,2432]{1,0:T(8,128)(2,1)S(1)} %get-tuple-element.23), channel_id=1, source_target_pairs={{0,12},{4,0},{8,4},{12,8},{1,13},{5,1},{9,5},{13,9},{2,14},{6,2},{... | collective-permute-start | bytes 116744 | tf_op jit(solution)/shard_map/clus_exchange/ppermute | solution.py:8
  27.3 5.0 %collective-permute-start.8 = (f32[1,8,128]{2,1,0:T(8,128)S(1)}, f32[1,8,128]{2,1,0:T(8,128)S(1)}, u32[]{:S(2)}, u32[]{:S(2)}) collective-permute-start(f32[1,8,128]{2,1,0:T(8,128)S(1)} %constant_dynamic-slice_fusion.1), channel_id=1, source_target_pairs={{0,2},{2,0},{1,3},{3,1},{4,6},{6,4},{5,7},{7,5},{8,10},{10,8},{9,1... | collective-permute-start | bytes 12296 | tf_op jit(solution)/shard_map/clus_exchange/ppermute | solution.py:8
  30.6 4.4 %collective-permute-start.7 = (f32[8,2176]{1,0:T(8,128)S(1)}, f32[8,2176]{1,0:T(8,128)S(1)}, u32[]{:S(2)}, u32[]{:S(2)}) collective-permute-start(f32[8,2176]{1,0:T(8,128)S(1)} %pad_maximum_fusion.4), channel_id=1, source_target_pairs={{0,2},{2,0},{1,3},{3,1},{4,6},{6,4},{5,7},{7,5},{8,10},{10,8},{9,1... | collective-permute-start | bytes 208904 | tf_op jit(solution)/shard_map/pair_sums/ppermute | solution.py:8
  32.3 4.5 %collective-permute-start.9 = (f32[8,128]{1,0:T(8,128)S(1)}, f32[8,128]{1,0:T(8,128)S(1)}, u32[]{:S(2)}, u32[]{:S(2)}) collective-permute-start(f32[8,128]{1,0:T(8,128)S(1)} %add_bitcast_fusion.1), channel_id=1, source_target_pairs={{0,8},{4,12},{8,0},{12,4},{1,9},{5,13},{9,1},{13,5},{2,10},{6,14},... | collective-permute-start | bytes 12296 | tf_op jit(solution)/shard_map/pair_sums/ppermute | solution.py:8
  38.0 5.9 %collective-permute-start.11 = (bf16[8,2432]{1,0:T(8,128)(2,1)S(1)}, bf16[8,2432]{1,0:T(8,128)(2,1)S(1)}, u32[]{:S(2)}, u32[]{:S(2)}) collective-permute-start(bf16[8,2432]{1,0:T(8,128)(2,1)S(1)} %get-tuple-element.20), channel_id=1, source_target_pairs={{0,4},{4,8},{8,12},{12,0},{1,5},{5,9},{9,13},{13,1},{2,6},{6,10},{... | collective-permute-start | bytes 116744 | tf_op jit(solution)/shard_map/clus_exchange/ppermute | solution.py:8
  39.5 4.4 %collective-permute-start.10 = (bf16[8,2432]{1,0:T(8,128)(2,1)S(1)}, bf16[8,2432]{1,0:T(8,128)(2,1)S(1)}, u32[]{:S(2)}, u32[]{:S(2)}) collective-permute-start(bf16[8,2432]{1,0:T(8,128)(2,1)S(1)} %get-tuple-element.21), channel_id=1, source_target_pairs={{0,12},{4,0},{8,4},{12,8},{1,13},{5,1},{9,5},{13,9},{2,14},{6,2},{... | collective-permute-start | bytes 116744 | tf_op jit(solution)/shard_map/clus_exchange/ppermute | solution.py:8
  41.9 3.7 %collective-permute-start.13 = (f32[1,8,128]{2,1,0:T(8,128)S(1)}, f32[1,8,128]{2,1,0:T(8,128)S(1)}, u32[]{:S(2)}, u32[]{:S(2)}) collective-permute-start(f32[1,8,128]{2,1,0:T(8,128)S(1)} %constant_dynamic-slice_fusion), channel_id=1, source_target_pairs={{0,2},{2,0},{1,3},{3,1},{4,6},{6,4},{5,7},{7,5},{8,10},{10,8},{9,1... | collective-permute-start | bytes 12296 | tf_op jit(solution)/shard_map/clus_exchange/ppermute | solution.py:8
  45.2 4.4 %collective-permute-start.12 = (f32[8,2176]{1,0:T(8,128)S(1)}, f32[8,2176]{1,0:T(8,128)S(1)}, u32[]{:S(2)}, u32[]{:S(2)}) collective-permute-start(f32[8,2176]{1,0:T(8,128)S(1)} %pad_maximum_fusion.5), channel_id=1, source_target_pairs={{0,2},{2,0},{1,3},{3,1},{4,6},{6,4},{5,7},{7,5},{8,10},{10,8},{9,1... | collective-permute-start | bytes 208904 | tf_op jit(solution)/shard_map/pair_sums/ppermute | solution.py:8
  45.6 4.5 %collective-permute-start.14 = (f32[8,128]{1,0:T(8,128)S(1)}, f32[8,128]{1,0:T(8,128)S(1)}, u32[]{:S(2)}, u32[]{:S(2)}) collective-permute-start(f32[8,128]{1,0:T(8,128)S(1)} %add_bitcast_fusion), channel_id=1, source_target_pairs={{0,8},{4,12},{8,0},{12,4},{1,9},{5,13},{9,1},{13,5},{2,10},{6,14},... | collective-permute-start | bytes 12296 | tf_op jit(solution)/shard_map/pair_sums/ppermute | solution.py:8

commit v16 on v14

--- a/solution.py
+++ b/solution.py
@@ -32,6 +32,21 @@
         return value + shift(value, "pair", 2, 1)
     received = [value] + [shift(value, "pair", pair_count, s) for s in range(1, pair_count)]
     stacked = jnp.stack(received)
+    order = (pair_index - jnp.arange(pair_count)) % pair_count
+    canonical = stacked[order]
+    total = canonical[0]
+    for q in range(1, pair_count):
+        total = total + canonical[q]
+    return total
+
+
+def pair_total_list(arrivals, pair_index):
+    pair_count = len(arrivals)
+    if pair_count == 1:
+        return arrivals[0]
+    if pair_count == 2:
+        return arrivals[0] + arrivals[1]
+    stacked = jnp.stack(arrivals)
     order = (pair_index - jnp.arange(pair_count)) % pair_count
     canonical = stacked[order]
     total = canonical[0]
@@ -109,8 +124,6 @@
                 if s == peer_count - 1:
                     from_plus = neighbour
                 far_mine = far_mine + join_three(incoming[:, iterate_size:])
-            if short_shifts:
-                far_pair = pair_total(partial_value, pair_count, pair_index)
         with jax.named_scope("near_partial"):
             extended = jnp.concatenate([iterate, from_plus, from_minus], axis=0)
             gathered = jnp.einsum(
@@ -136,9 +149,16 @@
             near_sum = packed[:, :iterate_size].reshape(clusters_here, rhs_here, leaf_size)
             coef_flat = packed[:, iterate_size:]
             for s in short_shifts:
-                coef_flat = coef_flat + shift(
-                    far_pair[(my_index + s) % peer_count], "clus", peer_count, s
-                )
+                outgoing = partial_value[(my_index + s) % peer_count]
+                arrivals = []
+                for t in range(pair_count):
+                    pairs = [
+                        (c * pair_count + p, ((c + s) % peer_count) * pair_count + (p + t) % pair_count)
+                        for c in range(peer_count)
+                        for p in range(pair_count)
+                    ]
+                    arrivals.append(lax.ppermute(outgoing, ("clus", "pair"), pairs))
+                coef_flat = coef_flat + pair_total_list(arrivals, pair_index)
             coef_sum = coef_flat.reshape(clusters_here, rhs_here, rank_size)
         with jax.named_scope("far_field"):
             far_field = jnp.einsum(

time: 51.3 us -> 56.7 us (1.11)
  waiting for transfers between devices: 9.79 us -> 13.8 us
  starting transfers between devices: 25 us -> 26.3 us
    ppermute x0 -> x6, starting transfers between devices: none -> 8.39 us  [shards(): arrivals.append(lax.ppermute(outgoing, ('clus', 'pair'), pairs))]
    ppermute x0 -> x6, waiting for transfers between devices: none -> 8.37 us  [shards(): arrivals.append(lax.ppermute(outgoing, ('clus', 'pair'), pairs))]
    ppermute x15 -> x9, starting transfers between devices: 25 us -> 17.9 us  [shift(): lax.ppermute(value, axis, [(i, (i + step) % count) for i in range(count)])]
    ppermute x15 -> x9, waiting for transfers between devices: 9.79 us -> 5.47 us  [shift(): lax.ppermute(value, axis, [(i, (i + step) % count) for i in range(count)])]
  transfers between devices with their start and end apart: 15 -> 15, of which waited for: 9 -> 8; matrix products, arithmetic and copies ran while one was open for 13% -> 5% of each run, Pallas kernels for 0% -> 0%
where the time goes in v16:
time: 56.7 us; the launch traced here: 56.4 us
  starting transfers between devices  26.3 us (46%)
  waiting for transfers between devices  13.8 us (24%)
  matrix products  8.39 us (15%)
  other arithmetic  4.51 us (8%)
  local copies, waits for them, and re-layouts  2.95 us (5%)
    ppermute x9, starting transfers between devices, shift(): lax.ppermute(value, axis, [(i, (i + step) % count) for i in range(count)])  17.9 us
    ppermute x6, starting transfers between devices, shards(): arrivals.append(lax.ppermute(outgoing, ('clus', 'pair'), pairs))  8.39 us
    ppermute x6, waiting for transfers between devices, shards(): arrivals.append(lax.ppermute(outgoing, ('clus', 'pair'), pairs))  8.37 us
    ppermute x9, waiting for transfers between devices, shift(): lax.ppermute(value, axis, [(i, (i + step) % count) for i in range(count)])  5.47 us
    mul x1, other arithmetic, shards(): scaled = [scales[d] * source for d in range(degree_top)]  1.96 us
    dot_general x3, matrix products, shards(): jnp.einsum('jrs,jts->jrt', gathered, near_blocks, preferred_element_type=...  1.93 us
    dot_general x3, matrix products, shards(): jnp.einsum('jrl,jkl->jrk', far_input, col_basis, preferred_element_type=j...  1.87 us
    convert_element_type x1, other arithmetic, shards(): iterate = (coefficients[degree_top] * source).astype(jnp.bfloat16)  1.49 us
  transfers between devices with their start and end apart: 15, of which 8 were waited for; matrix products, arithmetic and copies ran while one was open for 5% of the time, Pallas kernels for 0%

profile of v16, /device:TPU:0, one launch (start us, length us, event | category | flops | bytes accessed | tf_op | source)
XLA Modules:
  0.0 56.4 jit_solution(6495121478695273958)
XLA Ops:
  0.1 1.4 %slice.126 = f32[1]{0:T(128)} slice(f32[4]{0:T(128)} %param.10), slice={[3:4]} | slice | bytes 8 | tf_op jit(solution)/shard_map/slice | solution.py:88
  1.4 1.5 %multiply_convert_fusion = bf16[8,2048]{1,0:T(8,128)(2,1)S(1)} fusion(f32[8,2048]{1,0:T(8,128)} %param.9, f32[]{:T(128)} %bitcast.1), kind=kLoop, calls=%fused_computation.35 | loop fusion | flops 32768 | bytes 98308 | tf_op jit(solution)/shard_map/convert_element_type | solution.py:88
  2.9 0.7 %broadcast_subtract_fusion = s32[64]{0:T(128)S(1)} fusion(s32[64]{0:T(128)} %param.16, s32[]{:T(128)S(6)} %mul.50), kind=kLoop, calls=%fused_computation.136 | loop fusion | flops 64 | bytes 516 | tf_op jit(solution)/shard_map/sub | solution.py:81
  3.9 1.3 %fusion.4 = f32[64,8,16]{2,1,0:T(8,128)S(1)} fusion(bf16[64,16,256]{2,1,0:T(8,128)(2,1)} %param.15, bf16[64,8,256]{2,0,1:T(8,128)(2,1)S(1)} %fusion.28), kind=kOutput, calls=%fused_computation.4 | convolution fusion | flops 4194304 | bytes 819200 | tf_op jit(solution)/shard_map/far_partial/jrl,jkl->jrk/dot_general | solution.py:100
  5.3 0.8 %fusion.40 = f32[4,8,128]{2,1,0:T(8,128)S(1)} fusion(f32[64,128,1]{0,1,2:T(8,128)S(1)} %bitcast.182, s32[4,8]{1,0:T(4,128)S(1)} %multiply_add_fusion, s32[64]{0:T(128)} %param.17), kind=kOutput, calls=%fused_computation.57 | convolution fusion | flops 3147776 | bytes 49536 | tf_op jit(solution)/shard_map/far_partial/jc,jm->cm/dot_general | solution.py:104
  6.3 3.1 %collective-permute-start.1 = (bf16[8,2432]{1,0:T(8,128)(2,1)S(1)}, bf16[8,2432]{1,0:T(8,128)(2,1)S(1)}, u32[]{:S(2)}, u32[]{:S(2)}) collective-permute-start(bf16[8,2432]{1,0:T(8,128)(2,1)S(1)} %get-tuple-element.12), channel_id=1, source_target_pairs={{0,4},{4,8},{8,12},{12,0},{1,5},{5,9},{9,13},{13,1},{2,6},{6,10},{... | collective-permute-start | bytes 116744 | tf_op jit(solution)/shard_map/clus_exchange/ppermute | solution.py:8
  9.4 2.1 %collective-permute-start = (bf16[8,2432]{1,0:T(8,128)(2,1)S(1)}, bf16[8,2432]{1,0:T(8,128)(2,1)S(1)}, u32[]{:S(2)}, u32[]{:S(2)}) collective-permute-start(bf16[8,2432]{1,0:T(8,128)(2,1)S(1)} %get-tuple-element.24), channel_id=1, source_target_pairs={{0,12},{4,0},{8,4},{12,8},{1,13},{5,1},{9,5},{13,9},{2,14},{6,2},{... | collective-permute-start | bytes 116744 | tf_op jit(solution)/shard_map/clus_exchange/ppermute | solution.py:8
  11.5 0.7 %fusion.80 = (f32[1]{0:T(128)}, f32[1]{0:T(128)}, f32[1]{0:T(128)}) fusion(f32[4]{0:T(128)S(1)} %copy-done.5), kind=kLoop, calls=%fused_computation.142 | loop fusion | bytes 24 | tf_op jit(solution)/shard_map/clus_exchange/slice | solution.py:118
  12.2 2.0 %broadcast_multiply_fusion = (f32[8,2048]{1,0:T(8,128)S(1)}, f32[8,2048]{1,0:T(8,128)S(1)}, f32[8,2048]{1,0:T(8,128)S(1)}) fusion(f32[8,2048]{1,0:T(8,128)S(1)} %copy-done.3, f32[]{:T(128)} %bitcast.18, f32[]{:T(128)} %bitcast.12, f32[]{:T(128)} %bitcast.15), kind=kLoop, calls=%fused_computation.46 | loop fusion | flops 49152 | bytes 262156 | tf_op jit(solution)/shard_map/clus_exchange/mul | solution.py:118
  14.5 0.6 %fusion.19 = f32[16,8,256]{2,1,0:T(8,128)S(1)} fusion(bf16[16,256,256]{2,1,0:T(8,128)(2,1)S(1)} %copy-done, bf16[16,8,256]{2,0,1:T(8,128)(2,1)S(1)} %fusion.12), kind=kOutput, calls=%fused_computation.25 | convolution fusion | flops 16777216 | bytes 2293760 | tf_op jit(solution)/shard_map/near_partial/jrs,jts->jrt/dot_general | solution.py:135
  15.5 1.7 %collective-permute-start.2 = (f32[8,2176]{1,0:T(8,128)S(1)}, f32[8,2176]{1,0:T(8,128)S(1)}, u32[]{:S(2)}, u32[]{:S(2)}) collective-permute-start(f32[8,2176]{1,0:T(8,128)S(1)} %pad_maximum_fusion.3), channel_id=1, source_target_pairs={{0,2},{2,0},{1,3},{3,1},{4,6},{6,4},{5,7},{7,5},{8,10},{10,8},{9,1... | collective-permute-start | bytes 208904 | tf_op jit(solution)/shard_map/pair_sums/ppermute | solution.py:8
  17.2 1.5 %collective-permute-start.4 = (f32[8,128]{1,0:T(8,128)S(1)}, f32[8,128]{1,0:T(8,128)S(1)}, u32[]{:S(2)}, u32[]{:S(2)}) collective-permute-start(f32[8,128]{1,0:T(8,128)S(1)} %dynamic-slice_bitcast_fusion.2), channel_id=1, source_target_pairs={{0,10},{2,8},{4,14},{6,12},{8,2},{10,0},{12,6},{14,4},{1,11},{3,9}... | collective-permute-start | bytes 12296 | tf_op jit(solution)/shard_map/pair_sums/ppermute | solution.py:160
  18.7 1.2 %collective-permute-start.3 = (f32[8,128]{1,0:T(8,128)S(1)}, f32[8,128]{1,0:T(8,128)S(1)}, u32[]{:S(2)}, u32[]{:S(2)}) collective-permute-start(f32[8,128]{1,0:T(8,128)S(1)} %dynamic-slice_bitcast_fusion.2), channel_id=1, source_target_pairs={{0,8},{2,10},{4,12},{6,14},{8,0},{10,2},{12,4},{14,6},{1,9},{3,11}... | collective-permute-start | bytes 12296 | tf_op jit(solution)/shard_map/pair_sums/ppermute | solution.py:160
  20.0 2.7 %collective-permute-done.4 = f32[8,128]{1,0:T(8,128)S(1)} collective-permute-done((f32[8,128]{1,0:T(8,128)S(1)}, f32[8,128]{1,0:T(8,128)S(1)}, u32[]{:S(2)}, u32[]{:S(2)}) %collective-permute-start.4) | collective-permute-done | bytes 4128 | tf_op jit(solution)/shard_map/pair_sums/ppermute | solution.py:160
  24.5 1.9 %collective-permute-start.6 = (bf16[8,2432]{1,0:T(8,128)(2,1)S(1)}, bf16[8,2432]{1,0:T(8,128)(2,1)S(1)}, u32[]{:S(2)}, u32[]{:S(2)}) collective-permute-start(bf16[8,2432]{1,0:T(8,128)(2,1)S(1)} %get-tuple-element.22), channel_id=1, source_target_pairs={{0,4},{4,8},{8,12},{12,0},{1,5},{5,9},{9,13},{13,1},{2,6},{6,10},{... | collective-permute-start | bytes 116744 | tf_op jit(solution)/shard_map/clus_exchange/ppermute | solution.py:8
  26.4 2.0 %collective-permute-start.5 = (bf16[8,2432]{1,0:T(8,128)(2,1)S(1)}, bf16[8,2432]{1,0:T(8,128)(2,1)S(1)}, u32[]{:S(2)}, u32[]{:S(2)}) collective-permute-start(bf16[8,2432]{1,0:T(8,128)(2,1)S(1)} %get-tuple-element.23), channel_id=1, source_target_pairs={{0,12},{4,0},{8,4},{12,8},{1,13},{5,1},{9,5},{13,9},{2,14},{6,2},{... | collective-permute-start | bytes 116744 | tf_op jit(solution)/shard_map/clus_exchange/ppermute | solution.py:8
  28.4 2.0 %collective-permute-done.6 = bf16[8,2432]{1,0:T(8,128)(2,1)S(1)} collective-permute-done((bf16[8,2432]{1,0:T(8,128)(2,1)S(1)}, bf16[8,2432]{1,0:T(8,128)(2,1)S(1)}, u32[]{:S(2)}, u32[]{:S(2)}) %collective-permute-start.6) | collective-permute-done | bytes 38944 | tf_op jit(solution)/shard_map/clus_exchange/ppermute | solution.py:8
  31.0 0.6 %fusion.17 = f32[16,8,256]{2,1,0:T(8,128)S(1)} fusion(bf16[16,256,256]{2,1,0:T(8,128)(2,1)S(1)} %copy-done, bf16[16,8,256]{2,0,1:T(8,128)(2,1)S(1)} %fusion.9), kind=kOutput, calls=%fused_computation.23 | convolution fusion | flops 16777216 | bytes 2293760 | tf_op jit(solution)/shard_map/near_partial/jrs,jts->jrt/dot_general | solution.py:135
  32.0 1.7 %collective-permute-start.7 = (f32[8,2176]{1,0:T(8,128)S(1)}, f32[8,2176]{1,0:T(8,128)S(1)}, u32[]{:S(2)}, u32[]{:S(2)}) collective-permute-start(f32[8,2176]{1,0:T(8,128)S(1)} %pad_maximum_fusion.4), channel_id=1, source_target_pairs={{0,2},{2,0},{1,3},{3,1},{4,6},{6,4},{5,7},{7,5},{8,10},{10,8},{9,1... | collective-permute-start | bytes 208904 | tf_op jit(solution)/shard_map/pair_sums/ppermute | solution.py:8
  33.7 0.6 %collective-permute-start.9 = (f32[8,128]{1,0:T(8,128)S(1)}, f32[8,128]{1,0:T(8,128)S(1)}, u32[]{:S(2)}, u32[]{:S(2)}) collective-permute-start(f32[8,128]{1,0:T(8,128)S(1)} %dynamic-slice_bitcast_fusion.1), channel_id=1, source_target_pairs={{0,10},{2,8},{4,14},{6,12},{8,2},{10,0},{12,6},{14,4},{1,11},{3,9}... | collective-permute-start | bytes 12296 | tf_op jit(solution)/shard_map/pair_sums/ppermute | solution.py:160
  34.3 2.2 %collective-permute-start.8 = (f32[8,128]{1,0:T(8,128)S(1)}, f32[8,128]{1,0:T(8,128)S(1)}, u32[]{:S(2)}, u32[]{:S(2)}) collective-permute-start(f32[8,128]{1,0:T(8,128)S(1)} %dynamic-slice_bitcast_fusion.1), channel_id=1, source_target_pairs={{0,8},{2,10},{4,12},{6,14},{8,0},{10,2},{12,4},{14,6},{1,9},{3,11}... | collective-permute-start | bytes 12296 | tf_op jit(solution)/shard_map/pair_sums/ppermute | solution.py:160
  36.5 2.6 %collective-permute-done.9 = f32[8,128]{1,0:T(8,128)S(1)} collective-permute-done((f32[8,128]{1,0:T(8,128)S(1)}, f32[8,128]{1,0:T(8,128)S(1)}, u32[]{:S(2)}, u32[]{:S(2)}) %collective-permute-start.9) | collective-permute-done | bytes 4128 | tf_op jit(solution)/shard_map/pair_sums/ppermute | solution.py:160
  40.3 3.0 %collective-permute-start.11 = (bf16[8,2432]{1,0:T(8,128)(2,1)S(1)}, bf16[8,2432]{1,0:T(8,128)(2,1)S(1)}, u32[]{:S(2)}, u32[]{:S(2)}) collective-permute-start(bf16[8,2432]{1,0:T(8,128)(2,1)S(1)} %get-tuple-element.20), channel_id=1, source_target_pairs={{0,4},{4,8},{8,12},{12,0},{1,5},{5,9},{9,13},{13,1},{2,6},{6,10},{... | collective-permute-start | bytes 116744 | tf_op jit(solution)/shard_map/clus_exchange/ppermute | solution.py:8
  43.3 0.9 %collective-permute-start.10 = (bf16[8,2432]{1,0:T(8,128)(2,1)S(1)}, bf16[8,2432]{1,0:T(8,128)(2,1)S(1)}, u32[]{:S(2)}, u32[]{:S(2)}) collective-permute-start(bf16[8,2432]{1,0:T(8,128)(2,1)S(1)} %get-tuple-element.21), channel_id=1, source_target_pairs={{0,12},{4,0},{8,4},{12,8},{1,13},{5,1},{9,5},{13,9},{2,14},{6,2},{... | collective-permute-start | bytes 116744 | tf_op jit(solution)/shard_map/clus_exchange/ppermute | solution.py:8
  44.2 2.0 %collective-permute-done.11 = bf16[8,2432]{1,0:T(8,128)(2,1)S(1)} collective-permute-done((bf16[8,2432]{1,0:T(8,128)(2,1)S(1)}, bf16[8,2432]{1,0:T(8,128)(2,1)S(1)}, u32[]{:S(2)}, u32[]{:S(2)}) %collective-permute-start.11) | collective-permute-done | bytes 38944 | tf_op jit(solution)/shard_map/clus_exchange/ppermute | solution.py:8
  46.2 1.1 %collective-permute-done.10 = bf16[8,2432]{1,0:T(8,128)(2,1)S(1)} collective-permute-done((bf16[8,2432]{1,0:T(8,128)(2,1)S(1)}, bf16[8,2432]{1,0:T(8,128)(2,1)S(1)}, u32[]{:S(2)}, u32[]{:S(2)}) %collective-permute-start.10) | collective-permute-done | bytes 38944 | tf_op jit(solution)/shard_map/clus_exchange/ppermute | solution.py:8
  47.5 0.6 %fusion.15 = f32[16,8,256]{2,1,0:T(8,128)S(1)} fusion(bf16[16,256,256]{2,1,0:T(8,128)(2,1)S(1)} %copy-done, bf16[16,8,256]{2,0,1:T(8,128)(2,1)S(1)} %fusion.6), kind=kOutput, calls=%fused_computation.21 | convolution fusion | flops 16777216 | bytes 2293760 | tf_op jit(solution)/shard_map/near_partial/jrs,jts->jrt/dot_general | solution.py:135
  48.5 1.6 %collective-permute-start.12 = (f32[8,2176]{1,0:T(8,128)S(1)}, f32[8,2176]{1,0:T(8,128)S(1)}, u32[]{:S(2)}, u32[]{:S(2)}) collective-permute-start(f32[8,2176]{1,0:T(8,128)S(1)} %pad_maximum_fusion.5), channel_id=1, source_target_pairs={{0,2},{2,0},{1,3},{3,1},{4,6},{6,4},{5,7},{7,5},{8,10},{10,8},{9,1... | collective-permute-start | bytes 208904 | tf_op jit(solution)/shard_map/pair_sums/ppermute | solution.py:8
  50.1 0.9 %collective-permute-start.14 = (f32[8,128]{1,0:T(8,128)S(1)}, f32[8,128]{1,0:T(8,128)S(1)}, u32[]{:S(2)}, u32[]{:S(2)}) collective-permute-start(f32[8,128]{1,0:T(8,128)S(1)} %dynamic-slice_bitcast_fusion), channel_id=1, source_target_pairs={{0,10},{2,8},{4,14},{6,12},{8,2},{10,0},{12,6},{14,4},{1,11},{3,9}... | collective-permute-start | bytes 12296 | tf_op jit(solution)/shard_map/pair_sums/ppermute | solution.py:160
  51.0 2.0 %collective-permute-start.13 = (f32[8,128]{1,0:T(8,128)S(1)}, f32[8,128]{1,0:T(8,128)S(1)}, u32[]{:S(2)}, u32[]{:S(2)}) collective-permute-start(f32[8,128]{1,0:T(8,128)S(1)} %dynamic-slice_bitcast_fusion), channel_id=1, source_target_pairs={{0,8},{2,10},{4,12},{6,14},{8,0},{10,2},{12,4},{14,6},{1,9},{3,11}... | collective-permute-start | bytes 12296 | tf_op jit(solution)/shard_map/pair_sums/ppermute | solution.py:160
  53.0 2.5 %collective-permute-done.14 = f32[8,128]{1,0:T(8,128)S(1)} collective-permute-done((f32[8,128]{1,0:T(8,128)S(1)}, f32[8,128]{1,0:T(8,128)S(1)}, u32[]{:S(2)}, u32[]{:S(2)}) %collective-permute-start.14) | collective-permute-done | bytes 4128 | tf_op jit(solution)/shard_map/pair_sums/ppermute | solution.py:160
  55.6 0.8 %fusion.21 = f32[8,8,256]{2,1,0:T(8,128)} fusion(f32[8,8,256]{2,1,0:T(8,128)S(1)} %bitcast.188, f32[8,8,256]{2,0,1:T(8,128)S(1)} %bitcast.187, f32[8,8,16]{2,1,0:T(8,128)S(1)} %reshape.133, bf16[8,16,256]{2,1,0:T(8,128)(2,1)S(1)} %copy-done.2), kind=kOutput, calls=%fused_computation.28 | convolution fusion | flops 3178496 | bytes 266240 | tf_op jit(solution)/shard_map/far_field/crk,ckl->crl/dot_general | solution.py:164
  (88 shorter events, 5.8 us)
Async XLA Ops:
  0.0 14.4 %copy-start = (bf16[16,256,256]{2,1,0:T(8,128)(2,1)S(1)}, bf16[16,256,256]{2,1,0:T(8,128)(2,1)}, u32[]{:S(2)}) copy-start(bf16[16,256,256]{2,1,0:T(8,128)(2,1)} %param.11) | copy-start | bytes 6291460
  0.0 11.5 %copy-start.5 = (f32[4]{0:T(128)S(1)}, f32[4]{0:T(128)}, u32[]{:S(2)}) copy-start(f32[4]{0:T(128)} %param.10) | copy-start | bytes 52
  0.0 12.2 %copy-start.3 = (f32[8,2048]{1,0:T(8,128)S(1)}, f32[8,2048]{1,0:T(8,128)}, u32[]{:S(2)}) copy-start(f32[8,2048]{1,0:T(8,128)} %param.9) | copy-start | bytes 196612
  0.0 11.5 %copy-start.6 = (s32[16]{0:T(128)S(1)}, s32[16]{0:T(128)}, u32[]{:S(2)}) copy-start(s32[16]{0:T(128)} %param.13) | copy-start | bytes 196
  0.0 14.1 %copy-start.7 = (s32[16]{0:T(128)S(1)}, s32[16]{0:T(128)}, u32[]{:S(2)}) copy-start(s32[16]{0:T(128)} %param.12) | copy-start | bytes 196
  6.3 17.1 %copy-start.2 = (bf16[8,16,256]{2,1,0:T(8,128)(2,1)S(1)}, bf16[8,16,256]{2,1,0:T(8,128)(2,1)}, u32[]{:S(2)}) copy-start(bf16[8,16,256]{2,1,0:T(8,128)(2,1)} %param.14) | copy-start | bytes 196612
  6.3 7.9 %collective-permute-start.1 = (bf16[8,2432]{1,0:T(8,128)(2,1)S(1)}, bf16[8,2432]{1,0:T(8,128)(2,1)S(1)}, u32[]{:S(2)}, u32[]{:S(2)}) collective-permute-start(bf16[8,2432]{1,0:T(8,128)(2,1)S(1)} %get-tuple-element.12), channel_id=1, source_target_pairs={{0,4},{4,8},{8,12},{12,0},{1,5},{5,9},{9,13},{13,1},{2,6},{6,10},{... | collective-permute-start | bytes 116744 | tf_op jit(solution)/shard_map/clus_exchange/ppermute | solution.py:8
  9.4 4.8 %collective-permute-start = (bf16[8,2432]{1,0:T(8,128)(2,1)S(1)}, bf16[8,2432]{1,0:T(8,128)(2,1)S(1)}, u32[]{:S(2)}, u32[]{:S(2)}) collective-permute-start(bf16[8,2432]{1,0:T(8,128)(2,1)S(1)} %get-tuple-element.24), channel_id=1, source_target_pairs={{0,12},{4,0},{8,4},{12,8},{1,13},{5,1},{9,5},{13,9},{2,14},{6,2},{... | collective-permute-start | bytes 116744 | tf_op jit(solution)/shard_map/clus_exchange/ppermute | solution.py:8
  14.2 9.6 %copy-start.1 = (bf16[64,16,256]{2,1,0:T(8,128)(2,1)S(1)}, bf16[64,16,256]{2,1,0:T(8,128)(2,1)}, u32[]{:S(2)}) copy-start(bf16[64,16,256]{2,1,0:T(8,128)(2,1)} %param.15) | copy-start | bytes 1572868
  14.5 9.8 %copy-start.4 = (s32[64]{0:T(128)S(1)}, s32[64]{0:T(128)}, u32[]{:S(2)}) copy-start(s32[64]{0:T(128)} %param.17) | copy-start | bytes 772
  15.5 4.5 %collective-permute-start.2 = (f32[8,2176]{1,0:T(8,128)S(1)}, f32[8,2176]{1,0:T(8,128)S(1)}, u32[]{:S(2)}, u32[]{:S(2)}) collective-permute-start(f32[8,2176]{1,0:T(8,128)S(1)} %pad_maximum_fusion.3), channel_id=1, source_target_pairs={{0,2},{2,0},{1,3},{3,1},{4,6},{6,4},{5,7},{7,5},{8,10},{10,8},{9,1... | collective-permute-start | bytes 208904 | tf_op jit(solution)/shard_map/pair_sums/ppermute | solution.py:8
  17.2 5.5 %collective-permute-start.4 = (f32[8,128]{1,0:T(8,128)S(1)}, f32[8,128]{1,0:T(8,128)S(1)}, u32[]{:S(2)}, u32[]{:S(2)}) collective-permute-start(f32[8,128]{1,0:T(8,128)S(1)} %dynamic-slice_bitcast_fusion.2), channel_id=1, source_target_pairs={{0,10},{2,8},{4,14},{6,12},{8,2},{10,0},{12,6},{14,4},{1,11},{3,9}... | collective-permute-start | bytes 12296 | tf_op jit(solution)/shard_map/pair_sums/ppermute | solution.py:160
  18.7 4.5 %collective-permute-start.3 = (f32[8,128]{1,0:T(8,128)S(1)}, f32[8,128]{1,0:T(8,128)S(1)}, u32[]{:S(2)}, u32[]{:S(2)}) collective-permute-start(f32[8,128]{1,0:T(8,128)S(1)} %dynamic-slice_bitcast_fusion.2), channel_id=1, source_target_pairs={{0,8},{2,10},{4,12},{6,14},{8,0},{10,2},{12,4},{14,6},{1,9},{3,11}... | collective-permute-start | bytes 12296 | tf_op jit(solution)/shard_map/pair_sums/ppermute | solution.py:160
  24.5 5.9 %collective-permute-start.6 = (bf16[8,2432]{1,0:T(8,128)(2,1)S(1)}, bf16[8,2432]{1,0:T(8,128)(2,1)S(1)}, u32[]{:S(2)}, u32[]{:S(2)}) collective-permute-start(bf16[8,2432]{1,0:T(8,128)(2,1)S(1)} %get-tuple-element.22), channel_id=1, source_target_pairs={{0,4},{4,8},{8,12},{12,0},{1,5},{5,9},{9,13},{13,1},{2,6},{6,10},{... | collective-permute-start | bytes 116744 | tf_op jit(solution)/shard_map/clus_exchange/ppermute | solution.py:8
  26.4 4.3 %collective-permute-start.5 = (bf16[8,2432]{1,0:T(8,128)(2,1)S(1)}, bf16[8,2432]{1,0:T(8,128)(2,1)S(1)}, u32[]{:S(2)}, u32[]{:S(2)}) collective-permute-start(bf16[8,2432]{1,0:T(8,128)(2,1)S(1)} %get-tuple-element.23), channel_id=1, source_target_pairs={{0,12},{4,0},{8,4},{12,8},{1,13},{5,1},{9,5},{13,9},{2,14},{6,2},{... | collective-permute-start | bytes 116744 | tf_op jit(solution)/shard_map/clus_exchange/ppermute | solution.py:8
  32.0 4.5 %collective-permute-start.7 = (f32[8,2176]{1,0:T(8,128)S(1)}, f32[8,2176]{1,0:T(8,128)S(1)}, u32[]{:S(2)}, u32[]{:S(2)}) collective-permute-start(f32[8,2176]{1,0:T(8,128)S(1)} %pad_maximum_fusion.4), channel_id=1, source_target_pairs={{0,2},{2,0},{1,3},{3,1},{4,6},{6,4},{5,7},{7,5},{8,10},{10,8},{9,1... | collective-permute-start | bytes 208904 | tf_op jit(solution)/shard_map/pair_sums/ppermute | solution.py:8
  33.7 5.4 %collective-permute-start.9 = (f32[8,128]{1,0:T(8,128)S(1)}, f32[8,128]{1,0:T(8,128)S(1)}, u32[]{:S(2)}, u32[]{:S(2)}) collective-permute-start(f32[8,128]{1,0:T(8,128)S(1)} %dynamic-slice_bitcast_fusion.1), channel_id=1, source_target_pairs={{0,10},{2,8},{4,14},{6,12},{8,2},{10,0},{12,6},{14,4},{1,11},{3,9}... | collective-permute-start | bytes 12296 | tf_op jit(solution)/shard_map/pair_sums/ppermute | solution.py:160
  34.3 4.8 %collective-permute-start.8 = (f32[8,128]{1,0:T(8,128)S(1)}, f32[8,128]{1,0:T(8,128)S(1)}, u32[]{:S(2)}, u32[]{:S(2)}) collective-permute-start(f32[8,128]{1,0:T(8,128)S(1)} %dynamic-slice_bitcast_fusion.1), channel_id=1, source_target_pairs={{0,8},{2,10},{4,12},{6,14},{8,0},{10,2},{12,4},{14,6},{1,9},{3,11}... | collective-permute-start | bytes 12296 | tf_op jit(solution)/shard_map/pair_sums/ppermute | solution.py:160
  40.3 5.9 %collective-permute-start.11 = (bf16[8,2432]{1,0:T(8,128)(2,1)S(1)}, bf16[8,2432]{1,0:T(8,128)(2,1)S(1)}, u32[]{:S(2)}, u32[]{:S(2)}) collective-permute-start(bf16[8,2432]{1,0:T(8,128)(2,1)S(1)} %get-tuple-element.20), channel_id=1, source_target_pairs={{0,4},{4,8},{8,12},{12,0},{1,5},{5,9},{9,13},{13,1},{2,6},{6,10},{... | collective-permute-start | bytes 116744 | tf_op jit(solution)/shard_map/clus_exchange/ppermute | solution.py:8
  43.3 4.0 %collective-permute-start.10 = (bf16[8,2432]{1,0:T(8,128)(2,1)S(1)}, bf16[8,2432]{1,0:T(8,128)(2,1)S(1)}, u32[]{:S(2)}, u32[]{:S(2)}) collective-permute-start(bf16[8,2432]{1,0:T(8,128)(2,1)S(1)} %get-tuple-element.21), channel_id=1, source_target_pairs={{0,12},{4,0},{8,4},{12,8},{1,13},{5,1},{9,5},{13,9},{2,14},{6,2},{... | collective-permute-start | bytes 116744 | tf_op jit(solution)/shard_map/clus_exchange/ppermute | solution.py:8
  48.5 4.5 %collective-permute-start.12 = (f32[8,2176]{1,0:T(8,128)S(1)}, f32[8,2176]{1,0:T(8,128)S(1)}, u32[]{:S(2)}, u32[]{:S(2)}) collective-permute-start(f32[8,2176]{1,0:T(8,128)S(1)} %pad_maximum_fusion.5), channel_id=1, source_target_pairs={{0,2},{2,0},{1,3},{3,1},{4,6},{6,4},{5,7},{7,5},{8,10},{10,8},{9,1... | collective-permute-start | bytes 208904 | tf_op jit(solution)/shard_map/pair_sums/ppermute | solution.py:8
  50.1 5.4 %collective-permute-start.14 = (f32[8,128]{1,0:T(8,128)S(1)}, f32[8,128]{1,0:T(8,128)S(1)}, u32[]{:S(2)}, u32[]{:S(2)}) collective-permute-start(f32[8,128]{1,0:T(8,128)S(1)} %dynamic-slice_bitcast_fusion), channel_id=1, source_target_pairs={{0,10},{2,8},{4,14},{6,12},{8,2},{10,0},{12,6},{14,4},{1,11},{3,9}... | collective-permute-start | bytes 12296 | tf_op jit(solution)/shard_map/pair_sums/ppermute | solution.py:160
  51.0 4.5 %collective-permute-start.13 = (f32[8,128]{1,0:T(8,128)S(1)}, f32[8,128]{1,0:T(8,128)S(1)}, u32[]{:S(2)}, u32[]{:S(2)}) collective-permute-start(f32[8,128]{1,0:T(8,128)S(1)} %dynamic-slice_bitcast_fusion), channel_id=1, source_target_pairs={{0,8},{2,10},{4,12},{6,14},{8,0},{10,2},{12,4},{14,6},{1,9},{3,11}... | collective-permute-start | bytes 12296 | tf_op jit(solution)/shard_map/pair_sums/ppermute | solution.py:160

commit v17 on v15

--- a/solution.py
+++ b/solution.py
@@ -23,6 +23,15 @@
         parts[..., k * width : (k + 1) * width].astype(jnp.float32) for k in range(3)
     )
     return (high + middle) + low
+
+
+def one_hot_sum(hot, values):
+    summed = jnp.einsum(
+        "jc,jm->cm", hot.astype(jnp.bfloat16), split_three(values),
+        preferred_element_type=jnp.float32,
+    )
+    width = values.shape[-1]
+    return (summed[:, :width] + summed[:, width : 2 * width]) + summed[:, 2 * width :]
 
 
 def pair_total(value, pair_count, pair_index):
@@ -86,7 +95,7 @@
                 "jrl,jkl->jrk", far_input, col_basis, preferred_element_type=jnp.float32
             )
             coef = coef.reshape(coef.shape[0], coef_size)
-            partial_value = jnp.einsum("jc,jm->cm", far_hot, coef, precision=lax.Precision.HIGHEST)
+            partial_value = one_hot_sum(far_hot, coef)
             partial_value = partial_value.reshape(peer_count, clusters_here, coef_size)
         with jax.named_scope("clus_exchange"):
             far_mine = partial_value[my_index]
@@ -126,9 +135,7 @@
                 "jrs,jts->jrt", gathered, near_blocks, preferred_element_type=jnp.float32
             )
             contrib = contrib.reshape(contrib.shape[0], iterate_size)
-            near_part = jnp.einsum(
-                "jc,jm->cm", target_hot, contrib, precision=lax.Precision.HIGHEST
-            )
+            near_part = one_hot_sum(target_hot, contrib)
         with jax.named_scope("pair_sums"):
             if scaled is None:
                 scaled = [coefficients[d] * source for d in range(degree_top)]

time: 51.3 us -> 51.7 us (level)
  no operation moved by 1% of the time
where the time goes in v17:
time: 51.7 us; the launch traced here: 51.4 us
  starting transfers between devices  25.1 us (49%)
  waiting for transfers between devices  9.65 us (19%)
  matrix products  8.53 us (16%)
  other arithmetic  4.69 us (9%)
  local copies, waits for them, and re-layouts  2.94 us (6%)
    ppermute x15, starting transfers between devices, shift(): lax.ppermute(value, axis, [(i, (i + step) % count) for i in range(count)])  25.1 us
    ppermute x15, waiting for transfers between devices, shift(): lax.ppermute(value, axis, [(i, (i + step) % count) for i in range(count)])  9.65 us
    dot_general x6, matrix products, one_hot_sum(): jnp.einsum('jc,jm->cm', hot.astype(jnp.bfloat16), split_three(values), pr...  2.2 us
    mul x1, other arithmetic, shards(): scaled = [scales[d] * source for d in range(degree_top)]  2.01 us
    dot_general x3, matrix products, shards(): jnp.einsum('jrs,jts->jrt', gathered, near_blocks, preferred_element_type=...  1.93 us
    dot_general x3, matrix products, shards(): jnp.einsum('jrl,jkl->jrk', far_input, col_basis, preferred_element_type=j...  1.87 us
    convert_element_type x1, other arithmetic, shards(): iterate = (coefficients[degree_top] * source).astype(jnp.bfloat16)  1.49 us
    slice x1, local copies, waits for them, and re-layouts, shards(): iterate = (coefficients[degree_top] * source).astype(jnp.bfloat16)  1.38 us
  transfers between devices with their start and end apart: 15, of which 8 were waited for; matrix products, arithmetic and copies ran while one was open for 13% of the time, Pallas kernels for 0%

profile of v17, /device:TPU:0, one launch (start us, length us, event | category | flops | bytes accessed | tf_op | source)
XLA Modules:
  0.0 51.4 jit_solution(4673752028757408414)
XLA Ops:
  0.0 1.4 %slice.180 = f32[1]{0:T(128)} slice(f32[4]{0:T(128)} %param.10), slice={[3:4]} | slice | bytes 8 | tf_op jit(solution)/shard_map/slice | solution.py:82
  1.4 0.7 %broadcast_subtract_fusion = s32[64]{0:T(128)S(1)} fusion(s32[64]{0:T(128)} %param.16, s32[]{:T(128)S(6)} %mul.50), kind=kLoop, calls=%fused_computation.210 | loop fusion | flops 64 | bytes 516 | tf_op jit(solution)/shard_map/sub | solution.py:75
  2.1 1.5 %multiply_convert_fusion = bf16[8,2048]{1,0:T(8,128)(2,1)S(1)} fusion(f32[8,2048]{1,0:T(8,128)} %param.9, f32[]{:T(128)} %bitcast.1), kind=kLoop, calls=%fused_computation.107 | loop fusion | flops 32768 | bytes 98308 | tf_op jit(solution)/shard_map/convert_element_type | solution.py:82
  3.8 1.3 %fusion.4 = f32[64,8,16]{2,1,0:T(8,128)S(1)} fusion(bf16[64,16,256]{2,1,0:T(8,128)(2,1)} %param.15, bf16[64,8,256]{2,0,1:T(8,128)(2,1)S(1)} %fusion.70), kind=kOutput, calls=%fused_computation.4 | convolution fusion | flops 4194304 | bytes 819200 | tf_op jit(solution)/shard_map/far_partial/jrl,jkl->jrk/dot_general | solution.py:94
  5.3 0.9 %fusion.36 = f32[32,384]{1,0:T(8,128)S(1)} fusion(bf16[64,128]{0,1:T(8,128)(2,1)S(1)} %get-tuple-element.36, bf16[64,128]{0,1:T(8,128)(2,1)S(1)} %get-tuple-element.37, bf16[64,128]{0,1:T(8,128)(2,1)S(1)} %get-tuple-element.35, s32[64]{0:T(128)} %param.17), kind=kOutput, calls=%fused_computation.48 | convolution fusion | flops 1726464 | bytes 98560 | tf_op jit(solution)/shard_map/far_partial/jc,jm->cm/dot_general | solution.py:29
  6.3 3.0 %collective-permute-start.3 = (f32[1,8,128]{2,1,0:T(8,128)S(1)}, f32[1,8,128]{2,1,0:T(8,128)S(1)}, u32[]{:S(2)}, u32[]{:S(2)}) collective-permute-start(f32[1,8,128]{2,1,0:T(8,128)S(1)} %constant_dynamic-slice_fusion.2), channel_id=1, source_target_pairs={{0,2},{2,0},{1,3},{3,1},{4,6},{6,4},{5,7},{7,5},{8,10},{10,8},{9,1... | collective-permute-start | bytes 12296 | tf_op jit(solution)/shard_map/clus_exchange/ppermute | solution.py:8
  9.4 1.6 %collective-permute-start.1 = (bf16[8,2432]{1,0:T(8,128)(2,1)S(1)}, bf16[8,2432]{1,0:T(8,128)(2,1)S(1)}, u32[]{:S(2)}, u32[]{:S(2)}) collective-permute-start(bf16[8,2432]{1,0:T(8,128)(2,1)S(1)} %get-tuple-element.12), channel_id=1, source_target_pairs={{0,4},{4,8},{8,12},{12,0},{1,5},{5,9},{9,13},{13,1},{2,6},{6,10},{... | collective-permute-start | bytes 116744 | tf_op jit(solution)/shard_map/clus_exchange/ppermute | solution.py:8
  11.0 2.2 %collective-permute-start = (bf16[8,2432]{1,0:T(8,128)(2,1)S(1)}, bf16[8,2432]{1,0:T(8,128)(2,1)S(1)}, u32[]{:S(2)}, u32[]{:S(2)}) collective-permute-start(bf16[8,2432]{1,0:T(8,128)(2,1)S(1)} %get-tuple-element.42), channel_id=1, source_target_pairs={{0,12},{4,0},{8,4},{12,8},{1,13},{5,1},{9,5},{13,9},{2,14},{6,2},{... | collective-permute-start | bytes 116744 | tf_op jit(solution)/shard_map/clus_exchange/ppermute | solution.py:8
  13.3 0.7 %fusion.119 = (f32[1]{0:T(128)}, f32[1]{0:T(128)}, f32[1]{0:T(128)}) fusion(f32[4]{0:T(128)S(1)} %copy-done.4), kind=kLoop, calls=%fused_computation.222 | loop fusion | bytes 24 | tf_op jit(solution)/shard_map/clus_exchange/slice | solution.py:112
  13.9 2.0 %broadcast_multiply_fusion = (f32[8,2048]{1,0:T(8,128)S(1)}, f32[8,2048]{1,0:T(8,128)S(1)}, f32[8,2048]{1,0:T(8,128)S(1)}) fusion(f32[8,2048]{1,0:T(8,128)S(1)} %copy-done.3, f32[]{:T(128)} %bitcast.18, f32[]{:T(128)} %bitcast.12, f32[]{:T(128)} %bitcast.15), kind=kLoop, calls=%fused_computation.118 | loop fusion | flops 49152 | bytes 262156 | tf_op jit(solution)/shard_map/clus_exchange/mul | solution.py:112
  16.3 0.6 %fusion.61 = f32[16,8,256]{2,1,0:T(8,128)S(1)} fusion(bf16[16,256,256]{2,1,0:T(8,128)(2,1)S(1)} %copy-done, bf16[16,8,256]{2,0,1:T(8,128)(2,1)S(1)} %fusion.33), kind=kOutput, calls=%fused_computation.97 | convolution fusion | flops 16777216 | bytes 2293760 | tf_op jit(solution)/shard_map/near_partial/jrs,jts->jrt/dot_general | solution.py:134
  17.3 0.4 collective-permute-start.2
  17.8 1.7 %collective-permute-start.4 = (f32[8,128]{1,0:T(8,128)S(1)}, f32[8,128]{1,0:T(8,128)S(1)}, u32[]{:S(2)}, u32[]{:S(2)}) collective-permute-start(f32[8,128]{1,0:T(8,128)S(1)} %add_bitcast_fusion.2), channel_id=1, source_target_pairs={{0,8},{4,12},{8,0},{12,4},{1,9},{5,13},{9,1},{13,5},{2,10},{6,14},... | collective-permute-start | bytes 12296 | tf_op jit(solution)/shard_map/pair_sums/ppermute | solution.py:8
  19.5 2.2 %collective-permute-done.2 = f32[8,2176]{1,0:T(8,128)S(1)} collective-permute-done((f32[8,2176]{1,0:T(8,128)S(1)}, f32[8,2176]{1,0:T(8,128)S(1)}, u32[]{:S(2)}, u32[]{:S(2)}) %collective-permute-start.2) | collective-permute-done | bytes 69664 | tf_op jit(solution)/shard_map/pair_sums/ppermute | solution.py:8
  21.7 0.6 %collective-permute-done.4 = f32[8,128]{1,0:T(8,128)S(1)} collective-permute-done((f32[8,128]{1,0:T(8,128)S(1)}, f32[8,128]{1,0:T(8,128)S(1)}, u32[]{:S(2)}, u32[]{:S(2)}) %collective-permute-start.4) | collective-permute-done | bytes 4128 | tf_op jit(solution)/shard_map/pair_sums/ppermute | solution.py:8
  23.6 0.7 %collective-permute-start.6 = (bf16[8,2432]{1,0:T(8,128)(2,1)S(1)}, bf16[8,2432]{1,0:T(8,128)(2,1)S(1)}, u32[]{:S(2)}, u32[]{:S(2)}) collective-permute-start(bf16[8,2432]{1,0:T(8,128)(2,1)S(1)} %get-tuple-element.40), channel_id=1, source_target_pairs={{0,4},{4,8},{8,12},{12,0},{1,5},{5,9},{9,13},{13,1},{2,6},{6,10},{... | collective-permute-start | bytes 116744 | tf_op jit(solution)/shard_map/clus_exchange/ppermute | solution.py:8
  24.4 3.1 %collective-permute-start.5 = (bf16[8,2432]{1,0:T(8,128)(2,1)S(1)}, bf16[8,2432]{1,0:T(8,128)(2,1)S(1)}, u32[]{:S(2)}, u32[]{:S(2)}) collective-permute-start(bf16[8,2432]{1,0:T(8,128)(2,1)S(1)} %get-tuple-element.41), channel_id=1, source_target_pairs={{0,12},{4,0},{8,4},{12,8},{1,13},{5,1},{9,5},{13,9},{2,14},{6,2},{... | collective-permute-start | bytes 116744 | tf_op jit(solution)/shard_map/clus_exchange/ppermute | solution.py:8
  27.5 1.6 %collective-permute-start.8 = (f32[1,8,128]{2,1,0:T(8,128)S(1)}, f32[1,8,128]{2,1,0:T(8,128)S(1)}, u32[]{:S(2)}, u32[]{:S(2)}) collective-permute-start(f32[1,8,128]{2,1,0:T(8,128)S(1)} %constant_dynamic-slice_fusion.1), channel_id=1, source_target_pairs={{0,2},{2,0},{1,3},{3,1},{4,6},{6,4},{5,7},{7,5},{8,10},{10,8},{9,1... | collective-permute-start | bytes 12296 | tf_op jit(solution)/shard_map/clus_exchange/ppermute | solution.py:8
  29.8 0.6 %fusion.59 = f32[16,8,256]{2,1,0:T(8,128)S(1)} fusion(bf16[16,256,256]{2,1,0:T(8,128)(2,1)S(1)} %copy-done, bf16[16,8,256]{2,0,1:T(8,128)(2,1)S(1)} %fusion.30), kind=kOutput, calls=%fused_computation.95 | convolution fusion | flops 16777216 | bytes 2293760 | tf_op jit(solution)/shard_map/near_partial/jrs,jts->jrt/dot_general | solution.py:134
  30.9 1.7 %collective-permute-start.7 = (f32[8,2176]{1,0:T(8,128)S(1)}, f32[8,2176]{1,0:T(8,128)S(1)}, u32[]{:S(2)}, u32[]{:S(2)}) collective-permute-start(f32[8,2176]{1,0:T(8,128)S(1)} %pad_maximum_fusion.4), channel_id=1, source_target_pairs={{0,2},{2,0},{1,3},{3,1},{4,6},{6,4},{5,7},{7,5},{8,10},{10,8},{9,1... | collective-permute-start | bytes 208904 | tf_op jit(solution)/shard_map/pair_sums/ppermute | solution.py:8
  32.6 1.6 %collective-permute-start.9 = (f32[8,128]{1,0:T(8,128)S(1)}, f32[8,128]{1,0:T(8,128)S(1)}, u32[]{:S(2)}, u32[]{:S(2)}) collective-permute-start(f32[8,128]{1,0:T(8,128)S(1)} %add_bitcast_fusion.1), channel_id=1, source_target_pairs={{0,8},{4,12},{8,0},{12,4},{1,9},{5,13},{9,1},{13,5},{2,10},{6,14},... | collective-permute-start | bytes 12296 | tf_op jit(solution)/shard_map/pair_sums/ppermute | solution.py:8
  34.2 1.0 %collective-permute-done.7 = f32[8,2176]{1,0:T(8,128)S(1)} collective-permute-done((f32[8,2176]{1,0:T(8,128)S(1)}, f32[8,2176]{1,0:T(8,128)S(1)}, u32[]{:S(2)}, u32[]{:S(2)}) %collective-permute-start.7) | collective-permute-done | bytes 69664 | tf_op jit(solution)/shard_map/pair_sums/ppermute | solution.py:8
  35.3 1.8 %collective-permute-done.9 = f32[8,128]{1,0:T(8,128)S(1)} collective-permute-done((f32[8,128]{1,0:T(8,128)S(1)}, f32[8,128]{1,0:T(8,128)S(1)}, u32[]{:S(2)}, u32[]{:S(2)}) %collective-permute-start.9) | collective-permute-done | bytes 4128 | tf_op jit(solution)/shard_map/pair_sums/ppermute | solution.py:8
  38.4 1.4 %collective-permute-start.11 = (bf16[8,2432]{1,0:T(8,128)(2,1)S(1)}, bf16[8,2432]{1,0:T(8,128)(2,1)S(1)}, u32[]{:S(2)}, u32[]{:S(2)}) collective-permute-start(bf16[8,2432]{1,0:T(8,128)(2,1)S(1)} %get-tuple-element.38), channel_id=1, source_target_pairs={{0,4},{4,8},{8,12},{12,0},{1,5},{5,9},{9,13},{13,1},{2,6},{6,10},{... | collective-permute-start | bytes 116744 | tf_op jit(solution)/shard_map/clus_exchange/ppermute | solution.py:8
  39.8 2.4 %collective-permute-start.10 = (bf16[8,2432]{1,0:T(8,128)(2,1)S(1)}, bf16[8,2432]{1,0:T(8,128)(2,1)S(1)}, u32[]{:S(2)}, u32[]{:S(2)}) collective-permute-start(bf16[8,2432]{1,0:T(8,128)(2,1)S(1)} %get-tuple-element.39), channel_id=1, source_target_pairs={{0,12},{4,0},{8,4},{12,8},{1,13},{5,1},{9,5},{13,9},{2,14},{6,2},{... | collective-permute-start | bytes 116744 | tf_op jit(solution)/shard_map/clus_exchange/ppermute | solution.py:8
  42.7 1.6 %collective-permute-done.11 = bf16[8,2432]{1,0:T(8,128)(2,1)S(1)} collective-permute-done((bf16[8,2432]{1,0:T(8,128)(2,1)S(1)}, bf16[8,2432]{1,0:T(8,128)(2,1)S(1)}, u32[]{:S(2)}, u32[]{:S(2)}) %collective-permute-start.11) | collective-permute-done | bytes 38944 | tf_op jit(solution)/shard_map/clus_exchange/ppermute | solution.py:8
  44.5 0.6 %fusion.57 = f32[16,8,256]{2,1,0:T(8,128)S(1)} fusion(bf16[16,256,256]{2,1,0:T(8,128)(2,1)S(1)} %copy-done, bf16[16,8,256]{2,0,1:T(8,128)(2,1)S(1)} %fusion.27), kind=kOutput, calls=%fused_computation.93 | convolution fusion | flops 16777216 | bytes 2293760 | tf_op jit(solution)/shard_map/near_partial/jrs,jts->jrt/dot_general | solution.py:134
  45.6 0.4 collective-permute-start.12
  46.0 2.4 %collective-permute-start.14 = (f32[8,128]{1,0:T(8,128)S(1)}, f32[8,128]{1,0:T(8,128)S(1)}, u32[]{:S(2)}, u32[]{:S(2)}) collective-permute-start(f32[8,128]{1,0:T(8,128)S(1)} %add_bitcast_fusion), channel_id=1, source_target_pairs={{0,8},{4,12},{8,0},{12,4},{1,9},{5,13},{9,1},{13,5},{2,10},{6,14},... | collective-permute-start | bytes 12296 | tf_op jit(solution)/shard_map/pair_sums/ppermute | solution.py:8
  48.5 1.5 %collective-permute-done.12 = f32[8,2176]{1,0:T(8,128)S(1)} collective-permute-done((f32[8,2176]{1,0:T(8,128)S(1)}, f32[8,2176]{1,0:T(8,128)S(1)}, u32[]{:S(2)}, u32[]{:S(2)}) %collective-permute-start.12) | collective-permute-done | bytes 69664 | tf_op jit(solution)/shard_map/pair_sums/ppermute | solution.py:8
  50.0 0.5 %collective-permute-done.14 = f32[8,128]{1,0:T(8,128)S(1)} collective-permute-done((f32[8,128]{1,0:T(8,128)S(1)}, f32[8,128]{1,0:T(8,128)S(1)}, u32[]{:S(2)}, u32[]{:S(2)}) %collective-permute-start.14) | collective-permute-done | bytes 4128 | tf_op jit(solution)/shard_map/pair_sums/ppermute | solution.py:8
  50.6 0.8 %fusion.63 = f32[8,8,256]{2,1,0:T(8,128)} fusion(f32[8,8,256]{2,1,0:T(8,128)S(1)} %bitcast.197, f32[8,8,256]{2,0,1:T(8,128)S(1)} %bitcast.196, f32[8,8,16]{2,1,0:T(8,128)S(1)} %reshape.121, bf16[8,16,256]{2,1,0:T(8,128)(2,1)S(1)} %copy-done.2), kind=kOutput, calls=%fused_computation.100 | convolution fusion | flops 3178496 | bytes 266240 | tf_op jit(solution)/shard_map/far_field/crk,ckl->crl/dot_general | solution.py:152
  (102 shorter events, 5.9 us)
Async XLA Ops:
  0.0 16.2 %copy-start = (bf16[16,256,256]{2,1,0:T(8,128)(2,1)S(1)}, bf16[16,256,256]{2,1,0:T(8,128)(2,1)}, u32[]{:S(2)}) copy-start(bf16[16,256,256]{2,1,0:T(8,128)(2,1)} %param.11) | copy-start | bytes 6291460
  0.0 13.3 %copy-start.4 = (f32[4]{0:T(128)S(1)}, f32[4]{0:T(128)}, u32[]{:S(2)}) copy-start(f32[4]{0:T(128)} %param.10) | copy-start | bytes 52
  0.0 13.9 %copy-start.3 = (f32[8,2048]{1,0:T(8,128)S(1)}, f32[8,2048]{1,0:T(8,128)}, u32[]{:S(2)}) copy-start(f32[8,2048]{1,0:T(8,128)} %param.9) | copy-start | bytes 196612
  0.0 13.2 %copy-start.5 = (s32[16]{0:T(128)S(1)}, s32[16]{0:T(128)}, u32[]{:S(2)}) copy-start(s32[16]{0:T(128)} %param.13) | copy-start | bytes 196
  0.0 15.9 %copy-start.6 = (s32[16]{0:T(128)S(1)}, s32[16]{0:T(128)}, u32[]{:S(2)}) copy-start(s32[16]{0:T(128)} %param.12) | copy-start | bytes 196
  6.3 11.5 %collective-permute-start.3 = (f32[1,8,128]{2,1,0:T(8,128)S(1)}, f32[1,8,128]{2,1,0:T(8,128)S(1)}, u32[]{:S(2)}, u32[]{:S(2)}) collective-permute-start(f32[1,8,128]{2,1,0:T(8,128)S(1)} %constant_dynamic-slice_fusion.2), channel_id=1, source_target_pairs={{0,2},{2,0},{1,3},{3,1},{4,6},{6,4},{5,7},{7,5},{8,10},{10,8},{9,1... | collective-permute-start | bytes 12296 | tf_op jit(solution)/shard_map/clus_exchange/ppermute | solution.py:8
  9.4 6.6 %collective-permute-start.1 = (bf16[8,2432]{1,0:T(8,128)(2,1)S(1)}, bf16[8,2432]{1,0:T(8,128)(2,1)S(1)}, u32[]{:S(2)}, u32[]{:S(2)}) collective-permute-start(bf16[8,2432]{1,0:T(8,128)(2,1)S(1)} %get-tuple-element.12), channel_id=1, source_target_pairs={{0,4},{4,8},{8,12},{12,0},{1,5},{5,9},{9,13},{13,1},{2,6},{6,10},{... | collective-permute-start | bytes 116744 | tf_op jit(solution)/shard_map/clus_exchange/ppermute | solution.py:8
  11.0 5.0 %collective-permute-start = (bf16[8,2432]{1,0:T(8,128)(2,1)S(1)}, bf16[8,2432]{1,0:T(8,128)(2,1)S(1)}, u32[]{:S(2)}, u32[]{:S(2)}) collective-permute-start(bf16[8,2432]{1,0:T(8,128)(2,1)S(1)} %get-tuple-element.42), channel_id=1, source_target_pairs={{0,12},{4,0},{8,4},{12,8},{1,13},{5,1},{9,5},{13,9},{2,14},{6,2},{... | collective-permute-start | bytes 116744 | tf_op jit(solution)/shard_map/clus_exchange/ppermute | solution.py:8
  16.2 6.1 %copy-start.2 = (bf16[8,16,256]{2,1,0:T(8,128)(2,1)S(1)}, bf16[8,16,256]{2,1,0:T(8,128)(2,1)}, u32[]{:S(2)}) copy-start(bf16[8,16,256]{2,1,0:T(8,128)(2,1)} %param.14) | copy-start | bytes 196612
  16.2 6.6 %copy-start.1 = (bf16[64,16,256]{2,1,0:T(8,128)(2,1)S(1)}, bf16[64,16,256]{2,1,0:T(8,128)(2,1)}, u32[]{:S(2)}) copy-start(bf16[64,16,256]{2,1,0:T(8,128)(2,1)} %param.15) | copy-start | bytes 1572868
  16.9 6.4 %copy-start.7 = (s32[64]{0:T(128)S(1)}, s32[64]{0:T(128)}, u32[]{:S(2)}) copy-start(s32[64]{0:T(128)} %param.17) | copy-start | bytes 772
  17.3 4.4 %collective-permute-start.2 = (f32[8,2176]{1,0:T(8,128)S(1)}, f32[8,2176]{1,0:T(8,128)S(1)}, u32[]{:S(2)}, u32[]{:S(2)}) collective-permute-start(f32[8,2176]{1,0:T(8,128)S(1)} %pad_maximum_fusion.3), channel_id=1, source_target_pairs={{0,2},{2,0},{1,3},{3,1},{4,6},{6,4},{5,7},{7,5},{8,10},{10,8},{9,1... | collective-permute-start | bytes 208904 | tf_op jit(solution)/shard_map/pair_sums/ppermute | solution.py:8
  17.8 4.5 %collective-permute-start.4 = (f32[8,128]{1,0:T(8,128)S(1)}, f32[8,128]{1,0:T(8,128)S(1)}, u32[]{:S(2)}, u32[]{:S(2)}) collective-permute-start(f32[8,128]{1,0:T(8,128)S(1)} %add_bitcast_fusion.2), channel_id=1, source_target_pairs={{0,8},{4,12},{8,0},{12,4},{1,9},{5,13},{9,1},{13,5},{2,10},{6,14},... | collective-permute-start | bytes 12296 | tf_op jit(solution)/shard_map/pair_sums/ppermute | solution.py:8
  23.6 5.9 %collective-permute-start.6 = (bf16[8,2432]{1,0:T(8,128)(2,1)S(1)}, bf16[8,2432]{1,0:T(8,128)(2,1)S(1)}, u32[]{:S(2)}, u32[]{:S(2)}) collective-permute-start(bf16[8,2432]{1,0:T(8,128)(2,1)S(1)} %get-tuple-element.40), channel_id=1, source_target_pairs={{0,4},{4,8},{8,12},{12,0},{1,5},{5,9},{9,13},{13,1},{2,6},{6,10},{... | collective-permute-start | bytes 116744 | tf_op jit(solution)/shard_map/clus_exchange/ppermute | solution.py:8
  24.4 5.2 %collective-permute-start.5 = (bf16[8,2432]{1,0:T(8,128)(2,1)S(1)}, bf16[8,2432]{1,0:T(8,128)(2,1)S(1)}, u32[]{:S(2)}, u32[]{:S(2)}) collective-permute-start(bf16[8,2432]{1,0:T(8,128)(2,1)S(1)} %get-tuple-element.41), channel_id=1, source_target_pairs={{0,12},{4,0},{8,4},{12,8},{1,13},{5,1},{9,5},{13,9},{2,14},{6,2},{... | collective-permute-start | bytes 116744 | tf_op jit(solution)/shard_map/clus_exchange/ppermute | solution.py:8
  27.5 5.1 %collective-permute-start.8 = (f32[1,8,128]{2,1,0:T(8,128)S(1)}, f32[1,8,128]{2,1,0:T(8,128)S(1)}, u32[]{:S(2)}, u32[]{:S(2)}) collective-permute-start(f32[1,8,128]{2,1,0:T(8,128)S(1)} %constant_dynamic-slice_fusion.1), channel_id=1, source_target_pairs={{0,2},{2,0},{1,3},{3,1},{4,6},{6,4},{5,7},{7,5},{8,10},{10,8},{9,1... | collective-permute-start | bytes 12296 | tf_op jit(solution)/shard_map/clus_exchange/ppermute | solution.py:8
  30.9 4.4 %collective-permute-start.7 = (f32[8,2176]{1,0:T(8,128)S(1)}, f32[8,2176]{1,0:T(8,128)S(1)}, u32[]{:S(2)}, u32[]{:S(2)}) collective-permute-start(f32[8,2176]{1,0:T(8,128)S(1)} %pad_maximum_fusion.4), channel_id=1, source_target_pairs={{0,2},{2,0},{1,3},{3,1},{4,6},{6,4},{5,7},{7,5},{8,10},{10,8},{9,1... | collective-permute-start | bytes 208904 | tf_op jit(solution)/shard_map/pair_sums/ppermute | solution.py:8
  32.6 4.5 %collective-permute-start.9 = (f32[8,128]{1,0:T(8,128)S(1)}, f32[8,128]{1,0:T(8,128)S(1)}, u32[]{:S(2)}, u32[]{:S(2)}) collective-permute-start(f32[8,128]{1,0:T(8,128)S(1)} %add_bitcast_fusion.1), channel_id=1, source_target_pairs={{0,8},{4,12},{8,0},{12,4},{1,9},{5,13},{9,1},{13,5},{2,10},{6,14},... | collective-permute-start | bytes 12296 | tf_op jit(solution)/shard_map/pair_sums/ppermute | solution.py:8
  38.4 5.9 %collective-permute-start.11 = (bf16[8,2432]{1,0:T(8,128)(2,1)S(1)}, bf16[8,2432]{1,0:T(8,128)(2,1)S(1)}, u32[]{:S(2)}, u32[]{:S(2)}) collective-permute-start(bf16[8,2432]{1,0:T(8,128)(2,1)S(1)} %get-tuple-element.38), channel_id=1, source_target_pairs={{0,4},{4,8},{8,12},{12,0},{1,5},{5,9},{9,13},{13,1},{2,6},{6,10},{... | collective-permute-start | bytes 116744 | tf_op jit(solution)/shard_map/clus_exchange/ppermute | solution.py:8
  39.8 4.4 %collective-permute-start.10 = (bf16[8,2432]{1,0:T(8,128)(2,1)S(1)}, bf16[8,2432]{1,0:T(8,128)(2,1)S(1)}, u32[]{:S(2)}, u32[]{:S(2)}) collective-permute-start(bf16[8,2432]{1,0:T(8,128)(2,1)S(1)} %get-tuple-element.39), channel_id=1, source_target_pairs={{0,12},{4,0},{8,4},{12,8},{1,13},{5,1},{9,5},{13,9},{2,14},{6,2},{... | collective-permute-start | bytes 116744 | tf_op jit(solution)/shard_map/clus_exchange/ppermute | solution.py:8
  42.3 3.7 %collective-permute-start.13 = (f32[1,8,128]{2,1,0:T(8,128)S(1)}, f32[1,8,128]{2,1,0:T(8,128)S(1)}, u32[]{:S(2)}, u32[]{:S(2)}) collective-permute-start(f32[1,8,128]{2,1,0:T(8,128)S(1)} %constant_dynamic-slice_fusion), channel_id=1, source_target_pairs={{0,2},{2,0},{1,3},{3,1},{4,6},{6,4},{5,7},{7,5},{8,10},{10,8},{9,1... | collective-permute-start | bytes 12296 | tf_op jit(solution)/shard_map/clus_exchange/ppermute | solution.py:8
  45.6 4.4 %collective-permute-start.12 = (f32[8,2176]{1,0:T(8,128)S(1)}, f32[8,2176]{1,0:T(8,128)S(1)}, u32[]{:S(2)}, u32[]{:S(2)}) collective-permute-start(f32[8,2176]{1,0:T(8,128)S(1)} %pad_maximum_fusion.5), channel_id=1, source_target_pairs={{0,2},{2,0},{1,3},{3,1},{4,6},{6,4},{5,7},{7,5},{8,10},{10,8},{9,1... | collective-permute-start | bytes 208904 | tf_op jit(solution)/shard_map/pair_sums/ppermute | solution.py:8
  46.0 4.5 %collective-permute-start.14 = (f32[8,128]{1,0:T(8,128)S(1)}, f32[8,128]{1,0:T(8,128)S(1)}, u32[]{:S(2)}, u32[]{:S(2)}) collective-permute-start(f32[8,128]{1,0:T(8,128)S(1)} %add_bitcast_fusion), channel_id=1, source_target_pairs={{0,8},{4,12},{8,0},{12,4},{1,9},{5,13},{9,1},{13,5},{2,10},{6,14},... | collective-permute-start | bytes 12296 | tf_op jit(solution)/shard_map/pair_sums/ppermute | solution.py:8
